TPU v7x, 32 devices: a whole 2x2x4 slice. The times are simulated.
32 devices in a mesh: tm: 16 (over z, x, core), doc: 2 (over y).
Axes of the slice: x: 2, y: 2, z: 4, core: 2. Of those that a mesh axis runs over, the one named last changes fastest.
Arguments:
- beta: float32 [16, 4096, 128], P('tm', 'doc'), may hold values from -6 to 260
- word_ids: int32 [16, 8, 128], P('tm', 'doc'), may hold values from 0 to 4095
- word_counts: int32 [16, 8, 128], P('tm', 'doc'), may hold values from 1 to 8
- block_slot: int32 [32], replicated, may hold values from 0 to 31, each once
- topic_prior: float32 [128], replicated, may hold values from 0.05 to 0.5
- drift_var: float32 [128], replicated, may hold values from 0.0005 to 0.05
- obs_precision: float32 [16, 128], replicated, may hold values from 0.01 to 4
Outputs:
- smoothed_means: float32 [16, 4096, 128], P('tm', 'doc')
- doc_topics: float32 [16, 8, 128], P('tm', 'doc')
Inputs may be any that keep to these rules, and one draw needn't show every extreme that they name: `block_slot`: each block has its own position.
All inputs are finite; a program needn't handle non-finite values.
Results may differ from a plain program's by a relative error of at most 0.0012.
The roundings to bfloat16 on the way count: a program that leaves them out, or rounds other values in their place, can miss the bound.
Values may be sent and summed in bfloat16 or wider, within the bound.
No kernel may reach another device: no remote copies, remote signals or barrier semaphores. Data moves between devices by JAX's collectives and lax.ppermute only.
A program may use at most 192 MiB of HBM per device.

v0:
```python
import jax
import jax.numpy as jnp
from jax import lax
from jax.sharding import PartitionSpec as P

K = 128
BLOCK = 128
EITERS = 4


init_variance = 4.0


def joined(value, axis, combine):
    everything = jax.tree.map(lambda part: lax.all_gather(part, axis), value)
    initial = jax.tree.map(lambda part: part[0], everything)

    def step(k, so_far):
        return combine(so_far, jax.tree.map(lambda part: part[k], everything))

    return lax.fori_loop(1, lax.axis_size(axis), step, initial)


def entering(part, axis, combine, identity, reverse):
    count = lax.axis_size(axis)
    place = lax.axis_index(axis)
    ahead = count - 1 - place if reverse else place
    gathered = jax.tree.map(lambda a: lax.all_gather(a, axis), part)
    state = jax.tree.map(lambda a, e: jnp.zeros_like(a) + jnp.asarray(e, a.dtype), part, identity)

    def one(step, state):
        source = count - 1 - step if reverse else step
        return combine(
            state, jax.tree.map(lambda a: lax.dynamic_index_in_dim(a, source, 0, False), gathered)
        )

    return lax.fori_loop(0, ahead, one, state)


def variance_tables(obs_precision, drift_var):

    def forward_step(prior_var, precision):
        denominator = 1.0 + prior_var * precision
        gain_now = prior_var * precision / denominator
        filt_var = prior_var / denominator
        return (filt_var + drift_var, (gain_now, filt_var))

    start_var = jnp.full(drift_var.shape, init_variance, dtype=jnp.float32)
    last_var, (gains, filt_vars) = lax.scan(forward_step, start_var, obs_precision)

    def backward_step(info_next, precision):
        merged = info_next + precision
        shrink = 1.0 / (1.0 + drift_var * merged)
        info_now = merged * shrink
        return (info_now, (shrink, info_now))

    zero_info = jnp.zeros(drift_var.shape, dtype=jnp.float32)
    last_info, (shrinks, infos) = lax.scan(
        backward_step, zero_info, obs_precision[1:], reverse=True
    )
    shrinks = jnp.concatenate([shrinks, jnp.ones_like(zero_info)[None]], axis=0)
    infos = jnp.concatenate([infos, zero_info[None]], axis=0)
    return (gains, filt_vars, shrinks, infos)


def e_step(looked, word_counts, topic_prior):
    counts_float = word_counts.astype(jnp.float32)
    doc_topics = topic_prior + jnp.sum(counts_float, axis=-1, keepdims=True) / K
    scores = looked.astype(jnp.float32)
    for sweep in range(EITERS):
        resp = jax.nn.softmax(lax.digamma(doc_topics)[..., None, :] + scores, axis=-1)
        doc_topics = topic_prior + jnp.sum(counts_float[..., None] * resp, axis=-2)
    weighted = (counts_float[..., None] * resp).astype(jnp.bfloat16)
    return (doc_topics, weighted)


def combine_normalizer(first_part, second_part):
    peak_value = jnp.maximum(first_part[0], second_part[0])
    summed = first_part[1] * jnp.exp(first_part[0] - peak_value) + second_part[1] * jnp.exp(
        second_part[0] - peak_value
    )
    return (peak_value, summed)


def compose_maps(earlier, later):
    return (later[0] * earlier[0], later[0] * earlier[1] + later[1])


def pick_year(table_all, year_index):
    return lax.dynamic_index_in_dim(table_all, year_index, 0, keepdims=False)


def body(beta, word_ids, word_counts, block_slot, topic_prior, drift_var, obs_precision):
    local_beta = beta[0]
    own_words = local_beta.shape[0]
    topics = local_beta.shape[1]
    local_peak = jnp.max(local_beta, axis=0)
    local_total = jnp.sum(jnp.exp(local_beta - local_peak), axis=0)
    peak_value, total_value = joined((local_peak, local_total), "doc", combine_normalizer)
    table = (local_beta - (peak_value + jnp.log(total_value))).astype(jnp.bfloat16)
    slot_ids = word_ids[0]
    doc_count = slot_ids.shape[0]
    slot_width = slot_ids.shape[1]
    block_count = block_slot.shape[0]
    block_of = slot_ids // BLOCK
    block_match = block_of[..., None] == lax.iota(jnp.int32, block_count)
    columns = jnp.sum(jnp.where(block_match, block_slot, 0), axis=-1) * BLOCK + slot_ids % BLOCK
    flat_columns = columns.reshape(-1)
    slot_total = flat_columns.shape[0]
    piece = lax.all_gather(table, "doc", axis=0, tiled=True)
    inside = (flat_columns >= 0) & (flat_columns < piece.shape[0])
    picked = jnp.take(piece, jnp.clip(flat_columns, 0, piece.shape[0] - 1), axis=0)
    looked = jnp.where(inside[:, None], picked, jnp.zeros_like(picked)).reshape(
        doc_count, slot_width, topics
    )
    doc_topics, weighted = e_step(looked, word_counts[0], topic_prior)
    flat_weighted = weighted.reshape(slot_total, topics)
    row_words = lax.iota(jnp.int32, own_words * lax.axis_size("doc"))
    marks = (row_words[:, None] == flat_columns[None, :]).astype(jnp.bfloat16)
    counts = lax.psum_scatter(
        jnp.dot(marks, flat_weighted, preferred_element_type=jnp.float32).astype(jnp.bfloat16),
        "doc",
        scatter_dimension=0,
        tiled=True,
    ).astype(jnp.float32)
    pseudo = local_beta + jnp.log1p(counts)
    gains, filt_vars, shrinks, infos = variance_tables(obs_precision, drift_var)
    year_index = lax.axis_index("tm")
    years_total = obs_precision.shape[0]
    gain_now = pick_year(gains, year_index)
    filt_now = pick_year(filt_vars, year_index)
    keep_part = 1.0 - gain_now
    push_part = gain_now * pseudo
    identity_map = (jnp.ones_like(keep_part), jnp.zeros_like(push_part))
    before = entering((keep_part, push_part), "tm", compose_maps, identity_map, False)
    filtered = keep_part * before[1] + push_part
    pull_now = jnp.where(year_index == years_total - 1, 0.0, filt_now / (filt_now + drift_var))
    own_term = (1.0 - pull_now) * filtered
    after = entering((pull_now, own_term), "tm", compose_maps, identity_map, True)
    smoothed = pull_now * after[1] + own_term
    return (smoothed[None], doc_topics[None])


def solution(mesh):
    in_specs = (
        P("tm", "doc", None),
        P("tm", "doc", None),
        P("tm", "doc", None),
        P(),
        P(),
        P(),
        P(),
    )
    out_specs = (P("tm", "doc", None), P("tm", "doc", None))
    return jax.shard_map(body, mesh=mesh, in_specs=in_specs, out_specs=out_specs, check_vma=False)
```

profile of v0, /device:TPU:0, one launch (start us, length us, event | category | flops | bytes accessed | tf_op | source)
XLA Modules:
  0.0 387.6 jit_solution(6193052944169842220)
XLA Ops:
  7.2 1.6 reduce_max.53
  8.8 1.5 fusion.5
  10.3 5.2 %all-gather.8 = f32[2,1,128]{2,1,0:T(1,128)S(1)} all-gather(f32[1,1,128]{2,1,0:T(1,128)S(1)} %bitcast.211), channel_id=4, replica_groups=mesh['tm'=16,'doc'=2] {'doc'}, dimensions={0}, use_global_device_ids=true | all-gather | bytes 1536 | tf_op jit(solution)/shard_map/all_gather | solution.py:15
  15.5 4.2 %all-gather.7 = f32[2,1,128]{2,1,0:T(1,128)S(1)} all-gather(f32[1,1,128]{2,1,0:T(1,128)S(1)} %bitcast.210), channel_id=3, replica_groups=mesh['tm'=16,'doc'=2] {'doc'}, dimensions={0}, use_global_device_ids=true | all-gather | bytes 1536 | tf_op jit(solution)/shard_map/all_gather | solution.py:15
  19.8 2.1 fusion.6
  21.9 0.7 add_select_fusion.2
  22.6 0.7 select_reduce_fusion
  23.4 0.7 compare_and_fusion.3
  24.1 0.8 convert_reduce_fusion
  24.9 0.7 compare_select_fusion
  25.6 0.7 compare_and_fusion.1
  26.4 0.8 select_select_fusion.5
  27.1 0.7 convert_bitcast_fusion.1
  27.8 17.2 %all-gather.13.cloned.1.call-done = bf16[4096,128]{1,0:T(8,128)(2,1)} async-done(((bf16[2048,128]{1,0:T(8,128)(2,1)}), bf16[4096,128]{1,0:T(8,128)(2,1)}) %all-gather.13.cloned.1.call-update) | async-done | bytes 1048592 | tf_op jit(solution)/shard_map/all_gather | solution.py:110
  45.1 2.4 gather_fusion
  48.0 0.4 fusion.48
  48.5 0.7 select_select_fusion.4
  49.6 0.4 fusion.47
  50.0 0.7 select_select_fusion.3
  51.5 0.7 select_select_fusion.2
  53.1 2.4 fusion.2
  55.6 12.5 %while.49 = (s32[]{:T(128)}, f32[128]{0:T(128)S(1)}, f32[16,128]{1,0:T(8,128)S(1)}, f32[16,128]{1,0:T(8,128)S(1)}, f32[16,128]{1,0:T(8,128)}, /*index=5*/f32[128]{0:T(128)S(1)}, s32[]{:T(128)}, s32[]{:T(128)}) while((s32[]{:T(128)}, f32[128]{0:T(128)S(1)}, f32[16,128]{1,0:T(8,128)S(1)}, f32[16,128]{1,0:T(8,128)S(1)}, ...), condition=%wide.region_1.0_spmd.clone, body=%wide.region_0.0_spmd.clone.sunk | while | flops 771 | bytes 5235 | solution.py:49
  55.6 0.7 fusion.79
  56.3 0.7 fusion.79
  57.1 0.7 fusion.79
  57.9 0.7 fusion.79
  58.7 0.7 fusion.79
  59.5 0.7 fusion.79
  60.2 0.7 fusion.79
  61.0 0.7 fusion.79
  61.8 0.7 fusion.79
  62.6 0.7 fusion.79
  63.4 0.7 fusion.79
  64.2 0.7 fusion.79
  64.9 0.7 fusion.79
  65.7 0.7 fusion.79
  66.5 0.7 fusion.79
  67.3 0.7 fusion.79
  68.1 7.9 %reduce-scatter.2.cloned.1.call-done = bf16[2048,128]{1,0:T(8,128)(2,1)} async-done(((bf16[4096,128]{1,0:T(8,128)(2,1)}), bf16[2048,128]{1,0:T(8,128)(2,1)}) %reduce-scatter.2.cloned.1.call-update) | async-done | bytes 524304 | tf_op jit(solution)/shard_map/reduce_scatter | solution.py:120
  76.0 2.4 fusion.7
  78.5 21.7 %all-gather.6 = f32[16,1,128]{2,1,0:T(1,128)S(1)} all-gather(f32[1,1,128]{2,1,0:T(1,128)S(1)} %get-tuple-element.251), channel_id=1, replica_groups=mesh['tm'=16,'doc'=2] {'tm'}, dimensions={0}, use_global_device_ids=true | all-gather | bytes 8704 | tf_op jit(solution)/shard_map/all_gather | solution.py:28
  100.3 105.0 %all-gather.15.cloned.1.call-done = f32[32768,128]{1,0:T(8,128)} async-done(((f32[2048,128]{1,0:T(8,128)}), f32[32768,128]{1,0:T(8,128)}) %all-gather.15.cloned.1.call-update) | async-done | bytes 16777232 | tf_op jit(solution)/shard_map/all_gather | solution.py:28
  205.4 1.1 copy-done.2
  206.5 1.1 add_multiply_fusion
  207.6 40.6 %all-gather.5 = f32[16,1,128]{2,1,0:T(1,128)S(1)} all-gather(f32[1,1,128]{2,1,0:T(1,128)S(1)} %bitcast.209), channel_id=2, replica_groups=mesh['tm'=16,'doc'=2] {'tm'}, dimensions={0}, use_global_device_ids=true | all-gather | bytes 8704 | tf_op jit(solution)/shard_map/all_gather | solution.py:28
  248.6 0.6 bitcast_add_fusion.4
  249.2 106.2 %all-gather.17.cloned.1.call-done = f32[32768,128]{1,0:T(8,128)} async-done(((f32[2048,128]{1,0:T(8,128)}), f32[32768,128]{1,0:T(8,128)}) %all-gather.17.cloned.1.call-update) | async-done | bytes 16777232 | tf_op jit(solution)/shard_map/all_gather | solution.py:28
  355.5 24.4 %while.48 = (s32[]{:T(128)}, f32[2048,128]{1,0:T(8,128)S(1)}, s32[]{:T(128)}, f32[16,128]{1,0:T(8,128)S(1)}, f32[16,2048,128]{2,1,0:T(8,128)}, /*index=5*/s32[]{:T(128)}, s32[]{:T(128)}, s32[]{:T(128)}, s32[]{:T(128)}) while((s32[]{:T(128)}, f32[2048,128]{1,0:T(8,128)S(1)}, s32[]{:T(128)}, f32[16,128]{1,0:T(8,128)S(1)}, ...), condition=%wide.region_21.22_spmd, body=%wide.region_20.21_spmd.sunk | while | flops 524294 | bytes 3147419 | solution.py:37
  355.6 1.7 bitcast_add_fusion.8
  357.3 1.6 bitcast_add_fusion.8
  358.9 1.6 bitcast_add_fusion.8
  360.5 1.6 bitcast_add_fusion.8
  362.1 1.6 bitcast_add_fusion.8
  363.8 1.6 bitcast_add_fusion.8
  365.4 1.6 bitcast_add_fusion.8
  367.0 1.6 bitcast_add_fusion.8
  368.6 1.6 bitcast_add_fusion.8
  370.3 1.6 bitcast_add_fusion.8
  371.9 1.6 bitcast_add_fusion.8
  373.5 1.6 bitcast_add_fusion.8
  375.1 1.6 bitcast_add_fusion.8
  376.8 1.6 bitcast_add_fusion.8
  378.4 1.6 bitcast_add_fusion.8
  380.0 1.1 add_bitcast_fusion
  (90 shorter events, 4.5 us)
Async XLA Ops:
  7.2 68.9 %copy-start = (f32[1,2048,128]{2,1,0:T(8,128)S(1)}, f32[1,2048,128]{2,1,0:T(8,128)}, u32[]{:S(2)}) copy-start(f32[1,2048,128]{2,1,0:T(8,128)} %param.13) | copy-start | bytes 3145732
  7.2 48.4 %copy-start.3 = (f32[128]{0:T(128)S(1)}, f32[128]{0:T(128)}, u32[]{:S(2)}) copy-start(f32[128]{0:T(128)} %param.18) | copy-start | bytes 1540
  7.2 37.9 %all-gather.13.cloned.1.call-start = ((), (), s32[]{:S(2)}) async-start(), calls=%async_computation.1 | async-start | bytes 1572864 | tf_op jit(solution)/shard_map/all_gather | solution.py:110
  21.9 54.2 %reduce-scatter.2.cloned.1.call-start = ((), (), s32[]{:S(2)}) async-start(), calls=%async_computation.2 | async-start | bytes 1572864 | tf_op jit(solution)/shard_map/reduce_scatter | solution.py:120
  55.5 149.8 %all-gather.15.cloned.1.call-start = ((), (), s32[]{:S(2)}) async-start(), calls=%async_computation.3 | async-start | bytes 17825792 | tf_op jit(solution)/shard_map/all_gather | solution.py:28
  78.5 277.0 %all-gather.17.cloned.1.call-start = ((), (), s32[]{:S(2)}) async-start(), calls=%async_computation.4 | async-start | bytes 17825792 | tf_op jit(solution)/shard_map/all_gather | solution.py:28
  205.3 1.2 copy-start.2
  205.3 43.3 %copy-start.4 = (f32[128]{0:T(128)S(1)}, f32[128]{0:T(128)}, u32[]{:S(2)}) copy-start(f32[128]{0:T(128)} %param.17) | copy-start | bytes 1540
  355.5 24.5 %copy-start.1 = (f32[2048,128]{1,0:T(8,128)S(1)}, f32[2048,128]{1,0:T(8,128)}, u32[]{:S(2)}) copy-start(f32[2048,128]{1,0:T(8,128)} %add_multiply_fusion) | copy-start | bytes 3145732
Sparse Core Ops, SparseCore 0:
  22.0 23.0 all-gather.12
  55.6 20.3 reduce-scatter.1
  78.8 126.4 all-gather.14
  207.9 147.5 all-gather.16
where the time goes:
time: 389 us; the launch traced here: 388 us
  waiting for transfers between devices  236 us (61%)
  blocking collectives  71.7 us (18%)
  other arithmetic  57.4 us (15%)
  between operations  14 us (4%)
  local copies, waits for them, and re-layouts  4.73 us (1%)
    all_gather x2, waiting for transfers between devices, entering(): gathered = jax.tree.map(lambda a: lax.all_gather(a, axis), part)  211 us
    all_gather x2, blocking collectives, entering(): gathered = jax.tree.map(lambda a: lax.all_gather(a, axis), part)  62.3 us
    add x15, other arithmetic, compose_maps(): return (later[0] * earlier[0], later[0] * earlier[1] + later[1])  23.9 us
    all_gather x1, waiting for transfers between devices, body(): piece = lax.all_gather(table, 'doc', axis=0, tiled=True)  17.2 us
    add x16, other arithmetic, forward_step(): return (filt_var + drift_var, (gain_now, filt_var))  11.3 us
    all_gather x2, blocking collectives, joined(): everything = jax.tree.map(lambda part: lax.all_gather(part, axis), value)  9.41 us
    reduce_scatter x1, waiting for transfers between devices, body(): lax.psum_scatter(jnp.dot(marks, flat_weighted, preferred_element_type=jnp...  7.95 us
  transfers between devices with their start and end apart: 4, of which 4 were waited for; matrix products, arithmetic and copies ran while one was open for 5% of the time, Pallas kernels for 0%

commit v1 on v0

v1 whole, which is shorter than its diff:
```python
import jax
import jax.numpy as jnp
from jax import lax
from jax.sharding import PartitionSpec as P

K = 128
BLOCK = 128
EITERS = 4


init_variance = 4.0


def variance_tables(obs_precision, drift_var):

    def forward_step(prior_var, precision):
        denominator = 1.0 + prior_var * precision
        gain_now = prior_var * precision / denominator
        filt_var = prior_var / denominator
        return (filt_var + drift_var, (gain_now, filt_var))

    start_var = jnp.full(drift_var.shape, init_variance, dtype=jnp.float32)
    last_var, (gains, filt_vars) = lax.scan(forward_step, start_var, obs_precision)

    def backward_step(info_next, precision):
        merged = info_next + precision
        shrink = 1.0 / (1.0 + drift_var * merged)
        info_now = merged * shrink
        return (info_now, (shrink, info_now))

    zero_info = jnp.zeros(drift_var.shape, dtype=jnp.float32)
    last_info, (shrinks, infos) = lax.scan(
        backward_step, zero_info, obs_precision[1:], reverse=True
    )
    shrinks = jnp.concatenate([shrinks, jnp.ones_like(zero_info)[None]], axis=0)
    infos = jnp.concatenate([infos, zero_info[None]], axis=0)
    return (gains, filt_vars, shrinks, infos)


def e_step(looked, word_counts, topic_prior):
    counts_float = word_counts.astype(jnp.float32)
    doc_topics = topic_prior + jnp.sum(counts_float, axis=-1, keepdims=True) / K
    scores = looked.astype(jnp.float32)
    for sweep in range(EITERS):
        resp = jax.nn.softmax(lax.digamma(doc_topics)[..., None, :] + scores, axis=-1)
        doc_topics = topic_prior + jnp.sum(counts_float[..., None] * resp, axis=-2)
    weighted = (counts_float[..., None] * resp).astype(jnp.bfloat16)
    return (doc_topics, weighted)


def body(beta, word_ids, word_counts, block_slot, topic_prior, drift_var, obs_precision):
    local_beta = beta[0]
    own_words = local_beta.shape[0]
    topics = local_beta.shape[1]
    doc_devices = lax.axis_size("doc")
    doc_place = lax.axis_index("doc")
    local_peak = jnp.max(local_beta, axis=0)
    local_total = jnp.sum(jnp.exp(local_beta - local_peak), axis=0)

    slot_ids = word_ids[0]
    local_docs = slot_ids.shape[0]
    slot_width = slot_ids.shape[1]
    columns = jnp.take(block_slot, slot_ids // BLOCK) * BLOCK + slot_ids % BLOCK

    all_columns = lax.all_gather(columns, "doc", axis=0, tiled=True)
    all_counts = lax.all_gather(word_counts[0], "doc", axis=0, tiled=True)
    peaks = lax.all_gather(local_peak, "doc")
    totals = lax.all_gather(local_total, "doc")
    peak_value = jnp.max(peaks, axis=0)
    total_value = jnp.sum(totals * jnp.exp(peaks - peak_value), axis=0)
    normalizer = peak_value + jnp.log(total_value)

    flat_columns = all_columns.reshape(-1)
    local_columns = flat_columns - doc_place * own_words
    inside = (local_columns >= 0) & (local_columns < own_words)
    picked = jnp.take(local_beta, jnp.clip(local_columns, 0, own_words - 1), axis=0)
    partial = jnp.where(
        inside[:, None], (picked - normalizer).astype(jnp.bfloat16), jnp.zeros((), jnp.bfloat16)
    )
    looked = lax.psum(partial, "doc").reshape(local_docs * doc_devices, slot_width, topics)

    doc_topics_all, weighted = e_step(looked, all_counts, topic_prior)
    doc_topics = lax.dynamic_slice_in_dim(doc_topics_all, doc_place * local_docs, local_docs, 0)

    flat_weighted = weighted.reshape(-1, topics)
    row_words = lax.iota(jnp.int32, own_words)
    marks = (row_words[:, None] == local_columns[None, :]).astype(jnp.bfloat16)
    counts = jnp.dot(marks, flat_weighted, preferred_element_type=jnp.float32)
    pseudo = local_beta + jnp.log1p(counts)

    gains, filt_vars, shrinks, infos = variance_tables(obs_precision, drift_var)
    years_total = obs_precision.shape[0]
    pulls = filt_vars / (filt_vars + drift_var)
    pulls = pulls.at[-1].set(0.0)

    years = lax.axis_size("tm")
    chunk = own_words // years
    by_year = lax.all_to_all(
        pseudo.reshape(years, chunk, topics), "tm", split_axis=0, concat_axis=0, tiled=True
    )

    def filter_step(mean_prev, inputs):
        gain_now, pseudo_now = inputs
        mean_now = (1.0 - gain_now) * mean_prev + gain_now * pseudo_now
        return mean_now, mean_now

    zero_mean = jnp.zeros((chunk, topics), dtype=jnp.float32)
    last_mean, filtered = lax.scan(filter_step, zero_mean, (gains[:, None, :], by_year), unroll=True)

    def smooth_step(mean_next, inputs):
        pull_now, filt_now = inputs
        mean_now = pull_now * mean_next + (1.0 - pull_now) * filt_now
        return mean_now, mean_now

    first_mean, smoothed = lax.scan(
        smooth_step, zero_mean, (pulls[:, None, :], filtered), reverse=True, unroll=True
    )
    back = lax.all_to_all(smoothed, "tm", split_axis=0, concat_axis=0, tiled=True)
    return (back.reshape(own_words, topics)[None], doc_topics[None])


def solution(mesh):
    in_specs = (
        P("tm", "doc", None),
        P("tm", "doc", None),
        P("tm", "doc", None),
        P(),
        P(),
        P(),
        P(),
    )
    out_specs = (P("tm", "doc", None), P("tm", "doc", None))
    return jax.shard_map(body, mesh=mesh, in_specs=in_specs, out_specs=out_specs, check_vma=False)
```

time: 389 us -> 146 us (0.38)
  waiting for transfers between devices: 236 us -> 52.6 us
  blocking collectives: 71.7 us -> 18.1 us
  other arithmetic: 57.4 us -> 29.6 us
  starting transfers between devices: 0.16 us -> 12.6 us
  local copies, waits for them, and re-layouts: 4.73 us -> 13.1 us
    all_gather x3 -> x0, waiting for transfers between devices: 228 us -> none  [the longest x2 211 us: entering(): gathered = jax.tree.map(lambda a: lax.all_gather(a, axis), part)]
    all_gather x4, blocking collectives: 71.7 us -> 18.1 us  [the longest x1 5.18 us: body(): totals = lax.all_gather(local_total, 'doc')]
    all_to_all x0 -> x2, waiting for transfers between devices: none -> 32 us  [the longest x1 21.8 us: body(): lax.all_to_all(smoothed, 'tm', split_axis=0, concat_axis=0, tiled=True)]
    add x15 -> x1, other arithmetic: 23.9 us -> 0.01 us  [body(): normalizer = peak_value + jnp.log(total_value)]
    psum x0 -> x1, waiting for transfers between devices: none -> 20.5 us  [body(): lax.psum(partial, 'doc')]
    all_to_all x0 -> x2, starting transfers between devices: none -> 12.5 us  [the longest x1 6.79 us: body(): lax.all_to_all(smoothed, 'tm', split_axis=0, concat_axis=0, tiled=True)]
    reduce_scatter x1 -> x0, waiting for transfers between devices: 7.95 us -> none  [body(): lax.psum_scatter(jnp.dot(marks, flat_weighted, preferred_element_type=jnp...]
    unnamed x1 -> x10, other arithmetic: 0.01 us -> 5.43 us
  transfers between devices with their start and end apart: 4 -> 3, of which waited for: 4 -> 3; matrix products, arithmetic and copies ran while one was open for 5% -> 10% of each run, Pallas kernels for 0% -> 0%
where the time goes in v1:
time: 146 us; the launch traced here: 143 us
  waiting for transfers between devices  52.6 us (36%)
  other arithmetic  29.6 us (20%)
  blocking collectives  18.1 us (12%)
  between operations  14.4 us (10%)
  local copies, waits for them, and re-layouts  13.1 us (9%)
  starting transfers between devices  12.6 us (9%)
  matrix products  2.76 us (2%)
    all_to_all x1, waiting for transfers between devices, body(): lax.all_to_all(smoothed, 'tm', split_axis=0, concat_axis=0, tiled=True)  21.8 us
    psum x1, waiting for transfers between devices, body(): lax.psum(partial, 'doc')  20.5 us
    add x16, other arithmetic, forward_step(): return (filt_var + drift_var, (gain_now, filt_var))  11.4 us
    all_to_all x1, waiting for transfers between devices, body(): lax.all_to_all(pseudo.reshape(years, chunk, topics), 'tm', split_axis=0,...  10.3 us
    all_to_all x1, starting transfers between devices, body(): lax.all_to_all(smoothed, 'tm', split_axis=0, concat_axis=0, tiled=True)  6.79 us
    all_to_all x1, starting transfers between devices, body(): lax.all_to_all(pseudo.reshape(years, chunk, topics), 'tm', split_axis=0,...  5.75 us
    unnamed x22, local copies, waits for them, and re-layouts  5.44 us
    unnamed x10, other arithmetic  5.43 us
  transfers between devices with their start and end apart: 3, of which 3 were waited for; matrix products, arithmetic and copies ran while one was open for 10% of the time, Pallas kernels for 0%

profile of v1, /device:TPU:0, one launch (start us, length us, event | category | flops | bytes accessed | tf_op | source)
XLA Modules:
  0.0 143.4 jit_solution(16217126004983186146)
XLA Ops:
  7.2 1.6 %reduce_max.54 = f32[128]{0:T(128)S(1)} reduce(f32[1,2048,128]{2,1,0:T(8,128)} %param.11, f32[]{:T(128)} %constant.154.clone.1), dimensions={0,1}, to_apply=%region_3.4 | reduce | flops 262016 | bytes 1049092 | tf_op jit(solution)/shard_map/reduce_max | solution.py:57
  8.8 0.3 exponential_reduce_fusion
  9.1 5.2 %all-gather.5 = f32[2,1,128]{2,1,0:T(1,128)S(1)} all-gather(f32[1,1,128]{2,1,0:T(1,128)S(1)} %bitcast.281), channel_id=4, replica_groups=mesh['tm'=16,'doc'=2] {'doc'}, dimensions={0}, use_global_device_ids=true | all-gather | bytes 1536 | tf_op jit(solution)/shard_map/all_gather | solution.py:68
  14.3 4.2 %all-gather.4 = f32[2,1,128]{2,1,0:T(1,128)S(1)} all-gather(f32[1,1,128]{2,1,0:T(1,128)S(1)} %bitcast.278), channel_id=3, replica_groups=mesh['tm'=16,'doc'=2] {'doc'}, dimensions={0}, use_global_device_ids=true | all-gather | bytes 1536 | tf_op jit(solution)/shard_map/all_gather | solution.py:67
  18.6 3.3 %gather_fusion = s32[512]{0:T(512)S(1)} fusion(s32[32]{0:T(128)S(1)} %copy-done, s32[1024]{0:T(1024)S(1)} %pad_clamp_fusion), kind=kCustom, calls=%fused_computation | custom fusion | bytes 6144 | tf_op jit(solution)/shard_map/jit(_take)/gather | solution.py:63
  22.0 4.4 %all-gather.3 = s32[2,4,128]{2,1,0:T(4,128)S(1)} all-gather(s32[1,4,128]{2,1,0:T(4,128)S(1)} %fusion.120), channel_id=1, replica_groups=mesh['tm'=16,'doc'=2] {'doc'}, dimensions={0}, use_global_device_ids=true | all-gather | bytes 6144 | tf_op jit(solution)/shard_map/all_gather | solution.py:65
  26.4 2.8 %gather_fusion.1 = f32[1024,128]{1,0:T(8,128)S(1)} fusion(f32[2048,128]{1,0:T(8,128)S(1)} %bitcast.257, s32[1024]{0:T(1024)S(1)} %broadcast_clamp_fusion), kind=kCustom, calls=%fused_computation.1 | custom fusion | bytes 1052672 | tf_op jit(solution)/shard_map/jit(_take)/gather | solution.py:76
  29.3 1.0 fusion.24
  30.4 4.4 %all-gather = s32[1,8,128]{2,0,1:T(1,128)S(1)} all-gather(s32[1,4,128]{2,0,1:T(1,128)S(1)} %bitcast.279), channel_id=2, replica_groups=mesh['tm'=16,'doc'=2] {'doc'}, dimensions={1}, use_global_device_ids=true | all-gather | bytes 6144 | tf_op jit(solution)/shard_map/all_gather | solution.py:66
  34.7 0.1 convert_reduce_fusion
  35.0 20.5 %all-reduce.2.cloned.1.call-done = bf16[1024,128]{1,0:T(8,128)(2,1)} async-done(((bf16[1024,128]{1,0:T(8,128)(2,1)}), bf16[1024,128]{1,0:T(8,128)(2,1)}) %all-reduce.2.cloned.1.call-update) | async-done | bytes 262160 | tf_op jit(solution)/shard_map/psum | solution.py:80
  55.6 1.2 fusion.6
  56.8 1.3 fusion.23
  58.1 1.4 multiply_reduce_fusion.3
  59.6 1.2 fusion.8
  60.8 0.4 fusion.21
  61.2 0.5 multiply_reduce_fusion.2
  61.7 0.2 fusion.10
  62.0 0.4 fusion.19
  62.4 0.5 multiply_reduce_fusion.1
  62.9 0.2 fusion.12
  63.1 0.4 fusion.15
  63.5 0.5 fusion.17
  64.0 2.8 %fusion.4 = f32[2048,128]{1,0:T(8,128)} fusion(bf16[1024,128]{1,0:T(8,128)(2,1)S(1)} %fusion.17, s32[1024]{0:T(1024)S(1)} %bitcast.274, f32[1,2048,128]{2,1,0:T(8,128)S(1)} %copy-done.2), kind=kOutput, calls=%fused_computation.11 | convolution fusion | flops 539230208 | bytes 2363392 | tf_op jit(solution)/shard_map/dot_general | solution.py:88
  66.8 5.7 %all-to-all-start = ((f32[16,128,128]{2,1,0:T(8,128)}), f32[16,128,128]{2,1,0:T(8,128)S(1)}, u32[]{:S(2)}, u32[]{:S(2)}) async-start(f32[16,128,128]{2,1,0:T(8,128)} %bitcast.59), calls=%async_computation | async-start | bytes 2097152 | tf_op jit(solution)/shard_map/all_to_all | solution.py:98
  72.5 12.5 %while.16 = (s32[]{:T(128)}, f32[128]{0:T(128)S(1)}, f32[16,128]{1,0:T(8,128)S(1)}, f32[16,128]{1,0:T(8,128)S(1)}, f32[16,128]{1,0:T(8,128)}, /*index=5*/f32[128]{0:T(128)S(1)}, s32[]{:T(128)}, s32[]{:T(128)}) while((s32[]{:T(128)}, f32[128]{0:T(128)S(1)}, f32[16,128]{1,0:T(8,128)S(1)}, f32[16,128]{1,0:T(8,128)S(1)}, ...), condition=%wide.region_1.0_spmd.clone, body=%wide.region_0.0_spmd.clone.sunk | while | flops 771 | bytes 5235 | solution.py:23
  72.6 0.7 fusion.137
  73.3 0.7 fusion.137
  74.1 0.7 fusion.137
  74.9 0.7 fusion.137
  75.7 0.7 fusion.137
  76.5 0.7 fusion.137
  77.3 0.7 fusion.137
  78.0 0.7 fusion.137
  78.8 0.7 fusion.137
  79.6 0.7 fusion.137
  80.4 0.7 fusion.137
  81.2 0.7 fusion.137
  82.0 0.7 fusion.137
  82.7 0.7 fusion.137
  83.5 0.7 fusion.137
  84.3 0.7 fusion.137
  85.2 10.3 %all-to-all-done = f32[16,128,128]{2,1,0:T(8,128)S(1)} async-done(((f32[16,128,128]{2,1,0:T(8,128)}), f32[16,128,128]{2,1,0:T(8,128)S(1)}, u32[]{:S(2)}, u32[]{:S(2)}) %all-to-all-start) | async-done | bytes 1048608 | tf_op jit(solution)/shard_map/all_to_all | solution.py:98
  95.4 0.9 add_dynamic-update-slice_fusion
  96.4 0.6 constant_dynamic-update-slice_fusion.13
  97.0 0.6 constant_dynamic-update-slice_fusion.12
  97.6 0.6 constant_dynamic-update-slice_fusion.11
  98.3 0.6 constant_dynamic-update-slice_fusion.10
  98.9 0.6 constant_dynamic-update-slice_fusion.9
  99.6 0.6 constant_dynamic-update-slice_fusion.8
  100.2 0.6 constant_dynamic-update-slice_fusion.7
  100.8 0.6 constant_dynamic-update-slice_fusion.6
  101.5 0.6 constant_dynamic-update-slice_fusion.5
  102.1 0.6 constant_dynamic-update-slice_fusion.4
  102.7 0.6 constant_dynamic-update-slice_fusion.3
  103.4 0.6 constant_dynamic-update-slice_fusion.2
  104.0 0.6 constant_dynamic-update-slice_fusion.1
  104.6 0.6 constant_dynamic-update-slice_fusion
  105.3 0.6 fusion.41
  105.9 6.8 %all-to-all-start.1 = ((f32[16,128,128]{2,1,0:T(8,128)}), f32[16,128,128]{2,1,0:T(8,128)S(1)}, u32[]{:S(2)}, u32[]{:S(2)}) async-start(f32[16,128,128]{2,1,0:T(8,128)} %fusion.41), calls=%async_computation.1 | async-start | bytes 2097152 | tf_op jit(solution)/shard_map/all_to_all | solution.py:118
  112.7 0.5 multiply_reduce_fusion
  113.2 0.6 dynamic-slice_bitcast_fusion
  113.8 21.8 %all-to-all-done.1 = f32[16,128,128]{2,1,0:T(8,128)S(1)} async-done(((f32[16,128,128]{2,1,0:T(8,128)}), f32[16,128,128]{2,1,0:T(8,128)S(1)}, u32[]{:S(2)}, u32[]{:S(2)}) %all-to-all-start.1) | async-done | bytes 1048608 | tf_op jit(solution)/shard_map/all_to_all | solution.py:118
  135.6 1.0 copy.43
  (73 shorter events, 1.5 us)
Async XLA Ops:
  7.2 11.5 %copy-start = (s32[32]{0:T(128)S(1)}, s32[32]{0:T(128)}, u32[]{:S(2)}) copy-start(s32[32]{0:T(128)} %param.14) | copy-start | bytes 388
  7.2 1.7 %copy-start.2 = (f32[1,2048,128]{2,1,0:T(8,128)S(1)}, f32[1,2048,128]{2,1,0:T(8,128)}, u32[]{:S(2)}) copy-start(f32[1,2048,128]{2,1,0:T(8,128)} %param.11) | copy-start | bytes 3145732
  7.2 48.4 %all-reduce.2.cloned.1.call-start = ((), (), s32[]{:S(2)}) async-start(), calls=%async_computation.2 | async-start | bytes 524288 | tf_op jit(solution)/shard_map/psum | solution.py:80
  7.2 11.4 %copy-start.5 = (s32[1,4,128]{2,1,0:T(4,128)S(1)}, s32[1,4,128]{2,1,0:T(4,128)}, u32[]{:S(2)}) copy-start(s32[1,4,128]{2,1,0:T(4,128)} %param.12) | copy-start | bytes 6148
  29.3 1.1 copy-start.6
  29.3 5.6 %copy-start.4 = (f32[128]{0:T(128)S(1)}, f32[128]{0:T(128)}, u32[]{:S(2)}) copy-start(f32[128]{0:T(128)} %param.15) | copy-start | bytes 1540
  55.6 5.2 %copy-start.1 = (bf16[1024,128]{1,0:T(8,128)(2,1)S(1)}, bf16[1024,128]{1,0:T(8,128)(2,1)}, u32[]{:S(2)}) copy-start(bf16[1024,128]{1,0:T(8,128)(2,1)} %all-reduce.2.cloned.1.call-done) | copy-start | bytes 786436
  66.8 5.8 %copy-start.3 = (f32[128]{0:T(128)S(1)}, f32[128]{0:T(128)}, u32[]{:S(2)}) copy-start(f32[128]{0:T(128)} %param.16) | copy-start | bytes 1540
  66.8 28.6 %all-to-all-start = ((f32[16,128,128]{2,1,0:T(8,128)}), f32[16,128,128]{2,1,0:T(8,128)S(1)}, u32[]{:S(2)}, u32[]{:S(2)}) async-start(f32[16,128,128]{2,1,0:T(8,128)} %bitcast.59), calls=%async_computation | async-start | bytes 2097152 | tf_op jit(solution)/shard_map/all_to_all | solution.py:98
  105.9 29.7 %all-to-all-start.1 = ((f32[16,128,128]{2,1,0:T(8,128)}), f32[16,128,128]{2,1,0:T(8,128)S(1)}, u32[]{:S(2)}, u32[]{:S(2)}) async-start(f32[16,128,128]{2,1,0:T(8,128)} %fusion.41), calls=%async_computation.1 | async-start | bytes 2097152 | tf_op jit(solution)/shard_map/all_to_all | solution.py:118
Sparse Core Ops, SparseCore 0:
  30.5 25.0 all-reduce.1

commit v2 on v1

--- a/solution.py
+++ b/solution.py
@@ -1,6 +1,7 @@
 import jax
 import jax.numpy as jnp
 from jax import lax
+from jax.experimental import pallas as pl
 from jax.sharding import PartitionSpec as P
 
 K = 128
@@ -44,8 +45,31 @@
     for sweep in range(EITERS):
         resp = jax.nn.softmax(lax.digamma(doc_topics)[..., None, :] + scores, axis=-1)
         doc_topics = topic_prior + jnp.sum(counts_float[..., None] * resp, axis=-2)
-    weighted = (counts_float[..., None] * resp).astype(jnp.bfloat16)
+    weighted = to_bf16(counts_float[..., None] * resp)
     return (doc_topics, weighted)
+
+
+def to_bf16(value):
+    return lax.reduce_precision(value, exponent_bits=8, mantissa_bits=7).astype(jnp.bfloat16)
+
+
+def shift_doc(value, s):
+    count = lax.axis_size("doc")
+    return lax.ppermute(value, "doc", [(i, (i + s) % count) for i in range(count)])
+
+
+def kalman_kernel(gain_ref, pull_ref, pseudo_ref, out_ref):
+    years = pseudo_ref.shape[0]
+    mean = jnp.zeros(pseudo_ref.shape[1:], jnp.float32)
+    for t in range(years):
+        gain_now = gain_ref[pl.ds(t, 1), :]
+        mean = (1.0 - gain_now) * mean + gain_now * pseudo_ref[t]
+        out_ref[t] = mean
+    mean = jnp.zeros(pseudo_ref.shape[1:], jnp.float32)
+    for t in reversed(range(years)):
+        pull_now = pull_ref[pl.ds(t, 1), :]
+        mean = pull_now * mean + (1.0 - pull_now) * out_ref[t]
+        out_ref[t] = mean
 
 
 def body(beta, word_ids, word_counts, block_slot, topic_prior, drift_var, obs_precision):
@@ -62,10 +86,14 @@
     slot_width = slot_ids.shape[1]
     columns = jnp.take(block_slot, slot_ids // BLOCK) * BLOCK + slot_ids % BLOCK
 
-    all_columns = lax.all_gather(columns, "doc", axis=0, tiled=True)
-    all_counts = lax.all_gather(word_counts[0], "doc", axis=0, tiled=True)
-    peaks = lax.all_gather(local_peak, "doc")
-    totals = lax.all_gather(local_total, "doc")
+    ints = jnp.stack([columns, word_counts[0]])
+    stats = jnp.stack([local_peak, local_total])
+    ints_seen = [ints] + [shift_doc(ints, s) for s in range(1, doc_devices)]
+    stats_seen = jnp.stack([stats] + [shift_doc(stats, s) for s in range(1, doc_devices)])
+    all_columns = jnp.concatenate([part[0] for part in ints_seen], axis=0)
+    all_counts = jnp.concatenate([part[1] for part in ints_seen], axis=0)
+    peaks = stats_seen[:, 0]
+    totals = stats_seen[:, 1]
     peak_value = jnp.max(peaks, axis=0)
     total_value = jnp.sum(totals * jnp.exp(peaks - peak_value), axis=0)
     normalizer = peak_value + jnp.log(total_value)
@@ -75,12 +103,15 @@
     inside = (local_columns >= 0) & (local_columns < own_words)
     picked = jnp.take(local_beta, jnp.clip(local_columns, 0, own_words - 1), axis=0)
     partial = jnp.where(
-        inside[:, None], (picked - normalizer).astype(jnp.bfloat16), jnp.zeros((), jnp.bfloat16)
-    )
-    looked = lax.psum(partial, "doc").reshape(local_docs * doc_devices, slot_width, topics)
+        inside[:, None], to_bf16(picked - normalizer), jnp.zeros((), jnp.bfloat16)
+    ).reshape(doc_devices, local_docs * slot_width, topics)
+    looked = partial
+    for s in range(1, doc_devices):
+        looked = looked + jnp.roll(shift_doc(partial, s), s, axis=0)
+    looked = looked.reshape(local_docs * doc_devices, slot_width, topics)
 
     doc_topics_all, weighted = e_step(looked, all_counts, topic_prior)
-    doc_topics = lax.dynamic_slice_in_dim(doc_topics_all, doc_place * local_docs, local_docs, 0)
+    doc_topics = doc_topics_all[:local_docs]
 
     flat_weighted = weighted.reshape(-1, topics)
     row_words = lax.iota(jnp.int32, own_words)
@@ -99,22 +130,9 @@
         pseudo.reshape(years, chunk, topics), "tm", split_axis=0, concat_axis=0, tiled=True
     )
 
-    def filter_step(mean_prev, inputs):
-        gain_now, pseudo_now = inputs
-        mean_now = (1.0 - gain_now) * mean_prev + gain_now * pseudo_now
-        return mean_now, mean_now
-
-    zero_mean = jnp.zeros((chunk, topics), dtype=jnp.float32)
-    last_mean, filtered = lax.scan(filter_step, zero_mean, (gains[:, None, :], by_year), unroll=True)
-
-    def smooth_step(mean_next, inputs):
-        pull_now, filt_now = inputs
-        mean_now = pull_now * mean_next + (1.0 - pull_now) * filt_now
-        return mean_now, mean_now
-
-    first_mean, smoothed = lax.scan(
-        smooth_step, zero_mean, (pulls[:, None, :], filtered), reverse=True, unroll=True
-    )
+    smoothed = pl.pallas_call(
+        kalman_kernel, out_shape=jax.ShapeDtypeStruct(by_year.shape, jnp.float32)
+    )(gains, pulls, by_year)
     back = lax.all_to_all(smoothed, "tm", split_axis=0, concat_axis=0, tiled=True)
     return (back.reshape(own_words, topics)[None], doc_topics[None])
 

time: 146 us -> 106 us (0.73)
  blocking collectives: 18.1 us -> 0 us
  between operations: 14.4 us -> 0.99 us
  waiting for transfers between devices: 52.6 us -> 41.6 us
  starting transfers between devices: 12.6 us -> 16.1 us
  local copies, waits for them, and re-layouts: 13.1 us -> 9.71 us
  Pallas kernels: 0 us -> 2.47 us
    psum x1 -> x0, waiting for transfers between devices: 20.5 us -> none  [body(): lax.psum(partial, 'doc')]
    all_gather x4 -> x0, blocking collectives: 18.1 us -> none  [the longest x1 5.18 us: body(): totals = lax.all_gather(local_total, 'doc')]
    div x0 -> x3, other arithmetic: none -> 12 us  [e_step(): jax.nn.softmax(lax.digamma(doc_topics)[..., None, :] + scores, axis=-1)]
    ppermute x0 -> x3, waiting for transfers between devices: none -> 9.86 us  [shift_doc(): lax.ppermute(value, 'doc', [(i, (i + s) % count) for i in range(count)])]
    unnamed x10 -> x1, other arithmetic: 5.43 us -> 0.01 us
    unnamed x22 -> x17, local copies, waits for them, and re-layouts: 5.44 us -> 1.97 us
    ppermute x0 -> x3, starting transfers between devices: none -> 3.24 us  [shift_doc(): lax.ppermute(value, 'doc', [(i, (i + s) % count) for i in range(count)])]
    pallas_call x0 -> x1, Pallas kernels: none -> 2.47 us  [body(): pl.pallas_call(kalman_kernel, out_shape=jax.ShapeDtypeStruct(by_year.shap...]
  transfers between devices with their start and end apart: 3 -> 5, of which waited for: 3 -> 4; matrix products, arithmetic and copies ran while one was open for 10% -> 17% of each run, Pallas kernels for 0% -> 0%
where the time goes in v2:
time: 106 us; the launch traced here: 104 us
  waiting for transfers between devices  41.6 us (39%)
  other arithmetic  30.1 us (28%)
  starting transfers between devices  16.1 us (15%)
  local copies, waits for them, and re-layouts  9.71 us (9%)
  matrix products  2.76 us (3%)
  Pallas kernels  2.47 us (2%)
    all_to_all x1, waiting for transfers between devices, body(): lax.all_to_all(smoothed, 'tm', split_axis=0, concat_axis=0, tiled=True)  21.4 us
    div x3, other arithmetic, e_step(): jax.nn.softmax(lax.digamma(doc_topics)[..., None, :] + scores, axis=-1)  12 us
    add x16, other arithmetic, forward_step(): return (filt_var + drift_var, (gain_now, filt_var))  11.3 us
    all_to_all x1, waiting for transfers between devices, body(): lax.all_to_all(pseudo.reshape(years, chunk, topics), 'tm', split_axis=0,...  10.3 us
    ppermute x3, waiting for transfers between devices, shift_doc(): lax.ppermute(value, 'doc', [(i, (i + s) % count) for i in range(count)])  9.86 us
    all_to_all x1, starting transfers between devices, body(): lax.all_to_all(smoothed, 'tm', split_axis=0, concat_axis=0, tiled=True)  6.79 us
    all_to_all x1, starting transfers between devices, body(): lax.all_to_all(pseudo.reshape(years, chunk, topics), 'tm', split_axis=0,...  6.04 us
    gather x1, local copies, waits for them, and re-layouts, body(): columns = jnp.take(block_slot, slot_ids // BLOCK) * BLOCK + slot_ids % BLOCK  3.35 us
  transfers between devices with their start and end apart: 5, of which 4 were waited for; matrix products, arithmetic and copies ran while one was open for 17% of the time, Pallas kernels for 0%

profile of v2, /device:TPU:0, one launch (start us, length us, event | category | flops | bytes accessed | tf_op | source)
XLA Modules:
  0.0 104.0 jit_solution(13574735993315468097)
XLA Ops:
  0.6 0.0 copy-start
  0.6 0.0 copy-start.1
  0.7 0.0 copy-start.5
  0.7 1.6 %reduce_max.54 = f32[128]{0:T(128)S(1)} reduce(f32[1,2048,128]{2,1,0:T(8,128)} %param.11, f32[]{:T(128)} %constant.150.clone.1), dimensions={0,1}, to_apply=%region_3.4 | reduce | flops 262016 | bytes 1049092 | tf_op jit(solution)/shard_map/reduce_max | solution.py:81
  2.3 0.0 copy-done.1
  2.3 0.3 exponential_reduce_fusion
  2.6 3.1 %collective-permute-start.1 = (f32[2,128]{1,0:T(2,128)S(1)}, f32[2,128]{1,0:T(2,128)S(1)}, u32[]{:S(2)}, u32[]{:S(2)}) collective-permute-start(f32[2,128]{1,0:T(2,128)S(1)} %get-tuple-element.99), channel_id=1, source_target_pairs={{0,1},{1,0},{2,3},{3,2},{4,5},{5,4},{6,7},{7,6},{8,9},{9,8},{10,11... | collective-permute-start | bytes 3080 | tf_op jit(solution)/shard_map/ppermute | solution.py:58
  5.6 0.0 copy-done.5
  5.7 0.0 copy-done
  5.7 0.0 copy-start.4
  5.7 3.3 %gather_fusion = s32[512]{0:T(512)S(1)} fusion(s32[32]{0:T(128)S(1)} %copy-done, s32[1024]{0:T(1024)S(1)} %pad_clamp_fusion), kind=kCustom, calls=%fused_computation | custom fusion | bytes 6144 | tf_op jit(solution)/shard_map/jit(_take)/gather | solution.py:87
  9.1 0.0 copy-done.4
  9.1 0.1 collective-permute-start
  9.2 0.0 collective-permute-done.1
  9.3 3.4 %collective-permute-done = s32[2,4,128]{2,1,0:T(4,128)S(1)} collective-permute-done((s32[2,4,128]{2,1,0:T(4,128)S(1)}, s32[2,4,128]{2,1,0:T(4,128)S(1)}, u32[]{:S(2)}, u32[]{:S(2)}) %collective-permute-start) | collective-permute-done | bytes 4128 | tf_op jit(solution)/shard_map/ppermute | solution.py:58
  12.7 0.1 fusion.155
  13.0 0.0 copy-start.7
  13.0 2.8 %gather_fusion.1 = f32[1024,128]{1,0:T(8,128)S(1)} fusion(f32[2048,128]{1,0:T(8,128)S(1)} %bitcast.116, s32[1024]{0:T(1024)S(1)} %broadcast_clamp_fusion), kind=kCustom, calls=%fused_computation.1 | custom fusion | bytes 1052672 | tf_op jit(solution)/shard_map/jit(_take)/gather | solution.py:104
  15.8 0.3 fusion.52
  16.2 0.1 collective-permute-start.2
  16.3 0.0 copy-done.7
  16.3 0.1 fusion.65
  16.4 6.4 %collective-permute-done.2 = bf16[2,512,128]{2,1,0:T(8,128)(2,1)S(1)} collective-permute-done((bf16[2,512,128]{2,1,0:T(8,128)(2,1)S(1)}, bf16[2,512,128]{2,1,0:T(8,128)(2,1)S(1)}, u32[]{:S(2)}, u32[]{:S(2)}) %collective-permute-start.2) | collective-permute-done | bytes 262176 | tf_op jit(solution)/shard_map/ppermute | solution.py:58
  22.9 0.3 fusion.51
  23.3 0.5 fusion.15
  23.8 4.0 %fusion.161 = f32[8,128]{1,0:T(8,128)S(1)} fusion(bf16[8,128,128]{2,1,0:T(8,128)(2,1)S(1)} %get-tuple-element.87, f32[8,128]{1,0:T(8,128)S(1)} %get-tuple-element.86, f32[8,128]{1,0:T(8,128)S(1)} %fusion.65, bf16[8,128,128]{2,1,0:T(8,128)(2,1)S(1)} %fusion.51, f32[8,128]{1,0:T(8,128)S(1)} %add_convert_fusion.1), kind=kOutput, calls=%fused_computation.245 | output fusion | flops 1179775 | bytes 540672 | tf_op jit(solution)/shard_map/div | solution.py:46
  27.8 0.1 fusion.67
  27.8 0.2 fusion.17
  28.1 4.0 %fusion.162 = f32[8,128]{1,0:T(8,128)S(1)} fusion(bf16[8,128,128]{2,1,0:T(8,128)(2,1)S(1)} %get-tuple-element.87, f32[8,128]{1,0:T(8,128)S(1)} %fusion.17, f32[8,128]{1,0:T(8,128)S(1)} %fusion.67, bf16[8,128,128]{2,1,0:T(8,128)(2,1)S(1)} %fusion.51, f32[8,128]{1,0:T(8,128)S(1)} %add_convert_fusion.1), kind=kOutput, calls=%fused_computation.246 | output fusion | flops 1179775 | bytes 540672 | tf_op jit(solution)/shard_map/div | solution.py:46
  32.1 0.1 fusion.69
  32.1 0.2 fusion.19
  32.4 4.0 %fusion.163 = f32[8,128]{1,0:T(8,128)S(1)} fusion(bf16[8,128,128]{2,1,0:T(8,128)(2,1)S(1)} %get-tuple-element.87, f32[8,128]{1,0:T(8,128)S(1)} %fusion.19, f32[8,128]{1,0:T(8,128)S(1)} %fusion.69, bf16[8,128,128]{2,1,0:T(8,128)(2,1)S(1)} %fusion.51, f32[8,128]{1,0:T(8,128)S(1)} %add_convert_fusion.1), kind=kOutput, calls=%fused_computation.247 | output fusion | flops 1179775 | bytes 540672 | tf_op jit(solution)/shard_map/div | solution.py:46
  36.4 0.1 fusion.71
  36.4 0.2 fusion.21
  36.7 0.4 fusion.23
  37.1 1.1 %fusion.48 = bf16[1024,128]{1,0:T(8,128)(2,1)S(1)} fusion(f32[1024,128]{1,0:T(8,128)S(1)} %gather_fusion.1, bf16[2,512,128]{2,1,0:T(8,128)(2,1)S(1)} %pad_maximum_fusion, f32[1024]{0:T(1024)S(1)} %bitcast.125, f32[1024]{0:T(1024)S(1)} %bitcast.123, f32[128]{0:T(128)S(1)} %log_add_fusion, f32[8,128]{1,0:T(8,128)S(1)} %fusion.71, f32[1024]{0:T(1024)S(1)} %fusion.135, ...), kind=kLoop, calls=%fused_computation.62 | loop fusion | flops 1966080 | bytes 1067520 | tf_op jit(solution)/shard_map/convert_element_type | solution.py:53
  38.2 2.8 %fusion.7 = f32[2048,128]{1,0:T(8,128)} fusion(bf16[1024,128]{1,0:T(8,128)(2,1)S(1)} %fusion.48, s32[1024]{0:T(1024)S(1)} %get-tuple-element.85, f32[1,2048,128]{2,1,0:T(8,128)S(1)} %copy-done.1), kind=kOutput, calls=%fused_computation.14 | convolution fusion | flops 539230208 | bytes 2363392 | tf_op jit(solution)/shard_map/dot_general | solution.py:119
  41.0 6.0 %all-to-all-start = ((f32[16,128,128]{2,1,0:T(8,128)}), f32[16,128,128]{2,1,0:T(8,128)S(1)}, u32[]{:S(2)}, u32[]{:S(2)}) async-start(f32[16,128,128]{2,1,0:T(8,128)} %bitcast.28), calls=%async_computation | async-start | bytes 2097152 | tf_op jit(solution)/shard_map/all_to_all | solution.py:129
  47.0 0.0 copy-done.6
  47.0 12.5 %while.16 = (s32[]{:T(128)}, f32[128]{0:T(128)S(1)}, f32[16,128]{1,0:T(8,128)S(1)}, f32[16,128]{1,0:T(8,128)S(1)}, f32[16,128]{1,0:T(8,128)}, /*index=5*/f32[128]{0:T(128)S(1)}, s32[]{:T(128)}, s32[]{:T(128)}) while((s32[]{:T(128)}, f32[128]{0:T(128)S(1)}, f32[16,128]{1,0:T(8,128)S(1)}, f32[16,128]{1,0:T(8,128)S(1)}, ...), condition=%wide.region_1.0_spmd.clone, body=%wide.region_0.0_spmd.clone.sunk | while | flops 771 | bytes 5227 | solution.py:24
  47.0 0.7 fusion.166
  47.8 0.7 fusion.166
  48.6 0.7 fusion.166
  49.4 0.7 fusion.166
  50.1 0.7 fusion.166
  50.9 0.7 fusion.166
  51.7 0.7 fusion.166
  52.5 0.7 fusion.166
  53.3 0.7 fusion.166
  54.0 0.7 fusion.166
  54.8 0.7 fusion.166
  55.6 0.7 fusion.166
  56.4 0.7 fusion.166
  57.2 0.7 fusion.166
  58.0 0.7 fusion.166
  58.7 0.7 fusion.166
  59.6 10.3 %all-to-all-done.pseudo_ref = f32[16,128,128]{2,1,0:T(8,128)S(1)} async-done(((f32[16,128,128]{2,1,0:T(8,128)}), f32[16,128,128]{2,1,0:T(8,128)S(1)}, u32[]{:S(2)}, u32[]{:S(2)}) %all-to-all-start) | async-done | bytes 1048608 | tf_op jit(solution)/shard_map/all_to_all | solution.py:129
  69.9 1.0 copy-done.2
  70.9 2.5 %shard_map.86 = f32[16,128,128]{2,1,0:T(8,128)} custom-call(f32[16,128]{1,0:T(8,128)S(1)} %get-tuple-element.47.gain_ref, f32[16,128]{1,0:T(8,128)} %copy-done.3, f32[16,128,128]{2,1,0:T(8,128)} %copy-done.2), custom_call_target="tpu_custom_call" | custom-call | tf_op jit(solution)/shard_map/pallas_call | solution.py:133
  73.3 6.8 %all-to-all-start.1 = ((f32[16,128,128]{2,1,0:T(8,128)}), f32[16,128,128]{2,1,0:T(8,128)S(1)}, u32[]{:S(2)}, u32[]{:S(2)}) async-start(f32[16,128,128]{2,1,0:T(8,128)} %shard_map.86), calls=%async_computation.1 | async-start | bytes 2097152 | tf_op jit(solution)/shard_map/all_to_all | solution.py:136
  80.1 0.9 fusion.49
  81.0 0.6 slice_bitcast_fusion.1
  81.6 21.4 %all-to-all-done.1 = f32[16,128,128]{2,1,0:T(8,128)S(1)} async-done(((f32[16,128,128]{2,1,0:T(8,128)}), f32[16,128,128]{2,1,0:T(8,128)S(1)}, u32[]{:S(2)}, u32[]{:S(2)}) %all-to-all-start.1) | async-done | bytes 1048608 | tf_op jit(solution)/shard_map/all_to_all | solution.py:136
  103.0 1.0 copy.28
  (68 shorter events, 1.3 us)
Async XLA Ops:
  0.6 5.0 %copy-start = (s32[32]{0:T(128)S(1)}, s32[32]{0:T(128)}, u32[]{:S(2)}) copy-start(s32[32]{0:T(128)} %param.14) | copy-start | bytes 388
  0.6 1.6 %copy-start.1 = (f32[1,2048,128]{2,1,0:T(8,128)S(1)}, f32[1,2048,128]{2,1,0:T(8,128)}, u32[]{:S(2)}) copy-start(f32[1,2048,128]{2,1,0:T(8,128)} %param.11) | copy-start | bytes 3145732
  0.7 5.0 %copy-start.5 = (s32[1,4,128]{2,1,0:T(4,128)S(1)}, s32[1,4,128]{2,1,0:T(4,128)}, u32[]{:S(2)}) copy-start(s32[1,4,128]{2,1,0:T(4,128)} %param.12) | copy-start | bytes 6148
  2.6 6.7 %collective-permute-start.1 = (f32[2,128]{1,0:T(2,128)S(1)}, f32[2,128]{1,0:T(2,128)S(1)}, u32[]{:S(2)}, u32[]{:S(2)}) collective-permute-start(f32[2,128]{1,0:T(2,128)S(1)} %get-tuple-element.99), channel_id=1, source_target_pairs={{0,1},{1,0},{2,3},{3,2},{4,5},{5,4},{6,7},{7,6},{8,9},{9,8},{10,11... | collective-permute-start | bytes 3080 | tf_op jit(solution)/shard_map/ppermute | solution.py:58
  5.7 3.4 %copy-start.4 = (s32[1,4,128]{2,1,0:T(4,128)S(1)}, s32[1,4,128]{2,1,0:T(4,128)}, u32[]{:S(2)}) copy-start(s32[1,4,128]{2,1,0:T(4,128)} %param.13) | copy-start | bytes 6148
  9.1 3.7 %collective-permute-start = (s32[2,4,128]{2,1,0:T(4,128)S(1)}, s32[2,4,128]{2,1,0:T(4,128)S(1)}, u32[]{:S(2)}, u32[]{:S(2)}) collective-permute-start(s32[2,4,128]{2,1,0:T(4,128)S(1)} %pad_add_fusion), channel_id=1, source_target_pairs={{0,1},{1,0},{2,3},{3,2},{4,5},{5,4},{6,7},{7,6},{8,9},{9,8},{10,11... | collective-permute-start | bytes 12296 | tf_op jit(solution)/shard_map/ppermute | solution.py:58
  13.0 3.3 %copy-start.7 = (f32[128]{0:T(128)S(1)}, f32[128]{0:T(128)}, u32[]{:S(2)}) copy-start(f32[128]{0:T(128)} %param.15) | copy-start | bytes 1540
  16.2 6.7 %collective-permute-start.2 = (bf16[2,512,128]{2,1,0:T(8,128)(2,1)S(1)}, bf16[2,512,128]{2,1,0:T(8,128)(2,1)S(1)}, u32[]{:S(2)}, u32[]{:S(2)}) collective-permute-start(bf16[2,512,128]{2,1,0:T(8,128)(2,1)S(1)} %fusion.52), channel_id=1, source_target_pairs={{0,1},{1,0},{2,3},{3,2},{4,5},{5,4},{6,7},{7,6},{8,9},{9,8},{10,11... | collective-permute-start | bytes 786440 | tf_op jit(solution)/shard_map/ppermute | solution.py:58
  40.9 6.1 %copy-start.6 = (f32[128]{0:T(128)S(1)}, f32[128]{0:T(128)}, u32[]{:S(2)}) copy-start(f32[128]{0:T(128)} %param.16) | copy-start | bytes 1540
  41.0 28.9 %all-to-all-start = ((f32[16,128,128]{2,1,0:T(8,128)}), f32[16,128,128]{2,1,0:T(8,128)S(1)}, u32[]{:S(2)}, u32[]{:S(2)}) async-start(f32[16,128,128]{2,1,0:T(8,128)} %bitcast.28), calls=%async_computation | async-start | bytes 2097152 | tf_op jit(solution)/shard_map/all_to_all | solution.py:129
  59.6 10.3 %copy-start.3 = (f32[16,128]{1,0:T(8,128)}, f32[16,128]{1,0:T(8,128)S(1)}, u32[]{:S(2)}) copy-start(f32[16,128]{1,0:T(8,128)S(1)} %scatter.4.pull_ref) | copy-start | bytes 24580
  69.9 1.0 copy-start.2
  73.3 29.7 %all-to-all-start.1 = ((f32[16,128,128]{2,1,0:T(8,128)}), f32[16,128,128]{2,1,0:T(8,128)S(1)}, u32[]{:S(2)}, u32[]{:S(2)}) async-start(f32[16,128,128]{2,1,0:T(8,128)} %shard_map.86), calls=%async_computation.1 | async-start | bytes 2097152 | tf_op jit(solution)/shard_map/all_to_all | solution.py:136

commit v3 on v2

--- a/solution.py
+++ b/solution.py
@@ -43,7 +43,11 @@
     doc_topics = topic_prior + jnp.sum(counts_float, axis=-1, keepdims=True) / K
     scores = looked.astype(jnp.float32)
     for sweep in range(EITERS):
-        resp = jax.nn.softmax(lax.digamma(doc_topics)[..., None, :] + scores, axis=-1)
+        logits = lax.digamma(doc_topics)[..., None, :] + scores
+        peak = lax.optimization_barrier(jnp.max(logits, axis=-1, keepdims=True))
+        raised = jnp.exp(logits - peak)
+        total = lax.optimization_barrier(jnp.sum(raised, axis=-1, keepdims=True))
+        resp = raised / total
         doc_topics = topic_prior + jnp.sum(counts_float[..., None] * resp, axis=-2)
     weighted = to_bf16(counts_float[..., None] * resp)
     return (doc_topics, weighted)
@@ -84,13 +88,16 @@
     slot_ids = word_ids[0]
     local_docs = slot_ids.shape[0]
     slot_width = slot_ids.shape[1]
-    columns = jnp.take(block_slot, slot_ids // BLOCK) * BLOCK + slot_ids % BLOCK
 
-    ints = jnp.stack([columns, word_counts[0]])
+    ints = jnp.stack([slot_ids, word_counts[0]])
     stats = jnp.stack([local_peak, local_total])
     ints_seen = [ints] + [shift_doc(ints, s) for s in range(1, doc_devices)]
     stats_seen = jnp.stack([stats] + [shift_doc(stats, s) for s in range(1, doc_devices)])
-    all_columns = jnp.concatenate([part[0] for part in ints_seen], axis=0)
+    all_ids = jnp.concatenate([part[0] for part in ints_seen], axis=0)
+    block_match = (all_ids // BLOCK)[..., None] == lax.iota(jnp.int32, block_slot.shape[0])
+    all_columns = (
+        jnp.sum(jnp.where(block_match, block_slot, 0), axis=-1) * BLOCK + all_ids % BLOCK
+    )
     all_counts = jnp.concatenate([part[1] for part in ints_seen], axis=0)
     peaks = stats_seen[:, 0]
     totals = stats_seen[:, 1]

time: 106 us -> 93.5 us (0.88)
  the two profiles are of different devices: /device:TPU:0 before, /device:TPU:9 now
where the time goes in v3:
time: 93.5 us; the launch traced here: 92.6 us
  waiting for transfers between devices  43.9 us (47%)
  other arithmetic  20.5 us (22%)
  starting transfers between devices  15.4 us (16%)
  local copies, waits for them, and re-layouts  6.36 us (7%)
  matrix products  2.76 us (3%)
  Pallas kernels  2.47 us (3%)
    all_to_all x1, waiting for transfers between devices, body(): lax.all_to_all(smoothed, 'tm', split_axis=0, concat_axis=0, tiled=True)  23.8 us
    all_to_all x1, waiting for transfers between devices, body(): lax.all_to_all(pseudo.reshape(years, chunk, topics), 'tm', split_axis=0,...  12.3 us
    add x16, other arithmetic, forward_step(): return (filt_var + drift_var, (gain_now, filt_var))  11.3 us
    all_to_all x1, starting transfers between devices, body(): lax.all_to_all(pseudo.reshape(years, chunk, topics), 'tm', split_axis=0,...  8.88 us
    ppermute x3, waiting for transfers between devices, shift_doc(): lax.ppermute(value, 'doc', [(i, (i + s) % count) for i in range(count)])  7.75 us
    all_to_all x1, starting transfers between devices, body(): lax.all_to_all(smoothed, 'tm', split_axis=0, concat_axis=0, tiled=True)  4.76 us
    gather x1, local copies, waits for them, and re-layouts, body(): jnp.take(local_beta, jnp.clip(local_columns, 0, own_words - 1), axis=0)  2.81 us
    dot_general x1, matrix products, body(): counts = jnp.dot(marks, flat_weighted, preferred_element_type=jnp.float32)  2.76 us
  transfers between devices with their start and end apart: 5, of which 5 were waited for; matrix products, arithmetic and copies ran while one was open for 15% of the time, Pallas kernels for 0%

profile of v3, /device:TPU:9, one launch (start us, length us, event | category | flops | bytes accessed | tf_op | source)
XLA Modules:
  0.0 92.6 jit_solution(16380698718286904661)
XLA Ops:
  0.6 0.0 copy-start
  0.6 0.0 copy-start.3
  0.7 0.0 copy-start.4
  0.7 0.0 copy-start.7
  0.7 1.6 %reduce_max.54 = f32[128]{0:T(128)S(1)} reduce(f32[1,2048,128]{2,1,0:T(8,128)} %param.11, f32[]{:T(128)} %constant.137.clone.1), dimensions={0,1}, to_apply=%region_4.5 | reduce | flops 262016 | bytes 1049092 | tf_op jit(solution)/shard_map/reduce_max | solution.py:85
  2.3 0.0 copy-done
  2.3 0.3 exponential_reduce_fusion
  2.6 1.3 %collective-permute-start.1 = (f32[2,128]{1,0:T(2,128)S(1)}, f32[2,128]{1,0:T(2,128)S(1)}, u32[]{:S(2)}, u32[]{:S(2)}) collective-permute-start(f32[2,128]{1,0:T(2,128)S(1)} %get-tuple-element.104), channel_id=1, source_target_pairs={{0,1},{1,0},{2,3},{3,2},{4,5},{5,4},{6,7},{7,6},{8,9},{9,8},{10,11... | collective-permute-start | bytes 3080 | tf_op jit(solution)/shard_map/ppermute | solution.py:62
  3.9 0.3 collective-permute-start
  4.2 0.9 collective-permute-done.1
  5.1 1.4 %collective-permute-done = s32[2,4,128]{2,1,0:T(4,128)S(1)} collective-permute-done((s32[2,4,128]{2,1,0:T(4,128)S(1)}, s32[2,4,128]{2,1,0:T(4,128)S(1)}, u32[]{:S(2)}, u32[]{:S(2)}) %collective-permute-start) | collective-permute-done | bytes 4128 | tf_op jit(solution)/shard_map/ppermute | solution.py:62
  6.5 0.1 fusion.145
  6.6 0.0 copy-done.7
  6.6 0.1 select_reduce_fusion
  6.9 0.0 copy-start.6
  6.9 2.8 %gather_fusion = f32[1024,128]{1,0:T(8,128)S(1)} fusion(f32[2048,128]{1,0:T(8,128)S(1)} %bitcast.89, s32[1024]{0:T(1024)S(1)} %broadcast_clamp_fusion), kind=kCustom, calls=%fused_computation | custom fusion | bytes 1052672 | tf_op jit(solution)/shard_map/jit(_take)/gather | solution.py:111
  9.7 0.3 fusion.49
  10.1 0.2 collective-permute-start.2
  10.4 0.0 copy-done.6
  10.4 0.1 fusion.61
  10.5 5.5 %collective-permute-done.2 = bf16[2,512,128]{2,1,0:T(8,128)(2,1)S(1)} collective-permute-done((bf16[2,512,128]{2,1,0:T(8,128)(2,1)S(1)}, bf16[2,512,128]{2,1,0:T(8,128)(2,1)S(1)}, u32[]{:S(2)}, u32[]{:S(2)}) %collective-permute-start.2) | collective-permute-done | bytes 262176 | tf_op jit(solution)/shard_map/ppermute | solution.py:62
  16.1 0.5 fusion.6
  16.6 0.4 fusion.20
  17.0 0.9 fusion.46
  17.9 0.1 fusion.65
  17.9 0.2 fusion.8
  18.1 0.4 fusion.18
  18.5 0.5 fusion.45
  19.0 0.1 fusion.67
  19.1 0.2 fusion.10
  19.3 0.4 fusion.16
  19.7 0.5 fusion.44
  20.2 0.1 fusion.69
  20.2 0.2 fusion.12
  20.5 0.4 fusion.14
  20.8 1.1 %fusion.42 = bf16[1024,128]{1,0:T(8,128)(2,1)S(1)} fusion(f32[1024,128]{1,0:T(8,128)S(1)} %gather_fusion, bf16[2,512,128]{2,1,0:T(8,128)(2,1)S(1)} %pad_maximum_fusion, f32[1024]{0:T(1024)S(1)} %bitcast.97, f32[1024]{0:T(1024)S(1)} %bitcast.95, f32[128]{0:T(128)S(1)} %log_add_fusion, f32[8,128]{1,0:T(8,128)S(1)} %fusion.69, f32[1024]{0:T(1024)S(1)} %fusion.135, ...), kind=kLoop, calls=%fused_computation.58 | loop fusion | flops 1966080 | bytes 1067520 | tf_op jit(solution)/shard_map/convert_element_type | solution.py:57
  22.0 2.8 %fusion.4 = f32[2048,128]{1,0:T(8,128)} fusion(bf16[1024,128]{1,0:T(8,128)(2,1)S(1)} %fusion.42, s32[1024]{0:T(1024)S(1)} %get-tuple-element.85, f32[1,2048,128]{2,1,0:T(8,128)S(1)} %copy-done), kind=kOutput, calls=%fused_computation.10 | convolution fusion | flops 539230208 | bytes 2363392 | tf_op jit(solution)/shard_map/dot_general | solution.py:126
  24.7 8.9 %all-to-all-start = ((f32[16,128,128]{2,1,0:T(8,128)}), f32[16,128,128]{2,1,0:T(8,128)S(1)}, u32[]{:S(2)}, u32[]{:S(2)}) async-start(f32[16,128,128]{2,1,0:T(8,128)} %bitcast.41), calls=%async_computation | async-start | bytes 2097152 | tf_op jit(solution)/shard_map/all_to_all | solution.py:136
  33.6 0.0 copy-done.5
  33.6 12.5 %while.16 = (s32[]{:T(128)}, f32[128]{0:T(128)S(1)}, f32[16,128]{1,0:T(8,128)S(1)}, f32[16,128]{1,0:T(8,128)S(1)}, f32[16,128]{1,0:T(8,128)}, /*index=5*/f32[128]{0:T(128)S(1)}, s32[]{:T(128)}, s32[]{:T(128)}) while((s32[]{:T(128)}, f32[128]{0:T(128)S(1)}, f32[16,128]{1,0:T(8,128)S(1)}, f32[16,128]{1,0:T(8,128)S(1)}, ...), condition=%wide.region_1.0_spmd.clone, body=%wide.region_0.0_spmd.clone.sunk | while | flops 771 | bytes 5227 | solution.py:24
  33.6 0.7 fusion.155
  34.4 0.7 fusion.155
  35.2 0.7 fusion.155
  36.0 0.7 fusion.155
  36.7 0.7 fusion.155
  37.5 0.7 fusion.155
  38.3 0.7 fusion.155
  39.1 0.7 fusion.155
  39.9 0.7 fusion.155
  40.6 0.7 fusion.155
  41.4 0.7 fusion.155
  42.2 0.7 fusion.155
  43.0 0.7 fusion.155
  43.8 0.7 fusion.155
  44.6 0.7 fusion.155
  45.3 0.7 fusion.155
  46.2 12.3 %all-to-all-done.pseudo_ref = f32[16,128,128]{2,1,0:T(8,128)S(1)} async-done(((f32[16,128,128]{2,1,0:T(8,128)}), f32[16,128,128]{2,1,0:T(8,128)S(1)}, u32[]{:S(2)}, u32[]{:S(2)}) %all-to-all-start) | async-done | bytes 1048608 | tf_op jit(solution)/shard_map/all_to_all | solution.py:136
  58.5 1.0 %copy-done.1 = f32[16,128,128]{2,1,0:T(8,128)} copy-done((f32[16,128,128]{2,1,0:T(8,128)}, f32[16,128,128]{2,1,0:T(8,128)S(1)}, u32[]{:S(2)}) %copy-start.1) | copy-done | bytes 1048600
  59.5 2.5 %shard_map.86 = f32[16,128,128]{2,1,0:T(8,128)} custom-call(f32[16,128]{1,0:T(8,128)S(1)} %get-tuple-element.47.gain_ref, f32[16,128]{1,0:T(8,128)} %copy-done.2, f32[16,128,128]{2,1,0:T(8,128)} %copy-done.1), custom_call_target="tpu_custom_call" | custom-call | tf_op jit(solution)/shard_map/pallas_call | solution.py:140
  62.0 4.8 %all-to-all-start.1 = ((f32[16,128,128]{2,1,0:T(8,128)}), f32[16,128,128]{2,1,0:T(8,128)S(1)}, u32[]{:S(2)}, u32[]{:S(2)}) async-start(f32[16,128,128]{2,1,0:T(8,128)} %shard_map.86), calls=%async_computation.1 | async-start | bytes 2097152 | tf_op jit(solution)/shard_map/all_to_all | solution.py:143
  66.7 0.5 fusion.43
  67.2 0.6 slice_bitcast_fusion.1
  67.8 23.8 %all-to-all-done.1 = f32[16,128,128]{2,1,0:T(8,128)S(1)} async-done(((f32[16,128,128]{2,1,0:T(8,128)}), f32[16,128,128]{2,1,0:T(8,128)S(1)}, u32[]{:S(2)}, u32[]{:S(2)}) %all-to-all-start.1) | async-done | bytes 1048608 | tf_op jit(solution)/shard_map/all_to_all | solution.py:143
  91.6 1.0 %copy.28 = f32[1,2048,128]{2,1,0:T(8,128)} copy(f32[1,2048,128]{2,1,0:T(8,128)S(1)} %bitcast.92) | data formatting | bytes 2097152
  (70 shorter events, 1.3 us)
Async XLA Ops:
  0.6 1.6 %copy-start = (f32[1,2048,128]{2,1,0:T(8,128)S(1)}, f32[1,2048,128]{2,1,0:T(8,128)}, u32[]{:S(2)}) copy-start(f32[1,2048,128]{2,1,0:T(8,128)} %param.11) | copy-start | bytes 3145732
  0.6 3.2 %copy-start.3 = (s32[1,4,128]{2,1,0:T(4,128)S(1)}, s32[1,4,128]{2,1,0:T(4,128)}, u32[]{:S(2)}) copy-start(s32[1,4,128]{2,1,0:T(4,128)} %param.12) | copy-start | bytes 6148
  0.7 3.2 %copy-start.4 = (s32[1,4,128]{2,1,0:T(4,128)S(1)}, s32[1,4,128]{2,1,0:T(4,128)}, u32[]{:S(2)}) copy-start(s32[1,4,128]{2,1,0:T(4,128)} %param.13) | copy-start | bytes 6148
  0.7 6.0 %copy-start.7 = (s32[32]{0:T(128)S(1)}, s32[32]{0:T(128)}, u32[]{:S(2)}) copy-start(s32[32]{0:T(128)} %param.14) | copy-start | bytes 388
  2.6 2.5 %collective-permute-start.1 = (f32[2,128]{1,0:T(2,128)S(1)}, f32[2,128]{1,0:T(2,128)S(1)}, u32[]{:S(2)}, u32[]{:S(2)}) collective-permute-start(f32[2,128]{1,0:T(2,128)S(1)} %get-tuple-element.104), channel_id=1, source_target_pairs={{0,1},{1,0},{2,3},{3,2},{4,5},{5,4},{6,7},{7,6},{8,9},{9,8},{10,11... | collective-permute-start | bytes 3080 | tf_op jit(solution)/shard_map/ppermute | solution.py:62
  3.9 2.6 %collective-permute-start = (s32[2,4,128]{2,1,0:T(4,128)S(1)}, s32[2,4,128]{2,1,0:T(4,128)S(1)}, u32[]{:S(2)}, u32[]{:S(2)}) collective-permute-start(s32[2,4,128]{2,1,0:T(4,128)S(1)} %pad_add_fusion), channel_id=1, source_target_pairs={{0,1},{1,0},{2,3},{3,2},{4,5},{5,4},{6,7},{7,6},{8,9},{9,8},{10,11... | collective-permute-start | bytes 12296 | tf_op jit(solution)/shard_map/ppermute | solution.py:62
  6.9 3.5 %copy-start.6 = (f32[128]{0:T(128)S(1)}, f32[128]{0:T(128)}, u32[]{:S(2)}) copy-start(f32[128]{0:T(128)} %param.15) | copy-start | bytes 1540
  10.1 5.9 %collective-permute-start.2 = (bf16[2,512,128]{2,1,0:T(8,128)(2,1)S(1)}, bf16[2,512,128]{2,1,0:T(8,128)(2,1)S(1)}, u32[]{:S(2)}, u32[]{:S(2)}) collective-permute-start(bf16[2,512,128]{2,1,0:T(8,128)(2,1)S(1)} %fusion.49), channel_id=1, source_target_pairs={{0,1},{1,0},{2,3},{3,2},{4,5},{5,4},{6,7},{7,6},{8,9},{9,8},{10,11... | collective-permute-start | bytes 786440 | tf_op jit(solution)/shard_map/ppermute | solution.py:62
  24.7 8.9 %copy-start.5 = (f32[128]{0:T(128)S(1)}, f32[128]{0:T(128)}, u32[]{:S(2)}) copy-start(f32[128]{0:T(128)} %param.16) | copy-start | bytes 1540
  24.7 33.8 %all-to-all-start = ((f32[16,128,128]{2,1,0:T(8,128)}), f32[16,128,128]{2,1,0:T(8,128)S(1)}, u32[]{:S(2)}, u32[]{:S(2)}) async-start(f32[16,128,128]{2,1,0:T(8,128)} %bitcast.41), calls=%async_computation | async-start | bytes 2097152 | tf_op jit(solution)/shard_map/all_to_all | solution.py:136
  46.2 12.4 %copy-start.2 = (f32[16,128]{1,0:T(8,128)}, f32[16,128]{1,0:T(8,128)S(1)}, u32[]{:S(2)}) copy-start(f32[16,128]{1,0:T(8,128)S(1)} %scatter.4.pull_ref) | copy-start | bytes 24580
  58.5 1.0 %copy-start.1 = (f32[16,128,128]{2,1,0:T(8,128)}, f32[16,128,128]{2,1,0:T(8,128)S(1)}, u32[]{:S(2)}) copy-start(f32[16,128,128]{2,1,0:T(8,128)S(1)} %all-to-all-done.pseudo_ref) | copy-start | bytes 3145732
  62.0 29.7 %all-to-all-start.1 = ((f32[16,128,128]{2,1,0:T(8,128)}), f32[16,128,128]{2,1,0:T(8,128)S(1)}, u32[]{:S(2)}, u32[]{:S(2)}) async-start(f32[16,128,128]{2,1,0:T(8,128)} %shard_map.86), calls=%async_computation.1 | async-start | bytes 2097152 | tf_op jit(solution)/shard_map/all_to_all | solution.py:143

commit v4 on v3

--- a/solution.py
+++ b/solution.py
@@ -21,7 +21,7 @@
         return (filt_var + drift_var, (gain_now, filt_var))
 
     start_var = jnp.full(drift_var.shape, init_variance, dtype=jnp.float32)
-    last_var, (gains, filt_vars) = lax.scan(forward_step, start_var, obs_precision)
+    last_var, (gains, filt_vars) = lax.scan(forward_step, start_var, obs_precision, unroll=True)
 
     def backward_step(info_next, precision):
         merged = info_next + precision
@@ -57,23 +57,55 @@
     return lax.reduce_precision(value, exponent_bits=8, mantissa_bits=7).astype(jnp.bfloat16)
 
 
+def shift_axis(value, axis, s):
+    count = lax.axis_size(axis)
+    return lax.ppermute(value, axis, [(i, (i + s) % count) for i in range(count)])
+
+
 def shift_doc(value, s):
-    count = lax.axis_size("doc")
-    return lax.ppermute(value, "doc", [(i, (i + s) % count) for i in range(count)])
-
-
-def kalman_kernel(gain_ref, pull_ref, pseudo_ref, out_ref):
+    return shift_axis(value, "doc", s)
+
+
+def kalman_kernel(gain_ref, pull_ref, start_ref, after_ref, pseudo_ref, out_ref, last_ref):
     years = pseudo_ref.shape[0]
-    mean = jnp.zeros(pseudo_ref.shape[1:], jnp.float32)
+    mean = start_ref[...]
     for t in range(years):
         gain_now = gain_ref[pl.ds(t, 1), :]
         mean = (1.0 - gain_now) * mean + gain_now * pseudo_ref[t]
         out_ref[t] = mean
-    mean = jnp.zeros(pseudo_ref.shape[1:], jnp.float32)
+    last_ref[...] = mean
+    mean = after_ref[...]
     for t in reversed(range(years)):
         pull_now = pull_ref[pl.ds(t, 1), :]
         mean = pull_now * mean + (1.0 - pull_now) * out_ref[t]
         out_ref[t] = mean
+
+
+def kalman(gains, pulls, start, after, by_year):
+    return pl.pallas_call(
+        kalman_kernel,
+        out_shape=(
+            jax.ShapeDtypeStruct(by_year.shape, jnp.float32),
+            jax.ShapeDtypeStruct(start.shape, jnp.float32),
+        ),
+    )(gains, pulls, start, after, by_year)
+
+
+def group_maps(gains, pulls, groups):
+    gains_g = gains.reshape(groups, -1, gains.shape[-1])
+    pulls_g = pulls.reshape(groups, -1, pulls.shape[-1])
+    span = gains_g.shape[1]
+    carry = jnp.ones_like(gains_g[:, 0])
+    responses = []
+    for i in range(span):
+        carry = (1.0 - gains_g[:, i]) * carry
+        responses.append(carry)
+    from_start = jnp.zeros_like(carry)
+    from_after = jnp.ones_like(carry)
+    for i in reversed(range(span)):
+        from_start = pulls_g[:, i] * from_start + (1.0 - pulls_g[:, i]) * responses[i]
+        from_after = pulls_g[:, i] * from_after
+    return carry, from_start, from_after
 
 
 def body(beta, word_ids, word_counts, block_slot, topic_prior, drift_var, obs_precision):
@@ -131,28 +163,45 @@
     pulls = filt_vars / (filt_vars + drift_var)
     pulls = pulls.at[-1].set(0.0)
 
-    years = lax.axis_size("tm")
-    chunk = own_words // years
+    groups = lax.axis_size("tg")
+    span = lax.axis_size("tl")
+    group = lax.axis_index("tg")
+    chunk = own_words // span
     by_year = lax.all_to_all(
-        pseudo.reshape(years, chunk, topics), "tm", split_axis=0, concat_axis=0, tiled=True
+        pseudo.reshape(span, chunk, topics), "tl", split_axis=0, concat_axis=0, tiled=True
     )
-
-    smoothed = pl.pallas_call(
-        kalman_kernel, out_shape=jax.ShapeDtypeStruct(by_year.shape, jnp.float32)
-    )(gains, pulls, by_year)
-    back = lax.all_to_all(smoothed, "tm", split_axis=0, concat_axis=0, tiled=True)
+    gains_here = lax.dynamic_slice_in_dim(gains, group * span, span, 0)
+    pulls_here = lax.dynamic_slice_in_dim(pulls, group * span, span, 0)
+    zero_mean = jnp.zeros((chunk, topics), jnp.float32)
+    if groups == 1:
+        smoothed, _ = kalman(gains_here, pulls_here, zero_mean, zero_mean, by_year)
+    else:
+        local_smoothed, local_last = kalman(gains_here, pulls_here, zero_mean, zero_mean, by_year)
+        summary = jnp.stack([local_last, local_smoothed[0]])
+        seen = [summary] + [shift_axis(summary, "tg", s) for s in range(1, groups)]
+        ordered = jnp.stack(seen)[(group - jnp.arange(groups)) % groups]
+        carry, from_start, from_after = group_maps(gains, pulls, groups)
+        entering = [zero_mean]
+        for g in range(groups - 1):
+            entering.append(ordered[g, 0] + carry[g] * entering[g])
+        leaving = [zero_mean] * groups
+        for g in reversed(range(1, groups)):
+            leaving[g - 1] = (
+                ordered[g, 1] + from_start[g] * entering[g] + from_after[g] * leaving[g]
+            )
+        start = jnp.stack(entering)[group]
+        after = jnp.stack(leaving)[group]
+        smoothed, _ = kalman(gains_here, pulls_here, start, after, by_year)
+    back = lax.all_to_all(smoothed, "tl", split_axis=0, concat_axis=0, tiled=True)
     return (back.reshape(own_words, topics)[None], doc_topics[None])
 
 
 def solution(mesh):
-    in_specs = (
-        P("tm", "doc", None),
-        P("tm", "doc", None),
-        P("tm", "doc", None),
-        P(),
-        P(),
-        P(),
-        P(),
-    )
-    out_specs = (P("tm", "doc", None), P("tm", "doc", None))
-    return jax.shard_map(body, mesh=mesh, in_specs=in_specs, out_specs=out_specs, check_vma=False)
+    years = mesh.shape["tm"]
+    span = 8 if years % 8 == 0 else years
+    devices = mesh.devices.reshape(years // span, span, mesh.shape["doc"])
+    grouped = jax.sharding.Mesh(devices, ("tg", "tl", "doc"))
+    split = P(("tg", "tl"), "doc", None)
+    in_specs = (split, split, split, P(), P(), P(), P())
+    out_specs = (split, split)
+    return jax.shard_map(body, mesh=grouped, in_specs=in_specs, out_specs=out_specs, check_vma=False)

time: 93.5 us -> 90.5 us (0.968)
  the two profiles are of different devices: /device:TPU:9 before, /device:TPU:0 now
where the time goes in v4:
time: 90.5 us; the launch traced here: 90.1 us
  waiting for transfers between devices  48.3 us (53%)
  starting transfers between devices  13.3 us (15%)
  other arithmetic  10.4 us (11%)
  local copies, waits for them, and re-layouts  9.08 us (10%)
  Pallas kernels  5.29 us (6%)
  matrix products  2.76 us (3%)
  between operations  1.02 us (1%)
    ppermute x4, waiting for transfers between devices, shift_axis(): lax.ppermute(value, axis, [(i, (i + s) % count) for i in range(count)])  21.4 us
    all_to_all x1, waiting for transfers between devices, body(): lax.all_to_all(pseudo.reshape(span, chunk, topics), 'tl', split_axis=0, c...  13.6 us
    all_to_all x1, waiting for transfers between devices, body(): lax.all_to_all(smoothed, 'tl', split_axis=0, concat_axis=0, tiled=True)  13.3 us
    ppermute x4, starting transfers between devices, shift_axis(): lax.ppermute(value, axis, [(i, (i + s) % count) for i in range(count)])  5.92 us
    pallas_call x2, Pallas kernels, kalman(): pl.pallas_call(kalman_kernel, out_shape=(jax.ShapeDtypeStruct(by_year.sha...  5.29 us
    all_to_all x1, starting transfers between devices, body(): lax.all_to_all(pseudo.reshape(span, chunk, topics), 'tl', split_axis=0, c...  3.87 us
    all_to_all x1, starting transfers between devices, body(): lax.all_to_all(smoothed, 'tl', split_axis=0, concat_axis=0, tiled=True)  3.56 us
    gather x1, local copies, waits for them, and re-layouts, body(): jnp.take(local_beta, jnp.clip(local_columns, 0, own_words - 1), axis=0)  2.81 us
  transfers between devices with their start and end apart: 6, of which 6 were waited for; matrix products, arithmetic and copies ran while one was open for 3% of the time, Pallas kernels for 0%

profile of v4, /device:TPU:0, one launch (start us, length us, event | category | flops | bytes accessed | tf_op | source)
XLA Modules:
  0.0 90.1 jit_solution(6567386058448127054)
XLA Ops:
  0.6 0.0 copy-start
  0.6 0.0 copy-start.3
  0.7 0.0 copy-start.2
  0.7 0.0 copy-start.4
  0.7 0.0 copy-start.5
  0.7 0.0 copy-start.7
  0.7 1.6 %reduce_max.54 = f32[128]{0:T(128)S(1)} reduce(f32[1,2048,128]{2,1,0:T(8,128)} %param.9, f32[]{:T(128)} %constant.152.clone.1), dimensions={0,1}, to_apply=%region_2.3 | reduce | flops 262016 | bytes 1049092 | tf_op jit(solution)/shard_map/reduce_max | solution.py:117
  2.3 0.0 copy-done
  2.3 0.3 exponential_reduce_fusion
  2.6 3.1 %collective-permute-start.1 = (f32[2,128]{1,0:T(2,128)S(1)}, f32[2,128]{1,0:T(2,128)S(1)}, u32[]{:S(2)}, u32[]{:S(2)}) collective-permute-start(f32[2,128]{1,0:T(2,128)S(1)} %get-tuple-element.93), channel_id=1, source_target_pairs={{0,1},{1,0},{2,3},{3,2},{4,5},{5,4},{6,7},{7,6},{8,9},{9,8},{10,11... | collective-permute-start | bytes 3080 | tf_op jit(solution)/shard_map/ppermute | solution.py:62
  5.6 0.0 copy-done.3
  5.6 0.0 copy-done.2
  5.6 0.1 collective-permute-start
  5.8 0.0 copy-done.4
  5.8 0.0 copy-done.5
  5.8 0.1 fusion.166
  5.9 0.1 concatenate.60
  6.0 1.2 %collective-permute-done.1 = f32[2,128]{1,0:T(2,128)S(1)} collective-permute-done((f32[2,128]{1,0:T(2,128)S(1)}, f32[2,128]{1,0:T(2,128)S(1)}, u32[]{:S(2)}, u32[]{:S(2)}) %collective-permute-start.1) | collective-permute-done | bytes 1056 | tf_op jit(solution)/shard_map/ppermute | solution.py:62
  7.3 2.1 %collective-permute-done = s32[2,4,128]{2,1,0:T(4,128)S(1)} collective-permute-done((s32[2,4,128]{2,1,0:T(4,128)S(1)}, s32[2,4,128]{2,1,0:T(4,128)S(1)}, u32[]{:S(2)}, u32[]{:S(2)}) %collective-permute-start) | collective-permute-done | bytes 4128 | tf_op jit(solution)/shard_map/ppermute | solution.py:62
  9.3 0.1 fusion.168
  9.5 0.0 copy-done.7
  9.5 0.1 select_reduce_fusion
  9.8 0.0 copy-start.6
  9.8 2.8 %gather_fusion = f32[1024,128]{1,0:T(8,128)S(1)} fusion(f32[2048,128]{1,0:T(8,128)S(1)} %bitcast.358, s32[1024]{0:T(1024)S(1)} %broadcast_clamp_fusion), kind=kCustom, calls=%fused_computation | custom fusion | bytes 1052672 | tf_op jit(solution)/shard_map/jit(_take)/gather | solution.py:143
  12.6 0.3 fusion.48
  13.0 0.1 collective-permute-start.2
  13.1 0.1 fusion.65
  13.2 6.4 %collective-permute-done.2 = bf16[2,512,128]{2,1,0:T(8,128)(2,1)S(1)} collective-permute-done((bf16[2,512,128]{2,1,0:T(8,128)(2,1)S(1)}, bf16[2,512,128]{2,1,0:T(8,128)(2,1)S(1)}, u32[]{:S(2)}, u32[]{:S(2)}) %collective-permute-start.2) | collective-permute-done | bytes 262176 | tf_op jit(solution)/shard_map/ppermute | solution.py:62
  19.7 0.5 fusion.5
  20.2 0.4 fusion.19
  20.6 0.9 fusion.45
  21.5 0.1 fusion.69
  21.6 0.2 fusion.7
  21.8 0.4 fusion.17
  22.2 0.5 fusion.44
  22.7 0.1 fusion.71
  22.7 0.2 fusion.9
  22.9 0.4 fusion.15
  23.3 0.5 fusion.43
  23.8 0.1 fusion.73
  23.9 0.2 fusion.11
  24.1 0.4 fusion.13
  24.5 1.1 %fusion.41 = bf16[1024,128]{1,0:T(8,128)(2,1)S(1)} fusion(f32[1024,128]{1,0:T(8,128)S(1)} %gather_fusion, bf16[2,512,128]{2,1,0:T(8,128)(2,1)S(1)} %pad_maximum_fusion.1, f32[1024]{0:T(1024)S(1)} %bitcast.369, f32[1024]{0:T(1024)S(1)} %bitcast.366, f32[128]{0:T(128)S(1)} %log_add_fusion, f32[8,128]{1,0:T(8,128)S(1)} %fusion.73, f32[1024]{0:T(1024)S(1)} %fusion.139, ...), kind=kLoop, calls=%fused_computation.55 | loop fusion | flops 1966080 | bytes 1067520 | tf_op jit(solution)/shard_map/convert_element_type | solution.py:57
  25.6 2.8 %fusion.3 = f32[2048,128]{1,0:T(8,128)} fusion(bf16[1024,128]{1,0:T(8,128)(2,1)S(1)} %fusion.41, s32[1024]{0:T(1024)S(1)} %get-tuple-element.23, f32[1,2048,128]{2,1,0:T(8,128)S(1)} %copy-done), kind=kOutput, calls=%fused_computation.6 | convolution fusion | flops 539230208 | bytes 2363392 | tf_op jit(solution)/shard_map/dot_general | solution.py:158
  28.4 3.9 %all-to-all-start = ((f32[8,256,128]{2,1,0:T(8,128)}), f32[8,256,128]{2,1,0:T(8,128)S(1)}, u32[]{:S(2)}, u32[]{:S(2)}) async-start(f32[8,256,128]{2,1,0:T(8,128)} %bitcast.87), calls=%async_computation | async-start | bytes 2097152 | tf_op jit(solution)/shard_map/all_to_all | solution.py:170
  32.4 0.1 concatenate.59
  32.4 0.6 constant_dynamic-slice_fusion
  33.1 13.6 %all-to-all-done.pseudo_ref = f32[8,256,128]{2,1,0:T(8,128)S(1)} async-done(((f32[8,256,128]{2,1,0:T(8,128)}), f32[8,256,128]{2,1,0:T(8,128)S(1)}, u32[]{:S(2)}, u32[]{:S(2)}) %all-to-all-start) | async-done | bytes 1048608 | tf_op jit(solution)/shard_map/all_to_all | solution.py:170
  46.7 0.7 broadcast_in_dim.239.start_ref.after_ref
  47.4 0.3 copy-done.1
  47.7 2.6 %shard_map.86 = (f32[8,256,128]{2,1,0:T(8,128)}, f32[256,128]{1,0:T(8,128)}) custom-call(f32[8,128]{1,0:T(8,128)} %get-tuple-element.96.gain_ref, f32[8,128]{1,0:T(8,128)} %get-tuple-element.95.pull_ref, f32[256,128]{1,0:T(8,128)} %broadcast_in_dim.239.start_ref.after_ref, f32[256,128]{1,0:T(8,128)} %broadcast_in_dim.239.start_ref.after_ref, ...), custom_call_target="tpu_custom_call" | custom-call | tf_op jit(solution)/shard_map/pallas_call | solution.py:85
  50.4 0.9 %slice.190 = f32[1,256,128]{2,1,0:T(8,128)S(1)} slice(f32[8,256,128]{2,1,0:T(8,128)} %get-tuple-element.18), slice={[0:1], [0:256], [0:128]} | slice | bytes 262144 | tf_op jit(solution)/shard_map/slice | solution.py:180
  51.3 0.9 %fusion.169 = (f32[1,2,256,128]{3,2,1,0:T(8,128)S(1)}, f32[2,256,128]{2,1,0:T(8,128)S(1)}) fusion(f32[1,256,128]{2,1,0:T(8,128)S(1)} %slice.190, f32[1,256,128]{2,1,0:T(8,128)} %bitcast.365), kind=kLoop, calls=%fused_computation.323 | loop fusion | flops 65536 | bytes 786432 | tf_op jit(solution)/shard_map/stack | solution.py:182
  52.2 2.7 %collective-permute-start.3 = (f32[2,256,128]{2,1,0:T(8,128)S(1)}, f32[2,256,128]{2,1,0:T(8,128)S(1)}, u32[]{:S(2)}, u32[]{:S(2)}) collective-permute-start(f32[2,256,128]{2,1,0:T(8,128)S(1)} %get-tuple-element.49), channel_id=1, source_target_pairs={{0,16},{16,0},{1,17},{17,1},{2,18},{18,2},{3,19},{19,3},{4,20},{20... | collective-permute-start | bytes 786440 | tf_op jit(solution)/shard_map/ppermute | solution.py:62
  54.9 11.7 %collective-permute-done.3 = f32[2,256,128]{2,1,0:T(8,128)S(1)} collective-permute-done((f32[2,256,128]{2,1,0:T(8,128)S(1)}, f32[2,256,128]{2,1,0:T(8,128)S(1)}, u32[]{:S(2)}, u32[]{:S(2)}) %collective-permute-start.3) | collective-permute-done | bytes 262176 | tf_op jit(solution)/shard_map/ppermute | solution.py:62
  66.6 0.6 gather_fusion.1
  67.2 0.7 fusion.54.after_ref
  67.9 0.7 fusion.53.start_ref
  68.6 2.6 %shard_map.87 = (f32[8,256,128]{2,1,0:T(8,128)}, f32[256,128]{1,0:T(8,128)}) custom-call(f32[8,128]{1,0:T(8,128)} %get-tuple-element.96.gain_ref, f32[8,128]{1,0:T(8,128)} %get-tuple-element.95.pull_ref, f32[256,128]{1,0:T(8,128)} %fusion.53.start_ref, f32[256,128]{1,0:T(8,128)} %fusion.54.after_ref, f32[8,256,128]{2,1,0:T(8,128)} %copy-done.1), custom_call_target="tpu_custom_call" | custom-call | tf_op jit(solution)/shard_map/pallas_call | solution.py:85
  71.2 3.6 %all-to-all-start.1 = ((f32[8,256,128]{2,1,0:T(8,128)}), f32[8,256,128]{2,1,0:T(8,128)S(1)}, u32[]{:S(2)}, u32[]{:S(2)}) async-start(f32[8,256,128]{2,1,0:T(8,128)} %get-tuple-element.19), calls=%async_computation.1 | async-start | bytes 2097152 | tf_op jit(solution)/shard_map/all_to_all | solution.py:195
  74.8 0.5 fusion.42
  75.3 0.6 slice_bitcast_fusion.3
  75.9 13.3 %all-to-all-done.1 = f32[8,256,128]{2,1,0:T(8,128)S(1)} async-done(((f32[8,256,128]{2,1,0:T(8,128)}), f32[8,256,128]{2,1,0:T(8,128)S(1)}, u32[]{:S(2)}, u32[]{:S(2)}) %all-to-all-start.1) | async-done | bytes 1048608 | tf_op jit(solution)/shard_map/all_to_all | solution.py:195
  89.2 1.0 %copy.71 = f32[1,2048,128]{2,1,0:T(8,128)} copy(f32[1,2048,128]{2,1,0:T(8,128)S(1)} %bitcast.361) | data formatting | bytes 2097152
  (43 shorter events, 0.6 us)
Async XLA Ops:
  0.6 1.6 %copy-start = (f32[1,2048,128]{2,1,0:T(8,128)S(1)}, f32[1,2048,128]{2,1,0:T(8,128)}, u32[]{:S(2)}) copy-start(f32[1,2048,128]{2,1,0:T(8,128)} %param.9) | copy-start | bytes 3145732
  0.6 5.0 %copy-start.3 = (s32[1,4,128]{2,1,0:T(4,128)S(1)}, s32[1,4,128]{2,1,0:T(4,128)}, u32[]{:S(2)}) copy-start(s32[1,4,128]{2,1,0:T(4,128)} %param.11) | copy-start | bytes 6148
  0.7 5.0 %copy-start.2 = (s32[1,4,128]{2,1,0:T(4,128)S(1)}, s32[1,4,128]{2,1,0:T(4,128)}, u32[]{:S(2)}) copy-start(s32[1,4,128]{2,1,0:T(4,128)} %param.10) | copy-start | bytes 6148
  0.7 5.1 %copy-start.4 = (f32[16,128]{1,0:T(8,128)S(1)}, f32[16,128]{1,0:T(8,128)}, u32[]{:S(2)}) copy-start(f32[16,128]{1,0:T(8,128)} %param.15) | copy-start | bytes 24580
  0.7 5.1 %copy-start.5 = (f32[128]{0:T(128)S(1)}, f32[128]{0:T(128)}, u32[]{:S(2)}) copy-start(f32[128]{0:T(128)} %param.14) | copy-start | bytes 1540
  0.7 8.8 %copy-start.7 = (s32[32]{0:T(128)S(1)}, s32[32]{0:T(128)}, u32[]{:S(2)}) copy-start(s32[32]{0:T(128)} %param.12) | copy-start | bytes 388
  2.6 4.6 %collective-permute-start.1 = (f32[2,128]{1,0:T(2,128)S(1)}, f32[2,128]{1,0:T(2,128)S(1)}, u32[]{:S(2)}, u32[]{:S(2)}) collective-permute-start(f32[2,128]{1,0:T(2,128)S(1)} %get-tuple-element.93), channel_id=1, source_target_pairs={{0,1},{1,0},{2,3},{3,2},{4,5},{5,4},{6,7},{7,6},{8,9},{9,8},{10,11... | collective-permute-start | bytes 3080 | tf_op jit(solution)/shard_map/ppermute | solution.py:62
  5.6 3.7 %collective-permute-start = (s32[2,4,128]{2,1,0:T(4,128)S(1)}, s32[2,4,128]{2,1,0:T(4,128)S(1)}, u32[]{:S(2)}, u32[]{:S(2)}) collective-permute-start(s32[2,4,128]{2,1,0:T(4,128)S(1)} %pad_add_fusion), channel_id=1, source_target_pairs={{0,1},{1,0},{2,3},{3,2},{4,5},{5,4},{6,7},{7,6},{8,9},{9,8},{10,11... | collective-permute-start | bytes 12296 | tf_op jit(solution)/shard_map/ppermute | solution.py:62
  9.8 3.3 %copy-start.6 = (f32[128]{0:T(128)S(1)}, f32[128]{0:T(128)}, u32[]{:S(2)}) copy-start(f32[128]{0:T(128)} %param.13) | copy-start | bytes 1540
  13.0 6.7 %collective-permute-start.2 = (bf16[2,512,128]{2,1,0:T(8,128)(2,1)S(1)}, bf16[2,512,128]{2,1,0:T(8,128)(2,1)S(1)}, u32[]{:S(2)}, u32[]{:S(2)}) collective-permute-start(bf16[2,512,128]{2,1,0:T(8,128)(2,1)S(1)} %fusion.48), channel_id=1, source_target_pairs={{0,1},{1,0},{2,3},{3,2},{4,5},{5,4},{6,7},{7,6},{8,9},{9,8},{10,11... | collective-permute-start | bytes 786440 | tf_op jit(solution)/shard_map/ppermute | solution.py:62
  28.4 18.3 %all-to-all-start = ((f32[8,256,128]{2,1,0:T(8,128)}), f32[8,256,128]{2,1,0:T(8,128)S(1)}, u32[]{:S(2)}, u32[]{:S(2)}) async-start(f32[8,256,128]{2,1,0:T(8,128)} %bitcast.87), calls=%async_computation | async-start | bytes 2097152 | tf_op jit(solution)/shard_map/all_to_all | solution.py:170
  46.7 1.0 %copy-start.1 = (f32[8,256,128]{2,1,0:T(8,128)}, f32[8,256,128]{2,1,0:T(8,128)S(1)}, u32[]{:S(2)}) copy-start(f32[8,256,128]{2,1,0:T(8,128)S(1)} %all-to-all-done.pseudo_ref) | copy-start | bytes 3145732
  52.2 14.3 %collective-permute-start.3 = (f32[2,256,128]{2,1,0:T(8,128)S(1)}, f32[2,256,128]{2,1,0:T(8,128)S(1)}, u32[]{:S(2)}, u32[]{:S(2)}) collective-permute-start(f32[2,256,128]{2,1,0:T(8,128)S(1)} %get-tuple-element.49), channel_id=1, source_target_pairs={{0,16},{16,0},{1,17},{17,1},{2,18},{18,2},{3,19},{19,3},{4,20},{20... | collective-permute-start | bytes 786440 | tf_op jit(solution)/shard_map/ppermute | solution.py:62
  71.2 18.0 %all-to-all-start.1 = ((f32[8,256,128]{2,1,0:T(8,128)}), f32[8,256,128]{2,1,0:T(8,128)S(1)}, u32[]{:S(2)}, u32[]{:S(2)}) async-start(f32[8,256,128]{2,1,0:T(8,128)} %get-tuple-element.19), calls=%async_computation.1 | async-start | bytes 2097152 | tf_op jit(solution)/shard_map/all_to_all | solution.py:195

commit v5 on v4

--- a/solution.py
+++ b/solution.py
@@ -178,8 +178,16 @@
     else:
         local_smoothed, local_last = kalman(gains_here, pulls_here, zero_mean, zero_mean, by_year)
         summary = jnp.stack([local_last, local_smoothed[0]])
-        seen = [summary] + [shift_axis(summary, "tg", s) for s in range(1, groups)]
-        ordered = jnp.stack(seen)[(group - jnp.arange(groups)) % groups]
+        if groups == 2:
+            sent = jnp.where(group == 0, local_last, local_smoothed[0])
+            other = shift_axis(sent, "tg", 1)
+            ordered = jnp.where(
+                group == 0, jnp.stack([summary, jnp.stack([other, other])]),
+                jnp.stack([jnp.stack([other, other]), summary]),
+            )
+        else:
+            seen = [summary] + [shift_axis(summary, "tg", s) for s in range(1, groups)]
+            ordered = jnp.stack(seen)[(group - jnp.arange(groups)) % groups]
         carry, from_start, from_after = group_maps(gains, pulls, groups)
         entering = [zero_mean]
         for g in range(groups - 1):

time: 90.5 us -> 83.5 us (0.923)
  waiting for transfers between devices: 48.3 us -> 40.9 us
  other arithmetic: 10.4 us -> 11.4 us
    ppermute x4, waiting for transfers between devices: 21.4 us -> 14 us  [shift_axis(): lax.ppermute(value, axis, [(i, (i + s) % count) for i in range(count)])]
    select_n x1 -> x2, other arithmetic: 0.01 us -> 1.02 us  [the longest x1 0.98 us: body(): sent = jnp.where(group == 0, local_last, local_smoothed[0])]
  transfers between devices with their start and end apart: 6 -> 6, of which waited for: 6 -> 6; matrix products, arithmetic and copies ran while one was open for 3% -> 5% of each run, Pallas kernels for 0% -> 0%
where the time goes in v5:
time: 83.5 us; the launch traced here: 83.1 us
  waiting for transfers between devices  40.9 us (49%)
  starting transfers between devices  13.3 us (16%)
  other arithmetic  11.4 us (14%)
  local copies, waits for them, and re-layouts  8.49 us (10%)
  Pallas kernels  5.29 us (6%)
  matrix products  2.75 us (3%)
  between operations  1.01 us (1%)
    ppermute x4, waiting for transfers between devices, shift_axis(): lax.ppermute(value, axis, [(i, (i + s) % count) for i in range(count)])  14 us
    all_to_all x1, waiting for transfers between devices, body(): lax.all_to_all(pseudo.reshape(span, chunk, topics), 'tl', split_axis=0, c...  13.6 us
    all_to_all x1, waiting for transfers between devices, body(): lax.all_to_all(smoothed, 'tl', split_axis=0, concat_axis=0, tiled=True)  13.3 us
    ppermute x4, starting transfers between devices, shift_axis(): lax.ppermute(value, axis, [(i, (i + s) % count) for i in range(count)])  5.85 us
    pallas_call x2, Pallas kernels, kalman(): pl.pallas_call(kalman_kernel, out_shape=(jax.ShapeDtypeStruct(by_year.sha...  5.29 us
    all_to_all x1, starting transfers between devices, body(): lax.all_to_all(pseudo.reshape(span, chunk, topics), 'tl', split_axis=0, c...  3.87 us
    all_to_all x1, starting transfers between devices, body(): lax.all_to_all(smoothed, 'tl', split_axis=0, concat_axis=0, tiled=True)  3.56 us
    gather x1, local copies, waits for them, and re-layouts, body(): jnp.take(local_beta, jnp.clip(local_columns, 0, own_words - 1), axis=0)  2.81 us
  transfers between devices with their start and end apart: 6, of which 6 were waited for; matrix products, arithmetic and copies ran while one was open for 5% of the time, Pallas kernels for 0%

profile of v5, /device:TPU:0, one launch (start us, length us, event | category | flops | bytes accessed | tf_op | source)
XLA Modules:
  0.0 83.1 jit_solution(106419293909236288)
XLA Ops:
  0.6 0.0 copy-start
  0.6 0.0 copy-start.3
  0.7 0.0 copy-start.2
  0.7 0.0 copy-start.4
  0.7 0.0 copy-start.5
  0.7 0.0 copy-start.7
  0.7 1.6 %reduce_max.54 = f32[128]{0:T(128)S(1)} reduce(f32[1,2048,128]{2,1,0:T(8,128)} %param.9, f32[]{:T(128)} %constant.139.clone.1), dimensions={0,1}, to_apply=%region_2.3 | reduce | flops 262016 | bytes 1049092 | tf_op jit(solution)/shard_map/reduce_max | solution.py:117
  2.3 0.0 copy-done
  2.3 0.3 exponential_reduce_fusion
  2.6 3.1 %collective-permute-start.1 = (f32[2,128]{1,0:T(2,128)S(1)}, f32[2,128]{1,0:T(2,128)S(1)}, u32[]{:S(2)}, u32[]{:S(2)}) collective-permute-start(f32[2,128]{1,0:T(2,128)S(1)} %get-tuple-element.91), channel_id=1, source_target_pairs={{0,1},{1,0},{2,3},{3,2},{4,5},{5,4},{6,7},{7,6},{8,9},{9,8},{10,11... | collective-permute-start | bytes 3080 | tf_op jit(solution)/shard_map/ppermute | solution.py:62
  5.6 0.0 copy-done.3
  5.6 0.0 copy-done.2
  5.6 0.1 collective-permute-start
  5.8 0.0 copy-done.4
  5.8 0.0 copy-done.5
  5.8 0.1 fusion.164
  5.9 0.1 concatenate.60
  6.0 1.2 %collective-permute-done.1 = f32[2,128]{1,0:T(2,128)S(1)} collective-permute-done((f32[2,128]{1,0:T(2,128)S(1)}, f32[2,128]{1,0:T(2,128)S(1)}, u32[]{:S(2)}, u32[]{:S(2)}) %collective-permute-start.1) | collective-permute-done | bytes 1056 | tf_op jit(solution)/shard_map/ppermute | solution.py:62
  7.3 2.1 %collective-permute-done = s32[2,4,128]{2,1,0:T(4,128)S(1)} collective-permute-done((s32[2,4,128]{2,1,0:T(4,128)S(1)}, s32[2,4,128]{2,1,0:T(4,128)S(1)}, u32[]{:S(2)}, u32[]{:S(2)}) %collective-permute-start) | collective-permute-done | bytes 4128 | tf_op jit(solution)/shard_map/ppermute | solution.py:62
  9.3 0.1 fusion.166
  9.5 0.0 copy-done.7
  9.5 0.1 select_reduce_fusion
  9.8 0.0 copy-start.6
  9.8 2.8 %gather_fusion = f32[1024,128]{1,0:T(8,128)S(1)} fusion(f32[2048,128]{1,0:T(8,128)S(1)} %bitcast.360, s32[1024]{0:T(1024)S(1)} %broadcast_clamp_fusion), kind=kCustom, calls=%fused_computation | custom fusion | bytes 1052672 | tf_op jit(solution)/shard_map/jit(_take)/gather | solution.py:143
  12.6 0.3 fusion.48
  13.0 0.1 collective-permute-start.2
  13.1 0.1 fusion.65
  13.2 6.4 %collective-permute-done.2 = bf16[2,512,128]{2,1,0:T(8,128)(2,1)S(1)} collective-permute-done((bf16[2,512,128]{2,1,0:T(8,128)(2,1)S(1)}, bf16[2,512,128]{2,1,0:T(8,128)(2,1)S(1)}, u32[]{:S(2)}, u32[]{:S(2)}) %collective-permute-start.2) | collective-permute-done | bytes 262176 | tf_op jit(solution)/shard_map/ppermute | solution.py:62
  19.7 0.5 fusion.5
  20.2 0.4 fusion.19
  20.6 0.9 %fusion.45 = (f32[8,128]{1,0:T(8,128)S(1)}, bf16[8,128,128]{2,1,0:T(8,128)(2,1)S(1)}) fusion(f32[8,128]{1,0:T(8,128)S(1)} %fusion.19, f32[8,128]{1,0:T(8,128)S(1)} %get-tuple-element.26, f32[8,128]{1,0:T(8,128)S(1)} %fusion.65, f32[8,128]{1,0:T(8,128)S(1)} %get-tuple-element.95, bf16[8,128,128]{2,1,0:T(8,128)(2,1)S(1)} %bitcast.365, f32[128]{0:T(128)S(1)} %log_add_fusion, ...), kind=kLoop, calls=%fused_computation.62 | loop fusion | flops 1965056 | bytes 1071616 | tf_op jit(solution)/shard_map/reduce_sum | solution.py:51
  21.5 0.1 fusion.69
  21.6 0.2 fusion.7
  21.8 0.4 fusion.17
  22.2 0.5 fusion.44
  22.7 0.1 fusion.71
  22.7 0.2 fusion.9
  22.9 0.4 fusion.15
  23.3 0.5 fusion.43
  23.8 0.1 fusion.73
  23.9 0.2 fusion.11
  24.1 0.4 fusion.13
  24.5 1.1 %fusion.41 = bf16[1024,128]{1,0:T(8,128)(2,1)S(1)} fusion(f32[1024,128]{1,0:T(8,128)S(1)} %gather_fusion, bf16[2,512,128]{2,1,0:T(8,128)(2,1)S(1)} %pad_maximum_fusion, f32[1024]{0:T(1024)S(1)} %bitcast.371, f32[1024]{0:T(1024)S(1)} %bitcast.368, f32[128]{0:T(128)S(1)} %log_add_fusion, f32[8,128]{1,0:T(8,128)S(1)} %fusion.73, f32[1024]{0:T(1024)S(1)} %fusion.139, ...), kind=kLoop, calls=%fused_computation.54 | loop fusion | flops 1966080 | bytes 1067520 | tf_op jit(solution)/shard_map/convert_element_type | solution.py:57
  25.6 2.8 %fusion.3 = f32[2048,128]{1,0:T(8,128)} fusion(bf16[1024,128]{1,0:T(8,128)(2,1)S(1)} %fusion.41, s32[1024]{0:T(1024)S(1)} %get-tuple-element.23, f32[1,2048,128]{2,1,0:T(8,128)S(1)} %copy-done), kind=kOutput, calls=%fused_computation.5 | convolution fusion | flops 539230208 | bytes 2363392 | tf_op jit(solution)/shard_map/dot_general | solution.py:158
  28.4 3.9 %all-to-all-start = ((f32[8,256,128]{2,1,0:T(8,128)}), f32[8,256,128]{2,1,0:T(8,128)S(1)}, u32[]{:S(2)}, u32[]{:S(2)}) async-start(f32[8,256,128]{2,1,0:T(8,128)} %bitcast.87), calls=%async_computation | async-start | bytes 2097152 | tf_op jit(solution)/shard_map/all_to_all | solution.py:170
  32.4 0.1 concatenate.59
  32.4 0.6 constant_dynamic-slice_fusion
  33.1 13.6 %all-to-all-done.pseudo_ref = f32[8,256,128]{2,1,0:T(8,128)S(1)} async-done(((f32[8,256,128]{2,1,0:T(8,128)}), f32[8,256,128]{2,1,0:T(8,128)S(1)}, u32[]{:S(2)}, u32[]{:S(2)}) %all-to-all-start) | async-done | bytes 1048608 | tf_op jit(solution)/shard_map/all_to_all | solution.py:170
  46.7 0.7 broadcast_in_dim.238.start_ref.after_ref
  47.4 0.3 copy-done.1
  47.7 2.6 %shard_map.86 = (f32[8,256,128]{2,1,0:T(8,128)}, f32[256,128]{1,0:T(8,128)}) custom-call(f32[8,128]{1,0:T(8,128)} %get-tuple-element.94.gain_ref, f32[8,128]{1,0:T(8,128)} %get-tuple-element.93.pull_ref, f32[256,128]{1,0:T(8,128)} %broadcast_in_dim.238.start_ref.after_ref, f32[256,128]{1,0:T(8,128)} %broadcast_in_dim.238.start_ref.after_ref, ...), custom_call_target="tpu_custom_call" | custom-call | tf_op jit(solution)/shard_map/pallas_call | solution.py:85
  50.4 1.0 %bitcast_select_fusion = f32[256,128]{1,0:T(8,128)S(1)} fusion(f32[256,128]{1,0:T(8,128)} %get-tuple-element.17, pred[]{:T(512)S(6)} %eq.16, f32[8,256,128]{2,1,0:T(8,128)} %get-tuple-element.18), kind=kLoop, calls=%fused_computation.82 | loop fusion | flops 32768 | bytes 393217 | tf_op jit(solution)/shard_map/jit(_where)/select_n | solution.py:182
  51.4 2.6 %collective-permute-start.3 = (f32[256,128]{1,0:T(8,128)S(1)}, f32[256,128]{1,0:T(8,128)S(1)}, u32[]{:S(2)}, u32[]{:S(2)}) collective-permute-start(f32[256,128]{1,0:T(8,128)S(1)} %bitcast_select_fusion), channel_id=1, source_target_pairs={{0,16},{16,0},{1,17},{17,1},{2,18},{18,2},{3,19},{19,3},{4,20},{20... | collective-permute-start | bytes 393224 | tf_op jit(solution)/shard_map/ppermute | solution.py:62
  54.0 0.9 %slice.191 = f32[1,256,128]{2,1,0:T(8,128)S(1)} slice(f32[8,256,128]{2,1,0:T(8,128)} %get-tuple-element.18), slice={[0:1], [0:256], [0:128]} | slice | bytes 262144 | tf_op jit(solution)/shard_map/slice | solution.py:180
  54.9 0.9 %maximum_bitcast_fusion = f32[1,2,256,128]{3,2,1,0:T(8,128)S(1)} fusion(f32[1,256,128]{2,1,0:T(8,128)S(1)} %slice.191, f32[1,256,128]{2,1,0:T(8,128)} %bitcast.366), kind=kLoop, calls=%fused_computation.71 | loop fusion | flops 65536 | bytes 524288 | tf_op jit(solution)/shard_map/stack | solution.py:185
  55.8 4.3 %collective-permute-done.3 = f32[256,128]{1,0:T(8,128)S(1)} collective-permute-done((f32[256,128]{1,0:T(8,128)S(1)}, f32[256,128]{1,0:T(8,128)S(1)}, u32[]{:S(2)}, u32[]{:S(2)}) %collective-permute-start.3) | collective-permute-done | bytes 131104 | tf_op jit(solution)/shard_map/ppermute | solution.py:62
  60.2 0.7 fusion.54.after_ref
  60.9 0.7 fusion.53.start_ref
  61.5 2.6 %shard_map.87 = (f32[8,256,128]{2,1,0:T(8,128)}, f32[256,128]{1,0:T(8,128)}) custom-call(f32[8,128]{1,0:T(8,128)} %get-tuple-element.94.gain_ref, f32[8,128]{1,0:T(8,128)} %get-tuple-element.93.pull_ref, f32[256,128]{1,0:T(8,128)} %fusion.53.start_ref, f32[256,128]{1,0:T(8,128)} %fusion.54.after_ref, f32[8,256,128]{2,1,0:T(8,128)} %copy-done.1), custom_call_target="tpu_custom_call" | custom-call | tf_op jit(solution)/shard_map/pallas_call | solution.py:85
  64.2 3.6 %all-to-all-start.1 = ((f32[8,256,128]{2,1,0:T(8,128)}), f32[8,256,128]{2,1,0:T(8,128)S(1)}, u32[]{:S(2)}, u32[]{:S(2)}) async-start(f32[8,256,128]{2,1,0:T(8,128)} %get-tuple-element.19), calls=%async_computation.1 | async-start | bytes 2097152 | tf_op jit(solution)/shard_map/all_to_all | solution.py:203
  67.7 0.5 fusion.42
  68.2 0.6 slice_bitcast_fusion.3
  68.8 13.3 %all-to-all-done.1 = f32[8,256,128]{2,1,0:T(8,128)S(1)} async-done(((f32[8,256,128]{2,1,0:T(8,128)}), f32[8,256,128]{2,1,0:T(8,128)S(1)}, u32[]{:S(2)}, u32[]{:S(2)}) %all-to-all-start.1) | async-done | bytes 1048608 | tf_op jit(solution)/shard_map/all_to_all | solution.py:203
  82.1 1.0 %copy.71 = f32[1,2048,128]{2,1,0:T(8,128)} copy(f32[1,2048,128]{2,1,0:T(8,128)S(1)} %bitcast.363) | data formatting | bytes 2097152
  (42 shorter events, 0.6 us)
Async XLA Ops:
  0.6 1.6 %copy-start = (f32[1,2048,128]{2,1,0:T(8,128)S(1)}, f32[1,2048,128]{2,1,0:T(8,128)}, u32[]{:S(2)}) copy-start(f32[1,2048,128]{2,1,0:T(8,128)} %param.9) | copy-start | bytes 3145732
  0.6 5.0 %copy-start.3 = (s32[1,4,128]{2,1,0:T(4,128)S(1)}, s32[1,4,128]{2,1,0:T(4,128)}, u32[]{:S(2)}) copy-start(s32[1,4,128]{2,1,0:T(4,128)} %param.11) | copy-start | bytes 6148
  0.7 5.0 %copy-start.2 = (s32[1,4,128]{2,1,0:T(4,128)S(1)}, s32[1,4,128]{2,1,0:T(4,128)}, u32[]{:S(2)}) copy-start(s32[1,4,128]{2,1,0:T(4,128)} %param.10) | copy-start | bytes 6148
  0.7 5.1 %copy-start.4 = (f32[16,128]{1,0:T(8,128)S(1)}, f32[16,128]{1,0:T(8,128)}, u32[]{:S(2)}) copy-start(f32[16,128]{1,0:T(8,128)} %param.15) | copy-start | bytes 24580
  0.7 5.1 %copy-start.5 = (f32[128]{0:T(128)S(1)}, f32[128]{0:T(128)}, u32[]{:S(2)}) copy-start(f32[128]{0:T(128)} %param.14) | copy-start | bytes 1540
  0.7 8.8 %copy-start.7 = (s32[32]{0:T(128)S(1)}, s32[32]{0:T(128)}, u32[]{:S(2)}) copy-start(s32[32]{0:T(128)} %param.12) | copy-start | bytes 388
  2.6 4.6 %collective-permute-start.1 = (f32[2,128]{1,0:T(2,128)S(1)}, f32[2,128]{1,0:T(2,128)S(1)}, u32[]{:S(2)}, u32[]{:S(2)}) collective-permute-start(f32[2,128]{1,0:T(2,128)S(1)} %get-tuple-element.91), channel_id=1, source_target_pairs={{0,1},{1,0},{2,3},{3,2},{4,5},{5,4},{6,7},{7,6},{8,9},{9,8},{10,11... | collective-permute-start | bytes 3080 | tf_op jit(solution)/shard_map/ppermute | solution.py:62
  5.6 3.7 %collective-permute-start = (s32[2,4,128]{2,1,0:T(4,128)S(1)}, s32[2,4,128]{2,1,0:T(4,128)S(1)}, u32[]{:S(2)}, u32[]{:S(2)}) collective-permute-start(s32[2,4,128]{2,1,0:T(4,128)S(1)} %pad_add_fusion), channel_id=1, source_target_pairs={{0,1},{1,0},{2,3},{3,2},{4,5},{5,4},{6,7},{7,6},{8,9},{9,8},{10,11... | collective-permute-start | bytes 12296 | tf_op jit(solution)/shard_map/ppermute | solution.py:62
  9.8 3.3 %copy-start.6 = (f32[128]{0:T(128)S(1)}, f32[128]{0:T(128)}, u32[]{:S(2)}) copy-start(f32[128]{0:T(128)} %param.13) | copy-start | bytes 1540
  13.0 6.7 %collective-permute-start.2 = (bf16[2,512,128]{2,1,0:T(8,128)(2,1)S(1)}, bf16[2,512,128]{2,1,0:T(8,128)(2,1)S(1)}, u32[]{:S(2)}, u32[]{:S(2)}) collective-permute-start(bf16[2,512,128]{2,1,0:T(8,128)(2,1)S(1)} %fusion.48), channel_id=1, source_target_pairs={{0,1},{1,0},{2,3},{3,2},{4,5},{5,4},{6,7},{7,6},{8,9},{9,8},{10,11... | collective-permute-start | bytes 786440 | tf_op jit(solution)/shard_map/ppermute | solution.py:62
  28.4 18.3 %all-to-all-start = ((f32[8,256,128]{2,1,0:T(8,128)}), f32[8,256,128]{2,1,0:T(8,128)S(1)}, u32[]{:S(2)}, u32[]{:S(2)}) async-start(f32[8,256,128]{2,1,0:T(8,128)} %bitcast.87), calls=%async_computation | async-start | bytes 2097152 | tf_op jit(solution)/shard_map/all_to_all | solution.py:170
  46.7 1.0 %copy-start.1 = (f32[8,256,128]{2,1,0:T(8,128)}, f32[8,256,128]{2,1,0:T(8,128)S(1)}, u32[]{:S(2)}) copy-start(f32[8,256,128]{2,1,0:T(8,128)S(1)} %all-to-all-done.pseudo_ref) | copy-start | bytes 3145732
  51.4 8.7 %collective-permute-start.3 = (f32[256,128]{1,0:T(8,128)S(1)}, f32[256,128]{1,0:T(8,128)S(1)}, u32[]{:S(2)}, u32[]{:S(2)}) collective-permute-start(f32[256,128]{1,0:T(8,128)S(1)} %bitcast_select_fusion), channel_id=1, source_target_pairs={{0,16},{16,0},{1,17},{17,1},{2,18},{18,2},{3,19},{19,3},{4,20},{20... | collective-permute-start | bytes 393224 | tf_op jit(solution)/shard_map/ppermute | solution.py:62
  64.2 18.0 %all-to-all-start.1 = ((f32[8,256,128]{2,1,0:T(8,128)}), f32[8,256,128]{2,1,0:T(8,128)S(1)}, u32[]{:S(2)}, u32[]{:S(2)}) async-start(f32[8,256,128]{2,1,0:T(8,128)} %get-tuple-element.19), calls=%async_computation.1 | async-start | bytes 2097152 | tf_op jit(solution)/shard_map/all_to_all | solution.py:203

commit v6 on v5

--- a/solution.py
+++ b/solution.py
@@ -82,8 +82,16 @@
 
 
 def kalman(gains, pulls, start, after, by_year):
+    years, rows, topics = by_year.shape
+    block = 64 if rows % 64 == 0 else rows
+    whole = pl.BlockSpec((years, topics), lambda i: (0, 0))
+    edge = pl.BlockSpec((block, topics), lambda i: (i, 0))
+    stack = pl.BlockSpec((years, block, topics), lambda i: (0, i, 0))
     return pl.pallas_call(
         kalman_kernel,
+        grid=(rows // block,),
+        in_specs=[whole, whole, edge, edge, stack],
+        out_specs=(stack, edge),
         out_shape=(
             jax.ShapeDtypeStruct(by_year.shape, jnp.float32),
             jax.ShapeDtypeStruct(start.shape, jnp.float32),
@@ -139,11 +147,14 @@
 
     flat_columns = all_columns.reshape(-1)
     local_columns = flat_columns - doc_place * own_words
-    inside = (local_columns >= 0) & (local_columns < own_words)
-    picked = jnp.take(local_beta, jnp.clip(local_columns, 0, own_words - 1), axis=0)
-    partial = jnp.where(
-        inside[:, None], to_bf16(picked - normalizer), jnp.zeros((), jnp.bfloat16)
-    ).reshape(doc_devices, local_docs * slot_width, topics)
+    row_words = lax.iota(jnp.int32, own_words)
+    marks = (row_words[:, None] == local_columns[None, :]).astype(jnp.bfloat16)
+    table = to_bf16(local_beta - normalizer)
+    partial = (
+        lax.dot_general(marks, table, (((0,), (0,)), ((), ())), preferred_element_type=jnp.float32)
+        .astype(jnp.bfloat16)
+        .reshape(doc_devices, local_docs * slot_width, topics)
+    )
     looked = partial
     for s in range(1, doc_devices):
         looked = looked + jnp.roll(shift_doc(partial, s), s, axis=0)
@@ -153,8 +164,6 @@
     doc_topics = doc_topics_all[:local_docs]
 
     flat_weighted = weighted.reshape(-1, topics)
-    row_words = lax.iota(jnp.int32, own_words)
-    marks = (row_words[:, None] == local_columns[None, :]).astype(jnp.bfloat16)
     counts = jnp.dot(marks, flat_weighted, preferred_element_type=jnp.float32)
     pseudo = local_beta + jnp.log1p(counts)
 

time: 83.5 us -> 83 us (level)
  local copies, waits for them, and re-layouts: 8.49 us -> 5.62 us
  matrix products: 2.75 us -> 5.1 us
  Pallas kernels: 5.29 us -> 7.1 us
  other arithmetic: 11.4 us -> 9.6 us
    gather x1 -> x0, local copies, waits for them, and re-layouts: 2.81 us -> none  [body(): jnp.take(local_beta, jnp.clip(local_columns, 0, own_words - 1), axis=0)]
    dot_general x0 -> x1, matrix products: none -> 2.35 us  [body(): lax.dot_general(marks, table, (((0,), (0,)), ((), ())), preferred_element...]
    pallas_call x2, Pallas kernels: 5.29 us -> 7.1 us  [kalman(): pl.pallas_call(kalman_kernel, grid=(rows // block,), in_specs=[whole, who...]
where the time goes in v6:
time: 83 us; the launch traced here: 82.6 us
  waiting for transfers between devices  40.9 us (49%)
  starting transfers between devices  13.3 us (16%)
  other arithmetic  9.6 us (12%)
  Pallas kernels  7.1 us (9%)
  local copies, waits for them, and re-layouts  5.62 us (7%)
  matrix products  5.1 us (6%)
  between operations  0.93 us (1%)
    ppermute x4, waiting for transfers between devices, shift_axis(): lax.ppermute(value, axis, [(i, (i + s) % count) for i in range(count)])  14 us
    all_to_all x1, waiting for transfers between devices, body(): lax.all_to_all(pseudo.reshape(span, chunk, topics), 'tl', split_axis=0, c...  13.6 us
    all_to_all x1, waiting for transfers between devices, body(): lax.all_to_all(smoothed, 'tl', split_axis=0, concat_axis=0, tiled=True)  13.3 us
    pallas_call x2, Pallas kernels, kalman(): pl.pallas_call(kalman_kernel, grid=(rows // block,), in_specs=[whole, who...  7.1 us
    ppermute x4, starting transfers between devices, shift_axis(): lax.ppermute(value, axis, [(i, (i + s) % count) for i in range(count)])  5.85 us
    all_to_all x1, starting transfers between devices, body(): lax.all_to_all(pseudo.reshape(span, chunk, topics), 'tl', split_axis=0, c...  3.87 us
    all_to_all x1, starting transfers between devices, body(): lax.all_to_all(smoothed, 'tl', split_axis=0, concat_axis=0, tiled=True)  3.56 us
    dot_general x1, matrix products, body(): counts = jnp.dot(marks, flat_weighted, preferred_element_type=jnp.float32)  2.75 us
  transfers between devices with their start and end apart: 6, of which 6 were waited for; matrix products, arithmetic and copies ran while one was open for 5% of the time, Pallas kernels for 0%

profile of v6, /device:TPU:0, one launch (start us, length us, event | category | flops | bytes accessed | tf_op | source)
XLA Modules:
  0.0 82.6 jit_solution(7640729247107373936)
XLA Ops:
  0.6 0.0 copy-start.1
  0.6 0.0 copy-start.2
  0.7 0.0 copy-start.4
  0.7 0.0 copy-start.3
  0.7 0.0 copy-start.5
  0.7 0.0 copy-start.7
  0.7 1.6 %reduce_max.54 = f32[128]{0:T(128)S(1)} reduce(f32[1,2048,128]{2,1,0:T(8,128)} %param.9, f32[]{:T(128)} %constant.119.clone.1), dimensions={0,1}, to_apply=%region_2.3 | reduce | flops 262016 | bytes 1049092 | tf_op jit(solution)/shard_map/reduce_max | solution.py:125
  2.3 0.0 copy-done.1
  2.3 0.3 fusion.8
  2.6 3.1 %collective-permute-start.1 = (f32[2,128]{1,0:T(2,128)S(1)}, f32[2,128]{1,0:T(2,128)S(1)}, u32[]{:S(2)}, u32[]{:S(2)}) collective-permute-start(f32[2,128]{1,0:T(2,128)S(1)} %get-tuple-element.83), channel_id=1, source_target_pairs={{0,1},{1,0},{2,3},{3,2},{4,5},{5,4},{6,7},{7,6},{8,9},{9,8},{10,11... | collective-permute-start | bytes 3080 | tf_op jit(solution)/shard_map/ppermute | solution.py:62
  5.6 0.0 copy-done.2
  5.6 0.0 copy-done.4
  5.6 0.1 collective-permute-start
  5.8 0.0 copy-done.3
  5.8 0.0 copy-done.5
  5.8 0.1 fusion.157
  5.9 0.1 concatenate.56
  6.0 1.2 %collective-permute-done.1 = f32[2,128]{1,0:T(2,128)S(1)} collective-permute-done((f32[2,128]{1,0:T(2,128)S(1)}, f32[2,128]{1,0:T(2,128)S(1)}, u32[]{:S(2)}, u32[]{:S(2)}) %collective-permute-start.1) | collective-permute-done | bytes 1056 | tf_op jit(solution)/shard_map/ppermute | solution.py:62
  7.3 2.1 %collective-permute-done = s32[2,4,128]{2,1,0:T(4,128)S(1)} collective-permute-done((s32[2,4,128]{2,1,0:T(4,128)S(1)}, s32[2,4,128]{2,1,0:T(4,128)S(1)}, u32[]{:S(2)}, u32[]{:S(2)}) %collective-permute-start) | collective-permute-done | bytes 4128 | tf_op jit(solution)/shard_map/ppermute | solution.py:62
  9.3 0.1 fusion.159
  9.5 0.0 copy-done.7
  9.5 0.1 select_reduce_fusion
  9.6 0.0 copy-start.6
  9.6 2.4 %fusion.6 = bf16[1024,128]{1,0:T(8,128)(2,1)S(1)} fusion(s32[1024]{0:T(1024)S(1)} %fusion.62, f32[1,2048,128]{2,1,0:T(8,128)S(1)} %copy-done.1, f32[128]{0:T(128)S(1)} %log_add_fusion), kind=kOutput, calls=%fused_computation.7 | convolution fusion | flops 539885568 | bytes 1315328 | tf_op jit(solution)/shard_map/dot_general | solution.py:154
  12.0 0.1 collective-permute-start.2
  12.1 0.0 copy-done.6
  12.1 0.1 fusion.64
  12.2 6.4 %collective-permute-done.2 = bf16[2,512,128]{2,1,0:T(8,128)(2,1)S(1)} collective-permute-done((bf16[2,512,128]{2,1,0:T(8,128)(2,1)S(1)}, bf16[2,512,128]{2,1,0:T(8,128)(2,1)S(1)}, u32[]{:S(2)}, u32[]{:S(2)}) %collective-permute-start.2) | collective-permute-done | bytes 262176 | tf_op jit(solution)/shard_map/ppermute | solution.py:62
  18.7 0.2 fusion.45
  18.9 0.4 fusion.47
  19.3 0.5 fusion.52
  19.8 0.1 fusion.66
  19.9 0.2 fusion.41
  20.1 0.4 fusion.43
  20.5 0.5 fusion.51
  21.0 0.1 fusion.68
  21.0 0.2 fusion.37
  21.3 0.4 fusion.39
  21.6 0.5 fusion.50
  22.1 0.1 fusion.70
  22.2 0.2 fusion.29
  22.4 0.4 fusion.32
  22.8 0.5 fusion.35
  23.3 2.8 %fusion.5 = f32[2048,128]{1,0:T(8,128)} fusion(bf16[1024,128]{1,0:T(8,128)(2,1)S(1)} %fusion.35, s32[1024]{0:T(1024)S(1)} %fusion.62, f32[1,2048,128]{2,1,0:T(8,128)S(1)} %copy-done.1), kind=kOutput, calls=%fused_computation.6 | convolution fusion | flops 539230208 | bytes 2363392 | tf_op jit(solution)/shard_map/dot_general | solution.py:167
  26.0 3.9 %all-to-all-start = ((f32[8,256,128]{2,1,0:T(8,128)}), f32[8,256,128]{2,1,0:T(8,128)S(1)}, u32[]{:S(2)}, u32[]{:S(2)}) async-start(f32[8,256,128]{2,1,0:T(8,128)} %bitcast.89), calls=%async_computation | async-start | bytes 2097152 | tf_op jit(solution)/shard_map/all_to_all | solution.py:179
  30.0 0.1 concatenate.55
  30.1 0.6 constant_dynamic-slice_fusion
  30.8 13.6 %all-to-all-done.pseudo_ref = f32[8,256,128]{2,1,0:T(8,128)S(1)} async-done(((f32[8,256,128]{2,1,0:T(8,128)}), f32[8,256,128]{2,1,0:T(8,128)S(1)}, u32[]{:S(2)}, u32[]{:S(2)}) %all-to-all-start) | async-done | bytes 1048608 | tf_op jit(solution)/shard_map/all_to_all | solution.py:179
  44.4 0.7 broadcast_in_dim.191.start_ref.after_ref
  45.1 0.3 copy-done
  45.4 3.6 %shard_map.86 = (f32[8,256,128]{2,1,0:T(8,128)}, f32[256,128]{1,0:T(8,128)}) custom-call(f32[8,128]{1,0:T(8,128)} %get-tuple-element.86.gain_ref, f32[8,128]{1,0:T(8,128)} %get-tuple-element.85.pull_ref, f32[256,128]{1,0:T(8,128)} %broadcast_in_dim.191.start_ref.after_ref, f32[256,128]{1,0:T(8,128)} %broadcast_in_dim.191.start_ref.after_ref, ...), custom_call_target="tpu_custom_call" | custom-call | tf_op jit(solution)/shard_map/pallas_call | solution.py:90
  49.0 1.0 %bitcast_select_fusion = f32[256,128]{1,0:T(8,128)S(1)} fusion(f32[256,128]{1,0:T(8,128)} %get-tuple-element.17, pred[]{:T(512)S(6)} %eq.16, f32[8,256,128]{2,1,0:T(8,128)} %get-tuple-element.18), kind=kLoop, calls=%fused_computation.77 | loop fusion | flops 32768 | bytes 393217 | tf_op jit(solution)/shard_map/jit(_where)/select_n | solution.py:191
  49.9 2.6 %collective-permute-start.3 = (f32[256,128]{1,0:T(8,128)S(1)}, f32[256,128]{1,0:T(8,128)S(1)}, u32[]{:S(2)}, u32[]{:S(2)}) collective-permute-start(f32[256,128]{1,0:T(8,128)S(1)} %bitcast_select_fusion), channel_id=1, source_target_pairs={{0,16},{16,0},{1,17},{17,1},{2,18},{18,2},{3,19},{19,3},{4,20},{20... | collective-permute-start | bytes 393224 | tf_op jit(solution)/shard_map/ppermute | solution.py:62
  52.5 0.9 %slice.191 = f32[1,256,128]{2,1,0:T(8,128)S(1)} slice(f32[8,256,128]{2,1,0:T(8,128)} %get-tuple-element.18), slice={[0:1], [0:256], [0:128]} | slice | bytes 262144 | tf_op jit(solution)/shard_map/slice | solution.py:189
  53.5 0.9 %maximum_bitcast_fusion = f32[1,2,256,128]{3,2,1,0:T(8,128)S(1)} fusion(f32[1,256,128]{2,1,0:T(8,128)S(1)} %slice.191, f32[1,256,128]{2,1,0:T(8,128)} %bitcast.406), kind=kLoop, calls=%fused_computation.65 | loop fusion | flops 65536 | bytes 524288 | tf_op jit(solution)/shard_map/stack | solution.py:194
  54.4 4.3 %collective-permute-done.3 = f32[256,128]{1,0:T(8,128)S(1)} collective-permute-done((f32[256,128]{1,0:T(8,128)S(1)}, f32[256,128]{1,0:T(8,128)S(1)}, u32[]{:S(2)}, u32[]{:S(2)}) %collective-permute-start.3) | collective-permute-done | bytes 131104 | tf_op jit(solution)/shard_map/ppermute | solution.py:62
  58.8 0.7 fusion.54.after_ref
  59.4 0.7 fusion.53.start_ref
  60.1 3.6 %shard_map.87 = (f32[8,256,128]{2,1,0:T(8,128)}, f32[256,128]{1,0:T(8,128)}) custom-call(f32[8,128]{1,0:T(8,128)} %get-tuple-element.86.gain_ref, f32[8,128]{1,0:T(8,128)} %get-tuple-element.85.pull_ref, f32[256,128]{1,0:T(8,128)} %fusion.53.start_ref, f32[256,128]{1,0:T(8,128)} %fusion.54.after_ref, f32[8,256,128]{2,1,0:T(8,128)} %copy-done), custom_call_target="tpu_custom_call" | custom-call | tf_op jit(solution)/shard_map/pallas_call | solution.py:90
  63.6 3.6 %all-to-all-start.1 = ((f32[8,256,128]{2,1,0:T(8,128)}), f32[8,256,128]{2,1,0:T(8,128)S(1)}, u32[]{:S(2)}, u32[]{:S(2)}) async-start(f32[8,256,128]{2,1,0:T(8,128)} %get-tuple-element.19), calls=%async_computation.1 | async-start | bytes 2097152 | tf_op jit(solution)/shard_map/all_to_all | solution.py:212
  67.2 0.5 fusion.49
  67.7 0.6 slice_bitcast_fusion.3
  68.3 13.3 %all-to-all-done.1 = f32[8,256,128]{2,1,0:T(8,128)S(1)} async-done(((f32[8,256,128]{2,1,0:T(8,128)}), f32[8,256,128]{2,1,0:T(8,128)S(1)}, u32[]{:S(2)}, u32[]{:S(2)}) %all-to-all-start.1) | async-done | bytes 1048608 | tf_op jit(solution)/shard_map/all_to_all | solution.py:212
  81.6 1.0 %copy.71 = f32[1,2048,128]{2,1,0:T(8,128)} copy(f32[1,2048,128]{2,1,0:T(8,128)S(1)} %bitcast.403) | data formatting | bytes 2097152
  (29 shorter events, 0.4 us)
Async XLA Ops:
  0.6 1.6 %copy-start.1 = (f32[1,2048,128]{2,1,0:T(8,128)S(1)}, f32[1,2048,128]{2,1,0:T(8,128)}, u32[]{:S(2)}) copy-start(f32[1,2048,128]{2,1,0:T(8,128)} %param.9) | copy-start | bytes 3145732
  0.6 5.0 %copy-start.2 = (s32[1,4,128]{2,1,0:T(4,128)S(1)}, s32[1,4,128]{2,1,0:T(4,128)}, u32[]{:S(2)}) copy-start(s32[1,4,128]{2,1,0:T(4,128)} %param.11) | copy-start | bytes 6148
  0.7 5.0 %copy-start.4 = (s32[1,4,128]{2,1,0:T(4,128)S(1)}, s32[1,4,128]{2,1,0:T(4,128)}, u32[]{:S(2)}) copy-start(s32[1,4,128]{2,1,0:T(4,128)} %param.10) | copy-start | bytes 6148
  0.7 5.1 %copy-start.3 = (f32[16,128]{1,0:T(8,128)S(1)}, f32[16,128]{1,0:T(8,128)}, u32[]{:S(2)}) copy-start(f32[16,128]{1,0:T(8,128)} %param.15) | copy-start | bytes 24580
  0.7 5.1 %copy-start.5 = (f32[128]{0:T(128)S(1)}, f32[128]{0:T(128)}, u32[]{:S(2)}) copy-start(f32[128]{0:T(128)} %param.14) | copy-start | bytes 1540
  0.7 8.8 %copy-start.7 = (s32[32]{0:T(128)S(1)}, s32[32]{0:T(128)}, u32[]{:S(2)}) copy-start(s32[32]{0:T(128)} %param.12) | copy-start | bytes 388
  2.6 4.6 %collective-permute-start.1 = (f32[2,128]{1,0:T(2,128)S(1)}, f32[2,128]{1,0:T(2,128)S(1)}, u32[]{:S(2)}, u32[]{:S(2)}) collective-permute-start(f32[2,128]{1,0:T(2,128)S(1)} %get-tuple-element.83), channel_id=1, source_target_pairs={{0,1},{1,0},{2,3},{3,2},{4,5},{5,4},{6,7},{7,6},{8,9},{9,8},{10,11... | collective-permute-start | bytes 3080 | tf_op jit(solution)/shard_map/ppermute | solution.py:62
  5.6 3.7 %collective-permute-start = (s32[2,4,128]{2,1,0:T(4,128)S(1)}, s32[2,4,128]{2,1,0:T(4,128)S(1)}, u32[]{:S(2)}, u32[]{:S(2)}) collective-permute-start(s32[2,4,128]{2,1,0:T(4,128)S(1)} %pad_add_fusion), channel_id=1, source_target_pairs={{0,1},{1,0},{2,3},{3,2},{4,5},{5,4},{6,7},{7,6},{8,9},{9,8},{10,11... | collective-permute-start | bytes 12296 | tf_op jit(solution)/shard_map/ppermute | solution.py:62
  9.6 2.5 %copy-start.6 = (f32[128]{0:T(128)S(1)}, f32[128]{0:T(128)}, u32[]{:S(2)}) copy-start(f32[128]{0:T(128)} %param.13) | copy-start | bytes 1540
  12.0 6.7 %collective-permute-start.2 = (bf16[2,512,128]{2,1,0:T(8,128)(2,1)S(1)}, bf16[2,512,128]{2,1,0:T(8,128)(2,1)S(1)}, u32[]{:S(2)}, u32[]{:S(2)}) collective-permute-start(bf16[2,512,128]{2,1,0:T(8,128)(2,1)S(1)} %bitcast.405), channel_id=1, source_target_pairs={{0,1},{1,0},{2,3},{3,2},{4,5},{5,4},{6,7},{7,6},{8,9},{9,8},{10,11... | collective-permute-start | bytes 786440 | tf_op jit(solution)/shard_map/ppermute | solution.py:62
  26.0 18.3 %all-to-all-start = ((f32[8,256,128]{2,1,0:T(8,128)}), f32[8,256,128]{2,1,0:T(8,128)S(1)}, u32[]{:S(2)}, u32[]{:S(2)}) async-start(f32[8,256,128]{2,1,0:T(8,128)} %bitcast.89), calls=%async_computation | async-start | bytes 2097152 | tf_op jit(solution)/shard_map/all_to_all | solution.py:179
  44.4 1.0 %copy-start = (f32[8,256,128]{2,1,0:T(8,128)}, f32[8,256,128]{2,1,0:T(8,128)S(1)}, u32[]{:S(2)}) copy-start(f32[8,256,128]{2,1,0:T(8,128)S(1)} %all-to-all-done.pseudo_ref) | copy-start | bytes 3145732
  49.9 8.7 %collective-permute-start.3 = (f32[256,128]{1,0:T(8,128)S(1)}, f32[256,128]{1,0:T(8,128)S(1)}, u32[]{:S(2)}, u32[]{:S(2)}) collective-permute-start(f32[256,128]{1,0:T(8,128)S(1)} %bitcast_select_fusion), channel_id=1, source_target_pairs={{0,16},{16,0},{1,17},{17,1},{2,18},{18,2},{3,19},{19,3},{4,20},{20... | collective-permute-start | bytes 393224 | tf_op jit(solution)/shard_map/ppermute | solution.py:62
  63.6 18.0 %all-to-all-start.1 = ((f32[8,256,128]{2,1,0:T(8,128)}), f32[8,256,128]{2,1,0:T(8,128)S(1)}, u32[]{:S(2)}, u32[]{:S(2)}) async-start(f32[8,256,128]{2,1,0:T(8,128)} %get-tuple-element.19), calls=%async_computation.1 | async-start | bytes 2097152 | tf_op jit(solution)/shard_map/all_to_all | solution.py:212

commit v7 on v6

--- a/solution.py
+++ b/solution.py
@@ -7,6 +7,7 @@
 K = 128
 BLOCK = 128
 EITERS = 4
+PARTS = 2
 
 
 init_variance = 4.0
@@ -83,7 +84,7 @@
 
 def kalman(gains, pulls, start, after, by_year):
     years, rows, topics = by_year.shape
-    block = 64 if rows % 64 == 0 else rows
+    block = rows
     whole = pl.BlockSpec((years, topics), lambda i: (0, 0))
     edge = pl.BlockSpec((block, topics), lambda i: (i, 0))
     stack = pl.BlockSpec((years, block, topics), lambda i: (0, i, 0))
@@ -172,16 +173,26 @@
     pulls = filt_vars / (filt_vars + drift_var)
     pulls = pulls.at[-1].set(0.0)
 
+    span = lax.axis_size("tl")
+    chunk = own_words // span
+    by_dest = pseudo.reshape(span, chunk, topics)
+    parts = PARTS if chunk % (8 * PARTS) == 0 else 1
+    rows = chunk // parts
+    done = [
+        smooth_part(by_dest[:, i * rows:(i + 1) * rows], gains, pulls) for i in range(parts)
+    ]
+    back = jnp.concatenate(done, axis=1)
+    return (back.reshape(own_words, topics)[None], doc_topics[None])
+
+
+def smooth_part(by_dest, gains, pulls):
     groups = lax.axis_size("tg")
-    span = lax.axis_size("tl")
+    span, rows, topics = by_dest.shape
     group = lax.axis_index("tg")
-    chunk = own_words // span
-    by_year = lax.all_to_all(
-        pseudo.reshape(span, chunk, topics), "tl", split_axis=0, concat_axis=0, tiled=True
-    )
+    by_year = lax.all_to_all(by_dest, "tl", split_axis=0, concat_axis=0, tiled=True)
     gains_here = lax.dynamic_slice_in_dim(gains, group * span, span, 0)
     pulls_here = lax.dynamic_slice_in_dim(pulls, group * span, span, 0)
-    zero_mean = jnp.zeros((chunk, topics), jnp.float32)
+    zero_mean = jnp.zeros((rows, topics), jnp.float32)
     if groups == 1:
         smoothed, _ = kalman(gains_here, pulls_here, zero_mean, zero_mean, by_year)
     else:
@@ -209,8 +220,7 @@
         start = jnp.stack(entering)[group]
         after = jnp.stack(leaving)[group]
         smoothed, _ = kalman(gains_here, pulls_here, start, after, by_year)
-    back = lax.all_to_all(smoothed, "tl", split_axis=0, concat_axis=0, tiled=True)
-    return (back.reshape(own_words, topics)[None], doc_topics[None])
+    return lax.all_to_all(smoothed, "tl", split_axis=0, concat_axis=0, tiled=True)
 
 
 def solution(mesh):

time: 83 us -> 91 us (1.096)
  starting transfers between devices: 13.3 us -> 23.4 us
  waiting for transfers between devices: 40.9 us -> 34 us
  local copies, waits for them, and re-layouts: 5.62 us -> 8.1 us
  other arithmetic: 9.6 us -> 11.3 us
  Pallas kernels: 7.1 us -> 8.22 us
  matrix products: 5.1 us -> 4.12 us
    all_to_all x2 -> x4, starting transfers between devices: 7.43 us -> 14.4 us  [the longest x2 7.37 us: smooth_part(): lax.all_to_all(by_dest, 'tl', split_axis=0, concat_axis=0, tiled=True)]
    all_to_all x2 -> x4, waiting for transfers between devices: 26.9 us -> 22.9 us  [the longest x2 13.2 us: smooth_part(): lax.all_to_all(smoothed, 'tl', split_axis=0, concat_axis=0, tiled=True)]
    ppermute x4 -> x5, starting transfers between devices: 5.85 us -> 9.06 us  [shift_axis(): lax.ppermute(value, axis, [(i, (i + s) % count) for i in range(count)])]
    ppermute x4 -> x5, waiting for transfers between devices: 14 us -> 11.1 us  [shift_axis(): lax.ppermute(value, axis, [(i, (i + s) % count) for i in range(count)])]
    slice x1 -> x3, local copies, waits for them, and re-layouts: 0.91 us -> 2.76 us  [the longest x2 1.72 us: smooth_part(): summary = jnp.stack([local_last, local_smoothed[0]])]
    squeeze x2 -> x4, local copies, waits for them, and re-layouts: 1.33 us -> 2.5 us  [the longest x2 1.26 us: smooth_part(): after = jnp.stack(leaving)[group]]
    pallas_call x2 -> x4, Pallas kernels: 7.1 us -> 8.22 us  [kalman(): pl.pallas_call(kalman_kernel, grid=(rows // block,), in_specs=[whole, who...]
    concatenate x0 -> x1, other arithmetic: none -> 1.04 us  [body(): back = jnp.concatenate(done, axis=1)]
  transfers between devices with their start and end apart: 6 -> 9, of which waited for: 6 -> 8; matrix products, arithmetic and copies ran while one was open for 5% -> 9% of each run, Pallas kernels for 0% -> 7%
where the time goes in v7:
time: 91 us; the launch traced here: 90.2 us
  waiting for transfers between devices  34 us (37%)
  starting transfers between devices  23.4 us (26%)
  other arithmetic  11.3 us (12%)
  Pallas kernels  8.22 us (9%)
  local copies, waits for them, and re-layouts  8.1 us (9%)
  matrix products  4.12 us (5%)
  between operations  1 us (1%)
    all_to_all x2, waiting for transfers between devices, smooth_part(): lax.all_to_all(smoothed, 'tl', split_axis=0, concat_axis=0, tiled=True)  13.2 us
    ppermute x5, waiting for transfers between devices, shift_axis(): lax.ppermute(value, axis, [(i, (i + s) % count) for i in range(count)])  11.1 us
    all_to_all x2, waiting for transfers between devices, smooth_part(): lax.all_to_all(by_dest, 'tl', split_axis=0, concat_axis=0, tiled=True)  9.72 us
    ppermute x5, starting transfers between devices, shift_axis(): lax.ppermute(value, axis, [(i, (i + s) % count) for i in range(count)])  9.06 us
    pallas_call x4, Pallas kernels, kalman(): pl.pallas_call(kalman_kernel, grid=(rows // block,), in_specs=[whole, who...  8.22 us
    all_to_all x2, starting transfers between devices, smooth_part(): lax.all_to_all(by_dest, 'tl', split_axis=0, concat_axis=0, tiled=True)  7.37 us
    all_to_all x2, starting transfers between devices, smooth_part(): lax.all_to_all(smoothed, 'tl', split_axis=0, concat_axis=0, tiled=True)  6.99 us
    dot_general x1, matrix products, body(): lax.dot_general(marks, table, (((0,), (0,)), ((), ())), preferred_element...  2.35 us
  transfers between devices with their start and end apart: 9, of which 8 were waited for; matrix products, arithmetic and copies ran while one was open for 9% of the time, Pallas kernels for 7%

profile of v7, /device:TPU:0, one launch (start us, length us, event | category | flops | bytes accessed | tf_op | source)
XLA Modules:
  0.0 90.2 jit_solution(16717657706769554743)
XLA Ops:
  0.7 1.6 %reduce_max.54 = f32[128]{0:T(128)S(1)} reduce(f32[1,2048,128]{2,1,0:T(8,128)} %param.9, f32[]{:T(128)} %constant.119.clone.1), dimensions={0,1}, to_apply=%region_2.3 | reduce | flops 262016 | bytes 1049092 | tf_op jit(solution)/shard_map/reduce_max | solution.py:126
  2.3 0.3 fusion.8
  2.6 3.1 %collective-permute-start.1 = (f32[2,128]{1,0:T(2,128)S(1)}, f32[2,128]{1,0:T(2,128)S(1)}, u32[]{:S(2)}, u32[]{:S(2)}) collective-permute-start(f32[2,128]{1,0:T(2,128)S(1)} %get-tuple-element.95), channel_id=1, source_target_pairs={{0,1},{1,0},{2,3},{3,2},{4,5},{5,4},{6,7},{7,6},{8,9},{9,8},{10,11... | collective-permute-start | bytes 3080 | tf_op jit(solution)/shard_map/ppermute | solution.py:63
  5.6 0.1 collective-permute-start
  5.8 0.1 fusion.162
  5.9 0.1 concatenate.59
  6.0 1.2 %collective-permute-done.1 = f32[2,128]{1,0:T(2,128)S(1)} collective-permute-done((f32[2,128]{1,0:T(2,128)S(1)}, f32[2,128]{1,0:T(2,128)S(1)}, u32[]{:S(2)}, u32[]{:S(2)}) %collective-permute-start.1) | collective-permute-done | bytes 1056 | tf_op jit(solution)/shard_map/ppermute | solution.py:63
  7.3 2.1 %collective-permute-done = s32[2,4,128]{2,1,0:T(4,128)S(1)} collective-permute-done((s32[2,4,128]{2,1,0:T(4,128)S(1)}, s32[2,4,128]{2,1,0:T(4,128)S(1)}, u32[]{:S(2)}, u32[]{:S(2)}) %collective-permute-start) | collective-permute-done | bytes 4128 | tf_op jit(solution)/shard_map/ppermute | solution.py:63
  9.3 0.1 fusion.164
  9.5 0.1 select_reduce_fusion
  9.6 0.0 copy-start.8
  9.6 2.4 %fusion.6 = bf16[1024,128]{1,0:T(8,128)(2,1)S(1)} fusion(s32[1024]{0:T(1024)S(1)} %fusion.67, f32[1,2048,128]{2,1,0:T(8,128)S(1)} %copy-done.2, f32[128]{0:T(128)S(1)} %log_add_fusion), kind=kOutput, calls=%fused_computation.7 | convolution fusion | flops 539885568 | bytes 1315328 | tf_op jit(solution)/shard_map/dot_general | solution.py:155
  12.0 0.1 collective-permute-start.2
  12.1 0.1 fusion.69
  12.2 6.4 %collective-permute-done.2 = bf16[2,512,128]{2,1,0:T(8,128)(2,1)S(1)} collective-permute-done((bf16[2,512,128]{2,1,0:T(8,128)(2,1)S(1)}, bf16[2,512,128]{2,1,0:T(8,128)(2,1)S(1)}, u32[]{:S(2)}, u32[]{:S(2)}) %collective-permute-start.2) | collective-permute-done | bytes 262176 | tf_op jit(solution)/shard_map/ppermute | solution.py:63
  18.7 0.2 fusion.45
  18.9 0.4 fusion.47
  19.3 0.5 fusion.52
  19.8 0.1 fusion.71
  19.9 0.2 fusion.41
  20.1 0.4 fusion.43
  20.5 0.5 fusion.51
  21.0 0.1 fusion.73
  21.0 0.2 fusion.37
  21.3 0.4 fusion.39
  21.6 0.5 fusion.50
  22.1 0.1 fusion.75
  22.2 0.2 fusion.29
  22.4 0.4 fusion.32
  22.8 0.5 fusion.35
  23.3 1.8 %fusion.5 = f32[2048,128]{1,0:T(8,128)S(1)} fusion(bf16[1024,128]{1,0:T(8,128)(2,1)S(1)} %fusion.35, s32[1024]{0:T(1024)S(1)} %fusion.67, f32[1,2048,128]{2,1,0:T(8,128)S(1)} %copy-done.2), kind=kOutput, calls=%fused_computation.6 | convolution fusion | flops 539230208 | bytes 2363392 | tf_op jit(solution)/shard_map/dot_general | solution.py:168
  25.1 1.0 %fusion.167 = (f32[8,128,128]{2,1,0:T(8,128)}, f32[8,128,128]{2,1,0:T(8,128)}) fusion(f32[8,256,128]{2,1,0:T(8,128)S(1)} %bitcast.429), kind=kLoop, calls=%fused_computation.300 | loop fusion | bytes 2097152 | tf_op jit(solution)/shard_map/slice | solution.py:182
  26.1 3.9 %all-to-all-start.2 = ((f32[8,128,128]{2,1,0:T(8,128)}), f32[8,128,128]{2,1,0:T(8,128)S(1)}, u32[]{:S(2)}, u32[]{:S(2)}) async-start(f32[8,128,128]{2,1,0:T(8,128)} %get-tuple-element.51), calls=%async_computation.2 | async-start | bytes 1048576 | tf_op jit(solution)/shard_map/all_to_all | solution.py:192
  30.1 0.1 concatenate.58
  30.2 8.7 %all-to-all-done.2.pseudo_ref = f32[8,128,128]{2,1,0:T(8,128)S(1)} async-done(((f32[8,128,128]{2,1,0:T(8,128)}), f32[8,128,128]{2,1,0:T(8,128)S(1)}, u32[]{:S(2)}, u32[]{:S(2)}) %all-to-all-start.2) | async-done | bytes 524320 | tf_op jit(solution)/shard_map/all_to_all | solution.py:192
  38.8 3.5 %all-to-all-start = ((f32[8,128,128]{2,1,0:T(8,128)}), f32[8,128,128]{2,1,0:T(8,128)S(1)}, u32[]{:S(2)}, u32[]{:S(2)}) async-start(f32[8,128,128]{2,1,0:T(8,128)} %get-tuple-element.50), calls=%async_computation | async-start | bytes 1048576 | tf_op jit(solution)/shard_map/all_to_all | solution.py:192
  42.3 0.6 constant_dynamic-slice_fusion
  43.0 0.6 broadcast_34_start_ref_after_ref.2.start_ref.after_ref
  43.6 2.1 %shard_map.88 = (f32[8,128,128]{2,1,0:T(8,128)}, f32[128,128]{1,0:T(8,128)}) custom-call(f32[8,128]{1,0:T(8,128)} %get-tuple-element.98.gain_ref, f32[8,128]{1,0:T(8,128)} %get-tuple-element.97.pull_ref, f32[128,128]{1,0:T(8,128)} %broadcast_34_start_ref_after_ref.2.start_ref.after_ref, f32[128,128]{1,0:T(8,128)} %broadcast_34_start_ref_after_ref.2.start_ref.after_ref, ...), custom_call_target="tpu_custom_call" | custom-call | tf_op jit(solution)/shard_map/pallas_call | solution.py:91
  45.7 0.9 slice.266
  46.6 0.9 bitcast_select_fusion
  47.5 2.6 %collective-permute-start.4 = (f32[128,128]{1,0:T(8,128)S(1)}, f32[128,128]{1,0:T(8,128)S(1)}, u32[]{:S(2)}, u32[]{:S(2)}) collective-permute-start(f32[128,128]{1,0:T(8,128)S(1)} %bitcast_select_fusion), channel_id=1, source_target_pairs={{0,16},{16,0},{1,17},{17,1},{2,18},{18,2},{3,19},{19,3},{4,20},{20... | collective-permute-start | bytes 196616 | tf_op jit(solution)/shard_map/ppermute | solution.py:63
  50.1 1.1 %all-to-all-done.pseudo_ref = f32[8,128,128]{2,1,0:T(8,128)S(1)} async-done(((f32[8,128,128]{2,1,0:T(8,128)}), f32[8,128,128]{2,1,0:T(8,128)S(1)}, u32[]{:S(2)}, u32[]{:S(2)}) %all-to-all-start) | async-done | bytes 524320 | tf_op jit(solution)/shard_map/all_to_all | solution.py:192
  51.1 0.8 copy-done.1
  51.9 2.1 %shard_map.86 = (f32[8,128,128]{2,1,0:T(8,128)}, f32[128,128]{1,0:T(8,128)}) custom-call(f32[8,128]{1,0:T(8,128)} %get-tuple-element.98.gain_ref, f32[8,128]{1,0:T(8,128)} %get-tuple-element.97.pull_ref, f32[128,128]{1,0:T(8,128)} %broadcast_34_start_ref_after_ref.2.start_ref.after_ref, f32[128,128]{1,0:T(8,128)} %broadcast_34_start_ref_after_ref.2.start_ref.after_ref, ...), custom_call_target="tpu_custom_call" | custom-call | tf_op jit(solution)/shard_map/pallas_call | solution.py:91
  54.0 0.8 slice.243
  54.8 0.9 bitcast_select_fusion.1
  55.7 3.2 %collective-permute-start.3 = (f32[128,128]{1,0:T(8,128)S(1)}, f32[128,128]{1,0:T(8,128)S(1)}, u32[]{:S(2)}, u32[]{:S(2)}) collective-permute-start(f32[128,128]{1,0:T(8,128)S(1)} %bitcast_select_fusion.1), channel_id=1, source_target_pairs={{0,16},{16,0},{1,17},{17,1},{2,18},{18,2},{3,19},{19,3},{4,20},{20... | collective-permute-start | bytes 196616 | tf_op jit(solution)/shard_map/ppermute | solution.py:63
  58.9 0.9 maximum_bitcast_fusion
  59.8 0.0 collective-permute-done.4
  59.8 1.4 %collective-permute-done.3 = f32[128,128]{1,0:T(8,128)S(1)} collective-permute-done((f32[128,128]{1,0:T(8,128)S(1)}, f32[128,128]{1,0:T(8,128)S(1)}, u32[]{:S(2)}, u32[]{:S(2)}) %collective-permute-start.3) | collective-permute-done | bytes 65568 | tf_op jit(solution)/shard_map/ppermute | solution.py:63
  61.3 0.6 fusion.54.after_ref
  61.9 0.6 fusion.53.start_ref
  62.5 2.1 %shard_map.87 = (f32[8,128,128]{2,1,0:T(8,128)}, f32[128,128]{1,0:T(8,128)}) custom-call(f32[8,128]{1,0:T(8,128)} %get-tuple-element.98.gain_ref, f32[8,128]{1,0:T(8,128)} %get-tuple-element.97.pull_ref, f32[128,128]{1,0:T(8,128)} %fusion.53.start_ref, f32[128,128]{1,0:T(8,128)} %fusion.54.after_ref, f32[8,128,128]{2,1,0:T(8,128)} %copy-done.1), custom_call_target="tpu_custom_call" | custom-call | tf_op jit(solution)/shard_map/pallas_call | solution.py:91
  64.6 3.5 %all-to-all-start.1 = ((f32[8,128,128]{2,1,0:T(8,128)}), f32[8,128,128]{2,1,0:T(8,128)S(1)}, u32[]{:S(2)}, u32[]{:S(2)}) async-start(f32[8,128,128]{2,1,0:T(8,128)} %get-tuple-element.22), calls=%async_computation.1 | async-start | bytes 1048576 | tf_op jit(solution)/shard_map/all_to_all | solution.py:223
  68.1 0.6 fusion.56.after_ref
  68.7 0.6 fusion.55.start_ref
  69.3 2.0 %shard_map.89 = (f32[8,128,128]{2,1,0:T(8,128)}, f32[128,128]{1,0:T(8,128)}) custom-call(f32[8,128]{1,0:T(8,128)} %get-tuple-element.98.gain_ref, f32[8,128]{1,0:T(8,128)} %get-tuple-element.97.pull_ref, f32[128,128]{1,0:T(8,128)} %fusion.55.start_ref, f32[128,128]{1,0:T(8,128)} %fusion.56.after_ref, f32[8,128,128]{2,1,0:T(8,128)} %copy-done), custom_call_target="tpu_custom_call" | custom-call | tf_op jit(solution)/shard_map/pallas_call | solution.py:91
  71.4 5.5 %all-to-all-done.1 = f32[8,128,128]{2,1,0:T(8,128)S(1)} async-done(((f32[8,128,128]{2,1,0:T(8,128)}), f32[8,128,128]{2,1,0:T(8,128)S(1)}, u32[]{:S(2)}, u32[]{:S(2)}) %all-to-all-start.1) | async-done | bytes 524320 | tf_op jit(solution)/shard_map/all_to_all | solution.py:223
  76.9 3.5 %all-to-all-start.3 = ((f32[8,128,128]{2,1,0:T(8,128)}), f32[8,128,128]{2,1,0:T(8,128)S(1)}, u32[]{:S(2)}, u32[]{:S(2)}) async-start(f32[8,128,128]{2,1,0:T(8,128)} %get-tuple-element.25), calls=%async_computation.3 | async-start | bytes 1048576 | tf_op jit(solution)/shard_map/all_to_all | solution.py:223
  80.4 0.5 fusion.49
  80.9 0.6 slice_bitcast_fusion.5
  81.5 7.7 %all-to-all-done.3 = f32[8,128,128]{2,1,0:T(8,128)S(1)} async-done(((f32[8,128,128]{2,1,0:T(8,128)}), f32[8,128,128]{2,1,0:T(8,128)S(1)}, u32[]{:S(2)}, u32[]{:S(2)}) %all-to-all-start.3) | async-done | bytes 524320 | tf_op jit(solution)/shard_map/all_to_all | solution.py:223
  89.2 1.0 %pad_maximum_fusion = f32[8,256,128]{2,1,0:T(8,128)} fusion(f32[8,128,128]{2,1,0:T(8,128)S(1)} %all-to-all-done.3, f32[8,128,128]{2,1,0:T(8,128)S(1)} %all-to-all-done.1), kind=kLoop, calls=%fused_computation.8 | loop fusion | flops 262144 | bytes 2097152 | tf_op jit(solution)/shard_map/concatenate | solution.py:184
  (49 shorter events, 0.5 us)
Async XLA Ops:
  0.6 1.6 %copy-start.2 = (f32[1,2048,128]{2,1,0:T(8,128)S(1)}, f32[1,2048,128]{2,1,0:T(8,128)}, u32[]{:S(2)}) copy-start(f32[1,2048,128]{2,1,0:T(8,128)} %param.9) | copy-start | bytes 3145732
  0.6 5.0 %copy-start.4 = (s32[1,4,128]{2,1,0:T(4,128)S(1)}, s32[1,4,128]{2,1,0:T(4,128)}, u32[]{:S(2)}) copy-start(s32[1,4,128]{2,1,0:T(4,128)} %param.11) | copy-start | bytes 6148
  0.7 5.0 %copy-start.6 = (s32[1,4,128]{2,1,0:T(4,128)S(1)}, s32[1,4,128]{2,1,0:T(4,128)}, u32[]{:S(2)}) copy-start(s32[1,4,128]{2,1,0:T(4,128)} %param.10) | copy-start | bytes 6148
  0.7 5.1 %copy-start.5 = (f32[16,128]{1,0:T(8,128)S(1)}, f32[16,128]{1,0:T(8,128)}, u32[]{:S(2)}) copy-start(f32[16,128]{1,0:T(8,128)} %param.15) | copy-start | bytes 24580
  0.7 5.1 %copy-start.7 = (f32[128]{0:T(128)S(1)}, f32[128]{0:T(128)}, u32[]{:S(2)}) copy-start(f32[128]{0:T(128)} %param.14) | copy-start | bytes 1540
  0.7 8.8 %copy-start.9 = (s32[32]{0:T(128)S(1)}, s32[32]{0:T(128)}, u32[]{:S(2)}) copy-start(s32[32]{0:T(128)} %param.12) | copy-start | bytes 388
  2.6 4.6 %collective-permute-start.1 = (f32[2,128]{1,0:T(2,128)S(1)}, f32[2,128]{1,0:T(2,128)S(1)}, u32[]{:S(2)}, u32[]{:S(2)}) collective-permute-start(f32[2,128]{1,0:T(2,128)S(1)} %get-tuple-element.95), channel_id=1, source_target_pairs={{0,1},{1,0},{2,3},{3,2},{4,5},{5,4},{6,7},{7,6},{8,9},{9,8},{10,11... | collective-permute-start | bytes 3080 | tf_op jit(solution)/shard_map/ppermute | solution.py:63
  5.6 3.7 %collective-permute-start = (s32[2,4,128]{2,1,0:T(4,128)S(1)}, s32[2,4,128]{2,1,0:T(4,128)S(1)}, u32[]{:S(2)}, u32[]{:S(2)}) collective-permute-start(s32[2,4,128]{2,1,0:T(4,128)S(1)} %pad_add_fusion), channel_id=1, source_target_pairs={{0,1},{1,0},{2,3},{3,2},{4,5},{5,4},{6,7},{7,6},{8,9},{9,8},{10,11... | collective-permute-start | bytes 12296 | tf_op jit(solution)/shard_map/ppermute | solution.py:63
  9.6 2.5 %copy-start.8 = (f32[128]{0:T(128)S(1)}, f32[128]{0:T(128)}, u32[]{:S(2)}) copy-start(f32[128]{0:T(128)} %param.13) | copy-start | bytes 1540
  12.0 6.7 %collective-permute-start.2 = (bf16[2,512,128]{2,1,0:T(8,128)(2,1)S(1)}, bf16[2,512,128]{2,1,0:T(8,128)(2,1)S(1)}, u32[]{:S(2)}, u32[]{:S(2)}) collective-permute-start(bf16[2,512,128]{2,1,0:T(8,128)(2,1)S(1)} %bitcast.427), channel_id=1, source_target_pairs={{0,1},{1,0},{2,3},{3,2},{4,5},{5,4},{6,7},{7,6},{8,9},{9,8},{10,11... | collective-permute-start | bytes 786440 | tf_op jit(solution)/shard_map/ppermute | solution.py:63
  26.1 12.7 %all-to-all-start.2 = ((f32[8,128,128]{2,1,0:T(8,128)}), f32[8,128,128]{2,1,0:T(8,128)S(1)}, u32[]{:S(2)}, u32[]{:S(2)}) async-start(f32[8,128,128]{2,1,0:T(8,128)} %get-tuple-element.51), calls=%async_computation.2 | async-start | bytes 1048576 | tf_op jit(solution)/shard_map/all_to_all | solution.py:192
  38.8 4.8 %copy-start = (f32[8,128,128]{2,1,0:T(8,128)}, f32[8,128,128]{2,1,0:T(8,128)S(1)}, u32[]{:S(2)}) copy-start(f32[8,128,128]{2,1,0:T(8,128)S(1)} %all-to-all-done.2.pseudo_ref) | copy-start | bytes 1572868
  38.8 12.3 %all-to-all-start = ((f32[8,128,128]{2,1,0:T(8,128)}), f32[8,128,128]{2,1,0:T(8,128)S(1)}, u32[]{:S(2)}, u32[]{:S(2)}) async-start(f32[8,128,128]{2,1,0:T(8,128)} %get-tuple-element.50), calls=%async_computation | async-start | bytes 1048576 | tf_op jit(solution)/shard_map/all_to_all | solution.py:192
  45.7 13.2 %copy-start.3 = (f32[128,128]{1,0:T(8,128)S(1)}, f32[128,128]{1,0:T(8,128)}, u32[]{:S(2)}) copy-start(f32[128,128]{1,0:T(8,128)} %get-tuple-element.23) | copy-start | bytes 196612
  47.5 12.3 %collective-permute-start.4 = (f32[128,128]{1,0:T(8,128)S(1)}, f32[128,128]{1,0:T(8,128)S(1)}, u32[]{:S(2)}, u32[]{:S(2)}) collective-permute-start(f32[128,128]{1,0:T(8,128)S(1)} %bitcast_select_fusion), channel_id=1, source_target_pairs={{0,16},{16,0},{1,17},{17,1},{2,18},{18,2},{3,19},{19,3},{4,20},{20... | collective-permute-start | bytes 196616 | tf_op jit(solution)/shard_map/ppermute | solution.py:63
  51.1 0.8 copy-start.1
  55.7 5.4 %collective-permute-start.3 = (f32[128,128]{1,0:T(8,128)S(1)}, f32[128,128]{1,0:T(8,128)S(1)}, u32[]{:S(2)}, u32[]{:S(2)}) collective-permute-start(f32[128,128]{1,0:T(8,128)S(1)} %bitcast_select_fusion.1), channel_id=1, source_target_pairs={{0,16},{16,0},{1,17},{17,1},{2,18},{18,2},{3,19},{19,3},{4,20},{20... | collective-permute-start | bytes 196616 | tf_op jit(solution)/shard_map/ppermute | solution.py:63
  64.6 12.3 %all-to-all-start.1 = ((f32[8,128,128]{2,1,0:T(8,128)}), f32[8,128,128]{2,1,0:T(8,128)S(1)}, u32[]{:S(2)}, u32[]{:S(2)}) async-start(f32[8,128,128]{2,1,0:T(8,128)} %get-tuple-element.22), calls=%async_computation.1 | async-start | bytes 1048576 | tf_op jit(solution)/shard_map/all_to_all | solution.py:223
  76.9 12.3 %all-to-all-start.3 = ((f32[8,128,128]{2,1,0:T(8,128)}), f32[8,128,128]{2,1,0:T(8,128)S(1)}, u32[]{:S(2)}, u32[]{:S(2)}) async-start(f32[8,128,128]{2,1,0:T(8,128)} %get-tuple-element.25), calls=%async_computation.3 | async-start | bytes 1048576 | tf_op jit(solution)/shard_map/all_to_all | solution.py:223

commit v8 on v7

--- a/solution.py
+++ b/solution.py
@@ -7,7 +7,7 @@
 K = 128
 BLOCK = 128
 EITERS = 4
-PARTS = 2
+PARTS = 1
 
 
 init_variance = 4.0
@@ -130,10 +130,19 @@
     local_docs = slot_ids.shape[0]
     slot_width = slot_ids.shape[1]
 
-    ints = jnp.stack([slot_ids, word_counts[0]])
-    stats = jnp.stack([local_peak, local_total])
-    ints_seen = [ints] + [shift_doc(ints, s) for s in range(1, doc_devices)]
-    stats_seen = jnp.stack([stats] + [shift_doc(stats, s) for s in range(1, doc_devices)])
+    per_docs = local_docs * slot_width
+    message = jnp.concatenate([
+        slot_ids.reshape(-1).astype(jnp.float32),
+        word_counts[0].reshape(-1).astype(jnp.float32),
+        local_peak,
+        local_total,
+    ])
+    seen = jnp.stack([message] + [shift_doc(message, s) for s in range(1, doc_devices)])
+    ints_seen = [
+        seen[:, :2 * per_docs].astype(jnp.int32).reshape(doc_devices, 2, local_docs, slot_width)[i]
+        for i in range(doc_devices)
+    ]
+    stats_seen = seen[:, 2 * per_docs:].reshape(doc_devices, 2, topics)
     all_ids = jnp.concatenate([part[0] for part in ints_seen], axis=0)
     block_match = (all_ids // BLOCK)[..., None] == lax.iota(jnp.int32, block_slot.shape[0])
     all_columns = (

time: 91 us -> 80 us (0.88)
  starting transfers between devices: 23.4 us -> 15.3 us
  waiting for transfers between devices: 34 us -> 37.6 us
  Pallas kernels: 8.22 us -> 5.29 us
  local copies, waits for them, and re-layouts: 8.1 us -> 5.66 us
  other arithmetic: 11.3 us -> 9.63 us
  matrix products: 4.12 us -> 5.11 us
    all_to_all x2 -> x1, waiting for transfers between devices: 9.72 us -> 13.6 us  [smooth_part(): lax.all_to_all(by_dest, 'tl', split_axis=0, concat_axis=0, tiled=True)]
    all_to_all x2 -> x1, starting transfers between devices: 6.99 us -> 3.56 us  [smooth_part(): lax.all_to_all(smoothed, 'tl', split_axis=0, concat_axis=0, tiled=True)]
    all_to_all x2 -> x1, starting transfers between devices: 7.37 us -> 4 us  [smooth_part(): lax.all_to_all(by_dest, 'tl', split_axis=0, concat_axis=0, tiled=True)]
    pallas_call x4 -> x2, Pallas kernels: 8.22 us -> 5.29 us  [kalman(): pl.pallas_call(kalman_kernel, grid=(rows // block,), in_specs=[whole, who...]
    ppermute x5 -> x3, starting transfers between devices: 9.06 us -> 7.74 us  [shift_axis(): lax.ppermute(value, axis, [(i, (i + s) % count) for i in range(count)])]
    concatenate x1, other arithmetic: 1.04 us -> 0.01 us  [body(): jnp.concatenate([slot_ids.reshape(-1).astype(jnp.float32), word_counts[0]...]
    slice x1 -> x2, local copies, waits for them, and re-layouts: 1.04 us -> 0.02 us  [the longest x1 0.01 us: body(): all_ids = jnp.concatenate([part[0] for part in ints_seen], axis=0)]
    dot_general x1, matrix products: 1.77 us -> 2.76 us  [body(): counts = jnp.dot(marks, flat_weighted, preferred_element_type=jnp.float32)]
  transfers between devices with their start and end apart: 9 -> 5, of which waited for: 8 -> 5; matrix products, arithmetic and copies ran while one was open for 9% -> 5% of each run, Pallas kernels for 7% -> 0%
where the time goes in v8:
time: 80 us; the launch traced here: 79.6 us
  waiting for transfers between devices  37.6 us (47%)
  starting transfers between devices  15.3 us (19%)
  other arithmetic  9.63 us (12%)
  local copies, waits for them, and re-layouts  5.66 us (7%)
  Pallas kernels  5.29 us (7%)
  matrix products  5.11 us (6%)
  between operations  1 us (1%)
    all_to_all x1, waiting for transfers between devices, smooth_part(): lax.all_to_all(by_dest, 'tl', split_axis=0, concat_axis=0, tiled=True)  13.6 us
    all_to_all x1, waiting for transfers between devices, smooth_part(): lax.all_to_all(smoothed, 'tl', split_axis=0, concat_axis=0, tiled=True)  13.3 us
    ppermute x3, waiting for transfers between devices, shift_axis(): lax.ppermute(value, axis, [(i, (i + s) % count) for i in range(count)])  10.7 us
    ppermute x3, starting transfers between devices, shift_axis(): lax.ppermute(value, axis, [(i, (i + s) % count) for i in range(count)])  7.74 us
    pallas_call x2, Pallas kernels, kalman(): pl.pallas_call(kalman_kernel, grid=(rows // block,), in_specs=[whole, who...  5.29 us
    all_to_all x1, starting transfers between devices, smooth_part(): lax.all_to_all(by_dest, 'tl', split_axis=0, concat_axis=0, tiled=True)  4 us
    all_to_all x1, starting transfers between devices, smooth_part(): lax.all_to_all(smoothed, 'tl', split_axis=0, concat_axis=0, tiled=True)  3.56 us
    dot_general x1, matrix products, body(): counts = jnp.dot(marks, flat_weighted, preferred_element_type=jnp.float32)  2.76 us
  transfers between devices with their start and end apart: 5, of which 5 were waited for; matrix products, arithmetic and copies ran while one was open for 5% of the time, Pallas kernels for 0%

profile of v8, /device:TPU:0, one launch (start us, length us, event | category | flops | bytes accessed | tf_op | source)
XLA Modules:
  0.0 79.6 jit_solution(2984564221375219366)
XLA Ops:
  0.6 0.0 copy-start.1
  0.6 0.0 copy-start.5
  0.7 0.0 copy-start.6
  0.7 0.0 copy-start.2
  0.7 0.0 copy-start.3
  0.7 0.0 copy-start.7
  0.7 1.6 %reduce_max.54 = f32[128]{0:T(128)S(1)} reduce(f32[1,2048,128]{2,1,0:T(8,128)} %param.9, f32[]{:T(128)} %constant.112.clone.1), dimensions={0,1}, to_apply=%region_0.0 | reduce | flops 262016 | bytes 1049092 | tf_op jit(solution)/shard_map/reduce_max | solution.py:126
  2.3 0.0 copy-done.1
  2.3 0.3 fusion.8
  2.6 0.0 copy-done.5
  2.6 0.0 copy-done.6
  2.6 3.1 %collective-permute-start = (f32[1280]{0:T(1024)S(1)}, f32[1280]{0:T(1024)S(1)}, u32[]{:S(2)}, u32[]{:S(2)}) collective-permute-start(f32[1280]{0:T(1024)S(1)} %pad_maximum_fusion.1), channel_id=1, source_target_pairs={{0,1},{1,0},{2,3},{3,2},{4,5},{5,4},{6,7},{7,6},{8,9},{9,8},{10,11... | collective-permute-start | bytes 15368 | tf_op jit(solution)/shard_map/ppermute | solution.py:63
  5.7 0.0 copy-done.2
  5.7 0.0 copy-done.3
  5.7 0.1 fusion.161
  5.8 0.1 concatenate.59
  5.9 1.4 %collective-permute-done = f32[1280]{0:T(1024)S(1)} collective-permute-done((f32[1280]{0:T(1024)S(1)}, f32[1280]{0:T(1024)S(1)}, u32[]{:S(2)}, u32[]{:S(2)}) %collective-permute-start) | collective-permute-done | bytes 5152 | tf_op jit(solution)/shard_map/ppermute | solution.py:63
  7.4 0.1 fusion.162
  7.6 0.0 copy-done.7
  7.6 0.1 select_reduce_fusion
  7.7 0.0 copy-start.4
  7.7 2.4 %fusion.6 = bf16[1024,128]{1,0:T(8,128)(2,1)S(1)} fusion(s32[1024]{0:T(1024)S(1)} %fusion.64, f32[1,2048,128]{2,1,0:T(8,128)S(1)} %copy-done.1, f32[128]{0:T(128)S(1)} %log_add_fusion), kind=kOutput, calls=%fused_computation.7 | convolution fusion | flops 539885568 | bytes 1315328 | tf_op jit(solution)/shard_map/dot_general | solution.py:164
  10.1 2.1 %collective-permute-start.1 = (bf16[2,512,128]{2,1,0:T(8,128)(2,1)S(1)}, bf16[2,512,128]{2,1,0:T(8,128)(2,1)S(1)}, u32[]{:S(2)}, u32[]{:S(2)}) collective-permute-start(bf16[2,512,128]{2,1,0:T(8,128)(2,1)S(1)} %bitcast.408), channel_id=1, source_target_pairs={{0,1},{1,0},{2,3},{3,2},{4,5},{5,4},{6,7},{7,6},{8,9},{9,8},{10,11... | collective-permute-start | bytes 786440 | tf_op jit(solution)/shard_map/ppermute | solution.py:63
  12.2 0.0 copy-done.4
  12.2 0.1 fusion.66
  12.3 5.0 %collective-permute-done.1 = bf16[2,512,128]{2,1,0:T(8,128)(2,1)S(1)} collective-permute-done((bf16[2,512,128]{2,1,0:T(8,128)(2,1)S(1)}, bf16[2,512,128]{2,1,0:T(8,128)(2,1)S(1)}, u32[]{:S(2)}, u32[]{:S(2)}) %collective-permute-start.1) | collective-permute-done | bytes 262176 | tf_op jit(solution)/shard_map/ppermute | solution.py:63
  17.4 0.2 fusion.45
  17.6 0.4 fusion.47
  18.0 0.5 fusion.52
  18.5 0.1 fusion.68
  18.6 0.2 fusion.41
  18.8 0.4 fusion.43
  19.2 0.5 fusion.51
  19.7 0.1 fusion.70
  19.7 0.2 fusion.37
  20.0 0.4 fusion.39
  20.4 0.5 fusion.50
  20.8 0.1 fusion.72
  20.9 0.2 fusion.29
  21.1 0.4 fusion.32
  21.5 0.5 fusion.35
  22.0 2.8 %fusion.5 = f32[2048,128]{1,0:T(8,128)} fusion(bf16[1024,128]{1,0:T(8,128)(2,1)S(1)} %fusion.35, s32[1024]{0:T(1024)S(1)} %fusion.64, f32[1,2048,128]{2,1,0:T(8,128)S(1)} %copy-done.1), kind=kOutput, calls=%fused_computation.6 | convolution fusion | flops 539230208 | bytes 2363392 | tf_op jit(solution)/shard_map/dot_general | solution.py:177
  24.8 4.0 %all-to-all-start = ((f32[8,256,128]{2,1,0:T(8,128)}), f32[8,256,128]{2,1,0:T(8,128)S(1)}, u32[]{:S(2)}, u32[]{:S(2)}) async-start(f32[8,256,128]{2,1,0:T(8,128)} %bitcast.88), calls=%async_computation | async-start | bytes 2097152 | tf_op jit(solution)/shard_map/all_to_all | solution.py:201
  28.9 0.1 concatenate.58
  28.9 0.6 constant_dynamic-slice_fusion
  29.6 13.6 %all-to-all-done.pseudo_ref = f32[8,256,128]{2,1,0:T(8,128)S(1)} async-done(((f32[8,256,128]{2,1,0:T(8,128)}), f32[8,256,128]{2,1,0:T(8,128)S(1)}, u32[]{:S(2)}, u32[]{:S(2)}) %all-to-all-start) | async-done | bytes 1048608 | tf_op jit(solution)/shard_map/all_to_all | solution.py:201
  43.2 0.0 copy-start
  43.2 0.7 broadcast_in_dim.191.start_ref.after_ref
  43.9 0.3 copy-done
  44.2 2.6 %shard_map.86 = (f32[8,256,128]{2,1,0:T(8,128)}, f32[256,128]{1,0:T(8,128)}) custom-call(f32[8,128]{1,0:T(8,128)} %get-tuple-element.83.gain_ref, f32[8,128]{1,0:T(8,128)} %get-tuple-element.82.pull_ref, f32[256,128]{1,0:T(8,128)} %broadcast_in_dim.191.start_ref.after_ref, f32[256,128]{1,0:T(8,128)} %broadcast_in_dim.191.start_ref.after_ref, ...), custom_call_target="tpu_custom_call" | custom-call | tf_op jit(solution)/shard_map/pallas_call | solution.py:91
  46.9 1.0 %bitcast_select_fusion = f32[256,128]{1,0:T(8,128)S(1)} fusion(f32[256,128]{1,0:T(8,128)} %get-tuple-element.17, pred[]{:T(512)S(6)} %eq.16, f32[8,256,128]{2,1,0:T(8,128)} %get-tuple-element.18), kind=kLoop, calls=%fused_computation.77 | loop fusion | flops 32768 | bytes 393217 | tf_op jit(solution)/shard_map/jit(_where)/select_n | solution.py:211
  47.9 2.6 %collective-permute-start.2 = (f32[256,128]{1,0:T(8,128)S(1)}, f32[256,128]{1,0:T(8,128)S(1)}, u32[]{:S(2)}, u32[]{:S(2)}) collective-permute-start(f32[256,128]{1,0:T(8,128)S(1)} %bitcast_select_fusion), channel_id=1, source_target_pairs={{0,16},{16,0},{1,17},{17,1},{2,18},{18,2},{3,19},{19,3},{4,20},{20... | collective-permute-start | bytes 393224 | tf_op jit(solution)/shard_map/ppermute | solution.py:63
  50.5 0.9 %slice.220 = f32[1,256,128]{2,1,0:T(8,128)S(1)} slice(f32[8,256,128]{2,1,0:T(8,128)} %get-tuple-element.18), slice={[0:1], [0:256], [0:128]} | slice | bytes 262144 | tf_op jit(solution)/shard_map/slice | solution.py:209
  51.4 0.9 %maximum_bitcast_fusion = f32[1,2,256,128]{3,2,1,0:T(8,128)S(1)} fusion(f32[1,256,128]{2,1,0:T(8,128)S(1)} %slice.220, f32[1,256,128]{2,1,0:T(8,128)} %bitcast.409), kind=kLoop, calls=%fused_computation.65 | loop fusion | flops 65536 | bytes 524288 | tf_op jit(solution)/shard_map/stack | solution.py:214
  52.3 4.3 %collective-permute-done.2 = f32[256,128]{1,0:T(8,128)S(1)} collective-permute-done((f32[256,128]{1,0:T(8,128)S(1)}, f32[256,128]{1,0:T(8,128)S(1)}, u32[]{:S(2)}, u32[]{:S(2)}) %collective-permute-start.2) | collective-permute-done | bytes 131104 | tf_op jit(solution)/shard_map/ppermute | solution.py:63
  56.7 0.7 fusion.54.after_ref
  57.4 0.7 fusion.53.start_ref
  58.0 2.6 %shard_map.87 = (f32[8,256,128]{2,1,0:T(8,128)}, f32[256,128]{1,0:T(8,128)}) custom-call(f32[8,128]{1,0:T(8,128)} %get-tuple-element.83.gain_ref, f32[8,128]{1,0:T(8,128)} %get-tuple-element.82.pull_ref, f32[256,128]{1,0:T(8,128)} %fusion.53.start_ref, f32[256,128]{1,0:T(8,128)} %fusion.54.after_ref, f32[8,256,128]{2,1,0:T(8,128)} %copy-done), custom_call_target="tpu_custom_call" | custom-call | tf_op jit(solution)/shard_map/pallas_call | solution.py:91
  60.7 3.6 %all-to-all-start.1 = ((f32[8,256,128]{2,1,0:T(8,128)}), f32[8,256,128]{2,1,0:T(8,128)S(1)}, u32[]{:S(2)}, u32[]{:S(2)}) async-start(f32[8,256,128]{2,1,0:T(8,128)} %get-tuple-element.19), calls=%async_computation.1 | async-start | bytes 2097152 | tf_op jit(solution)/shard_map/all_to_all | solution.py:232
  64.2 0.5 fusion.49
  64.7 0.6 slice_bitcast_fusion.2
  65.3 13.3 %all-to-all-done.1 = f32[8,256,128]{2,1,0:T(8,128)S(1)} async-done(((f32[8,256,128]{2,1,0:T(8,128)}), f32[8,256,128]{2,1,0:T(8,128)S(1)}, u32[]{:S(2)}, u32[]{:S(2)}) %all-to-all-start.1) | async-done | bytes 1048608 | tf_op jit(solution)/shard_map/all_to_all | solution.py:232
  78.6 1.0 %copy.70 = f32[1,2048,128]{2,1,0:T(8,128)} copy(f32[1,2048,128]{2,1,0:T(8,128)S(1)} %bitcast.406) | data formatting | bytes 2097152
  (35 shorter events, 0.5 us)
Async XLA Ops:
  0.6 1.6 %copy-start.1 = (f32[1,2048,128]{2,1,0:T(8,128)S(1)}, f32[1,2048,128]{2,1,0:T(8,128)}, u32[]{:S(2)}) copy-start(f32[1,2048,128]{2,1,0:T(8,128)} %param.9) | copy-start | bytes 3145732
  0.6 1.9 %copy-start.5 = (s32[1,4,128]{2,1,0:T(4,128)S(1)}, s32[1,4,128]{2,1,0:T(4,128)}, u32[]{:S(2)}) copy-start(s32[1,4,128]{2,1,0:T(4,128)} %param.11) | copy-start | bytes 6148
  0.7 1.9 %copy-start.6 = (s32[1,4,128]{2,1,0:T(4,128)S(1)}, s32[1,4,128]{2,1,0:T(4,128)}, u32[]{:S(2)}) copy-start(s32[1,4,128]{2,1,0:T(4,128)} %param.10) | copy-start | bytes 6148
  0.7 5.0 %copy-start.2 = (f32[16,128]{1,0:T(8,128)S(1)}, f32[16,128]{1,0:T(8,128)}, u32[]{:S(2)}) copy-start(f32[16,128]{1,0:T(8,128)} %param.15) | copy-start | bytes 24580
  0.7 5.0 %copy-start.3 = (f32[128]{0:T(128)S(1)}, f32[128]{0:T(128)}, u32[]{:S(2)}) copy-start(f32[128]{0:T(128)} %param.14) | copy-start | bytes 1540
  0.7 6.9 %copy-start.7 = (s32[32]{0:T(128)S(1)}, s32[32]{0:T(128)}, u32[]{:S(2)}) copy-start(s32[32]{0:T(128)} %param.12) | copy-start | bytes 388
  2.6 4.7 %collective-permute-start = (f32[1280]{0:T(1024)S(1)}, f32[1280]{0:T(1024)S(1)}, u32[]{:S(2)}, u32[]{:S(2)}) collective-permute-start(f32[1280]{0:T(1024)S(1)} %pad_maximum_fusion.1), channel_id=1, source_target_pairs={{0,1},{1,0},{2,3},{3,2},{4,5},{5,4},{6,7},{7,6},{8,9},{9,8},{10,11... | collective-permute-start | bytes 15368 | tf_op jit(solution)/shard_map/ppermute | solution.py:63
  7.7 4.5 %copy-start.4 = (f32[128]{0:T(128)S(1)}, f32[128]{0:T(128)}, u32[]{:S(2)}) copy-start(f32[128]{0:T(128)} %param.13) | copy-start | bytes 1540
  10.1 7.2 %collective-permute-start.1 = (bf16[2,512,128]{2,1,0:T(8,128)(2,1)S(1)}, bf16[2,512,128]{2,1,0:T(8,128)(2,1)S(1)}, u32[]{:S(2)}, u32[]{:S(2)}) collective-permute-start(bf16[2,512,128]{2,1,0:T(8,128)(2,1)S(1)} %bitcast.408), channel_id=1, source_target_pairs={{0,1},{1,0},{2,3},{3,2},{4,5},{5,4},{6,7},{7,6},{8,9},{9,8},{10,11... | collective-permute-start | bytes 786440 | tf_op jit(solution)/shard_map/ppermute | solution.py:63
  24.8 18.5 %all-to-all-start = ((f32[8,256,128]{2,1,0:T(8,128)}), f32[8,256,128]{2,1,0:T(8,128)S(1)}, u32[]{:S(2)}, u32[]{:S(2)}) async-start(f32[8,256,128]{2,1,0:T(8,128)} %bitcast.88), calls=%async_computation | async-start | bytes 2097152 | tf_op jit(solution)/shard_map/all_to_all | solution.py:201
  43.2 1.0 %copy-start = (f32[8,256,128]{2,1,0:T(8,128)}, f32[8,256,128]{2,1,0:T(8,128)S(1)}, u32[]{:S(2)}) copy-start(f32[8,256,128]{2,1,0:T(8,128)S(1)} %all-to-all-done.pseudo_ref) | copy-start | bytes 3145732
  47.9 8.7 %collective-permute-start.2 = (f32[256,128]{1,0:T(8,128)S(1)}, f32[256,128]{1,0:T(8,128)S(1)}, u32[]{:S(2)}, u32[]{:S(2)}) collective-permute-start(f32[256,128]{1,0:T(8,128)S(1)} %bitcast_select_fusion), channel_id=1, source_target_pairs={{0,16},{16,0},{1,17},{17,1},{2,18},{18,2},{3,19},{19,3},{4,20},{20... | collective-permute-start | bytes 393224 | tf_op jit(solution)/shard_map/ppermute | solution.py:63
  60.7 18.0 %all-to-all-start.1 = ((f32[8,256,128]{2,1,0:T(8,128)}), f32[8,256,128]{2,1,0:T(8,128)S(1)}, u32[]{:S(2)}, u32[]{:S(2)}) async-start(f32[8,256,128]{2,1,0:T(8,128)} %get-tuple-element.19), calls=%async_computation.1 | async-start | bytes 2097152 | tf_op jit(solution)/shard_map/all_to_all | solution.py:232

commit v9 on v8

--- a/solution.py
+++ b/solution.py
@@ -2,6 +2,7 @@
 import jax.numpy as jnp
 from jax import lax
 from jax.experimental import pallas as pl
+from jax.experimental.pallas import tpu as pltpu
 from jax.sharding import PartitionSpec as P
 
 K = 128
@@ -98,6 +99,55 @@
             jax.ShapeDtypeStruct(start.shape, jnp.float32),
         ),
     )(gains, pulls, start, after, by_year)
+
+
+def first_pass_kernel(gain_ref, pull_ref, weight_ref, pseudo_ref, sent_ref, last_ref, filt_ref):
+    years = pseudo_ref.shape[0]
+    mean = jnp.zeros(pseudo_ref.shape[1:], jnp.float32)
+    for t in range(years):
+        gain_now = gain_ref[pl.ds(t, 1), :]
+        mean = (1.0 - gain_now) * mean + gain_now * pseudo_ref[t]
+        filt_ref[t] = mean
+    last = mean
+    mean = jnp.zeros(pseudo_ref.shape[1:], jnp.float32)
+    for t in reversed(range(years)):
+        pull_now = pull_ref[pl.ds(t, 1), :]
+        mean = pull_now * mean + (1.0 - pull_now) * filt_ref[t]
+    weight = weight_ref[...]
+    sent_ref[...] = weight * last + (1.0 - weight) * mean
+    last_ref[...] = last
+
+
+def second_pass_kernel(
+    gain_ref, pull_ref, weight_ref, reach_ref, other_ref, last_ref, pseudo_ref, out_ref
+):
+    years = pseudo_ref.shape[0]
+    weight = weight_ref[...]
+    other = other_ref[...]
+    mean = (1.0 - weight) * other
+    for t in range(years):
+        gain_now = gain_ref[pl.ds(t, 1), :]
+        mean = (1.0 - gain_now) * mean + gain_now * pseudo_ref[t]
+        out_ref[t] = mean
+    mean = weight * (other + reach_ref[...] * last_ref[...])
+    for t in reversed(range(years)):
+        pull_now = pull_ref[pl.ds(t, 1), :]
+        mean = pull_now * mean + (1.0 - pull_now) * out_ref[t]
+        out_ref[t] = mean
+
+
+def two_group_kalman(gains_here, pulls_here, weight, reach, by_year):
+    years, rows, topics = by_year.shape
+    edge = jax.ShapeDtypeStruct((rows, topics), jnp.float32)
+    sent, last = pl.pallas_call(
+        first_pass_kernel,
+        out_shape=(edge, edge),
+        scratch_shapes=[pltpu.VMEM(by_year.shape, jnp.float32)],
+    )(gains_here, pulls_here, weight, by_year)
+    other = shift_axis(sent, "tg", 1)
+    return pl.pallas_call(
+        second_pass_kernel, out_shape=jax.ShapeDtypeStruct(by_year.shape, jnp.float32)
+    )(gains_here, pulls_here, weight, reach, other, last, by_year)
 
 
 def group_maps(gains, pulls, groups):
@@ -204,6 +254,10 @@
     zero_mean = jnp.zeros((rows, topics), jnp.float32)
     if groups == 1:
         smoothed, _ = kalman(gains_here, pulls_here, zero_mean, zero_mean, by_year)
+    elif groups == 2:
+        carry, from_start, from_after = group_maps(gains, pulls, groups)
+        weight = jnp.where(group == 0, 1.0, 0.0) * jnp.ones((1, topics), jnp.float32)
+        smoothed = two_group_kalman(gains_here, pulls_here, weight, from_start[1:2], by_year)
     else:
         local_smoothed, local_last = kalman(gains_here, pulls_here, zero_mean, zero_mean, by_year)
         summary = jnp.stack([local_last, local_smoothed[0]])

time: 80 us -> 77.9 us (0.974)
  other arithmetic: 9.63 us -> 7.63 us
  waiting for transfers between devices: 37.6 us -> 39 us
  local copies, waits for them, and re-layouts: 5.66 us -> 4.61 us
    ppermute x3, waiting for transfers between devices: 10.7 us -> 12.3 us  [shift_axis(): lax.ppermute(value, axis, [(i, (i + s) % count) for i in range(count)])]
    squeeze x2 -> x0, local copies, waits for them, and re-layouts: 1.33 us -> none  [the longest x1 0.67 us: smooth_part(): after = jnp.stack(leaving)[group]]
    select_n x2 -> x0, other arithmetic: 1.02 us -> none  [the longest x1 0.98 us: smooth_part(): sent = jnp.where(group == 0, local_last, local_smoothed[0])]
    another operation x2 -> x0, other arithmetic: 0.94 us -> none  [smooth_part(): jnp.stack([summary, jnp.stack([other, other])])]
    unnamed x17 -> x19, local copies, waits for them, and re-layouts: 1.31 us -> 2.08 us
  transfers between devices with their start and end apart: 5 -> 5, of which waited for: 5 -> 5; matrix products, arithmetic and copies ran while one was open for 5% -> 4% of each run, Pallas kernels for 0% -> 0%
where the time goes in v9:
time: 77.9 us; the launch traced here: 77.6 us
  waiting for transfers between devices  39 us (50%)
  starting transfers between devices  15.4 us (20%)
  other arithmetic  7.63 us (10%)
  matrix products  5.1 us (7%)
  Pallas kernels  4.84 us (6%)
  local copies, waits for them, and re-layouts  4.61 us (6%)
  between operations  0.95 us (1%)
    all_to_all x1, waiting for transfers between devices, smooth_part(): lax.all_to_all(by_dest, 'tl', split_axis=0, concat_axis=0, tiled=True)  13.4 us
    all_to_all x1, waiting for transfers between devices, smooth_part(): lax.all_to_all(smoothed, 'tl', split_axis=0, concat_axis=0, tiled=True)  13.3 us
    ppermute x3, waiting for transfers between devices, shift_axis(): lax.ppermute(value, axis, [(i, (i + s) % count) for i in range(count)])  12.3 us
    ppermute x3, starting transfers between devices, shift_axis(): lax.ppermute(value, axis, [(i, (i + s) % count) for i in range(count)])  7.74 us
    all_to_all x1, starting transfers between devices, smooth_part(): lax.all_to_all(by_dest, 'tl', split_axis=0, concat_axis=0, tiled=True)  4.13 us
    all_to_all x1, starting transfers between devices, smooth_part(): lax.all_to_all(smoothed, 'tl', split_axis=0, concat_axis=0, tiled=True)  3.56 us
    dot_general x1, matrix products, body(): counts = jnp.dot(marks, flat_weighted, preferred_element_type=jnp.float32)  2.75 us
    pallas_call x1, Pallas kernels, two_group_kalman(): pl.pallas_call(second_pass_kernel, out_shape=jax.ShapeDtypeStruct(by_year...  2.68 us
  transfers between devices with their start and end apart: 5, of which 5 were waited for; matrix products, arithmetic and copies ran while one was open for 4% of the time, Pallas kernels for 0%

profile of v9, /device:TPU:0, one launch (start us, length us, event | category | flops | bytes accessed | tf_op | source)
XLA Modules:
  0.0 77.6 jit_solution(3614546778013127247)
XLA Ops:
  0.6 0.0 copy-start.1
  0.6 0.0 copy-start.6
  0.7 0.0 copy-start.7
  0.7 0.0 copy-start.8
  0.7 1.6 %reduce_max.54 = f32[128]{0:T(128)S(1)} reduce(f32[1,2048,128]{2,1,0:T(8,128)} %param.9, f32[]{:T(128)} %constant.110.clone.1), dimensions={0,1}, to_apply=%region_0.0 | reduce | flops 262016 | bytes 1049092 | tf_op jit(solution)/shard_map/reduce_max | solution.py:176
  2.3 0.0 copy-done.1
  2.3 0.3 fusion.8
  2.6 0.0 copy-done.6
  2.6 0.0 copy-done.7
  2.6 3.1 %collective-permute-start = (f32[1280]{0:T(1024)S(1)}, f32[1280]{0:T(1024)S(1)}, u32[]{:S(2)}, u32[]{:S(2)}) collective-permute-start(f32[1280]{0:T(1024)S(1)} %pad_maximum_fusion.1), channel_id=1, source_target_pairs={{0,1},{1,0},{2,3},{3,2},{4,5},{5,4},{6,7},{7,6},{8,9},{9,8},{10,11... | collective-permute-start | bytes 15368 | tf_op jit(solution)/shard_map/ppermute | solution.py:64
  5.7 1.6 %collective-permute-done = f32[1280]{0:T(1024)S(1)} collective-permute-done((f32[1280]{0:T(1024)S(1)}, f32[1280]{0:T(1024)S(1)}, u32[]{:S(2)}, u32[]{:S(2)}) %collective-permute-start) | collective-permute-done | bytes 5152 | tf_op jit(solution)/shard_map/ppermute | solution.py:64
  7.4 0.1 fusion.163
  7.6 0.0 copy-done.8
  7.6 0.1 select_reduce_fusion
  7.7 0.0 copy-start.5
  7.7 2.4 %fusion.6 = bf16[1024,128]{1,0:T(8,128)(2,1)S(1)} fusion(s32[1024]{0:T(1024)S(1)} %fusion.59, f32[1,2048,128]{2,1,0:T(8,128)S(1)} %copy-done.1, f32[128]{0:T(128)S(1)} %log_add_fusion), kind=kOutput, calls=%fused_computation.7 | convolution fusion | flops 539885568 | bytes 1315328 | tf_op jit(solution)/shard_map/dot_general | solution.py:214
  10.1 2.1 %collective-permute-start.1 = (bf16[2,512,128]{2,1,0:T(8,128)(2,1)S(1)}, bf16[2,512,128]{2,1,0:T(8,128)(2,1)S(1)}, u32[]{:S(2)}, u32[]{:S(2)}) collective-permute-start(bf16[2,512,128]{2,1,0:T(8,128)(2,1)S(1)} %bitcast.369), channel_id=1, source_target_pairs={{0,1},{1,0},{2,3},{3,2},{4,5},{5,4},{6,7},{7,6},{8,9},{9,8},{10,11... | collective-permute-start | bytes 786440 | tf_op jit(solution)/shard_map/ppermute | solution.py:64
  12.2 0.0 copy-done.5
  12.2 0.1 fusion.61
  12.3 5.0 %collective-permute-done.1 = bf16[2,512,128]{2,1,0:T(8,128)(2,1)S(1)} collective-permute-done((bf16[2,512,128]{2,1,0:T(8,128)(2,1)S(1)}, bf16[2,512,128]{2,1,0:T(8,128)(2,1)S(1)}, u32[]{:S(2)}, u32[]{:S(2)}) %collective-permute-start.1) | collective-permute-done | bytes 262176 | tf_op jit(solution)/shard_map/ppermute | solution.py:64
  17.4 0.2 fusion.45
  17.6 0.4 fusion.47
  18.0 0.5 fusion.52
  18.5 0.1 fusion.63
  18.5 0.2 fusion.41
  18.8 0.4 fusion.43
  19.2 0.5 fusion.51
  19.7 0.1 fusion.65
  19.7 0.2 fusion.37
  19.9 0.4 fusion.39
  20.3 0.5 fusion.50
  20.8 0.1 fusion.67
  20.9 0.2 fusion.29
  21.1 0.4 fusion.32
  21.5 0.5 fusion.35
  22.0 2.8 %fusion.5 = f32[2048,128]{1,0:T(8,128)} fusion(bf16[1024,128]{1,0:T(8,128)(2,1)S(1)} %fusion.35, s32[1024]{0:T(1024)S(1)} %fusion.59, f32[1,2048,128]{2,1,0:T(8,128)S(1)} %copy-done.1), kind=kOutput, calls=%fused_computation.6 | convolution fusion | flops 539230208 | bytes 2363392 | tf_op jit(solution)/shard_map/dot_general | solution.py:227
  24.7 0.0 copy-start.3
  24.7 0.0 copy-start.4
  24.7 4.1 %all-to-all-start = ((f32[8,256,128]{2,1,0:T(8,128)}), f32[8,256,128]{2,1,0:T(8,128)S(1)}, u32[]{:S(2)}, u32[]{:S(2)}) async-start(f32[8,256,128]{2,1,0:T(8,128)} %bitcast.107), calls=%async_computation | async-start | bytes 2097152 | tf_op jit(solution)/shard_map/all_to_all | solution.py:251
  28.9 0.0 copy-done.3
  28.9 0.0 copy-done.4
  28.9 0.1 fusion.162
  29.0 0.1 concatenate.59
  29.2 0.1 concatenate.58
  29.3 0.6 constant_dynamic-slice_fusion
  29.9 13.4 %all-to-all-done.pseudo_ref = f32[8,256,128]{2,1,0:T(8,128)S(1)} async-done(((f32[8,256,128]{2,1,0:T(8,128)}), f32[8,256,128]{2,1,0:T(8,128)S(1)}, u32[]{:S(2)}, u32[]{:S(2)}) %all-to-all-start) | async-done | bytes 1048608 | tf_op jit(solution)/shard_map/all_to_all | solution.py:251
  43.3 0.0 copy-start
  43.3 0.5 mul.208.weight_ref
  43.9 0.4 copy-done
  44.3 2.2 %shard_map.86 = (f32[256,128]{1,0:T(8,128)}, f32[256,128]{1,0:T(8,128)}) custom-call(f32[8,128]{1,0:T(8,128)} %get-tuple-element.76.gain_ref, f32[8,128]{1,0:T(8,128)} %get-tuple-element.75.pull_ref, f32[1,128]{1,0:T(1,128)} %mul.208.weight_ref, f32[8,256,128]{2,1,0:T(8,128)} %copy-done), custom_call_target="tpu_custom_call" | custom-call | tf_op jit(solution)/shard_map/pallas_call | solution.py:142
  46.5 2.6 %collective-permute-start.2 = (f32[256,128]{1,0:T(8,128)}, f32[256,128]{1,0:T(8,128)S(1)}, u32[]{:S(2)}, u32[]{:S(2)}) collective-permute-start(f32[256,128]{1,0:T(8,128)} %get-tuple-element.16), channel_id=1, source_target_pairs={{0,16},{16,0},{1,17},{17,1},{2,18},{18,2},{3,19},{19,3},{4,20},{20... | collective-permute-start | bytes 393224 | tf_op jit(solution)/shard_map/ppermute | solution.py:64
  49.1 0.6 slice.202.reach_ref
  49.7 5.7 %collective-permute-done.2.other_ref = f32[256,128]{1,0:T(8,128)S(1)} collective-permute-done((f32[256,128]{1,0:T(8,128)}, f32[256,128]{1,0:T(8,128)S(1)}, u32[]{:S(2)}, u32[]{:S(2)}) %collective-permute-start.2) | collective-permute-done | bytes 131104 | tf_op jit(solution)/shard_map/ppermute | solution.py:64
  55.3 0.0 copy-start.2
  55.3 0.7 copy-done.2
  56.0 2.7 %shard_map.87 = f32[8,256,128]{2,1,0:T(8,128)} custom-call(f32[8,128]{1,0:T(8,128)} %get-tuple-element.76.gain_ref, f32[8,128]{1,0:T(8,128)} %get-tuple-element.75.pull_ref, f32[1,128]{1,0:T(1,128)} %mul.208.weight_ref, f32[1,128]{1,0:T(1,128)} %slice.202.reach_ref, f32[256,128]{1,0:T(8,128)} %copy-done.2, f32[256,128]{1,0:T(8,128)} %get-tuple-element.17.last_ref, ...), custom_call_target="tpu_custom_call" | custom-call | tf_op jit(solution)/shard_map/pallas_call | solution.py:148
  58.7 3.6 %all-to-all-start.1 = ((f32[8,256,128]{2,1,0:T(8,128)}), f32[8,256,128]{2,1,0:T(8,128)S(1)}, u32[]{:S(2)}, u32[]{:S(2)}) async-start(f32[8,256,128]{2,1,0:T(8,128)} %shard_map.87), calls=%async_computation.1 | async-start | bytes 2097152 | tf_op jit(solution)/shard_map/all_to_all | solution.py:286
  62.2 0.5 fusion.49
  62.7 0.6 slice_bitcast_fusion
  63.3 13.3 %all-to-all-done.1 = f32[8,256,128]{2,1,0:T(8,128)S(1)} async-done(((f32[8,256,128]{2,1,0:T(8,128)}), f32[8,256,128]{2,1,0:T(8,128)S(1)}, u32[]{:S(2)}, u32[]{:S(2)}) %all-to-all-start.1) | async-done | bytes 1048608 | tf_op jit(solution)/shard_map/all_to_all | solution.py:286
  76.6 1.0 %copy.62 = f32[1,2048,128]{2,1,0:T(8,128)} copy(f32[1,2048,128]{2,1,0:T(8,128)S(1)} %bitcast.367) | data formatting | bytes 2097152
  (30 shorter events, 0.4 us)
Async XLA Ops:
  0.6 1.6 %copy-start.1 = (f32[1,2048,128]{2,1,0:T(8,128)S(1)}, f32[1,2048,128]{2,1,0:T(8,128)}, u32[]{:S(2)}) copy-start(f32[1,2048,128]{2,1,0:T(8,128)} %param.9) | copy-start | bytes 3145732
  0.6 1.9 %copy-start.6 = (s32[1,4,128]{2,1,0:T(4,128)S(1)}, s32[1,4,128]{2,1,0:T(4,128)}, u32[]{:S(2)}) copy-start(s32[1,4,128]{2,1,0:T(4,128)} %param.11) | copy-start | bytes 6148
  0.7 1.9 %copy-start.7 = (s32[1,4,128]{2,1,0:T(4,128)S(1)}, s32[1,4,128]{2,1,0:T(4,128)}, u32[]{:S(2)}) copy-start(s32[1,4,128]{2,1,0:T(4,128)} %param.10) | copy-start | bytes 6148
  0.7 6.9 %copy-start.8 = (s32[32]{0:T(128)S(1)}, s32[32]{0:T(128)}, u32[]{:S(2)}) copy-start(s32[32]{0:T(128)} %param.12) | copy-start | bytes 388
  2.6 4.7 %collective-permute-start = (f32[1280]{0:T(1024)S(1)}, f32[1280]{0:T(1024)S(1)}, u32[]{:S(2)}, u32[]{:S(2)}) collective-permute-start(f32[1280]{0:T(1024)S(1)} %pad_maximum_fusion.1), channel_id=1, source_target_pairs={{0,1},{1,0},{2,3},{3,2},{4,5},{5,4},{6,7},{7,6},{8,9},{9,8},{10,11... | collective-permute-start | bytes 15368 | tf_op jit(solution)/shard_map/ppermute | solution.py:64
  7.7 4.5 %copy-start.5 = (f32[128]{0:T(128)S(1)}, f32[128]{0:T(128)}, u32[]{:S(2)}) copy-start(f32[128]{0:T(128)} %param.13) | copy-start | bytes 1540
  10.1 7.2 %collective-permute-start.1 = (bf16[2,512,128]{2,1,0:T(8,128)(2,1)S(1)}, bf16[2,512,128]{2,1,0:T(8,128)(2,1)S(1)}, u32[]{:S(2)}, u32[]{:S(2)}) collective-permute-start(bf16[2,512,128]{2,1,0:T(8,128)(2,1)S(1)} %bitcast.369), channel_id=1, source_target_pairs={{0,1},{1,0},{2,3},{3,2},{4,5},{5,4},{6,7},{7,6},{8,9},{9,8},{10,11... | collective-permute-start | bytes 786440 | tf_op jit(solution)/shard_map/ppermute | solution.py:64
  24.7 4.1 %copy-start.3 = (f32[16,128]{1,0:T(8,128)S(1)}, f32[16,128]{1,0:T(8,128)}, u32[]{:S(2)}) copy-start(f32[16,128]{1,0:T(8,128)} %param.15) | copy-start | bytes 24580
  24.7 4.1 %copy-start.4 = (f32[128]{0:T(128)S(1)}, f32[128]{0:T(128)}, u32[]{:S(2)}) copy-start(f32[128]{0:T(128)} %param.14) | copy-start | bytes 1540
  24.7 18.6 %all-to-all-start = ((f32[8,256,128]{2,1,0:T(8,128)}), f32[8,256,128]{2,1,0:T(8,128)S(1)}, u32[]{:S(2)}, u32[]{:S(2)}) async-start(f32[8,256,128]{2,1,0:T(8,128)} %bitcast.107), calls=%async_computation | async-start | bytes 2097152 | tf_op jit(solution)/shard_map/all_to_all | solution.py:251
  43.3 1.0 %copy-start = (f32[8,256,128]{2,1,0:T(8,128)}, f32[8,256,128]{2,1,0:T(8,128)S(1)}, u32[]{:S(2)}) copy-start(f32[8,256,128]{2,1,0:T(8,128)S(1)} %all-to-all-done.pseudo_ref) | copy-start | bytes 3145732
  46.5 8.9 %collective-permute-start.2 = (f32[256,128]{1,0:T(8,128)}, f32[256,128]{1,0:T(8,128)S(1)}, u32[]{:S(2)}, u32[]{:S(2)}) collective-permute-start(f32[256,128]{1,0:T(8,128)} %get-tuple-element.16), channel_id=1, source_target_pairs={{0,16},{16,0},{1,17},{17,1},{2,18},{18,2},{3,19},{19,3},{4,20},{20... | collective-permute-start | bytes 393224 | tf_op jit(solution)/shard_map/ppermute | solution.py:64
  55.3 0.7 copy-start.2
  58.7 18.0 %all-to-all-start.1 = ((f32[8,256,128]{2,1,0:T(8,128)}), f32[8,256,128]{2,1,0:T(8,128)S(1)}, u32[]{:S(2)}, u32[]{:S(2)}) async-start(f32[8,256,128]{2,1,0:T(8,128)} %shard_map.87), calls=%async_computation.1 | async-start | bytes 2097152 | tf_op jit(solution)/shard_map/all_to_all | solution.py:286

commit v10 on v9

--- a/solution.py
+++ b/solution.py
@@ -101,53 +101,64 @@
     )(gains, pulls, start, after, by_year)
 
 
-def first_pass_kernel(gain_ref, pull_ref, weight_ref, pseudo_ref, sent_ref, last_ref, filt_ref):
+def first_pass_kernel(gain_ref, pull_ref, pseudo_ref, sent_ref, last_ref, filt_ref):
     years = pseudo_ref.shape[0]
+    group = lax.axis_index("tg")
+    base = group * years
     mean = jnp.zeros(pseudo_ref.shape[1:], jnp.float32)
     for t in range(years):
-        gain_now = gain_ref[pl.ds(t, 1), :]
+        gain_now = gain_ref[pl.ds(base + t, 1), :]
         mean = (1.0 - gain_now) * mean + gain_now * pseudo_ref[t]
         filt_ref[t] = mean
     last = mean
     mean = jnp.zeros(pseudo_ref.shape[1:], jnp.float32)
     for t in reversed(range(years)):
-        pull_now = pull_ref[pl.ds(t, 1), :]
+        pull_now = pull_ref[pl.ds(base + t, 1), :]
         mean = pull_now * mean + (1.0 - pull_now) * filt_ref[t]
-    weight = weight_ref[...]
+    weight = jnp.where(group == 0, 1.0, 0.0)
     sent_ref[...] = weight * last + (1.0 - weight) * mean
     last_ref[...] = last
 
 
-def second_pass_kernel(
-    gain_ref, pull_ref, weight_ref, reach_ref, other_ref, last_ref, pseudo_ref, out_ref
-):
+def second_pass_kernel(gain_ref, pull_ref, other_ref, last_ref, pseudo_ref, out_ref):
     years = pseudo_ref.shape[0]
-    weight = weight_ref[...]
+    group = lax.axis_index("tg")
+    base = group * years
+    weight = jnp.where(group == 0, 1.0, 0.0)
+    carry = jnp.ones((1, gain_ref.shape[1]), jnp.float32)
+    responses = []
+    for t in range(years):
+        carry = (1.0 - gain_ref[pl.ds(years + t, 1), :]) * carry
+        responses.append(carry)
+    reach = jnp.zeros_like(carry)
+    for t in reversed(range(years)):
+        pull_now = pull_ref[pl.ds(years + t, 1), :]
+        reach = pull_now * reach + (1.0 - pull_now) * responses[t]
     other = other_ref[...]
     mean = (1.0 - weight) * other
     for t in range(years):
-        gain_now = gain_ref[pl.ds(t, 1), :]
+        gain_now = gain_ref[pl.ds(base + t, 1), :]
         mean = (1.0 - gain_now) * mean + gain_now * pseudo_ref[t]
         out_ref[t] = mean
-    mean = weight * (other + reach_ref[...] * last_ref[...])
+    mean = weight * (other + reach * last_ref[...])
     for t in reversed(range(years)):
-        pull_now = pull_ref[pl.ds(t, 1), :]
+        pull_now = pull_ref[pl.ds(base + t, 1), :]
         mean = pull_now * mean + (1.0 - pull_now) * out_ref[t]
         out_ref[t] = mean
 
 
-def two_group_kalman(gains_here, pulls_here, weight, reach, by_year):
+def two_group_kalman(gains, pulls, by_year):
     years, rows, topics = by_year.shape
     edge = jax.ShapeDtypeStruct((rows, topics), jnp.float32)
     sent, last = pl.pallas_call(
         first_pass_kernel,
         out_shape=(edge, edge),
         scratch_shapes=[pltpu.VMEM(by_year.shape, jnp.float32)],
-    )(gains_here, pulls_here, weight, by_year)
+    )(gains, pulls, by_year)
     other = shift_axis(sent, "tg", 1)
     return pl.pallas_call(
         second_pass_kernel, out_shape=jax.ShapeDtypeStruct(by_year.shape, jnp.float32)
-    )(gains_here, pulls_here, weight, reach, other, last, by_year)
+    )(gains, pulls, other, last, by_year)
 
 
 def group_maps(gains, pulls, groups):
@@ -255,9 +266,7 @@
     if groups == 1:
         smoothed, _ = kalman(gains_here, pulls_here, zero_mean, zero_mean, by_year)
     elif groups == 2:
-        carry, from_start, from_after = group_maps(gains, pulls, groups)
-        weight = jnp.where(group == 0, 1.0, 0.0) * jnp.ones((1, topics), jnp.float32)
-        smoothed = two_group_kalman(gains_here, pulls_here, weight, from_start[1:2], by_year)
+        smoothed = two_group_kalman(gains, pulls, by_year)
     else:
         local_smoothed, local_last = kalman(gains_here, pulls_here, zero_mean, zero_mean, by_year)
         summary = jnp.stack([local_last, local_smoothed[0]])

time: 77.9 us -> 78 us (level)
    concatenate x2, local copies, waits for them, and re-layouts: 0.12 us -> 1.29 us  [variance_tables(): lax.scan(forward_step, start_var, obs_precision, unroll=True)]
    unnamed x19 -> x21, local copies, waits for them, and re-layouts: 2.08 us -> 2.63 us
where the time goes in v10:
time: 78 us; the launch traced here: 77.6 us
  waiting for transfers between devices  39.1 us (50%)
  starting transfers between devices  15.4 us (20%)
  other arithmetic  7.6 us (10%)
  matrix products  5.1 us (7%)
  Pallas kernels  4.87 us (6%)
  local copies, waits for them, and re-layouts  4.59 us (6%)
  between operations  0.94 us (1%)
    all_to_all x1, waiting for transfers between devices, smooth_part(): lax.all_to_all(smoothed, 'tl', split_axis=0, concat_axis=0, tiled=True)  13.3 us
    ppermute x3, waiting for transfers between devices, shift_axis(): lax.ppermute(value, axis, [(i, (i + s) % count) for i in range(count)])  12.9 us
    all_to_all x1, waiting for transfers between devices, smooth_part(): lax.all_to_all(by_dest, 'tl', split_axis=0, concat_axis=0, tiled=True)  12.9 us
    ppermute x3, starting transfers between devices, shift_axis(): lax.ppermute(value, axis, [(i, (i + s) % count) for i in range(count)])  7.74 us
    all_to_all x1, starting transfers between devices, smooth_part(): lax.all_to_all(by_dest, 'tl', split_axis=0, concat_axis=0, tiled=True)  4.13 us
    all_to_all x1, starting transfers between devices, smooth_part(): lax.all_to_all(smoothed, 'tl', split_axis=0, concat_axis=0, tiled=True)  3.56 us
    dot_general x1, matrix products, body(): counts = jnp.dot(marks, flat_weighted, preferred_element_type=jnp.float32)  2.75 us
    pallas_call x1, Pallas kernels, two_group_kalman(): pl.pallas_call(second_pass_kernel, out_shape=jax.ShapeDtypeStruct(by_year...  2.69 us
  transfers between devices with their start and end apart: 5, of which 5 were waited for; matrix products, arithmetic and copies ran while one was open for 4% of the time, Pallas kernels for 0%

profile of v10, /device:TPU:0, one launch (start us, length us, event | category | flops | bytes accessed | tf_op | source)
XLA Modules:
  0.0 77.6 jit_solution(6903965784372379879)
XLA Ops:
  0.6 0.0 copy-start.1
  0.6 0.0 copy-start.7
  0.7 0.0 copy-start.8
  0.7 0.0 copy-start.9
  0.7 1.6 %reduce_max.54 = f32[128]{0:T(128)S(1)} reduce(f32[1,2048,128]{2,1,0:T(8,128)} %param.9, f32[]{:T(128)} %constant.98.clone.1), dimensions={0,1}, to_apply=%region_0.0 | reduce | flops 262016 | bytes 1049092 | tf_op jit(solution)/shard_map/reduce_max | solution.py:187
  2.3 0.0 copy-done.1
  2.3 0.3 fusion.8
  2.6 0.0 copy-done.7
  2.6 0.0 copy-done.8
  2.6 3.1 %collective-permute-start = (f32[1280]{0:T(1024)S(1)}, f32[1280]{0:T(1024)S(1)}, u32[]{:S(2)}, u32[]{:S(2)}) collective-permute-start(f32[1280]{0:T(1024)S(1)} %pad_maximum_fusion.1), channel_id=1, source_target_pairs={{0,1},{1,0},{2,3},{3,2},{4,5},{5,4},{6,7},{7,6},{8,9},{9,8},{10,11... | collective-permute-start | bytes 15368 | tf_op jit(solution)/shard_map/ppermute | solution.py:64
  5.7 1.6 %collective-permute-done = f32[1280]{0:T(1024)S(1)} collective-permute-done((f32[1280]{0:T(1024)S(1)}, f32[1280]{0:T(1024)S(1)}, u32[]{:S(2)}, u32[]{:S(2)}) %collective-permute-start) | collective-permute-done | bytes 5152 | tf_op jit(solution)/shard_map/ppermute | solution.py:64
  7.4 0.1 fusion.156
  7.6 0.0 copy-done.9
  7.6 0.1 select_reduce_fusion
  7.7 0.0 copy-start.6
  7.7 2.4 %fusion.6 = bf16[1024,128]{1,0:T(8,128)(2,1)S(1)} fusion(s32[1024]{0:T(1024)S(1)} %fusion.59, f32[1,2048,128]{2,1,0:T(8,128)S(1)} %copy-done.1, f32[128]{0:T(128)S(1)} %log_add_fusion), kind=kOutput, calls=%fused_computation.7 | convolution fusion | flops 539885568 | bytes 1315328 | tf_op jit(solution)/shard_map/dot_general | solution.py:225
  10.1 2.1 %collective-permute-start.1 = (bf16[2,512,128]{2,1,0:T(8,128)(2,1)S(1)}, bf16[2,512,128]{2,1,0:T(8,128)(2,1)S(1)}, u32[]{:S(2)}, u32[]{:S(2)}) collective-permute-start(bf16[2,512,128]{2,1,0:T(8,128)(2,1)S(1)} %bitcast.282), channel_id=1, source_target_pairs={{0,1},{1,0},{2,3},{3,2},{4,5},{5,4},{6,7},{7,6},{8,9},{9,8},{10,11... | collective-permute-start | bytes 786440 | tf_op jit(solution)/shard_map/ppermute | solution.py:64
  12.2 0.0 copy-done.6
  12.2 0.1 fusion.61
  12.3 5.0 %collective-permute-done.1 = bf16[2,512,128]{2,1,0:T(8,128)(2,1)S(1)} collective-permute-done((bf16[2,512,128]{2,1,0:T(8,128)(2,1)S(1)}, bf16[2,512,128]{2,1,0:T(8,128)(2,1)S(1)}, u32[]{:S(2)}, u32[]{:S(2)}) %collective-permute-start.1) | collective-permute-done | bytes 262176 | tf_op jit(solution)/shard_map/ppermute | solution.py:64
  17.4 0.2 fusion.45
  17.6 0.4 fusion.47
  18.0 0.5 fusion.52
  18.5 0.1 fusion.63
  18.5 0.2 fusion.41
  18.8 0.4 fusion.43
  19.2 0.5 fusion.51
  19.7 0.1 fusion.65
  19.7 0.2 fusion.37
  19.9 0.4 fusion.39
  20.3 0.5 fusion.50
  20.8 0.1 fusion.67
  20.9 0.2 fusion.29
  21.1 0.4 fusion.32
  21.5 0.5 fusion.35
  22.0 2.8 %fusion.5 = f32[2048,128]{1,0:T(8,128)} fusion(bf16[1024,128]{1,0:T(8,128)(2,1)S(1)} %fusion.35, s32[1024]{0:T(1024)S(1)} %fusion.59, f32[1,2048,128]{2,1,0:T(8,128)S(1)} %copy-done.1), kind=kOutput, calls=%fused_computation.6 | convolution fusion | flops 539230208 | bytes 2363392 | tf_op jit(solution)/shard_map/dot_general | solution.py:238
  24.7 0.0 copy-start.4
  24.7 0.0 copy-start.5
  24.7 4.1 %all-to-all-start = ((f32[8,256,128]{2,1,0:T(8,128)}), f32[8,256,128]{2,1,0:T(8,128)S(1)}, u32[]{:S(2)}, u32[]{:S(2)}) async-start(f32[8,256,128]{2,1,0:T(8,128)} %bitcast.88), calls=%async_computation | async-start | bytes 2097152 | tf_op jit(solution)/shard_map/all_to_all | solution.py:262
  28.9 0.0 copy-done.4
  28.9 0.0 copy-done.5
  28.9 0.1 fusion.155
  29.0 0.1 concatenate.59
  29.2 0.0 copy-start.3
  29.2 1.2 %concatenate.58.gain_ref = f32[16,128]{1,0:T(8,128)} concatenate(f32[1,128]{1,0:T(1,128)S(1)} %add_divide_fusion.32, f32[1,128]{1,0:T(1,128)S(1)} %get-tuple-element.54, f32[1,128]{1,0:T(1,128)S(1)} %get-tuple-element.53, f32[1,128]{1,0:T(1,128)S(1)} %get-tuple-element.52, f32[1,128]{1,0:T(1,128)S(1)} %get-tuple-element.51, f32[1,128]{1,0:T(1,128)S(1)} %get-tuple-element.50, ...), dimensions={0} | concatenate | bytes 16384 | tf_op jit(solution)/shard_map/concatenate | solution.py:26
  30.5 12.9 %all-to-all-done.pseudo_ref = f32[8,256,128]{2,1,0:T(8,128)S(1)} async-done(((f32[8,256,128]{2,1,0:T(8,128)}), f32[8,256,128]{2,1,0:T(8,128)S(1)}, u32[]{:S(2)}, u32[]{:S(2)}) %all-to-all-start) | async-done | bytes 1048608 | tf_op jit(solution)/shard_map/all_to_all | solution.py:262
  43.3 0.0 copy-done.3
  43.3 0.0 copy-start
  43.3 1.0 %copy-done = f32[8,256,128]{2,1,0:T(8,128)} copy-done((f32[8,256,128]{2,1,0:T(8,128)}, f32[8,256,128]{2,1,0:T(8,128)S(1)}, u32[]{:S(2)}) %copy-start) | copy-done | bytes 1048600
  44.3 2.2 %shard_map.86 = (f32[256,128]{1,0:T(8,128)}, f32[256,128]{1,0:T(8,128)}) custom-call(f32[16,128]{1,0:T(8,128)} %concatenate.58.gain_ref, f32[16,128]{1,0:T(8,128)} %copy-done.3, f32[8,256,128]{2,1,0:T(8,128)} %copy-done), custom_call_target="tpu_custom_call" | custom-call | tf_op jit(solution)/shard_map/pallas_call | solution.py:153
  46.5 2.6 %collective-permute-start.2 = (f32[256,128]{1,0:T(8,128)}, f32[256,128]{1,0:T(8,128)S(1)}, u32[]{:S(2)}, u32[]{:S(2)}) collective-permute-start(f32[256,128]{1,0:T(8,128)} %get-tuple-element.16), channel_id=1, source_target_pairs={{0,16},{16,0},{1,17},{17,1},{2,18},{18,2},{3,19},{19,3},{4,20},{20... | collective-permute-start | bytes 393224 | tf_op jit(solution)/shard_map/ppermute | solution.py:64
  49.1 6.3 %collective-permute-done.2.other_ref = f32[256,128]{1,0:T(8,128)S(1)} collective-permute-done((f32[256,128]{1,0:T(8,128)}, f32[256,128]{1,0:T(8,128)S(1)}, u32[]{:S(2)}, u32[]{:S(2)}) %collective-permute-start.2) | collective-permute-done | bytes 131104 | tf_op jit(solution)/shard_map/ppermute | solution.py:64
  55.4 0.0 copy-start.2
  55.4 0.7 copy-done.2
  56.0 2.7 %shard_map.87 = f32[8,256,128]{2,1,0:T(8,128)} custom-call(f32[16,128]{1,0:T(8,128)} %concatenate.58.gain_ref, f32[16,128]{1,0:T(8,128)} %copy-done.3, f32[256,128]{1,0:T(8,128)} %copy-done.2, f32[256,128]{1,0:T(8,128)} %get-tuple-element.17.last_ref, f32[8,256,128]{2,1,0:T(8,128)} %copy-done), custom_call_target="tpu_custom_call" | custom-call | tf_op jit(solution)/shard_map/pallas_call | solution.py:159
  58.7 3.6 %all-to-all-start.1 = ((f32[8,256,128]{2,1,0:T(8,128)}), f32[8,256,128]{2,1,0:T(8,128)S(1)}, u32[]{:S(2)}, u32[]{:S(2)}) async-start(f32[8,256,128]{2,1,0:T(8,128)} %shard_map.87), calls=%async_computation.1 | async-start | bytes 2097152 | tf_op jit(solution)/shard_map/all_to_all | solution.py:295
  62.3 0.5 fusion.49
  62.8 0.6 slice_bitcast_fusion
  63.3 13.3 %all-to-all-done.1 = f32[8,256,128]{2,1,0:T(8,128)S(1)} async-done(((f32[8,256,128]{2,1,0:T(8,128)}), f32[8,256,128]{2,1,0:T(8,128)S(1)}, u32[]{:S(2)}, u32[]{:S(2)}) %all-to-all-start.1) | async-done | bytes 1048608 | tf_op jit(solution)/shard_map/all_to_all | solution.py:295
  76.7 1.0 %copy.13 = f32[1,2048,128]{2,1,0:T(8,128)} copy(f32[1,2048,128]{2,1,0:T(8,128)S(1)} %bitcast.280) | data formatting | bytes 2097152
  (27 shorter events, 0.3 us)
Async XLA Ops:
  0.6 1.6 %copy-start.1 = (f32[1,2048,128]{2,1,0:T(8,128)S(1)}, f32[1,2048,128]{2,1,0:T(8,128)}, u32[]{:S(2)}) copy-start(f32[1,2048,128]{2,1,0:T(8,128)} %param.9) | copy-start | bytes 3145732
  0.6 1.9 %copy-start.7 = (s32[1,4,128]{2,1,0:T(4,128)S(1)}, s32[1,4,128]{2,1,0:T(4,128)}, u32[]{:S(2)}) copy-start(s32[1,4,128]{2,1,0:T(4,128)} %param.11) | copy-start | bytes 6148
  0.7 1.9 %copy-start.8 = (s32[1,4,128]{2,1,0:T(4,128)S(1)}, s32[1,4,128]{2,1,0:T(4,128)}, u32[]{:S(2)}) copy-start(s32[1,4,128]{2,1,0:T(4,128)} %param.10) | copy-start | bytes 6148
  0.7 6.9 %copy-start.9 = (s32[32]{0:T(128)S(1)}, s32[32]{0:T(128)}, u32[]{:S(2)}) copy-start(s32[32]{0:T(128)} %param.12) | copy-start | bytes 388
  2.6 4.7 %collective-permute-start = (f32[1280]{0:T(1024)S(1)}, f32[1280]{0:T(1024)S(1)}, u32[]{:S(2)}, u32[]{:S(2)}) collective-permute-start(f32[1280]{0:T(1024)S(1)} %pad_maximum_fusion.1), channel_id=1, source_target_pairs={{0,1},{1,0},{2,3},{3,2},{4,5},{5,4},{6,7},{7,6},{8,9},{9,8},{10,11... | collective-permute-start | bytes 15368 | tf_op jit(solution)/shard_map/ppermute | solution.py:64
  7.7 4.5 %copy-start.6 = (f32[128]{0:T(128)S(1)}, f32[128]{0:T(128)}, u32[]{:S(2)}) copy-start(f32[128]{0:T(128)} %param.13) | copy-start | bytes 1540
  10.1 7.2 %collective-permute-start.1 = (bf16[2,512,128]{2,1,0:T(8,128)(2,1)S(1)}, bf16[2,512,128]{2,1,0:T(8,128)(2,1)S(1)}, u32[]{:S(2)}, u32[]{:S(2)}) collective-permute-start(bf16[2,512,128]{2,1,0:T(8,128)(2,1)S(1)} %bitcast.282), channel_id=1, source_target_pairs={{0,1},{1,0},{2,3},{3,2},{4,5},{5,4},{6,7},{7,6},{8,9},{9,8},{10,11... | collective-permute-start | bytes 786440 | tf_op jit(solution)/shard_map/ppermute | solution.py:64
  24.7 4.1 %copy-start.4 = (f32[16,128]{1,0:T(8,128)S(1)}, f32[16,128]{1,0:T(8,128)}, u32[]{:S(2)}) copy-start(f32[16,128]{1,0:T(8,128)} %param.15) | copy-start | bytes 24580
  24.7 4.1 %copy-start.5 = (f32[128]{0:T(128)S(1)}, f32[128]{0:T(128)}, u32[]{:S(2)}) copy-start(f32[128]{0:T(128)} %param.14) | copy-start | bytes 1540
  24.7 18.6 %all-to-all-start = ((f32[8,256,128]{2,1,0:T(8,128)}), f32[8,256,128]{2,1,0:T(8,128)S(1)}, u32[]{:S(2)}, u32[]{:S(2)}) async-start(f32[8,256,128]{2,1,0:T(8,128)} %bitcast.88), calls=%async_computation | async-start | bytes 2097152 | tf_op jit(solution)/shard_map/all_to_all | solution.py:262
  29.2 14.2 %copy-start.3 = (f32[16,128]{1,0:T(8,128)}, f32[16,128]{1,0:T(8,128)S(1)}, u32[]{:S(2)}) copy-start(f32[16,128]{1,0:T(8,128)S(1)} %scatter.4.pull_ref) | copy-start | bytes 24580
  43.3 1.0 %copy-start = (f32[8,256,128]{2,1,0:T(8,128)}, f32[8,256,128]{2,1,0:T(8,128)S(1)}, u32[]{:S(2)}) copy-start(f32[8,256,128]{2,1,0:T(8,128)S(1)} %all-to-all-done.pseudo_ref) | copy-start | bytes 3145732
  46.5 8.9 %collective-permute-start.2 = (f32[256,128]{1,0:T(8,128)}, f32[256,128]{1,0:T(8,128)S(1)}, u32[]{:S(2)}, u32[]{:S(2)}) collective-permute-start(f32[256,128]{1,0:T(8,128)} %get-tuple-element.16), channel_id=1, source_target_pairs={{0,16},{16,0},{1,17},{17,1},{2,18},{18,2},{3,19},{19,3},{4,20},{20... | collective-permute-start | bytes 393224 | tf_op jit(solution)/shard_map/ppermute | solution.py:64
  55.4 0.7 copy-start.2
  58.7 18.0 %all-to-all-start.1 = ((f32[8,256,128]{2,1,0:T(8,128)}), f32[8,256,128]{2,1,0:T(8,128)S(1)}, u32[]{:S(2)}, u32[]{:S(2)}) async-start(f32[8,256,128]{2,1,0:T(8,128)} %shard_map.87), calls=%async_computation.1 | async-start | bytes 2097152 | tf_op jit(solution)/shard_map/all_to_all | solution.py:295

commit v11 on v10

--- a/solution.py
+++ b/solution.py
@@ -48,9 +48,13 @@
         logits = lax.digamma(doc_topics)[..., None, :] + scores
         peak = lax.optimization_barrier(jnp.max(logits, axis=-1, keepdims=True))
         raised = jnp.exp(logits - peak)
-        total = lax.optimization_barrier(jnp.sum(raised, axis=-1, keepdims=True))
-        resp = raised / total
-        doc_topics = topic_prior + jnp.sum(counts_float[..., None] * resp, axis=-2)
+        total = jnp.sum(raised, axis=-1)
+        if sweep < EITERS - 1:
+            share = counts_float / total
+            doc_topics = topic_prior + jnp.sum(share[..., None] * raised, axis=-2)
+        else:
+            resp = raised / total[..., None]
+            doc_topics = topic_prior + jnp.sum(counts_float[..., None] * resp, axis=-2)
     weighted = to_bf16(counts_float[..., None] * resp)
     return (doc_topics, weighted)
 

time: 78 us -> 77.6 us (level)
    reduce_sum x4 -> x1, other arithmetic: 1.92 us -> 0.48 us  [e_step(): doc_topics = topic_prior + jnp.sum(counts_float[..., None] * resp, axis=-2)]
    reduce_sum x4 -> x7, other arithmetic: 1.56 us -> 2.62 us  [the longest x4 1.56 us: e_step(): total = jnp.sum(raised, axis=-1)]
where the time goes in v11:
time: 77.6 us; the launch traced here: 77.3 us
  waiting for transfers between devices  39.1 us (50%)
  starting transfers between devices  15.4 us (20%)
  other arithmetic  7.25 us (9%)
  matrix products  5.1 us (7%)
  Pallas kernels  4.87 us (6%)
  local copies, waits for them, and re-layouts  4.59 us (6%)
  between operations  0.96 us (1%)
    all_to_all x1, waiting for transfers between devices, smooth_part(): lax.all_to_all(smoothed, 'tl', split_axis=0, concat_axis=0, tiled=True)  13.3 us
    ppermute x3, waiting for transfers between devices, shift_axis(): lax.ppermute(value, axis, [(i, (i + s) % count) for i in range(count)])  12.9 us
    all_to_all x1, waiting for transfers between devices, smooth_part(): lax.all_to_all(by_dest, 'tl', split_axis=0, concat_axis=0, tiled=True)  12.9 us
    ppermute x3, starting transfers between devices, shift_axis(): lax.ppermute(value, axis, [(i, (i + s) % count) for i in range(count)])  7.74 us
    all_to_all x1, starting transfers between devices, smooth_part(): lax.all_to_all(by_dest, 'tl', split_axis=0, concat_axis=0, tiled=True)  4.13 us
    all_to_all x1, starting transfers between devices, smooth_part(): lax.all_to_all(smoothed, 'tl', split_axis=0, concat_axis=0, tiled=True)  3.56 us
    dot_general x1, matrix products, body(): counts = jnp.dot(marks, flat_weighted, preferred_element_type=jnp.float32)  2.76 us
    pallas_call x1, Pallas kernels, two_group_kalman(): pl.pallas_call(second_pass_kernel, out_shape=jax.ShapeDtypeStruct(by_year...  2.69 us
  transfers between devices with their start and end apart: 5, of which 5 were waited for; matrix products, arithmetic and copies ran while one was open for 4% of the time, Pallas kernels for 0%

profile of v11, /device:TPU:0, one launch (start us, length us, event | category | flops | bytes accessed | tf_op | source)
XLA Modules:
  0.0 77.3 jit_solution(17283444102225564719)
XLA Ops:
  0.6 0.0 copy-start.1
  0.6 0.0 copy-start.7
  0.7 0.0 copy-start.8
  0.7 0.0 copy-start.9
  0.7 1.6 %reduce_max.54 = f32[128]{0:T(128)S(1)} reduce(f32[1,2048,128]{2,1,0:T(8,128)} %param.9, f32[]{:T(128)} %constant.98.clone.1), dimensions={0,1}, to_apply=%region_0.0 | reduce | flops 262016 | bytes 1049092 | tf_op jit(solution)/shard_map/reduce_max | solution.py:191
  2.3 0.0 copy-done.1
  2.3 0.3 fusion.8
  2.6 0.0 copy-done.7
  2.6 0.0 copy-done.8
  2.6 3.1 %collective-permute-start = (f32[1280]{0:T(1024)S(1)}, f32[1280]{0:T(1024)S(1)}, u32[]{:S(2)}, u32[]{:S(2)}) collective-permute-start(f32[1280]{0:T(1024)S(1)} %pad_maximum_fusion.1), channel_id=1, source_target_pairs={{0,1},{1,0},{2,3},{3,2},{4,5},{5,4},{6,7},{7,6},{8,9},{9,8},{10,11... | collective-permute-start | bytes 15368 | tf_op jit(solution)/shard_map/ppermute | solution.py:68
  5.7 1.6 %collective-permute-done = f32[1280]{0:T(1024)S(1)} collective-permute-done((f32[1280]{0:T(1024)S(1)}, f32[1280]{0:T(1024)S(1)}, u32[]{:S(2)}, u32[]{:S(2)}) %collective-permute-start) | collective-permute-done | bytes 5152 | tf_op jit(solution)/shard_map/ppermute | solution.py:68
  7.4 0.1 fusion.153
  7.6 0.0 copy-done.9
  7.6 0.1 select_reduce_fusion
  7.7 0.0 copy-start.6
  7.7 2.3 %fusion.6 = bf16[1024,128]{1,0:T(8,128)(2,1)S(1)} fusion(s32[1024]{0:T(1024)S(1)} %fusion.56, f32[1,2048,128]{2,1,0:T(8,128)S(1)} %copy-done.1, f32[128]{0:T(128)S(1)} %log_add_fusion), kind=kOutput, calls=%fused_computation.7 | convolution fusion | flops 539885568 | bytes 1315328 | tf_op jit(solution)/shard_map/dot_general | solution.py:229
  10.1 2.1 %collective-permute-start.1 = (bf16[2,512,128]{2,1,0:T(8,128)(2,1)S(1)}, bf16[2,512,128]{2,1,0:T(8,128)(2,1)S(1)}, u32[]{:S(2)}, u32[]{:S(2)}) collective-permute-start(bf16[2,512,128]{2,1,0:T(8,128)(2,1)S(1)} %bitcast.280), channel_id=1, source_target_pairs={{0,1},{1,0},{2,3},{3,2},{4,5},{5,4},{6,7},{7,6},{8,9},{9,8},{10,11... | collective-permute-start | bytes 786440 | tf_op jit(solution)/shard_map/ppermute | solution.py:68
  12.2 0.0 copy-done.6
  12.2 0.1 fusion.58
  12.3 5.0 %collective-permute-done.1 = bf16[2,512,128]{2,1,0:T(8,128)(2,1)S(1)} collective-permute-done((bf16[2,512,128]{2,1,0:T(8,128)(2,1)S(1)}, bf16[2,512,128]{2,1,0:T(8,128)(2,1)S(1)}, u32[]{:S(2)}, u32[]{:S(2)}) %collective-permute-start.1) | collective-permute-done | bytes 262176 | tf_op jit(solution)/shard_map/ppermute | solution.py:68
  17.4 0.2 fusion.45
  17.6 0.4 fusion.47
  18.0 0.4 fusion.14
  18.4 0.1 fusion.60
  18.4 0.2 fusion.41
  18.7 0.4 fusion.43
  19.1 0.3 fusion.18
  19.4 0.1 fusion.62
  19.5 0.2 fusion.37
  19.7 0.4 fusion.39
  20.1 0.3 fusion.22
  20.5 0.1 fusion.64
  20.5 0.2 fusion.29
  20.8 0.4 fusion.32
  21.1 0.5 fusion.35
  21.6 2.8 %fusion.5 = f32[2048,128]{1,0:T(8,128)} fusion(bf16[1024,128]{1,0:T(8,128)(2,1)S(1)} %fusion.35, s32[1024]{0:T(1024)S(1)} %fusion.56, f32[1,2048,128]{2,1,0:T(8,128)S(1)} %copy-done.1), kind=kOutput, calls=%fused_computation.6 | convolution fusion | flops 539230208 | bytes 2363392 | tf_op jit(solution)/shard_map/dot_general | solution.py:242
  24.4 0.0 copy-start.4
  24.4 0.0 copy-start.5
  24.4 4.1 %all-to-all-start = ((f32[8,256,128]{2,1,0:T(8,128)}), f32[8,256,128]{2,1,0:T(8,128)S(1)}, u32[]{:S(2)}, u32[]{:S(2)}) async-start(f32[8,256,128]{2,1,0:T(8,128)} %bitcast.83), calls=%async_computation | async-start | bytes 2097152 | tf_op jit(solution)/shard_map/all_to_all | solution.py:266
  28.5 0.0 copy-done.4
  28.5 0.0 copy-done.5
  28.5 0.1 fusion.152
  28.7 0.1 concatenate.68
  28.8 0.0 copy-start.3
  28.9 1.2 %concatenate.67.gain_ref = f32[16,128]{1,0:T(8,128)} concatenate(f32[1,128]{1,0:T(1,128)S(1)} %add_divide_fusion.32, f32[1,128]{1,0:T(1,128)S(1)} %get-tuple-element.54, f32[1,128]{1,0:T(1,128)S(1)} %get-tuple-element.53, f32[1,128]{1,0:T(1,128)S(1)} %get-tuple-element.52, f32[1,128]{1,0:T(1,128)S(1)} %get-tuple-element.51, f32[1,128]{1,0:T(1,128)S(1)} %get-tuple-element.50, ...), dimensions={0} | concatenate | bytes 16384 | tf_op jit(solution)/shard_map/concatenate | solution.py:26
  30.1 12.9 %all-to-all-done.pseudo_ref = f32[8,256,128]{2,1,0:T(8,128)S(1)} async-done(((f32[8,256,128]{2,1,0:T(8,128)}), f32[8,256,128]{2,1,0:T(8,128)S(1)}, u32[]{:S(2)}, u32[]{:S(2)}) %all-to-all-start) | async-done | bytes 1048608 | tf_op jit(solution)/shard_map/all_to_all | solution.py:266
  43.0 0.0 copy-done.3
  43.0 0.0 copy-start
  43.0 1.0 %copy-done = f32[8,256,128]{2,1,0:T(8,128)} copy-done((f32[8,256,128]{2,1,0:T(8,128)}, f32[8,256,128]{2,1,0:T(8,128)S(1)}, u32[]{:S(2)}) %copy-start) | copy-done | bytes 1048600
  44.0 2.2 %shard_map.86 = (f32[256,128]{1,0:T(8,128)}, f32[256,128]{1,0:T(8,128)}) custom-call(f32[16,128]{1,0:T(8,128)} %concatenate.67.gain_ref, f32[16,128]{1,0:T(8,128)} %copy-done.3, f32[8,256,128]{2,1,0:T(8,128)} %copy-done), custom_call_target="tpu_custom_call" | custom-call | tf_op jit(solution)/shard_map/pallas_call | solution.py:157
  46.1 2.6 %collective-permute-start.2 = (f32[256,128]{1,0:T(8,128)}, f32[256,128]{1,0:T(8,128)S(1)}, u32[]{:S(2)}, u32[]{:S(2)}) collective-permute-start(f32[256,128]{1,0:T(8,128)} %get-tuple-element.16), channel_id=1, source_target_pairs={{0,16},{16,0},{1,17},{17,1},{2,18},{18,2},{3,19},{19,3},{4,20},{20... | collective-permute-start | bytes 393224 | tf_op jit(solution)/shard_map/ppermute | solution.py:68
  48.7 6.3 %collective-permute-done.2.other_ref = f32[256,128]{1,0:T(8,128)S(1)} collective-permute-done((f32[256,128]{1,0:T(8,128)}, f32[256,128]{1,0:T(8,128)S(1)}, u32[]{:S(2)}, u32[]{:S(2)}) %collective-permute-start.2) | collective-permute-done | bytes 131104 | tf_op jit(solution)/shard_map/ppermute | solution.py:68
  55.0 0.0 copy-start.2
  55.0 0.7 copy-done.2
  55.7 2.7 %shard_map.87 = f32[8,256,128]{2,1,0:T(8,128)} custom-call(f32[16,128]{1,0:T(8,128)} %concatenate.67.gain_ref, f32[16,128]{1,0:T(8,128)} %copy-done.3, f32[256,128]{1,0:T(8,128)} %copy-done.2, f32[256,128]{1,0:T(8,128)} %get-tuple-element.17.last_ref, f32[8,256,128]{2,1,0:T(8,128)} %copy-done), custom_call_target="tpu_custom_call" | custom-call | tf_op jit(solution)/shard_map/pallas_call | solution.py:163
  58.4 3.6 %all-to-all-start.1 = ((f32[8,256,128]{2,1,0:T(8,128)}), f32[8,256,128]{2,1,0:T(8,128)S(1)}, u32[]{:S(2)}, u32[]{:S(2)}) async-start(f32[8,256,128]{2,1,0:T(8,128)} %shard_map.87), calls=%async_computation.1 | async-start | bytes 2097152 | tf_op jit(solution)/shard_map/all_to_all | solution.py:299
  61.9 0.5 fusion.49
  62.4 0.6 slice_bitcast_fusion
  63.0 13.3 %all-to-all-done.1 = f32[8,256,128]{2,1,0:T(8,128)S(1)} async-done(((f32[8,256,128]{2,1,0:T(8,128)}), f32[8,256,128]{2,1,0:T(8,128)S(1)}, u32[]{:S(2)}, u32[]{:S(2)}) %all-to-all-start.1) | async-done | bytes 1048608 | tf_op jit(solution)/shard_map/all_to_all | solution.py:299
  76.3 1.0 %copy.13 = f32[1,2048,128]{2,1,0:T(8,128)} copy(f32[1,2048,128]{2,1,0:T(8,128)S(1)} %bitcast.278) | data formatting | bytes 2097152
  (30 shorter events, 0.4 us)
Async XLA Ops:
  0.6 1.6 %copy-start.1 = (f32[1,2048,128]{2,1,0:T(8,128)S(1)}, f32[1,2048,128]{2,1,0:T(8,128)}, u32[]{:S(2)}) copy-start(f32[1,2048,128]{2,1,0:T(8,128)} %param.9) | copy-start | bytes 3145732
  0.6 1.9 %copy-start.7 = (s32[1,4,128]{2,1,0:T(4,128)S(1)}, s32[1,4,128]{2,1,0:T(4,128)}, u32[]{:S(2)}) copy-start(s32[1,4,128]{2,1,0:T(4,128)} %param.11) | copy-start | bytes 6148
  0.7 1.9 %copy-start.8 = (s32[1,4,128]{2,1,0:T(4,128)S(1)}, s32[1,4,128]{2,1,0:T(4,128)}, u32[]{:S(2)}) copy-start(s32[1,4,128]{2,1,0:T(4,128)} %param.10) | copy-start | bytes 6148
  0.7 6.9 %copy-start.9 = (s32[32]{0:T(128)S(1)}, s32[32]{0:T(128)}, u32[]{:S(2)}) copy-start(s32[32]{0:T(128)} %param.12) | copy-start | bytes 388
  2.6 4.7 %collective-permute-start = (f32[1280]{0:T(1024)S(1)}, f32[1280]{0:T(1024)S(1)}, u32[]{:S(2)}, u32[]{:S(2)}) collective-permute-start(f32[1280]{0:T(1024)S(1)} %pad_maximum_fusion.1), channel_id=1, source_target_pairs={{0,1},{1,0},{2,3},{3,2},{4,5},{5,4},{6,7},{7,6},{8,9},{9,8},{10,11... | collective-permute-start | bytes 15368 | tf_op jit(solution)/shard_map/ppermute | solution.py:68
  7.7 4.5 %copy-start.6 = (f32[128]{0:T(128)S(1)}, f32[128]{0:T(128)}, u32[]{:S(2)}) copy-start(f32[128]{0:T(128)} %param.13) | copy-start | bytes 1540
  10.1 7.2 %collective-permute-start.1 = (bf16[2,512,128]{2,1,0:T(8,128)(2,1)S(1)}, bf16[2,512,128]{2,1,0:T(8,128)(2,1)S(1)}, u32[]{:S(2)}, u32[]{:S(2)}) collective-permute-start(bf16[2,512,128]{2,1,0:T(8,128)(2,1)S(1)} %bitcast.280), channel_id=1, source_target_pairs={{0,1},{1,0},{2,3},{3,2},{4,5},{5,4},{6,7},{7,6},{8,9},{9,8},{10,11... | collective-permute-start | bytes 786440 | tf_op jit(solution)/shard_map/ppermute | solution.py:68
  24.4 4.1 %copy-start.4 = (f32[16,128]{1,0:T(8,128)S(1)}, f32[16,128]{1,0:T(8,128)}, u32[]{:S(2)}) copy-start(f32[16,128]{1,0:T(8,128)} %param.15) | copy-start | bytes 24580
  24.4 4.1 %copy-start.5 = (f32[128]{0:T(128)S(1)}, f32[128]{0:T(128)}, u32[]{:S(2)}) copy-start(f32[128]{0:T(128)} %param.14) | copy-start | bytes 1540
  24.4 18.6 %all-to-all-start = ((f32[8,256,128]{2,1,0:T(8,128)}), f32[8,256,128]{2,1,0:T(8,128)S(1)}, u32[]{:S(2)}, u32[]{:S(2)}) async-start(f32[8,256,128]{2,1,0:T(8,128)} %bitcast.83), calls=%async_computation | async-start | bytes 2097152 | tf_op jit(solution)/shard_map/all_to_all | solution.py:266
  28.8 14.2 %copy-start.3 = (f32[16,128]{1,0:T(8,128)}, f32[16,128]{1,0:T(8,128)S(1)}, u32[]{:S(2)}) copy-start(f32[16,128]{1,0:T(8,128)S(1)} %scatter.4.pull_ref) | copy-start | bytes 24580
  43.0 1.0 %copy-start = (f32[8,256,128]{2,1,0:T(8,128)}, f32[8,256,128]{2,1,0:T(8,128)S(1)}, u32[]{:S(2)}) copy-start(f32[8,256,128]{2,1,0:T(8,128)S(1)} %all-to-all-done.pseudo_ref) | copy-start | bytes 3145732
  46.1 8.9 %collective-permute-start.2 = (f32[256,128]{1,0:T(8,128)}, f32[256,128]{1,0:T(8,128)S(1)}, u32[]{:S(2)}, u32[]{:S(2)}) collective-permute-start(f32[256,128]{1,0:T(8,128)} %get-tuple-element.16), channel_id=1, source_target_pairs={{0,16},{16,0},{1,17},{17,1},{2,18},{18,2},{3,19},{19,3},{4,20},{20... | collective-permute-start | bytes 393224 | tf_op jit(solution)/shard_map/ppermute | solution.py:68
  55.0 0.7 copy-start.2
  58.4 18.0 %all-to-all-start.1 = ((f32[8,256,128]{2,1,0:T(8,128)}), f32[8,256,128]{2,1,0:T(8,128)S(1)}, u32[]{:S(2)}, u32[]{:S(2)}) async-start(f32[8,256,128]{2,1,0:T(8,128)} %shard_map.87), calls=%async_computation.1 | async-start | bytes 2097152 | tf_op jit(solution)/shard_map/all_to_all | solution.py:299

commit v12 on v11

--- a/solution.py
+++ b/solution.py
@@ -154,11 +154,19 @@
 def two_group_kalman(gains, pulls, by_year):
     years, rows, topics = by_year.shape
     edge = jax.ShapeDtypeStruct((rows, topics), jnp.float32)
-    sent, last = pl.pallas_call(
-        first_pass_kernel,
-        out_shape=(edge, edge),
-        scratch_shapes=[pltpu.VMEM(by_year.shape, jnp.float32)],
-    )(gains, pulls, by_year)
+    group = lax.axis_index("tg")
+    gains_here = lax.dynamic_slice_in_dim(gains, group * years, years, 0)
+    pulls_here = lax.dynamic_slice_in_dim(pulls, group * years, years, 0)
+    mean = jnp.zeros((rows, topics), jnp.float32)
+    filtered = []
+    for t in range(years):
+        mean = (1.0 - gains_here[t]) * mean + gains_here[t] * by_year[t]
+        filtered.append(mean)
+    last = mean
+    mean = jnp.zeros((rows, topics), jnp.float32)
+    for t in reversed(range(years)):
+        mean = pulls_here[t] * mean + (1.0 - pulls_here[t]) * filtered[t]
+    sent = jnp.where(group == 0, last, mean)
     other = shift_axis(sent, "tg", 1)
     return pl.pallas_call(
         second_pass_kernel, out_shape=jax.ShapeDtypeStruct(by_year.shape, jnp.float32)

time: 77.6 us -> 75.2 us (0.969)
  Pallas kernels: 4.87 us -> 2.69 us
  local copies, waits for them, and re-layouts: 4.59 us -> 2.45 us
  other arithmetic: 7.25 us -> 8.27 us
  waiting for transfers between devices: 39.1 us -> 40 us
    pallas_call x1 -> x0, Pallas kernels: 2.18 us -> none  [two_group_kalman(): pl.pallas_call(first_pass_kernel, out_shape=(edge, edge), scratch_shapes=...]
    concatenate x2, local copies, waits for them, and re-layouts: 1.29 us -> 0.12 us  [variance_tables(): lax.scan(forward_step, start_var, obs_precision, unroll=True)]
    all_to_all x1, waiting for transfers between devices: 12.9 us -> 14 us  [smooth_part(): lax.all_to_all(by_dest, 'tl', split_axis=0, concat_axis=0, tiled=True)]
    select_n x0 -> x1, other arithmetic: none -> 0.99 us  [two_group_kalman(): sent = jnp.where(group == 0, last, mean)]
    unnamed x21 -> x23, local copies, waits for them, and re-layouts: 2.63 us -> 1.65 us
  transfers between devices with their start and end apart: 5 -> 5, of which waited for: 5 -> 5; matrix products, arithmetic and copies ran while one was open for 4% -> 2% of each run, Pallas kernels for 0% -> 0%
where the time goes in v12:
time: 75.2 us; the launch traced here: 74.9 us
  waiting for transfers between devices  40 us (53%)
  starting transfers between devices  15.4 us (20%)
  other arithmetic  8.27 us (11%)
  matrix products  5.11 us (7%)
  Pallas kernels  2.69 us (4%)
  local copies, waits for them, and re-layouts  2.45 us (3%)
  between operations  0.99 us (1%)
    all_to_all x1, waiting for transfers between devices, smooth_part(): lax.all_to_all(by_dest, 'tl', split_axis=0, concat_axis=0, tiled=True)  14 us
    all_to_all x1, waiting for transfers between devices, smooth_part(): lax.all_to_all(smoothed, 'tl', split_axis=0, concat_axis=0, tiled=True)  13.3 us
    ppermute x3, waiting for transfers between devices, shift_axis(): lax.ppermute(value, axis, [(i, (i + s) % count) for i in range(count)])  12.7 us
    ppermute x3, starting transfers between devices, shift_axis(): lax.ppermute(value, axis, [(i, (i + s) % count) for i in range(count)])  7.74 us
    all_to_all x1, starting transfers between devices, smooth_part(): lax.all_to_all(by_dest, 'tl', split_axis=0, concat_axis=0, tiled=True)  4.13 us
    all_to_all x1, starting transfers between devices, smooth_part(): lax.all_to_all(smoothed, 'tl', split_axis=0, concat_axis=0, tiled=True)  3.56 us
    dot_general x1, matrix products, body(): counts = jnp.dot(marks, flat_weighted, preferred_element_type=jnp.float32)  2.76 us
    pallas_call x1, Pallas kernels, two_group_kalman(): pl.pallas_call(second_pass_kernel, out_shape=jax.ShapeDtypeStruct(by_year...  2.69 us
  transfers between devices with their start and end apart: 5, of which 5 were waited for; matrix products, arithmetic and copies ran while one was open for 2% of the time, Pallas kernels for 0%

profile of v12, /device:TPU:0, one launch (start us, length us, event | category | flops | bytes accessed | tf_op | source)
XLA Modules:
  0.0 74.9 jit_solution(5274737004338444000)
XLA Ops:
  0.6 0.0 copy-start.1
  0.6 0.0 copy-start.8
  0.7 0.0 copy-start.9
  0.7 0.0 copy-start.10
  0.7 1.6 %reduce_max.54 = f32[128]{0:T(128)S(1)} reduce(f32[1,2048,128]{2,1,0:T(8,128)} %param.9, f32[]{:T(128)} %constant.108.clone.1), dimensions={0,1}, to_apply=%region_0.0 | reduce | flops 262016 | bytes 1049092 | tf_op jit(solution)/shard_map/reduce_max | solution.py:199
  2.3 0.0 copy-done.1
  2.3 0.3 fusion.8
  2.6 0.0 copy-done.8
  2.6 0.0 copy-done.9
  2.6 3.1 %collective-permute-start = (f32[1280]{0:T(1024)S(1)}, f32[1280]{0:T(1024)S(1)}, u32[]{:S(2)}, u32[]{:S(2)}) collective-permute-start(f32[1280]{0:T(1024)S(1)} %pad_maximum_fusion.1), channel_id=1, source_target_pairs={{0,1},{1,0},{2,3},{3,2},{4,5},{5,4},{6,7},{7,6},{8,9},{9,8},{10,11... | collective-permute-start | bytes 15368 | tf_op jit(solution)/shard_map/ppermute | solution.py:68
  5.7 1.6 %collective-permute-done = f32[1280]{0:T(1024)S(1)} collective-permute-done((f32[1280]{0:T(1024)S(1)}, f32[1280]{0:T(1024)S(1)}, u32[]{:S(2)}, u32[]{:S(2)}) %collective-permute-start) | collective-permute-done | bytes 5152 | tf_op jit(solution)/shard_map/ppermute | solution.py:68
  7.4 0.1 fusion.169
  7.6 0.0 copy-done.10
  7.6 0.1 select_reduce_fusion
  7.7 0.0 copy-start.7
  7.7 2.4 %fusion.6 = bf16[1024,128]{1,0:T(8,128)(2,1)S(1)} fusion(s32[1024]{0:T(1024)S(1)} %fusion.72, f32[1,2048,128]{2,1,0:T(8,128)S(1)} %copy-done.1, f32[128]{0:T(128)S(1)} %log_add_fusion), kind=kOutput, calls=%fused_computation.7 | convolution fusion | flops 539885568 | bytes 1315328 | tf_op jit(solution)/shard_map/dot_general | solution.py:237
  10.1 2.1 %collective-permute-start.1 = (bf16[2,512,128]{2,1,0:T(8,128)(2,1)S(1)}, bf16[2,512,128]{2,1,0:T(8,128)(2,1)S(1)}, u32[]{:S(2)}, u32[]{:S(2)}) collective-permute-start(bf16[2,512,128]{2,1,0:T(8,128)(2,1)S(1)} %bitcast.428), channel_id=1, source_target_pairs={{0,1},{1,0},{2,3},{3,2},{4,5},{5,4},{6,7},{7,6},{8,9},{9,8},{10,11... | collective-permute-start | bytes 786440 | tf_op jit(solution)/shard_map/ppermute | solution.py:68
  12.2 0.0 copy-done.7
  12.2 0.1 fusion.74
  12.3 5.0 %collective-permute-done.1 = bf16[2,512,128]{2,1,0:T(8,128)(2,1)S(1)} collective-permute-done((bf16[2,512,128]{2,1,0:T(8,128)(2,1)S(1)}, bf16[2,512,128]{2,1,0:T(8,128)(2,1)S(1)}, u32[]{:S(2)}, u32[]{:S(2)}) %collective-permute-start.1) | collective-permute-done | bytes 262176 | tf_op jit(solution)/shard_map/ppermute | solution.py:68
  17.4 0.2 fusion.45
  17.6 0.4 fusion.47
  18.0 0.4 fusion.14
  18.4 0.1 fusion.76
  18.4 0.2 fusion.41
  18.7 0.4 fusion.43
  19.1 0.3 fusion.18
  19.4 0.1 fusion.78
  19.5 0.2 fusion.37
  19.7 0.4 fusion.39
  20.1 0.3 fusion.22
  20.5 0.1 fusion.80
  20.5 0.2 fusion.29
  20.8 0.4 fusion.32
  21.1 0.5 fusion.35
  21.6 2.8 %fusion.5 = f32[2048,128]{1,0:T(8,128)} fusion(bf16[1024,128]{1,0:T(8,128)(2,1)S(1)} %fusion.35, s32[1024]{0:T(1024)S(1)} %fusion.72, f32[1,2048,128]{2,1,0:T(8,128)S(1)} %copy-done.1), kind=kOutput, calls=%fused_computation.6 | convolution fusion | flops 539230208 | bytes 2363392 | tf_op jit(solution)/shard_map/dot_general | solution.py:250
  24.4 0.0 copy-start.5
  24.4 0.0 copy-start.6
  24.4 4.1 %all-to-all-start = ((f32[8,256,128]{2,1,0:T(8,128)}), f32[8,256,128]{2,1,0:T(8,128)S(1)}, u32[]{:S(2)}, u32[]{:S(2)}) async-start(f32[8,256,128]{2,1,0:T(8,128)} %bitcast.92), calls=%async_computation | async-start | bytes 2097152 | tf_op jit(solution)/shard_map/all_to_all | solution.py:274
  28.5 0.0 copy-done.5
  28.5 0.0 copy-done.6
  28.5 0.1 fusion.168
  28.7 0.1 concatenate.68
  28.8 0.0 copy-start.4
  28.9 0.1 concatenate.67.gain_ref
  28.9 0.0 copy-start.3
  29.0 14.0 %all-to-all-done.pseudo_ref = f32[8,256,128]{2,1,0:T(8,128)S(1)} async-done(((f32[8,256,128]{2,1,0:T(8,128)}), f32[8,256,128]{2,1,0:T(8,128)S(1)}, u32[]{:S(2)}, u32[]{:S(2)}) %all-to-all-start) | async-done | bytes 1048608 | tf_op jit(solution)/shard_map/all_to_all | solution.py:274
  43.0 0.0 copy-start
  43.0 1.0 %add_select_fusion = (f32[256,128]{1,0:T(8,128)S(1)}, f32[256,128]{1,0:T(8,128)}) fusion(f32[8,256,128]{2,1,0:T(8,128)S(1)} %all-to-all-done.pseudo_ref, f32[128]{0:T(128)S(1)} %get-tuple-element.74, f32[128]{0:T(128)S(1)} %get-tuple-element.75, f32[128]{0:T(128)S(1)} %get-tuple-element.76, f32[128]{0:T(128)S(1)} %get-tuple-element.77, ...), kind=kLoop, calls=%fused_computation.86 | loop fusion | flops 1540096 | bytes 1327105 | tf_op jit(solution)/shard_map/jit(_where)/select_n | solution.py:169
  44.0 2.6 %collective-permute-start.2 = (f32[256,128]{1,0:T(8,128)S(1)}, f32[256,128]{1,0:T(8,128)S(1)}, u32[]{:S(2)}, u32[]{:S(2)}) collective-permute-start(f32[256,128]{1,0:T(8,128)S(1)} %get-tuple-element.14), channel_id=1, source_target_pairs={{0,16},{16,0},{1,17},{17,1},{2,18},{18,2},{3,19},{19,3},{4,20},{20... | collective-permute-start | bytes 393224 | tf_op jit(solution)/shard_map/ppermute | solution.py:68
  46.6 6.1 %collective-permute-done.2.other_ref = f32[256,128]{1,0:T(8,128)S(1)} collective-permute-done((f32[256,128]{1,0:T(8,128)S(1)}, f32[256,128]{1,0:T(8,128)S(1)}, u32[]{:S(2)}, u32[]{:S(2)}) %collective-permute-start.2) | collective-permute-done | bytes 131104 | tf_op jit(solution)/shard_map/ppermute | solution.py:68
  52.6 0.0 copy-start.2
  52.6 0.0 copy-done.4
  52.6 0.0 copy-done.3
  52.6 0.0 copy-done
  52.6 0.6 copy-done.2
  53.3 2.7 %shard_map.86 = f32[8,256,128]{2,1,0:T(8,128)} custom-call(f32[16,128]{1,0:T(8,128)} %copy-done.3, f32[16,128]{1,0:T(8,128)} %copy-done.4, f32[256,128]{1,0:T(8,128)} %copy-done.2, f32[256,128]{1,0:T(8,128)} %get-tuple-element.15.last_ref, f32[8,256,128]{2,1,0:T(8,128)} %copy-done), custom_call_target="tpu_custom_call" | custom-call | tf_op jit(solution)/shard_map/pallas_call | solution.py:171
  56.0 3.6 %all-to-all-start.1 = ((f32[8,256,128]{2,1,0:T(8,128)}), f32[8,256,128]{2,1,0:T(8,128)S(1)}, u32[]{:S(2)}, u32[]{:S(2)}) async-start(f32[8,256,128]{2,1,0:T(8,128)} %shard_map.86), calls=%async_computation.1 | async-start | bytes 2097152 | tf_op jit(solution)/shard_map/all_to_all | solution.py:307
  59.6 0.5 fusion.49
  60.1 0.6 slice_bitcast_fusion.8
  60.6 13.3 %all-to-all-done.1 = f32[8,256,128]{2,1,0:T(8,128)S(1)} async-done(((f32[8,256,128]{2,1,0:T(8,128)}), f32[8,256,128]{2,1,0:T(8,128)S(1)}, u32[]{:S(2)}, u32[]{:S(2)}) %all-to-all-start.1) | async-done | bytes 1048608 | tf_op jit(solution)/shard_map/all_to_all | solution.py:307
  73.9 1.0 %copy.13 = f32[1,2048,128]{2,1,0:T(8,128)} copy(f32[1,2048,128]{2,1,0:T(8,128)S(1)} %bitcast.426) | data formatting | bytes 2097152
  (33 shorter events, 0.4 us)
Async XLA Ops:
  0.6 1.6 %copy-start.1 = (f32[1,2048,128]{2,1,0:T(8,128)S(1)}, f32[1,2048,128]{2,1,0:T(8,128)}, u32[]{:S(2)}) copy-start(f32[1,2048,128]{2,1,0:T(8,128)} %param.9) | copy-start | bytes 3145732
  0.6 1.9 %copy-start.8 = (s32[1,4,128]{2,1,0:T(4,128)S(1)}, s32[1,4,128]{2,1,0:T(4,128)}, u32[]{:S(2)}) copy-start(s32[1,4,128]{2,1,0:T(4,128)} %param.11) | copy-start | bytes 6148
  0.7 1.9 %copy-start.9 = (s32[1,4,128]{2,1,0:T(4,128)S(1)}, s32[1,4,128]{2,1,0:T(4,128)}, u32[]{:S(2)}) copy-start(s32[1,4,128]{2,1,0:T(4,128)} %param.10) | copy-start | bytes 6148
  0.7 6.9 %copy-start.10 = (s32[32]{0:T(128)S(1)}, s32[32]{0:T(128)}, u32[]{:S(2)}) copy-start(s32[32]{0:T(128)} %param.12) | copy-start | bytes 388
  2.6 4.7 %collective-permute-start = (f32[1280]{0:T(1024)S(1)}, f32[1280]{0:T(1024)S(1)}, u32[]{:S(2)}, u32[]{:S(2)}) collective-permute-start(f32[1280]{0:T(1024)S(1)} %pad_maximum_fusion.1), channel_id=1, source_target_pairs={{0,1},{1,0},{2,3},{3,2},{4,5},{5,4},{6,7},{7,6},{8,9},{9,8},{10,11... | collective-permute-start | bytes 15368 | tf_op jit(solution)/shard_map/ppermute | solution.py:68
  7.7 4.5 %copy-start.7 = (f32[128]{0:T(128)S(1)}, f32[128]{0:T(128)}, u32[]{:S(2)}) copy-start(f32[128]{0:T(128)} %param.13) | copy-start | bytes 1540
  10.1 7.2 %collective-permute-start.1 = (bf16[2,512,128]{2,1,0:T(8,128)(2,1)S(1)}, bf16[2,512,128]{2,1,0:T(8,128)(2,1)S(1)}, u32[]{:S(2)}, u32[]{:S(2)}) collective-permute-start(bf16[2,512,128]{2,1,0:T(8,128)(2,1)S(1)} %bitcast.428), channel_id=1, source_target_pairs={{0,1},{1,0},{2,3},{3,2},{4,5},{5,4},{6,7},{7,6},{8,9},{9,8},{10,11... | collective-permute-start | bytes 786440 | tf_op jit(solution)/shard_map/ppermute | solution.py:68
  24.4 4.1 %copy-start.5 = (f32[16,128]{1,0:T(8,128)S(1)}, f32[16,128]{1,0:T(8,128)}, u32[]{:S(2)}) copy-start(f32[16,128]{1,0:T(8,128)} %param.15) | copy-start | bytes 24580
  24.4 4.1 %copy-start.6 = (f32[128]{0:T(128)S(1)}, f32[128]{0:T(128)}, u32[]{:S(2)}) copy-start(f32[128]{0:T(128)} %param.14) | copy-start | bytes 1540
  24.4 18.6 %all-to-all-start = ((f32[8,256,128]{2,1,0:T(8,128)}), f32[8,256,128]{2,1,0:T(8,128)S(1)}, u32[]{:S(2)}, u32[]{:S(2)}) async-start(f32[8,256,128]{2,1,0:T(8,128)} %bitcast.92), calls=%async_computation | async-start | bytes 2097152 | tf_op jit(solution)/shard_map/all_to_all | solution.py:274
  28.8 23.8 %copy-start.4 = (f32[16,128]{1,0:T(8,128)}, f32[16,128]{1,0:T(8,128)S(1)}, u32[]{:S(2)}) copy-start(f32[16,128]{1,0:T(8,128)S(1)} %scatter.4.pull_ref) | copy-start | bytes 24580
  28.9 23.7 %copy-start.3 = (f32[16,128]{1,0:T(8,128)}, f32[16,128]{1,0:T(8,128)S(1)}, u32[]{:S(2)}) copy-start(f32[16,128]{1,0:T(8,128)S(1)} %concatenate.67.gain_ref) | copy-start | bytes 24580
  43.0 9.7 %copy-start = (f32[8,256,128]{2,1,0:T(8,128)}, f32[8,256,128]{2,1,0:T(8,128)S(1)}, u32[]{:S(2)}) copy-start(f32[8,256,128]{2,1,0:T(8,128)S(1)} %all-to-all-done.pseudo_ref) | copy-start | bytes 3145732
  44.0 8.6 %collective-permute-start.2 = (f32[256,128]{1,0:T(8,128)S(1)}, f32[256,128]{1,0:T(8,128)S(1)}, u32[]{:S(2)}, u32[]{:S(2)}) collective-permute-start(f32[256,128]{1,0:T(8,128)S(1)} %get-tuple-element.14), channel_id=1, source_target_pairs={{0,16},{16,0},{1,17},{17,1},{2,18},{18,2},{3,19},{19,3},{4,20},{20... | collective-permute-start | bytes 393224 | tf_op jit(solution)/shard_map/ppermute | solution.py:68
  52.6 0.7 copy-start.2
  56.0 18.0 %all-to-all-start.1 = ((f32[8,256,128]{2,1,0:T(8,128)}), f32[8,256,128]{2,1,0:T(8,128)S(1)}, u32[]{:S(2)}, u32[]{:S(2)}) async-start(f32[8,256,128]{2,1,0:T(8,128)} %shard_map.86), calls=%async_computation.1 | async-start | bytes 2097152 | tf_op jit(solution)/shard_map/all_to_all | solution.py:307

commit v13 on v12

--- a/solution.py
+++ b/solution.py
@@ -168,9 +168,33 @@
         mean = pulls_here[t] * mean + (1.0 - pulls_here[t]) * filtered[t]
     sent = jnp.where(group == 0, last, mean)
     other = shift_axis(sent, "tg", 1)
-    return pl.pallas_call(
-        second_pass_kernel, out_shape=jax.ShapeDtypeStruct(by_year.shape, jnp.float32)
-    )(gains, pulls, other, last, by_year)
+    carry = jnp.ones((topics,), jnp.float32)
+    responses = []
+    for t in range(years):
+        carry = (1.0 - gains[years + t]) * carry
+        responses.append(carry)
+    reach = jnp.zeros_like(carry)
+    for t in reversed(range(years)):
+        reach = pulls[years + t] * reach + (1.0 - pulls[years + t]) * responses[t]
+    weight = jnp.where(group == 0, 1.0, 0.0)
+    start = (1.0 - weight) * other
+    after = weight * (other + reach * last)
+    unit = jnp.eye(years + 2, dtype=jnp.float32)[:, :, None]
+    state = unit[years]
+    filtered = []
+    for t in range(years):
+        state = (1.0 - gains_here[t]) * state + gains_here[t] * unit[t]
+        filtered.append(state)
+    state = unit[years + 1]
+    maps = [None] * years
+    for t in reversed(range(years)):
+        state = pulls_here[t] * state + (1.0 - pulls_here[t]) * filtered[t]
+        maps[t] = state
+    maps = jnp.stack(maps)
+    smoothed = maps[:, years, None, :] * start + maps[:, years + 1, None, :] * after
+    for s in range(years):
+        smoothed = smoothed + maps[:, s, None, :] * by_year[s]
+    return smoothed
 
 
 def group_maps(gains, pulls, groups):

time: 75.2 us -> 72.8 us (0.968)
  Pallas kernels: 2.69 us -> 0 us
  other arithmetic: 8.27 us -> 9.59 us
    pallas_call x1 -> x0, Pallas kernels: 2.69 us -> none  [two_group_kalman(): pl.pallas_call(second_pass_kernel, out_shape=jax.ShapeDtypeStruct(by_year...]
    add x0 -> x4, other arithmetic: none -> 2.05 us  [the longest x1 1.71 us: two_group_kalman(): smoothed = smoothed + maps[:, s, None, :] * by_year[s]]
    select_n x1, other arithmetic: 0.99 us -> 0.24 us  [two_group_kalman(): sent = jnp.where(group == 0, last, mean)]
    unnamed x23 -> x15, local copies, waits for them, and re-layouts: 1.65 us -> 1 us
  transfers between devices with their start and end apart: 5 -> 5, of which waited for: 5 -> 5; matrix products, arithmetic and copies ran while one was open for 2% -> 3% of each run, Pallas kernels for 0% -> 0%
where the time goes in v13:
time: 72.8 us; the launch traced here: 72.5 us
  waiting for transfers between devices  39.5 us (54%)
  starting transfers between devices  15.4 us (21%)
  other arithmetic  9.59 us (13%)
  matrix products  5.11 us (7%)
  local copies, waits for them, and re-layouts  1.95 us (3%)
  between operations  1.03 us (1%)
    all_to_all x1, waiting for transfers between devices, smooth_part(): lax.all_to_all(by_dest, 'tl', split_axis=0, concat_axis=0, tiled=True)  14 us
    all_to_all x1, waiting for transfers between devices, smooth_part(): lax.all_to_all(smoothed, 'tl', split_axis=0, concat_axis=0, tiled=True)  13.3 us
    ppermute x3, waiting for transfers between devices, shift_axis(): lax.ppermute(value, axis, [(i, (i + s) % count) for i in range(count)])  12.2 us
    ppermute x3, starting transfers between devices, shift_axis(): lax.ppermute(value, axis, [(i, (i + s) % count) for i in range(count)])  7.8 us
    all_to_all x1, starting transfers between devices, smooth_part(): lax.all_to_all(by_dest, 'tl', split_axis=0, concat_axis=0, tiled=True)  4 us
    all_to_all x1, starting transfers between devices, smooth_part(): lax.all_to_all(smoothed, 'tl', split_axis=0, concat_axis=0, tiled=True)  3.56 us
    dot_general x1, matrix products, body(): counts = jnp.dot(marks, flat_weighted, preferred_element_type=jnp.float32)  2.76 us
    dot_general x1, matrix products, body(): lax.dot_general(marks, table, (((0,), (0,)), ((), ())), preferred_element...  2.35 us
  transfers between devices with their start and end apart: 5, of which 5 were waited for; matrix products, arithmetic and copies ran while one was open for 3% of the time, Pallas kernels for 0%

profile of v13, /device:TPU:0, one launch (start us, length us, event | category | flops | bytes accessed | tf_op | source)
XLA Modules:
  0.0 72.5 jit_solution(3184534530075856885)
XLA Ops:
  0.6 0.0 copy-start
  0.6 0.0 copy-start.4
  0.7 0.0 copy-start.5
  0.7 0.0 copy-start.1
  0.7 0.0 copy-start.2
  0.7 0.0 copy-start.6
  0.7 1.6 %reduce_max.54 = f32[128]{0:T(128)S(1)} reduce(f32[1,2048,128]{2,1,0:T(8,128)} %param.9, f32[]{:T(128)} %constant.110.clone.1), dimensions={0,1}, to_apply=%region_0.0 | reduce | flops 262016 | bytes 1049092 | tf_op jit(solution)/shard_map/reduce_max | solution.py:223
  2.3 0.0 copy-done
  2.3 0.3 fusion.8
  2.6 0.0 copy-done.4
  2.6 0.0 copy-done.5
  2.6 3.1 %collective-permute-start = (f32[1280]{0:T(1024)S(1)}, f32[1280]{0:T(1024)S(1)}, u32[]{:S(2)}, u32[]{:S(2)}) collective-permute-start(f32[1280]{0:T(1024)S(1)} %pad_maximum_fusion.1), channel_id=1, source_target_pairs={{0,1},{1,0},{2,3},{3,2},{4,5},{5,4},{6,7},{7,6},{8,9},{9,8},{10,11... | collective-permute-start | bytes 15368 | tf_op jit(solution)/shard_map/ppermute | solution.py:68
  5.7 0.0 copy-done.1
  5.7 0.0 copy-done.2
  5.7 0.1 fusion.145
  5.9 0.1 concatenate.67
  6.1 0.1 concatenate.68
  6.1 1.2 %collective-permute-done = f32[1280]{0:T(1024)S(1)} collective-permute-done((f32[1280]{0:T(1024)S(1)}, f32[1280]{0:T(1024)S(1)}, u32[]{:S(2)}, u32[]{:S(2)}) %collective-permute-start) | collective-permute-done | bytes 5152 | tf_op jit(solution)/shard_map/ppermute | solution.py:68
  7.4 0.1 fusion.146
  7.6 0.0 copy-done.6
  7.6 0.1 select_reduce_fusion
  7.7 0.0 copy-start.3
  7.7 2.4 %fusion.6 = bf16[1024,128]{1,0:T(8,128)(2,1)S(1)} fusion(s32[1024]{0:T(1024)S(1)} %fusion.57, f32[1,2048,128]{2,1,0:T(8,128)S(1)} %copy-done, f32[128]{0:T(128)S(1)} %log_add_fusion), kind=kOutput, calls=%fused_computation.7 | convolution fusion | flops 539885568 | bytes 1315328 | tf_op jit(solution)/shard_map/dot_general | solution.py:261
  10.1 2.1 %collective-permute-start.1 = (bf16[2,512,128]{2,1,0:T(8,128)(2,1)S(1)}, bf16[2,512,128]{2,1,0:T(8,128)(2,1)S(1)}, u32[]{:S(2)}, u32[]{:S(2)}) collective-permute-start(bf16[2,512,128]{2,1,0:T(8,128)(2,1)S(1)} %bitcast.470), channel_id=1, source_target_pairs={{0,1},{1,0},{2,3},{3,2},{4,5},{5,4},{6,7},{7,6},{8,9},{9,8},{10,11... | collective-permute-start | bytes 786440 | tf_op jit(solution)/shard_map/ppermute | solution.py:68
  12.2 0.0 copy-done.3
  12.2 0.1 fusion.59
  12.3 5.0 %collective-permute-done.1 = bf16[2,512,128]{2,1,0:T(8,128)(2,1)S(1)} collective-permute-done((bf16[2,512,128]{2,1,0:T(8,128)(2,1)S(1)}, bf16[2,512,128]{2,1,0:T(8,128)(2,1)S(1)}, u32[]{:S(2)}, u32[]{:S(2)}) %collective-permute-start.1) | collective-permute-done | bytes 262176 | tf_op jit(solution)/shard_map/ppermute | solution.py:68
  17.4 0.2 fusion.45
  17.6 0.4 fusion.47
  18.0 0.4 fusion.14
  18.4 0.1 fusion.61
  18.5 0.2 fusion.41
  18.7 0.4 fusion.43
  19.1 0.3 fusion.18
  19.4 0.1 fusion.63
  19.5 0.2 fusion.37
  19.7 0.4 fusion.39
  20.1 0.3 fusion.22
  20.5 0.1 fusion.65
  20.5 0.2 fusion.29
  20.8 0.4 fusion.32
  21.2 0.5 fusion.35
  21.6 2.8 %fusion.5 = f32[2048,128]{1,0:T(8,128)} fusion(bf16[1024,128]{1,0:T(8,128)(2,1)S(1)} %fusion.35, s32[1024]{0:T(1024)S(1)} %fusion.57, f32[1,2048,128]{2,1,0:T(8,128)S(1)} %copy-done), kind=kOutput, calls=%fused_computation.6 | convolution fusion | flops 539230208 | bytes 2363392 | tf_op jit(solution)/shard_map/dot_general | solution.py:274
  24.4 4.0 %all-to-all-start = ((f32[8,256,128]{2,1,0:T(8,128)}), f32[8,256,128]{2,1,0:T(8,128)S(1)}, u32[]{:S(2)}, u32[]{:S(2)}) async-start(f32[8,256,128]{2,1,0:T(8,128)} %bitcast.126), calls=%async_computation | async-start | bytes 2097152 | tf_op jit(solution)/shard_map/all_to_all | solution.py:298
  28.5 0.2 multiply_add_fusion.17
  28.6 0.1 multiply_add_fusion.9
  28.8 0.1 stack.8
  28.9 14.0 %all-to-all-done = f32[8,256,128]{2,1,0:T(8,128)S(1)} async-done(((f32[8,256,128]{2,1,0:T(8,128)}), f32[8,256,128]{2,1,0:T(8,128)S(1)}, u32[]{:S(2)}, u32[]{:S(2)}) %all-to-all-start) | async-done | bytes 1048608 | tf_op jit(solution)/shard_map/all_to_all | solution.py:298
  42.9 0.2 add_select_fusion
  43.1 2.7 %collective-permute-start.2 = (f32[256,128]{1,0:T(8,128)S(1)}, f32[256,128]{1,0:T(8,128)S(1)}, u32[]{:S(2)}, u32[]{:S(2)}) collective-permute-start(f32[256,128]{1,0:T(8,128)S(1)} %get-tuple-element.23), channel_id=1, source_target_pairs={{0,16},{16,0},{1,17},{17,1},{2,18},{18,2},{3,19},{19,3},{4,20},{20... | collective-permute-start | bytes 393224 | tf_op jit(solution)/shard_map/ppermute | solution.py:68
  45.8 0.1 slice_bitcast_fusion.7
  45.8 6.0 %collective-permute-done.2 = f32[256,128]{1,0:T(8,128)S(1)} collective-permute-done((f32[256,128]{1,0:T(8,128)S(1)}, f32[256,128]{1,0:T(8,128)S(1)}, u32[]{:S(2)}, u32[]{:S(2)}) %collective-permute-start.2) | collective-permute-done | bytes 131104 | tf_op jit(solution)/shard_map/ppermute | solution.py:68
  51.9 1.7 %multiply_add_fusion = f32[8,256,128]{2,1,0:T(8,128)} fusion(f32[256,128]{1,0:T(8,128)S(1)} %get-tuple-element.60, f32[8,128]{1,0:T(8,128)S(1)} %get-tuple-element.72, f32[256,128]{1,0:T(8,128)S(1)} %get-tuple-element.61, f32[8,128]{1,0:T(8,128)S(1)} %get-tuple-element.73, f32[256,128]{1,0:T(8,128)S(1)} %get-tuple-element.62, ...), kind=kLoop, calls=%fused_computation.14 | loop fusion | flops 4980736 | bytes 2400256 | tf_op jit(solution)/shard_map/add | solution.py:196
  53.6 3.6 %all-to-all-start.1 = ((f32[8,256,128]{2,1,0:T(8,128)}), f32[8,256,128]{2,1,0:T(8,128)S(1)}, u32[]{:S(2)}, u32[]{:S(2)}) async-start(f32[8,256,128]{2,1,0:T(8,128)} %multiply_add_fusion), calls=%async_computation.1 | async-start | bytes 2097152 | tf_op jit(solution)/shard_map/all_to_all | solution.py:331
  57.1 0.5 fusion.49
  57.6 0.6 slice_bitcast_fusion.18
  58.2 13.3 %all-to-all-done.1 = f32[8,256,128]{2,1,0:T(8,128)S(1)} async-done(((f32[8,256,128]{2,1,0:T(8,128)}), f32[8,256,128]{2,1,0:T(8,128)S(1)}, u32[]{:S(2)}, u32[]{:S(2)}) %all-to-all-start.1) | async-done | bytes 1048608 | tf_op jit(solution)/shard_map/all_to_all | solution.py:331
  71.5 1.0 %copy.13 = f32[1,2048,128]{2,1,0:T(8,128)} copy(f32[1,2048,128]{2,1,0:T(8,128)S(1)} %bitcast.468) | data formatting | bytes 2097152
  (39 shorter events, 0.5 us)
Async XLA Ops:
  0.6 1.6 %copy-start = (f32[1,2048,128]{2,1,0:T(8,128)S(1)}, f32[1,2048,128]{2,1,0:T(8,128)}, u32[]{:S(2)}) copy-start(f32[1,2048,128]{2,1,0:T(8,128)} %param.9) | copy-start | bytes 3145732
  0.6 1.9 %copy-start.4 = (s32[1,4,128]{2,1,0:T(4,128)S(1)}, s32[1,4,128]{2,1,0:T(4,128)}, u32[]{:S(2)}) copy-start(s32[1,4,128]{2,1,0:T(4,128)} %param.11) | copy-start | bytes 6148
  0.7 1.9 %copy-start.5 = (s32[1,4,128]{2,1,0:T(4,128)S(1)}, s32[1,4,128]{2,1,0:T(4,128)}, u32[]{:S(2)}) copy-start(s32[1,4,128]{2,1,0:T(4,128)} %param.10) | copy-start | bytes 6148
  0.7 5.0 %copy-start.1 = (f32[16,128]{1,0:T(8,128)S(1)}, f32[16,128]{1,0:T(8,128)}, u32[]{:S(2)}) copy-start(f32[16,128]{1,0:T(8,128)} %param.15) | copy-start | bytes 24580
  0.7 5.0 %copy-start.2 = (f32[128]{0:T(128)S(1)}, f32[128]{0:T(128)}, u32[]{:S(2)}) copy-start(f32[128]{0:T(128)} %param.14) | copy-start | bytes 1540
  0.7 6.9 %copy-start.6 = (s32[32]{0:T(128)S(1)}, s32[32]{0:T(128)}, u32[]{:S(2)}) copy-start(s32[32]{0:T(128)} %param.12) | copy-start | bytes 388
  2.6 4.7 %collective-permute-start = (f32[1280]{0:T(1024)S(1)}, f32[1280]{0:T(1024)S(1)}, u32[]{:S(2)}, u32[]{:S(2)}) collective-permute-start(f32[1280]{0:T(1024)S(1)} %pad_maximum_fusion.1), channel_id=1, source_target_pairs={{0,1},{1,0},{2,3},{3,2},{4,5},{5,4},{6,7},{7,6},{8,9},{9,8},{10,11... | collective-permute-start | bytes 15368 | tf_op jit(solution)/shard_map/ppermute | solution.py:68
  7.7 4.5 %copy-start.3 = (f32[128]{0:T(128)S(1)}, f32[128]{0:T(128)}, u32[]{:S(2)}) copy-start(f32[128]{0:T(128)} %param.13) | copy-start | bytes 1540
  10.1 7.2 %collective-permute-start.1 = (bf16[2,512,128]{2,1,0:T(8,128)(2,1)S(1)}, bf16[2,512,128]{2,1,0:T(8,128)(2,1)S(1)}, u32[]{:S(2)}, u32[]{:S(2)}) collective-permute-start(bf16[2,512,128]{2,1,0:T(8,128)(2,1)S(1)} %bitcast.470), channel_id=1, source_target_pairs={{0,1},{1,0},{2,3},{3,2},{4,5},{5,4},{6,7},{7,6},{8,9},{9,8},{10,11... | collective-permute-start | bytes 786440 | tf_op jit(solution)/shard_map/ppermute | solution.py:68
  24.4 18.5 %all-to-all-start = ((f32[8,256,128]{2,1,0:T(8,128)}), f32[8,256,128]{2,1,0:T(8,128)S(1)}, u32[]{:S(2)}, u32[]{:S(2)}) async-start(f32[8,256,128]{2,1,0:T(8,128)} %bitcast.126), calls=%async_computation | async-start | bytes 2097152 | tf_op jit(solution)/shard_map/all_to_all | solution.py:298
  43.1 8.7 %collective-permute-start.2 = (f32[256,128]{1,0:T(8,128)S(1)}, f32[256,128]{1,0:T(8,128)S(1)}, u32[]{:S(2)}, u32[]{:S(2)}) collective-permute-start(f32[256,128]{1,0:T(8,128)S(1)} %get-tuple-element.23), channel_id=1, source_target_pairs={{0,16},{16,0},{1,17},{17,1},{2,18},{18,2},{3,19},{19,3},{4,20},{20... | collective-permute-start | bytes 393224 | tf_op jit(solution)/shard_map/ppermute | solution.py:68
  53.6 18.0 %all-to-all-start.1 = ((f32[8,256,128]{2,1,0:T(8,128)}), f32[8,256,128]{2,1,0:T(8,128)S(1)}, u32[]{:S(2)}, u32[]{:S(2)}) async-start(f32[8,256,128]{2,1,0:T(8,128)} %multiply_add_fusion), calls=%async_computation.1 | async-start | bytes 2097152 | tf_op jit(solution)/shard_map/all_to_all | solution.py:331

commit v14 on v13

--- a/solution.py
+++ b/solution.py
@@ -177,8 +177,6 @@
     for t in reversed(range(years)):
         reach = pulls[years + t] * reach + (1.0 - pulls[years + t]) * responses[t]
     weight = jnp.where(group == 0, 1.0, 0.0)
-    start = (1.0 - weight) * other
-    after = weight * (other + reach * last)
     unit = jnp.eye(years + 2, dtype=jnp.float32)[:, :, None]
     state = unit[years]
     filtered = []
@@ -191,10 +189,11 @@
         state = pulls_here[t] * state + (1.0 - pulls_here[t]) * filtered[t]
         maps[t] = state
     maps = jnp.stack(maps)
-    smoothed = maps[:, years, None, :] * start + maps[:, years + 1, None, :] * after
+    smoothed = maps[:, years + 1, None, :] * (weight * reach * last)
     for s in range(years):
         smoothed = smoothed + maps[:, s, None, :] * by_year[s]
-    return smoothed
+    via_other = (1.0 - weight) * maps[:, years] + weight * maps[:, years + 1]
+    return smoothed + via_other[:, None, :] * other
 
 
 def group_maps(gains, pulls, groups):

time: 72.8 us -> 72.7 us (level)
    add x2 -> x1, other arithmetic: 1.76 us -> 1.71 us  [two_group_kalman(): return smoothed + via_other[:, None, :] * other]
where the time goes in v14:
time: 72.7 us; the launch traced here: 72.5 us
  waiting for transfers between devices  39.3 us (54%)
  starting transfers between devices  15.4 us (21%)
  other arithmetic  9.7 us (13%)
  matrix products  5.11 us (7%)
  local copies, waits for them, and re-layouts  1.94 us (3%)
  between operations  1.03 us (1%)
    all_to_all x1, waiting for transfers between devices, smooth_part(): lax.all_to_all(by_dest, 'tl', split_axis=0, concat_axis=0, tiled=True)  14 us
    all_to_all x1, waiting for transfers between devices, smooth_part(): lax.all_to_all(smoothed, 'tl', split_axis=0, concat_axis=0, tiled=True)  13.3 us
    ppermute x3, waiting for transfers between devices, shift_axis(): lax.ppermute(value, axis, [(i, (i + s) % count) for i in range(count)])  12 us
    ppermute x3, starting transfers between devices, shift_axis(): lax.ppermute(value, axis, [(i, (i + s) % count) for i in range(count)])  7.8 us
    all_to_all x1, starting transfers between devices, smooth_part(): lax.all_to_all(by_dest, 'tl', split_axis=0, concat_axis=0, tiled=True)  4 us
    all_to_all x1, starting transfers between devices, smooth_part(): lax.all_to_all(smoothed, 'tl', split_axis=0, concat_axis=0, tiled=True)  3.56 us
    dot_general x1, matrix products, body(): counts = jnp.dot(marks, flat_weighted, preferred_element_type=jnp.float32)  2.76 us
    dot_general x1, matrix products, body(): lax.dot_general(marks, table, (((0,), (0,)), ((), ())), preferred_element...  2.35 us
  transfers between devices with their start and end apart: 5, of which 5 were waited for; matrix products, arithmetic and copies ran while one was open for 3% of the time, Pallas kernels for 0%

profile of v14, /device:TPU:0, one launch (start us, length us, event | category | flops | bytes accessed | tf_op | source)
XLA Modules:
  0.0 72.5 jit_solution(16660055403490017344)
XLA Ops:
  0.6 0.0 copy-start
  0.6 0.0 copy-start.4
  0.7 0.0 copy-start.5
  0.7 0.0 copy-start.1
  0.7 0.0 copy-start.2
  0.7 0.0 copy-start.6
  0.7 1.6 %reduce_max.54 = f32[128]{0:T(128)S(1)} reduce(f32[1,2048,128]{2,1,0:T(8,128)} %param.9, f32[]{:T(128)} %constant.110.clone.1), dimensions={0,1}, to_apply=%region_0.0 | reduce | flops 262016 | bytes 1049092 | tf_op jit(solution)/shard_map/reduce_max | solution.py:222
  2.3 0.0 copy-done
  2.3 0.3 fusion.8
  2.6 0.0 copy-done.4
  2.6 0.0 copy-done.5
  2.6 3.1 %collective-permute-start = (f32[1280]{0:T(1024)S(1)}, f32[1280]{0:T(1024)S(1)}, u32[]{:S(2)}, u32[]{:S(2)}) collective-permute-start(f32[1280]{0:T(1024)S(1)} %pad_maximum_fusion.1), channel_id=1, source_target_pairs={{0,1},{1,0},{2,3},{3,2},{4,5},{5,4},{6,7},{7,6},{8,9},{9,8},{10,11... | collective-permute-start | bytes 15368 | tf_op jit(solution)/shard_map/ppermute | solution.py:68
  5.7 0.0 copy-done.1
  5.7 0.0 copy-done.2
  5.7 0.1 fusion.146
  5.8 0.1 fusion.147
  5.9 0.1 concatenate.67
  6.1 0.1 concatenate.68
  6.1 1.2 %collective-permute-done = f32[1280]{0:T(1024)S(1)} collective-permute-done((f32[1280]{0:T(1024)S(1)}, f32[1280]{0:T(1024)S(1)}, u32[]{:S(2)}, u32[]{:S(2)}) %collective-permute-start) | collective-permute-done | bytes 5152 | tf_op jit(solution)/shard_map/ppermute | solution.py:68
  7.4 0.1 fusion.148
  7.6 0.0 copy-done.6
  7.6 0.1 select_reduce_fusion
  7.7 0.0 copy-start.3
  7.7 2.4 %fusion.6 = bf16[1024,128]{1,0:T(8,128)(2,1)S(1)} fusion(s32[1024]{0:T(1024)S(1)} %fusion.57, f32[1,2048,128]{2,1,0:T(8,128)S(1)} %copy-done, f32[128]{0:T(128)S(1)} %log_add_fusion), kind=kOutput, calls=%fused_computation.7 | convolution fusion | flops 539885568 | bytes 1315328 | tf_op jit(solution)/shard_map/dot_general | solution.py:260
  10.1 2.1 %collective-permute-start.1 = (bf16[2,512,128]{2,1,0:T(8,128)(2,1)S(1)}, bf16[2,512,128]{2,1,0:T(8,128)(2,1)S(1)}, u32[]{:S(2)}, u32[]{:S(2)}) collective-permute-start(bf16[2,512,128]{2,1,0:T(8,128)(2,1)S(1)} %bitcast.450), channel_id=1, source_target_pairs={{0,1},{1,0},{2,3},{3,2},{4,5},{5,4},{6,7},{7,6},{8,9},{9,8},{10,11... | collective-permute-start | bytes 786440 | tf_op jit(solution)/shard_map/ppermute | solution.py:68
  12.2 0.0 copy-done.3
  12.2 0.1 fusion.59
  12.3 5.0 %collective-permute-done.1 = bf16[2,512,128]{2,1,0:T(8,128)(2,1)S(1)} collective-permute-done((bf16[2,512,128]{2,1,0:T(8,128)(2,1)S(1)}, bf16[2,512,128]{2,1,0:T(8,128)(2,1)S(1)}, u32[]{:S(2)}, u32[]{:S(2)}) %collective-permute-start.1) | collective-permute-done | bytes 262176 | tf_op jit(solution)/shard_map/ppermute | solution.py:68
  17.4 0.2 fusion.45
  17.6 0.4 fusion.47
  18.0 0.4 fusion.14
  18.4 0.1 fusion.61
  18.5 0.2 fusion.41
  18.7 0.4 fusion.43
  19.1 0.3 fusion.18
  19.4 0.1 fusion.63
  19.5 0.2 fusion.37
  19.7 0.4 fusion.39
  20.1 0.3 fusion.22
  20.5 0.1 fusion.65
  20.5 0.2 fusion.29
  20.8 0.4 fusion.32
  21.2 0.5 fusion.35
  21.6 2.8 %fusion.5 = f32[2048,128]{1,0:T(8,128)} fusion(bf16[1024,128]{1,0:T(8,128)(2,1)S(1)} %fusion.35, s32[1024]{0:T(1024)S(1)} %fusion.57, f32[1,2048,128]{2,1,0:T(8,128)S(1)} %copy-done), kind=kOutput, calls=%fused_computation.6 | convolution fusion | flops 539230208 | bytes 2363392 | tf_op jit(solution)/shard_map/dot_general | solution.py:273
  24.4 4.0 %all-to-all-start = ((f32[8,256,128]{2,1,0:T(8,128)}), f32[8,256,128]{2,1,0:T(8,128)S(1)}, u32[]{:S(2)}, u32[]{:S(2)}) async-start(f32[8,256,128]{2,1,0:T(8,128)} %bitcast.133), calls=%async_computation | async-start | bytes 2097152 | tf_op jit(solution)/shard_map/all_to_all | solution.py:297
  28.5 0.2 multiply_add_fusion.9
  28.6 0.1 multiply_add_fusion.1
  28.8 0.1 stack.8
  28.9 14.0 %all-to-all-done = f32[8,256,128]{2,1,0:T(8,128)S(1)} async-done(((f32[8,256,128]{2,1,0:T(8,128)}), f32[8,256,128]{2,1,0:T(8,128)S(1)}, u32[]{:S(2)}, u32[]{:S(2)}) %all-to-all-start) | async-done | bytes 1048608 | tf_op jit(solution)/shard_map/all_to_all | solution.py:297
  42.9 0.2 add_select_fusion
  43.1 2.7 %collective-permute-start.2 = (f32[256,128]{1,0:T(8,128)S(1)}, f32[256,128]{1,0:T(8,128)S(1)}, u32[]{:S(2)}, u32[]{:S(2)}) collective-permute-start(f32[256,128]{1,0:T(8,128)S(1)} %add_select_fusion), channel_id=1, source_target_pairs={{0,16},{16,0},{1,17},{17,1},{2,18},{18,2},{3,19},{19,3},{4,20},{20... | collective-permute-start | bytes 393224 | tf_op jit(solution)/shard_map/ppermute | solution.py:68
  45.8 0.1 slice_bitcast_fusion.7
  45.8 0.1 multiply_bitcast_fusion
  46.0 5.9 %collective-permute-done.2 = f32[256,128]{1,0:T(8,128)S(1)} collective-permute-done((f32[256,128]{1,0:T(8,128)S(1)}, f32[256,128]{1,0:T(8,128)S(1)}, u32[]{:S(2)}, u32[]{:S(2)}) %collective-permute-start.2) | collective-permute-done | bytes 131104 | tf_op jit(solution)/shard_map/ppermute | solution.py:68
  51.8 1.7 %multiply_add_fusion = f32[8,256,128]{2,1,0:T(8,128)} fusion(f32[256,128]{1,0:T(8,128)S(1)} %collective-permute-done.2, f32[8,128]{1,0:T(8,128)S(1)} %get-tuple-element.69, f32[256,128]{1,0:T(8,128)S(1)} %get-tuple-element.59, f32[8,128]{1,0:T(8,128)S(1)} %get-tuple-element.70, f32[256,128]{1,0:T(8,128)S(1)} %get-tuple-element.60, ...), kind=kLoop, calls=%fused_computation.14 | loop fusion | flops 4980736 | bytes 2400256 | tf_op jit(solution)/shard_map/add | solution.py:196
  53.5 3.6 %all-to-all-start.1 = ((f32[8,256,128]{2,1,0:T(8,128)}), f32[8,256,128]{2,1,0:T(8,128)S(1)}, u32[]{:S(2)}, u32[]{:S(2)}) async-start(f32[8,256,128]{2,1,0:T(8,128)} %multiply_add_fusion), calls=%async_computation.1 | async-start | bytes 2097152 | tf_op jit(solution)/shard_map/all_to_all | solution.py:330
  57.1 0.5 fusion.49
  57.6 0.6 slice_bitcast_fusion.17
  58.2 13.3 %all-to-all-done.1 = f32[8,256,128]{2,1,0:T(8,128)S(1)} async-done(((f32[8,256,128]{2,1,0:T(8,128)}), f32[8,256,128]{2,1,0:T(8,128)S(1)}, u32[]{:S(2)}, u32[]{:S(2)}) %all-to-all-start.1) | async-done | bytes 1048608 | tf_op jit(solution)/shard_map/all_to_all | solution.py:330
  71.5 1.0 %copy.13 = f32[1,2048,128]{2,1,0:T(8,128)} copy(f32[1,2048,128]{2,1,0:T(8,128)S(1)} %bitcast.448) | data formatting | bytes 2097152
  (38 shorter events, 0.5 us)
Async XLA Ops:
  0.6 1.6 %copy-start = (f32[1,2048,128]{2,1,0:T(8,128)S(1)}, f32[1,2048,128]{2,1,0:T(8,128)}, u32[]{:S(2)}) copy-start(f32[1,2048,128]{2,1,0:T(8,128)} %param.9) | copy-start | bytes 3145732
  0.6 1.9 %copy-start.4 = (s32[1,4,128]{2,1,0:T(4,128)S(1)}, s32[1,4,128]{2,1,0:T(4,128)}, u32[]{:S(2)}) copy-start(s32[1,4,128]{2,1,0:T(4,128)} %param.11) | copy-start | bytes 6148
  0.7 1.9 %copy-start.5 = (s32[1,4,128]{2,1,0:T(4,128)S(1)}, s32[1,4,128]{2,1,0:T(4,128)}, u32[]{:S(2)}) copy-start(s32[1,4,128]{2,1,0:T(4,128)} %param.10) | copy-start | bytes 6148
  0.7 5.0 %copy-start.1 = (f32[16,128]{1,0:T(8,128)S(1)}, f32[16,128]{1,0:T(8,128)}, u32[]{:S(2)}) copy-start(f32[16,128]{1,0:T(8,128)} %param.15) | copy-start | bytes 24580
  0.7 5.0 %copy-start.2 = (f32[128]{0:T(128)S(1)}, f32[128]{0:T(128)}, u32[]{:S(2)}) copy-start(f32[128]{0:T(128)} %param.14) | copy-start | bytes 1540
  0.7 6.9 %copy-start.6 = (s32[32]{0:T(128)S(1)}, s32[32]{0:T(128)}, u32[]{:S(2)}) copy-start(s32[32]{0:T(128)} %param.12) | copy-start | bytes 388
  2.6 4.7 %collective-permute-start = (f32[1280]{0:T(1024)S(1)}, f32[1280]{0:T(1024)S(1)}, u32[]{:S(2)}, u32[]{:S(2)}) collective-permute-start(f32[1280]{0:T(1024)S(1)} %pad_maximum_fusion.1), channel_id=1, source_target_pairs={{0,1},{1,0},{2,3},{3,2},{4,5},{5,4},{6,7},{7,6},{8,9},{9,8},{10,11... | collective-permute-start | bytes 15368 | tf_op jit(solution)/shard_map/ppermute | solution.py:68
  7.7 4.5 %copy-start.3 = (f32[128]{0:T(128)S(1)}, f32[128]{0:T(128)}, u32[]{:S(2)}) copy-start(f32[128]{0:T(128)} %param.13) | copy-start | bytes 1540
  10.1 7.2 %collective-permute-start.1 = (bf16[2,512,128]{2,1,0:T(8,128)(2,1)S(1)}, bf16[2,512,128]{2,1,0:T(8,128)(2,1)S(1)}, u32[]{:S(2)}, u32[]{:S(2)}) collective-permute-start(bf16[2,512,128]{2,1,0:T(8,128)(2,1)S(1)} %bitcast.450), channel_id=1, source_target_pairs={{0,1},{1,0},{2,3},{3,2},{4,5},{5,4},{6,7},{7,6},{8,9},{9,8},{10,11... | collective-permute-start | bytes 786440 | tf_op jit(solution)/shard_map/ppermute | solution.py:68
  24.4 18.5 %all-to-all-start = ((f32[8,256,128]{2,1,0:T(8,128)}), f32[8,256,128]{2,1,0:T(8,128)S(1)}, u32[]{:S(2)}, u32[]{:S(2)}) async-start(f32[8,256,128]{2,1,0:T(8,128)} %bitcast.133), calls=%async_computation | async-start | bytes 2097152 | tf_op jit(solution)/shard_map/all_to_all | solution.py:297
  43.1 8.7 %collective-permute-start.2 = (f32[256,128]{1,0:T(8,128)S(1)}, f32[256,128]{1,0:T(8,128)S(1)}, u32[]{:S(2)}, u32[]{:S(2)}) collective-permute-start(f32[256,128]{1,0:T(8,128)S(1)} %add_select_fusion), channel_id=1, source_target_pairs={{0,16},{16,0},{1,17},{17,1},{2,18},{18,2},{3,19},{19,3},{4,20},{20... | collective-permute-start | bytes 393224 | tf_op jit(solution)/shard_map/ppermute | solution.py:68
  53.5 18.0 %all-to-all-start.1 = ((f32[8,256,128]{2,1,0:T(8,128)}), f32[8,256,128]{2,1,0:T(8,128)S(1)}, u32[]{:S(2)}, u32[]{:S(2)}) async-start(f32[8,256,128]{2,1,0:T(8,128)} %multiply_add_fusion), calls=%async_computation.1 | async-start | bytes 2097152 | tf_op jit(solution)/shard_map/all_to_all | solution.py:330

commit v15 on v14

--- a/solution.py
+++ b/solution.py
@@ -192,6 +192,7 @@
     smoothed = maps[:, years + 1, None, :] * (weight * reach * last)
     for s in range(years):
         smoothed = smoothed + maps[:, s, None, :] * by_year[s]
+    smoothed = lax.optimization_barrier(smoothed)
     via_other = (1.0 - weight) * maps[:, years] + weight * maps[:, years + 1]
     return smoothed + via_other[:, None, :] * other
 

time: 72.7 us -> 72.1 us (level)
  transfers between devices with their start and end apart: 5 -> 5, of which waited for: 5 -> 5; matrix products, arithmetic and copies ran while one was open for 3% -> 4% of each run, Pallas kernels for 0% -> 0%
where the time goes in v15:
time: 72.1 us; the launch traced here: 71.8 us
  waiting for transfers between devices  38.7 us (54%)
  starting transfers between devices  15.4 us (21%)
  other arithmetic  9.69 us (13%)
  matrix products  5.11 us (7%)
  local copies, waits for them, and re-layouts  1.94 us (3%)
  between operations  1.02 us (1%)
    all_to_all x1, waiting for transfers between devices, smooth_part(): lax.all_to_all(by_dest, 'tl', split_axis=0, concat_axis=0, tiled=True)  14 us
    all_to_all x1, waiting for transfers between devices, smooth_part(): lax.all_to_all(smoothed, 'tl', split_axis=0, concat_axis=0, tiled=True)  13.3 us
    ppermute x3, waiting for transfers between devices, shift_axis(): lax.ppermute(value, axis, [(i, (i + s) % count) for i in range(count)])  11.4 us
    ppermute x3, starting transfers between devices, shift_axis(): lax.ppermute(value, axis, [(i, (i + s) % count) for i in range(count)])  7.8 us
    all_to_all x1, starting transfers between devices, smooth_part(): lax.all_to_all(by_dest, 'tl', split_axis=0, concat_axis=0, tiled=True)  4 us
    all_to_all x1, starting transfers between devices, smooth_part(): lax.all_to_all(smoothed, 'tl', split_axis=0, concat_axis=0, tiled=True)  3.56 us
    dot_general x1, matrix products, body(): counts = jnp.dot(marks, flat_weighted, preferred_element_type=jnp.float32)  2.76 us
    dot_general x1, matrix products, body(): lax.dot_general(marks, table, (((0,), (0,)), ((), ())), preferred_element...  2.35 us
  transfers between devices with their start and end apart: 5, of which 5 were waited for; matrix products, arithmetic and copies ran while one was open for 4% of the time, Pallas kernels for 0%

profile of v15, /device:TPU:0, one launch (start us, length us, event | category | flops | bytes accessed | tf_op | source)
XLA Modules:
  0.0 71.8 jit_solution(752648949117470867)
XLA Ops:
  0.6 0.0 copy-start
  0.6 0.0 copy-start.4
  0.7 0.0 copy-start.5
  0.7 0.0 copy-start.1
  0.7 0.0 copy-start.2
  0.7 0.0 copy-start.6
  0.7 1.6 %reduce_max.54 = f32[128]{0:T(128)S(1)} reduce(f32[1,2048,128]{2,1,0:T(8,128)} %param.9, f32[]{:T(128)} %constant.110.clone.1), dimensions={0,1}, to_apply=%region_0.0 | reduce | flops 262016 | bytes 1049092 | tf_op jit(solution)/shard_map/reduce_max | solution.py:223
  2.3 0.0 copy-done
  2.3 0.3 fusion.8
  2.6 0.0 copy-done.4
  2.6 0.0 copy-done.5
  2.6 3.1 %collective-permute-start = (f32[1280]{0:T(1024)S(1)}, f32[1280]{0:T(1024)S(1)}, u32[]{:S(2)}, u32[]{:S(2)}) collective-permute-start(f32[1280]{0:T(1024)S(1)} %pad_maximum_fusion.1), channel_id=1, source_target_pairs={{0,1},{1,0},{2,3},{3,2},{4,5},{5,4},{6,7},{7,6},{8,9},{9,8},{10,11... | collective-permute-start | bytes 15368 | tf_op jit(solution)/shard_map/ppermute | solution.py:68
  5.7 0.0 copy-done.1
  5.7 0.0 copy-done.2
  5.7 0.1 fusion.147
  5.9 0.1 concatenate.67
  6.1 0.1 concatenate.68
  6.1 1.2 %collective-permute-done = f32[1280]{0:T(1024)S(1)} collective-permute-done((f32[1280]{0:T(1024)S(1)}, f32[1280]{0:T(1024)S(1)}, u32[]{:S(2)}, u32[]{:S(2)}) %collective-permute-start) | collective-permute-done | bytes 5152 | tf_op jit(solution)/shard_map/ppermute | solution.py:68
  7.4 0.1 fusion.148
  7.6 0.0 copy-done.6
  7.6 0.1 select_reduce_fusion
  7.7 0.0 copy-start.3
  7.7 2.4 %fusion.6 = bf16[1024,128]{1,0:T(8,128)(2,1)S(1)} fusion(s32[1024]{0:T(1024)S(1)} %fusion.57, f32[1,2048,128]{2,1,0:T(8,128)S(1)} %copy-done, f32[128]{0:T(128)S(1)} %log_add_fusion), kind=kOutput, calls=%fused_computation.7 | convolution fusion | flops 539885568 | bytes 1315328 | tf_op jit(solution)/shard_map/dot_general | solution.py:261
  10.1 2.1 %collective-permute-start.1 = (bf16[2,512,128]{2,1,0:T(8,128)(2,1)S(1)}, bf16[2,512,128]{2,1,0:T(8,128)(2,1)S(1)}, u32[]{:S(2)}, u32[]{:S(2)}) collective-permute-start(bf16[2,512,128]{2,1,0:T(8,128)(2,1)S(1)} %bitcast.450), channel_id=1, source_target_pairs={{0,1},{1,0},{2,3},{3,2},{4,5},{5,4},{6,7},{7,6},{8,9},{9,8},{10,11... | collective-permute-start | bytes 786440 | tf_op jit(solution)/shard_map/ppermute | solution.py:68
  12.2 0.0 copy-done.3
  12.2 0.1 fusion.59
  12.3 5.0 %collective-permute-done.1 = bf16[2,512,128]{2,1,0:T(8,128)(2,1)S(1)} collective-permute-done((bf16[2,512,128]{2,1,0:T(8,128)(2,1)S(1)}, bf16[2,512,128]{2,1,0:T(8,128)(2,1)S(1)}, u32[]{:S(2)}, u32[]{:S(2)}) %collective-permute-start.1) | collective-permute-done | bytes 262176 | tf_op jit(solution)/shard_map/ppermute | solution.py:68
  17.4 0.2 fusion.45
  17.6 0.4 fusion.47
  18.0 0.4 fusion.14
  18.4 0.1 fusion.61
  18.5 0.2 fusion.41
  18.7 0.4 fusion.43
  19.1 0.3 fusion.18
  19.4 0.1 fusion.63
  19.5 0.2 fusion.37
  19.7 0.4 fusion.39
  20.1 0.3 fusion.22
  20.5 0.1 fusion.65
  20.5 0.2 fusion.29
  20.8 0.4 fusion.32
  21.2 0.5 fusion.35
  21.6 2.8 %fusion.5 = f32[2048,128]{1,0:T(8,128)} fusion(bf16[1024,128]{1,0:T(8,128)(2,1)S(1)} %fusion.35, s32[1024]{0:T(1024)S(1)} %fusion.57, f32[1,2048,128]{2,1,0:T(8,128)S(1)} %copy-done), kind=kOutput, calls=%fused_computation.6 | convolution fusion | flops 539230208 | bytes 2363392 | tf_op jit(solution)/shard_map/dot_general | solution.py:274
  24.4 4.0 %all-to-all-start = ((f32[8,256,128]{2,1,0:T(8,128)}), f32[8,256,128]{2,1,0:T(8,128)S(1)}, u32[]{:S(2)}, u32[]{:S(2)}) async-start(f32[8,256,128]{2,1,0:T(8,128)} %bitcast.133), calls=%async_computation | async-start | bytes 2097152 | tf_op jit(solution)/shard_map/all_to_all | solution.py:298
  28.5 0.2 multiply_add_fusion.10
  28.6 0.1 multiply_add_fusion.2
  28.8 0.1 stack.8
  28.9 14.0 %all-to-all-done = f32[8,256,128]{2,1,0:T(8,128)S(1)} async-done(((f32[8,256,128]{2,1,0:T(8,128)}), f32[8,256,128]{2,1,0:T(8,128)S(1)}, u32[]{:S(2)}, u32[]{:S(2)}) %all-to-all-start) | async-done | bytes 1048608 | tf_op jit(solution)/shard_map/all_to_all | solution.py:298
  42.9 0.2 add_select_fusion
  43.1 2.7 %collective-permute-start.2 = (f32[256,128]{1,0:T(8,128)S(1)}, f32[256,128]{1,0:T(8,128)S(1)}, u32[]{:S(2)}, u32[]{:S(2)}) collective-permute-start(f32[256,128]{1,0:T(8,128)S(1)} %add_select_fusion), channel_id=1, source_target_pairs={{0,16},{16,0},{1,17},{17,1},{2,18},{18,2},{3,19},{19,3},{4,20},{20... | collective-permute-start | bytes 393224 | tf_op jit(solution)/shard_map/ppermute | solution.py:68
  45.8 0.1 slice_bitcast_fusion.7
  45.8 0.1 multiply_bitcast_fusion
  46.0 0.6 multiply_add_fusion.1
  46.6 5.2 %collective-permute-done.2 = f32[256,128]{1,0:T(8,128)S(1)} collective-permute-done((f32[256,128]{1,0:T(8,128)S(1)}, f32[256,128]{1,0:T(8,128)S(1)}, u32[]{:S(2)}, u32[]{:S(2)}) %collective-permute-start.2) | collective-permute-done | bytes 131104 | tf_op jit(solution)/shard_map/ppermute | solution.py:68
  51.8 1.1 %multiply_add_fusion = f32[8,256,128]{2,1,0:T(8,128)} fusion(f32[8,256,128]{2,1,0:T(8,128)S(1)} %multiply_add_fusion.1, f32[256,128]{1,0:T(8,128)S(1)} %collective-permute-done.2, f32[8,128]{1,0:T(8,128)S(1)} %get-tuple-element.67), kind=kLoop, calls=%fused_computation.14 | loop fusion | flops 524288 | bytes 2232320 | tf_op jit(solution)/shard_map/add | solution.py:197
  52.9 3.6 %all-to-all-start.1 = ((f32[8,256,128]{2,1,0:T(8,128)}), f32[8,256,128]{2,1,0:T(8,128)S(1)}, u32[]{:S(2)}, u32[]{:S(2)}) async-start(f32[8,256,128]{2,1,0:T(8,128)} %multiply_add_fusion), calls=%async_computation.1 | async-start | bytes 2097152 | tf_op jit(solution)/shard_map/all_to_all | solution.py:331
  56.5 0.5 fusion.49
  57.0 0.6 slice_bitcast_fusion.17
  57.5 13.3 %all-to-all-done.1 = f32[8,256,128]{2,1,0:T(8,128)S(1)} async-done(((f32[8,256,128]{2,1,0:T(8,128)}), f32[8,256,128]{2,1,0:T(8,128)S(1)}, u32[]{:S(2)}, u32[]{:S(2)}) %all-to-all-start.1) | async-done | bytes 1048608 | tf_op jit(solution)/shard_map/all_to_all | solution.py:331
  70.9 1.0 %copy.13 = f32[1,2048,128]{2,1,0:T(8,128)} copy(f32[1,2048,128]{2,1,0:T(8,128)S(1)} %bitcast.448) | data formatting | bytes 2097152
  (38 shorter events, 0.5 us)
Async XLA Ops:
  0.6 1.6 %copy-start = (f32[1,2048,128]{2,1,0:T(8,128)S(1)}, f32[1,2048,128]{2,1,0:T(8,128)}, u32[]{:S(2)}) copy-start(f32[1,2048,128]{2,1,0:T(8,128)} %param.9) | copy-start | bytes 3145732
  0.6 1.9 %copy-start.4 = (s32[1,4,128]{2,1,0:T(4,128)S(1)}, s32[1,4,128]{2,1,0:T(4,128)}, u32[]{:S(2)}) copy-start(s32[1,4,128]{2,1,0:T(4,128)} %param.11) | copy-start | bytes 6148
  0.7 1.9 %copy-start.5 = (s32[1,4,128]{2,1,0:T(4,128)S(1)}, s32[1,4,128]{2,1,0:T(4,128)}, u32[]{:S(2)}) copy-start(s32[1,4,128]{2,1,0:T(4,128)} %param.10) | copy-start | bytes 6148
  0.7 5.0 %copy-start.1 = (f32[16,128]{1,0:T(8,128)S(1)}, f32[16,128]{1,0:T(8,128)}, u32[]{:S(2)}) copy-start(f32[16,128]{1,0:T(8,128)} %param.15) | copy-start | bytes 24580
  0.7 5.0 %copy-start.2 = (f32[128]{0:T(128)S(1)}, f32[128]{0:T(128)}, u32[]{:S(2)}) copy-start(f32[128]{0:T(128)} %param.14) | copy-start | bytes 1540
  0.7 6.9 %copy-start.6 = (s32[32]{0:T(128)S(1)}, s32[32]{0:T(128)}, u32[]{:S(2)}) copy-start(s32[32]{0:T(128)} %param.12) | copy-start | bytes 388
  2.6 4.7 %collective-permute-start = (f32[1280]{0:T(1024)S(1)}, f32[1280]{0:T(1024)S(1)}, u32[]{:S(2)}, u32[]{:S(2)}) collective-permute-start(f32[1280]{0:T(1024)S(1)} %pad_maximum_fusion.1), channel_id=1, source_target_pairs={{0,1},{1,0},{2,3},{3,2},{4,5},{5,4},{6,7},{7,6},{8,9},{9,8},{10,11... | collective-permute-start | bytes 15368 | tf_op jit(solution)/shard_map/ppermute | solution.py:68
  7.7 4.5 %copy-start.3 = (f32[128]{0:T(128)S(1)}, f32[128]{0:T(128)}, u32[]{:S(2)}) copy-start(f32[128]{0:T(128)} %param.13) | copy-start | bytes 1540
  10.1 7.2 %collective-permute-start.1 = (bf16[2,512,128]{2,1,0:T(8,128)(2,1)S(1)}, bf16[2,512,128]{2,1,0:T(8,128)(2,1)S(1)}, u32[]{:S(2)}, u32[]{:S(2)}) collective-permute-start(bf16[2,512,128]{2,1,0:T(8,128)(2,1)S(1)} %bitcast.450), channel_id=1, source_target_pairs={{0,1},{1,0},{2,3},{3,2},{4,5},{5,4},{6,7},{7,6},{8,9},{9,8},{10,11... | collective-permute-start | bytes 786440 | tf_op jit(solution)/shard_map/ppermute | solution.py:68
  24.4 18.5 %all-to-all-start = ((f32[8,256,128]{2,1,0:T(8,128)}), f32[8,256,128]{2,1,0:T(8,128)S(1)}, u32[]{:S(2)}, u32[]{:S(2)}) async-start(f32[8,256,128]{2,1,0:T(8,128)} %bitcast.133), calls=%async_computation | async-start | bytes 2097152 | tf_op jit(solution)/shard_map/all_to_all | solution.py:298
  43.1 8.7 %collective-permute-start.2 = (f32[256,128]{1,0:T(8,128)S(1)}, f32[256,128]{1,0:T(8,128)S(1)}, u32[]{:S(2)}, u32[]{:S(2)}) collective-permute-start(f32[256,128]{1,0:T(8,128)S(1)} %add_select_fusion), channel_id=1, source_target_pairs={{0,16},{16,0},{1,17},{17,1},{2,18},{18,2},{3,19},{19,3},{4,20},{20... | collective-permute-start | bytes 393224 | tf_op jit(solution)/shard_map/ppermute | solution.py:68
  52.9 18.0 %all-to-all-start.1 = ((f32[8,256,128]{2,1,0:T(8,128)}), f32[8,256,128]{2,1,0:T(8,128)S(1)}, u32[]{:S(2)}, u32[]{:S(2)}) async-start(f32[8,256,128]{2,1,0:T(8,128)} %multiply_add_fusion), calls=%async_computation.1 | async-start | bytes 2097152 | tf_op jit(solution)/shard_map/all_to_all | solution.py:331

commit v16 on v15

--- a/solution.py
+++ b/solution.py
@@ -271,7 +271,11 @@
     doc_topics = doc_topics_all[:local_docs]
 
     flat_weighted = weighted.reshape(-1, topics)
-    counts = jnp.dot(marks, flat_weighted, preferred_element_type=jnp.float32)
+    held_columns = lax.optimization_barrier(local_columns)
+    held_marks = lax.optimization_barrier(
+        (row_words[:, None] == held_columns[None, :]).astype(jnp.bfloat16)
+    )
+    counts = jnp.dot(held_marks, flat_weighted, preferred_element_type=jnp.float32)
     pseudo = local_beta + jnp.log1p(counts)
 
     gains, filt_vars, shrinks, infos = variance_tables(obs_precision, drift_var)

time: 72.1 us -> 78.8 us (1.093)
  other arithmetic: 9.69 us -> 18.5 us
  starting transfers between devices: 15.4 us -> 13.1 us
  waiting for transfers between devices: 38.7 us -> 37.9 us
    convert_element_type x0 -> x1, other arithmetic: none -> 2.09 us  [body(): (row_words[:, None] == held_columns[None, :]).astype(jnp.bfloat16)]
    ppermute x3, starting transfers between devices: 7.8 us -> 5.79 us  [shift_axis(): lax.ppermute(value, axis, [(i, (i + s) % count) for i in range(count)])]
    broadcast_in_dim x2, other arithmetic: 0.17 us -> 2.11 us  [variance_tables(): lax.scan(forward_step, start_var, obs_precision, unroll=True)]
    dot_general x1, matrix products: 2.35 us -> 3.58 us  [body(): lax.dot_general(marks, table, (((0,), (0,)), ((), ())), preferred_element...]
    reduce_sum x1, other arithmetic: 0.29 us -> 1.52 us  [body(): local_total = jnp.sum(jnp.exp(local_beta - local_peak), axis=0)]
    mul x2, other arithmetic: 0.17 us -> 1.15 us  [two_group_kalman(): smoothed = maps[:, years + 1, None, :] * (weight * reach * last)]
    ppermute x3, waiting for transfers between devices: 11.4 us -> 10.6 us  [shift_axis(): lax.ppermute(value, axis, [(i, (i + s) % count) for i in range(count)])]
  transfers between devices with their start and end apart: 5 -> 5, of which waited for: 5 -> 4; matrix products, arithmetic and copies ran while one was open for 4% -> 12% of each run, Pallas kernels for 0% -> 0%
where the time goes in v16:
time: 78.8 us; the launch traced here: 78.2 us
  waiting for transfers between devices  37.9 us (48%)
  other arithmetic  18.5 us (23%)
  starting transfers between devices  13.1 us (17%)
  matrix products  5.81 us (7%)
  local copies, waits for them, and re-layouts  1.91 us (2%)
  between operations  0.98 us (1%)
    all_to_all x1, waiting for transfers between devices, smooth_part(): lax.all_to_all(by_dest, 'tl', split_axis=0, concat_axis=0, tiled=True)  14 us
    all_to_all x1, waiting for transfers between devices, smooth_part(): lax.all_to_all(smoothed, 'tl', split_axis=0, concat_axis=0, tiled=True)  13.3 us
    ppermute x3, waiting for transfers between devices, shift_axis(): lax.ppermute(value, axis, [(i, (i + s) % count) for i in range(count)])  10.6 us
    ppermute x3, starting transfers between devices, shift_axis(): lax.ppermute(value, axis, [(i, (i + s) % count) for i in range(count)])  5.79 us
    all_to_all x1, starting transfers between devices, smooth_part(): lax.all_to_all(by_dest, 'tl', split_axis=0, concat_axis=0, tiled=True)  3.79 us
    dot_general x1, matrix products, body(): lax.dot_general(marks, table, (((0,), (0,)), ((), ())), preferred_element...  3.58 us
    all_to_all x1, starting transfers between devices, smooth_part(): lax.all_to_all(smoothed, 'tl', split_axis=0, concat_axis=0, tiled=True)  3.56 us
    dot_general x1, matrix products, body(): jnp.dot(held_marks, flat_weighted, preferred_element_type=jnp.float32)  2.23 us
  transfers between devices with their start and end apart: 5, of which 4 were waited for; matrix products, arithmetic and copies ran while one was open for 12% of the time, Pallas kernels for 0%

profile of v16, /device:TPU:0, one launch (start us, length us, event | category | flops | bytes accessed | tf_op | source)
XLA Modules:
  0.0 78.2 jit_solution(11668607567182197833)
XLA Ops:
  0.6 1.5 %reduce_max.54 = f32[128]{0:T(128)S(1)} reduce(f32[1,2048,128]{2,1,0:T(8,128)} %param.9, f32[]{:T(128)} %constant.112.clone.1), dimensions={0,1}, to_apply=%region_0.0 | reduce | flops 262016 | bytes 1049092 | tf_op jit(solution)/shard_map/reduce_max | solution.py:223
  2.1 1.5 %fusion.6 = f32[128]{0:T(128)S(1)} fusion(f32[1,2048,128]{2,1,0:T(8,128)} %param.9, f32[128]{0:T(128)S(1)} %reduce_max.54), kind=kLoop, calls=%fused_computation.11 | loop fusion | flops 524160 | bytes 1049600 | tf_op jit(solution)/shard_map/reduce_sum | solution.py:224
  3.7 0.7 convert_bitcast_fusion
  4.4 3.1 %collective-permute-start = (f32[1280]{0:T(1024)S(1)}, f32[1280]{0:T(1024)S(1)}, u32[]{:S(2)}, u32[]{:S(2)}) collective-permute-start(f32[1280]{0:T(1024)S(1)} %pad_maximum_fusion.1), channel_id=1, source_target_pairs={{0,1},{1,0},{2,3},{3,2},{4,5},{5,4},{6,7},{7,6},{8,9},{9,8},{10,11... | collective-permute-start | bytes 15368 | tf_op jit(solution)/shard_map/ppermute | solution.py:68
  7.4 0.7 add_divide_fusion.31
  8.1 1.1 %fusion.145 = (f32[1,128]{1,0:T(1,128)S(1)}, f32[128]{0:T(128)S(1)}, f32[128]{0:T(128)S(1)}, f32[128]{0:T(128)S(1)}, f32[128]{0:T(128)S(1)}, /*index=5*/f32[128]...) fusion(f32[16,128]{1,0:T(8,128)} %param.15, ...), kind=kLoop, calls=%fused_computation.326 | loop fusion | flops 8064 | bytes 16896 | tf_op jit(solution)/shard_map/broadcast_in_dim | solution.py:26
  9.3 1.0 %fusion.144 = (f32[1,128]{1,0:T(1,128)S(1)}, f32[1,128]{1,0:T(1,128)S(1)}, f32[1,128]{1,0:T(1,128)S(1)}, f32[1,128]{1,0:T(1,128)S(1)}, f32[1,128]{1,0:T(1,128)S(...) fusion(f32[16,128]{1,0:T(8,128)} %param.15, f32[128]{0:T(128)S(1)} %get-tuple-element.40, f32[128]{0:T(128)} %param.14, ...), kind=kLoop, calls=%fused_computation.271 | loop fusion | flops 3584 | bytes 11264 | tf_op jit(solution)/shard_map/broadcast_in_dim | solution.py:26
  10.2 0.1 concatenate.67
  10.3 0.7 add_divide_fusion
  11.0 1.0 %add_multiply_fusion = (f32[128]{0:T(128)S(1)}, f32[128]{0:T(128)S(1)}, f32[128]{0:T(128)S(1)}, f32[128]{0:T(128)S(1)}, f32[128]{0:T(128)S(1)}, /*index=5*/f32[1...) fusion(f32[16,128]{1,0:T(8,128)S(1)} %scatter.4, f32[]{:T(128)S(6)} %select_n.42, f32[16,128]{1,0:T(8,128)} %param.15, ...), kind=kLoop, calls=%fused_computation.306 | loop fusion | flops 9728 | bytes 16900 | tf_op jit(solution)/shard_map/mul | solution.py:192
  12.0 0.1 concatenate.68
  12.1 0.0 collective-permute-done
  12.3 0.7 select_reduce_fusion
  13.0 0.0 copy-start.1
  13.1 3.6 %fusion.4 = bf16[1024,128]{1,0:T(8,128)(2,1)S(1)} fusion(s32[1024]{0:T(1024)S(1)} %fusion.55, f32[1,2048,128]{2,1,0:T(8,128)} %param.9, f32[128]{0:T(128)S(1)} %log_add_fusion), kind=kOutput, calls=%fused_computation.7 | convolution fusion | flops 539885568 | bytes 1315328 | tf_op jit(solution)/shard_map/dot_general | solution.py:261
  16.6 0.1 collective-permute-start.1
  16.7 0.1 fusion.146
  16.9 0.0 copy-start
  16.9 2.1 %fusion = bf16[2048,1024]{1,0:T(8,128)(2,1)S(1)} fusion(s32[1024]{0:T(1024)S(1)} %fusion.55), kind=kLoop, calls=%fused_computation.2 | loop fusion | flops 4194304 | bytes 4198400 | tf_op jit(solution)/shard_map/convert_element_type | solution.py:276
  19.0 0.0 copy-done.1
  19.0 0.1 fusion.57
  19.1 5.4 %collective-permute-done.1 = bf16[2,512,128]{2,1,0:T(8,128)(2,1)S(1)} collective-permute-done((bf16[2,512,128]{2,1,0:T(8,128)(2,1)S(1)}, bf16[2,512,128]{2,1,0:T(8,128)(2,1)S(1)}, u32[]{:S(2)}, u32[]{:S(2)}) %collective-permute-start.1) | collective-permute-done | bytes 262176 | tf_op jit(solution)/shard_map/ppermute | solution.py:68
  24.5 0.2 fusion.43
  24.8 0.4 fusion.45
  25.2 0.4 fusion.12
  25.5 0.1 fusion.59
  25.6 0.2 fusion.39
  25.8 0.4 fusion.41
  26.2 0.3 fusion.16
  26.6 0.1 fusion.61
  26.6 0.2 fusion.35
  26.9 0.4 fusion.37
  27.3 0.3 fusion.20
  27.6 0.1 fusion.63
  27.7 0.2 fusion.27
  27.9 0.4 fusion.30
  28.3 0.5 fusion.33
  28.8 0.0 copy-done
  28.8 2.2 %fusion.3 = f32[2048,128]{1,0:T(8,128)} fusion(bf16[2048,1024]{1,0:T(8,128)(2,1)S(1)} %fusion, bf16[1024,128]{1,0:T(8,128)(2,1)S(1)} %fusion.33, f32[1,2048,128]{2,1,0:T(8,128)S(1)} %copy-done), kind=kOutput, calls=%fused_computation.6 | convolution fusion | flops 537133056 | bytes 6553600 | tf_op jit(solution)/shard_map/dot_general | solution.py:278
  31.0 3.8 %all-to-all-start = ((f32[8,256,128]{2,1,0:T(8,128)}), f32[8,256,128]{2,1,0:T(8,128)S(1)}, u32[]{:S(2)}, u32[]{:S(2)}) async-start(f32[8,256,128]{2,1,0:T(8,128)} %bitcast.133), calls=%async_computation | async-start | bytes 2097152 | tf_op jit(solution)/shard_map/all_to_all | solution.py:302
  34.9 0.2 multiply_add_fusion.10
  35.0 0.1 multiply_add_fusion.2
  35.2 0.1 stack.8
  35.3 14.0 %all-to-all-done = f32[8,256,128]{2,1,0:T(8,128)S(1)} async-done(((f32[8,256,128]{2,1,0:T(8,128)}), f32[8,256,128]{2,1,0:T(8,128)S(1)}, u32[]{:S(2)}, u32[]{:S(2)}) %all-to-all-start) | async-done | bytes 1048608 | tf_op jit(solution)/shard_map/all_to_all | solution.py:302
  49.3 0.2 add_select_fusion
  49.5 2.6 %collective-permute-start.2 = (f32[256,128]{1,0:T(8,128)S(1)}, f32[256,128]{1,0:T(8,128)S(1)}, u32[]{:S(2)}, u32[]{:S(2)}) collective-permute-start(f32[256,128]{1,0:T(8,128)S(1)} %add_select_fusion), channel_id=1, source_target_pairs={{0,16},{16,0},{1,17},{17,1},{2,18},{18,2},{3,19},{19,3},{4,20},{20... | collective-permute-start | bytes 393224 | tf_op jit(solution)/shard_map/ppermute | solution.py:68
  52.2 0.1 slice_bitcast_fusion.7
  52.2 0.1 multiply_bitcast_fusion
  52.4 0.6 multiply_add_fusion.1
  53.0 5.2 %collective-permute-done.2 = f32[256,128]{1,0:T(8,128)S(1)} collective-permute-done((f32[256,128]{1,0:T(8,128)S(1)}, f32[256,128]{1,0:T(8,128)S(1)}, u32[]{:S(2)}, u32[]{:S(2)}) %collective-permute-start.2) | collective-permute-done | bytes 131104 | tf_op jit(solution)/shard_map/ppermute | solution.py:68
  58.2 1.1 %multiply_add_fusion = f32[8,256,128]{2,1,0:T(8,128)} fusion(f32[8,256,128]{2,1,0:T(8,128)S(1)} %multiply_add_fusion.1, f32[256,128]{1,0:T(8,128)S(1)} %collective-permute-done.2, f32[8,128]{1,0:T(8,128)S(1)} %get-tuple-element.67), kind=kLoop, calls=%fused_computation.14 | loop fusion | flops 524288 | bytes 2232320 | tf_op jit(solution)/shard_map/add | solution.py:197
  59.3 3.6 %all-to-all-start.1 = ((f32[8,256,128]{2,1,0:T(8,128)}), f32[8,256,128]{2,1,0:T(8,128)S(1)}, u32[]{:S(2)}, u32[]{:S(2)}) async-start(f32[8,256,128]{2,1,0:T(8,128)} %multiply_add_fusion), calls=%async_computation.1 | async-start | bytes 2097152 | tf_op jit(solution)/shard_map/all_to_all | solution.py:335
  62.9 0.5 fusion.47
  63.4 0.6 slice_bitcast_fusion.17
  64.0 13.3 %all-to-all-done.1 = f32[8,256,128]{2,1,0:T(8,128)S(1)} async-done(((f32[8,256,128]{2,1,0:T(8,128)}), f32[8,256,128]{2,1,0:T(8,128)S(1)}, u32[]{:S(2)}, u32[]{:S(2)}) %all-to-all-start.1) | async-done | bytes 1048608 | tf_op jit(solution)/shard_map/all_to_all | solution.py:335
  77.3 1.0 %copy.13 = f32[1,2048,128]{2,1,0:T(8,128)} copy(f32[1,2048,128]{2,1,0:T(8,128)S(1)} %bitcast.449) | data formatting | bytes 2097152
  (33 shorter events, 0.4 us)
Async XLA Ops:
  4.4 7.7 %collective-permute-start = (f32[1280]{0:T(1024)S(1)}, f32[1280]{0:T(1024)S(1)}, u32[]{:S(2)}, u32[]{:S(2)}) collective-permute-start(f32[1280]{0:T(1024)S(1)} %pad_maximum_fusion.1), channel_id=1, source_target_pairs={{0,1},{1,0},{2,3},{3,2},{4,5},{5,4},{6,7},{7,6},{8,9},{9,8},{10,11... | collective-permute-start | bytes 15368 | tf_op jit(solution)/shard_map/ppermute | solution.py:68
  13.0 5.9 %copy-start.1 = (f32[128]{0:T(128)S(1)}, f32[128]{0:T(128)}, u32[]{:S(2)}) copy-start(f32[128]{0:T(128)} %param.13) | copy-start | bytes 1540
  16.6 7.8 %collective-permute-start.1 = (bf16[2,512,128]{2,1,0:T(8,128)(2,1)S(1)}, bf16[2,512,128]{2,1,0:T(8,128)(2,1)S(1)}, u32[]{:S(2)}, u32[]{:S(2)}) collective-permute-start(bf16[2,512,128]{2,1,0:T(8,128)(2,1)S(1)} %bitcast.451), channel_id=1, source_target_pairs={{0,1},{1,0},{2,3},{3,2},{4,5},{5,4},{6,7},{7,6},{8,9},{9,8},{10,11... | collective-permute-start | bytes 786440 | tf_op jit(solution)/shard_map/ppermute | solution.py:68
  16.9 11.9 %copy-start = (f32[1,2048,128]{2,1,0:T(8,128)S(1)}, f32[1,2048,128]{2,1,0:T(8,128)}, u32[]{:S(2)}) copy-start(f32[1,2048,128]{2,1,0:T(8,128)} %param.9) | copy-start | bytes 3145732
  31.0 18.3 %all-to-all-start = ((f32[8,256,128]{2,1,0:T(8,128)}), f32[8,256,128]{2,1,0:T(8,128)S(1)}, u32[]{:S(2)}, u32[]{:S(2)}) async-start(f32[8,256,128]{2,1,0:T(8,128)} %bitcast.133), calls=%async_computation | async-start | bytes 2097152 | tf_op jit(solution)/shard_map/all_to_all | solution.py:302
  49.5 8.7 %collective-permute-start.2 = (f32[256,128]{1,0:T(8,128)S(1)}, f32[256,128]{1,0:T(8,128)S(1)}, u32[]{:S(2)}, u32[]{:S(2)}) collective-permute-start(f32[256,128]{1,0:T(8,128)S(1)} %add_select_fusion), channel_id=1, source_target_pairs={{0,16},{16,0},{1,17},{17,1},{2,18},{18,2},{3,19},{19,3},{4,20},{20... | collective-permute-start | bytes 393224 | tf_op jit(solution)/shard_map/ppermute | solution.py:68
  59.3 18.0 %all-to-all-start.1 = ((f32[8,256,128]{2,1,0:T(8,128)}), f32[8,256,128]{2,1,0:T(8,128)S(1)}, u32[]{:S(2)}, u32[]{:S(2)}) async-start(f32[8,256,128]{2,1,0:T(8,128)} %multiply_add_fusion), calls=%async_computation.1 | async-start | bytes 2097152 | tf_op jit(solution)/shard_map/all_to_all | solution.py:335

commit v17 on v16

--- a/solution.py
+++ b/solution.py
@@ -278,6 +278,7 @@
     counts = jnp.dot(held_marks, flat_weighted, preferred_element_type=jnp.float32)
     pseudo = local_beta + jnp.log1p(counts)
 
+    obs_precision, drift_var, pseudo = lax.optimization_barrier((obs_precision, drift_var, pseudo))
     gains, filt_vars, shrinks, infos = variance_tables(obs_precision, drift_var)
     years_total = obs_precision.shape[0]
     pulls = filt_vars / (filt_vars + drift_var)

time: 78.8 us -> 75.6 us (0.959)
  other arithmetic: 18.5 us -> 14.3 us
  starting transfers between devices: 13.1 us -> 15.4 us
  waiting for transfers between devices: 37.9 us -> 36.8 us
    ppermute x3, starting transfers between devices: 5.79 us -> 7.8 us  [shift_axis(): lax.ppermute(value, axis, [(i, (i + s) % count) for i in range(count)])]
    broadcast_in_dim x2, other arithmetic: 2.11 us -> 0.17 us  [variance_tables(): lax.scan(forward_step, start_var, obs_precision, unroll=True)]
    ppermute x3, waiting for transfers between devices: 10.6 us -> 9.58 us  [shift_axis(): lax.ppermute(value, axis, [(i, (i + s) % count) for i in range(count)])]
    mul x2, other arithmetic: 1.15 us -> 0.17 us  [two_group_kalman(): smoothed = maps[:, years + 1, None, :] * (weight * reach * last)]
  transfers between devices with their start and end apart: 5 -> 5, of which waited for: 4 -> 5; matrix products, arithmetic and copies ran while one was open for 12% -> 6% of each run, Pallas kernels for 0% -> 0%
where the time goes in v17:
time: 75.6 us; the launch traced here: 75.2 us
  waiting for transfers between devices  36.8 us (49%)
  starting transfers between devices  15.4 us (20%)
  other arithmetic  14.3 us (19%)
  matrix products  5.82 us (8%)
  local copies, waits for them, and re-layouts  1.95 us (3%)
  between operations  1 us (1%)
    all_to_all x1, waiting for transfers between devices, smooth_part(): lax.all_to_all(by_dest, 'tl', split_axis=0, concat_axis=0, tiled=True)  13.9 us
    all_to_all x1, waiting for transfers between devices, smooth_part(): lax.all_to_all(smoothed, 'tl', split_axis=0, concat_axis=0, tiled=True)  13.3 us
    ppermute x3, waiting for transfers between devices, shift_axis(): lax.ppermute(value, axis, [(i, (i + s) % count) for i in range(count)])  9.58 us
    ppermute x3, starting transfers between devices, shift_axis(): lax.ppermute(value, axis, [(i, (i + s) % count) for i in range(count)])  7.8 us
    all_to_all x1, starting transfers between devices, smooth_part(): lax.all_to_all(by_dest, 'tl', split_axis=0, concat_axis=0, tiled=True)  4.01 us
    dot_general x1, matrix products, body(): lax.dot_general(marks, table, (((0,), (0,)), ((), ())), preferred_element...  3.58 us
    all_to_all x1, starting transfers between devices, smooth_part(): lax.all_to_all(smoothed, 'tl', split_axis=0, concat_axis=0, tiled=True)  3.56 us
    dot_general x1, matrix products, body(): jnp.dot(held_marks, flat_weighted, preferred_element_type=jnp.float32)  2.24 us
  transfers between devices with their start and end apart: 5, of which 5 were waited for; matrix products, arithmetic and copies ran while one was open for 6% of the time, Pallas kernels for 0%

profile of v17, /device:TPU:0, one launch (start us, length us, event | category | flops | bytes accessed | tf_op | source)
XLA Modules:
  0.0 75.2 jit_solution(17778913499464768395)
XLA Ops:
  0.6 1.5 %reduce_max.54 = f32[128]{0:T(128)S(1)} reduce(f32[1,2048,128]{2,1,0:T(8,128)} %param.9, f32[]{:T(128)} %constant.104.clone.1), dimensions={0,1}, to_apply=%region_0.0 | reduce | flops 262016 | bytes 1049092 | tf_op jit(solution)/shard_map/reduce_max | solution.py:223
  2.1 1.5 %fusion.6 = f32[128]{0:T(128)S(1)} fusion(f32[1,2048,128]{2,1,0:T(8,128)} %param.9, f32[128]{0:T(128)S(1)} %reduce_max.54), kind=kLoop, calls=%fused_computation.11 | loop fusion | flops 524160 | bytes 1049600 | tf_op jit(solution)/shard_map/reduce_sum | solution.py:224
  3.7 0.7 convert_bitcast_fusion
  4.4 3.1 %collective-permute-start = (f32[1280]{0:T(1024)S(1)}, f32[1280]{0:T(1024)S(1)}, u32[]{:S(2)}, u32[]{:S(2)}) collective-permute-start(f32[1280]{0:T(1024)S(1)} %pad_maximum_fusion.1), channel_id=1, source_target_pairs={{0,1},{1,0},{2,3},{3,2},{4,5},{5,4},{6,7},{7,6},{8,9},{9,8},{10,11... | collective-permute-start | bytes 15368 | tf_op jit(solution)/shard_map/ppermute | solution.py:68
  7.5 1.6 %collective-permute-done = f32[1280]{0:T(1024)S(1)} collective-permute-done((f32[1280]{0:T(1024)S(1)}, f32[1280]{0:T(1024)S(1)}, u32[]{:S(2)}, u32[]{:S(2)}) %collective-permute-start) | collective-permute-done | bytes 5152 | tf_op jit(solution)/shard_map/ppermute | solution.py:68
  9.2 0.7 select_reduce_fusion
  10.0 0.0 copy-start.3
  10.0 3.6 %fusion.4 = bf16[1024,128]{1,0:T(8,128)(2,1)S(1)} fusion(s32[1024]{0:T(1024)S(1)} %fusion.55, f32[1,2048,128]{2,1,0:T(8,128)} %param.9, f32[128]{0:T(128)S(1)} %log_add_fusion), kind=kOutput, calls=%fused_computation.7 | convolution fusion | flops 539885568 | bytes 1315328 | tf_op jit(solution)/shard_map/dot_general | solution.py:261
  13.6 2.1 %collective-permute-start.1 = (bf16[2,512,128]{2,1,0:T(8,128)(2,1)S(1)}, bf16[2,512,128]{2,1,0:T(8,128)(2,1)S(1)}, u32[]{:S(2)}, u32[]{:S(2)}) collective-permute-start(bf16[2,512,128]{2,1,0:T(8,128)(2,1)S(1)} %bitcast.451), channel_id=1, source_target_pairs={{0,1},{1,0},{2,3},{3,2},{4,5},{5,4},{6,7},{7,6},{8,9},{9,8},{10,11... | collective-permute-start | bytes 786440 | tf_op jit(solution)/shard_map/ppermute | solution.py:68
  15.7 0.1 fusion.146
  15.8 0.0 copy-start
  15.8 2.1 %fusion = bf16[2048,1024]{1,0:T(8,128)(2,1)S(1)} fusion(s32[1024]{0:T(1024)S(1)} %fusion.55), kind=kLoop, calls=%fused_computation.2 | loop fusion | flops 4194304 | bytes 4198400 | tf_op jit(solution)/shard_map/convert_element_type | solution.py:276
  17.9 0.0 copy-done.3
  17.9 0.1 fusion.57
  18.1 2.8 %collective-permute-done.1 = bf16[2,512,128]{2,1,0:T(8,128)(2,1)S(1)} collective-permute-done((bf16[2,512,128]{2,1,0:T(8,128)(2,1)S(1)}, bf16[2,512,128]{2,1,0:T(8,128)(2,1)S(1)}, u32[]{:S(2)}, u32[]{:S(2)}) %collective-permute-start.1) | collective-permute-done | bytes 262176 | tf_op jit(solution)/shard_map/ppermute | solution.py:68
  20.9 0.2 fusion.43
  21.1 0.4 fusion.45
  21.5 0.4 fusion.12
  21.9 0.1 fusion.59
  22.0 0.2 fusion.39
  22.2 0.4 fusion.41
  22.6 0.3 fusion.16
  22.9 0.1 fusion.61
  23.0 0.2 fusion.35
  23.2 0.4 fusion.37
  23.6 0.3 fusion.20
  24.0 0.1 fusion.63
  24.1 0.2 fusion.27
  24.3 0.4 fusion.30
  24.7 0.5 fusion.33
  25.2 0.0 copy-done
  25.2 0.0 copy-start.1
  25.2 0.0 copy-start.2
  25.2 2.2 %fusion.3 = f32[2048,128]{1,0:T(8,128)} fusion(bf16[2048,1024]{1,0:T(8,128)(2,1)S(1)} %fusion, bf16[1024,128]{1,0:T(8,128)(2,1)S(1)} %fusion.33, f32[1,2048,128]{2,1,0:T(8,128)S(1)} %copy-done), kind=kOutput, calls=%fused_computation.6 | convolution fusion | flops 537133056 | bytes 6553600 | tf_op jit(solution)/shard_map/dot_general | solution.py:278
  27.4 0.0 copy-done.1
  27.4 0.0 copy-done.2
  27.4 0.1 fusion.145
  27.6 0.1 concatenate.81
  27.8 4.0 %all-to-all-start = ((f32[8,256,128]{2,1,0:T(8,128)}), f32[8,256,128]{2,1,0:T(8,128)S(1)}, u32[]{:S(2)}, u32[]{:S(2)}) async-start(f32[8,256,128]{2,1,0:T(8,128)} %bitcast.133), calls=%async_computation | async-start | bytes 2097152 | tf_op jit(solution)/shard_map/all_to_all | solution.py:303
  31.8 0.1 concatenate.82
  31.9 0.2 multiply_add_fusion.10
  32.1 0.1 multiply_add_fusion.2
  32.2 0.1 stack.11
  32.3 13.9 %all-to-all-done = f32[8,256,128]{2,1,0:T(8,128)S(1)} async-done(((f32[8,256,128]{2,1,0:T(8,128)}), f32[8,256,128]{2,1,0:T(8,128)S(1)}, u32[]{:S(2)}, u32[]{:S(2)}) %all-to-all-start) | async-done | bytes 1048608 | tf_op jit(solution)/shard_map/all_to_all | solution.py:303
  46.3 0.2 add_select_fusion
  46.5 2.7 %collective-permute-start.2 = (f32[256,128]{1,0:T(8,128)S(1)}, f32[256,128]{1,0:T(8,128)S(1)}, u32[]{:S(2)}, u32[]{:S(2)}) collective-permute-start(f32[256,128]{1,0:T(8,128)S(1)} %add_select_fusion), channel_id=1, source_target_pairs={{0,16},{16,0},{1,17},{17,1},{2,18},{18,2},{3,19},{19,3},{4,20},{20... | collective-permute-start | bytes 393224 | tf_op jit(solution)/shard_map/ppermute | solution.py:68
  49.1 0.1 slice_bitcast_fusion.7
  49.2 0.1 multiply_bitcast_fusion
  49.3 0.6 multiply_add_fusion.1
  50.0 5.2 %collective-permute-done.2 = f32[256,128]{1,0:T(8,128)S(1)} collective-permute-done((f32[256,128]{1,0:T(8,128)S(1)}, f32[256,128]{1,0:T(8,128)S(1)}, u32[]{:S(2)}, u32[]{:S(2)}) %collective-permute-start.2) | collective-permute-done | bytes 131104 | tf_op jit(solution)/shard_map/ppermute | solution.py:68
  55.2 1.1 %multiply_add_fusion = f32[8,256,128]{2,1,0:T(8,128)} fusion(f32[8,256,128]{2,1,0:T(8,128)S(1)} %multiply_add_fusion.1, f32[256,128]{1,0:T(8,128)S(1)} %collective-permute-done.2, f32[8,128]{1,0:T(8,128)S(1)} %get-tuple-element.73), kind=kLoop, calls=%fused_computation.14 | loop fusion | flops 524288 | bytes 2232320 | tf_op jit(solution)/shard_map/add | solution.py:197
  56.3 3.6 %all-to-all-start.1 = ((f32[8,256,128]{2,1,0:T(8,128)}), f32[8,256,128]{2,1,0:T(8,128)S(1)}, u32[]{:S(2)}, u32[]{:S(2)}) async-start(f32[8,256,128]{2,1,0:T(8,128)} %multiply_add_fusion), calls=%async_computation.1 | async-start | bytes 2097152 | tf_op jit(solution)/shard_map/all_to_all | solution.py:336
  59.8 0.5 fusion.47
  60.3 0.6 slice_bitcast_fusion.17
  60.9 13.3 %all-to-all-done.1 = f32[8,256,128]{2,1,0:T(8,128)S(1)} async-done(((f32[8,256,128]{2,1,0:T(8,128)}), f32[8,256,128]{2,1,0:T(8,128)S(1)}, u32[]{:S(2)}, u32[]{:S(2)}) %all-to-all-start.1) | async-done | bytes 1048608 | tf_op jit(solution)/shard_map/all_to_all | solution.py:336
  74.2 1.0 %copy.13 = f32[1,2048,128]{2,1,0:T(8,128)} copy(f32[1,2048,128]{2,1,0:T(8,128)S(1)} %bitcast.449) | data formatting | bytes 2097152
  (38 shorter events, 0.5 us)
Async XLA Ops:
  4.4 4.7 %collective-permute-start = (f32[1280]{0:T(1024)S(1)}, f32[1280]{0:T(1024)S(1)}, u32[]{:S(2)}, u32[]{:S(2)}) collective-permute-start(f32[1280]{0:T(1024)S(1)} %pad_maximum_fusion.1), channel_id=1, source_target_pairs={{0,1},{1,0},{2,3},{3,2},{4,5},{5,4},{6,7},{7,6},{8,9},{9,8},{10,11... | collective-permute-start | bytes 15368 | tf_op jit(solution)/shard_map/ppermute | solution.py:68
  10.0 7.9 %copy-start.3 = (f32[128]{0:T(128)S(1)}, f32[128]{0:T(128)}, u32[]{:S(2)}) copy-start(f32[128]{0:T(128)} %param.13) | copy-start | bytes 1540
  13.6 7.2 %collective-permute-start.1 = (bf16[2,512,128]{2,1,0:T(8,128)(2,1)S(1)}, bf16[2,512,128]{2,1,0:T(8,128)(2,1)S(1)}, u32[]{:S(2)}, u32[]{:S(2)}) collective-permute-start(bf16[2,512,128]{2,1,0:T(8,128)(2,1)S(1)} %bitcast.451), channel_id=1, source_target_pairs={{0,1},{1,0},{2,3},{3,2},{4,5},{5,4},{6,7},{7,6},{8,9},{9,8},{10,11... | collective-permute-start | bytes 786440 | tf_op jit(solution)/shard_map/ppermute | solution.py:68
  15.8 9.3 %copy-start = (f32[1,2048,128]{2,1,0:T(8,128)S(1)}, f32[1,2048,128]{2,1,0:T(8,128)}, u32[]{:S(2)}) copy-start(f32[1,2048,128]{2,1,0:T(8,128)} %param.9) | copy-start | bytes 3145732
  25.2 2.3 %copy-start.1 = (f32[16,128]{1,0:T(8,128)S(1)}, f32[16,128]{1,0:T(8,128)}, u32[]{:S(2)}) copy-start(f32[16,128]{1,0:T(8,128)} %param.15) | copy-start | bytes 24580
  25.2 2.3 %copy-start.2 = (f32[128]{0:T(128)S(1)}, f32[128]{0:T(128)}, u32[]{:S(2)}) copy-start(f32[128]{0:T(128)} %param.14) | copy-start | bytes 1540
  27.8 18.5 %all-to-all-start = ((f32[8,256,128]{2,1,0:T(8,128)}), f32[8,256,128]{2,1,0:T(8,128)S(1)}, u32[]{:S(2)}, u32[]{:S(2)}) async-start(f32[8,256,128]{2,1,0:T(8,128)} %bitcast.133), calls=%async_computation | async-start | bytes 2097152 | tf_op jit(solution)/shard_map/all_to_all | solution.py:303
  46.5 8.7 %collective-permute-start.2 = (f32[256,128]{1,0:T(8,128)S(1)}, f32[256,128]{1,0:T(8,128)S(1)}, u32[]{:S(2)}, u32[]{:S(2)}) collective-permute-start(f32[256,128]{1,0:T(8,128)S(1)} %add_select_fusion), channel_id=1, source_target_pairs={{0,16},{16,0},{1,17},{17,1},{2,18},{18,2},{3,19},{19,3},{4,20},{20... | collective-permute-start | bytes 393224 | tf_op jit(solution)/shard_map/ppermute | solution.py:68
  56.3 18.0 %all-to-all-start.1 = ((f32[8,256,128]{2,1,0:T(8,128)}), f32[8,256,128]{2,1,0:T(8,128)S(1)}, u32[]{:S(2)}, u32[]{:S(2)}) async-start(f32[8,256,128]{2,1,0:T(8,128)} %multiply_add_fusion), calls=%async_computation.1 | async-start | bytes 2097152 | tf_op jit(solution)/shard_map/all_to_all | solution.py:336

commit v18 on v15

--- a/solution.py
+++ b/solution.py
@@ -257,8 +257,9 @@
     row_words = lax.iota(jnp.int32, own_words)
     marks = (row_words[:, None] == local_columns[None, :]).astype(jnp.bfloat16)
     table = to_bf16(local_beta - normalizer)
+    slot_marks = (local_columns[:, None] == row_words[None, :]).astype(jnp.bfloat16)
     partial = (
-        lax.dot_general(marks, table, (((0,), (0,)), ((), ())), preferred_element_type=jnp.float32)
+        jnp.dot(slot_marks, table, preferred_element_type=jnp.float32)
         .astype(jnp.bfloat16)
         .reshape(doc_devices, local_docs * slot_width, topics)
     )

time: 72.1 us -> 71.3 us (0.989)
  matrix products: 5.11 us -> 4.28 us
    dot_general x1, matrix products: 2.35 us -> 1.52 us  [body(): jnp.dot(slot_marks, table, preferred_element_type=jnp.float32)]
where the time goes in v18:
time: 71.3 us; the launch traced here: 71 us
  waiting for transfers between devices  38.7 us (54%)
  starting transfers between devices  15.4 us (22%)
  other arithmetic  9.69 us (14%)
  matrix products  4.28 us (6%)
  local copies, waits for them, and re-layouts  1.94 us (3%)
  between operations  1.02 us (1%)
    all_to_all x1, waiting for transfers between devices, smooth_part(): lax.all_to_all(by_dest, 'tl', split_axis=0, concat_axis=0, tiled=True)  14 us
    all_to_all x1, waiting for transfers between devices, smooth_part(): lax.all_to_all(smoothed, 'tl', split_axis=0, concat_axis=0, tiled=True)  13.3 us
    ppermute x3, waiting for transfers between devices, shift_axis(): lax.ppermute(value, axis, [(i, (i + s) % count) for i in range(count)])  11.4 us
    ppermute x3, starting transfers between devices, shift_axis(): lax.ppermute(value, axis, [(i, (i + s) % count) for i in range(count)])  7.8 us
    all_to_all x1, starting transfers between devices, smooth_part(): lax.all_to_all(by_dest, 'tl', split_axis=0, concat_axis=0, tiled=True)  4 us
    all_to_all x1, starting transfers between devices, smooth_part(): lax.all_to_all(smoothed, 'tl', split_axis=0, concat_axis=0, tiled=True)  3.56 us
    dot_general x1, matrix products, body(): counts = jnp.dot(marks, flat_weighted, preferred_element_type=jnp.float32)  2.75 us
    reduce_max x1, other arithmetic, body(): local_peak = jnp.max(local_beta, axis=0)  1.59 us
  transfers between devices with their start and end apart: 5, of which 5 were waited for; matrix products, arithmetic and copies ran while one was open for 4% of the time, Pallas kernels for 0%

profile of v18, /device:TPU:0, one launch (start us, length us, event | category | flops | bytes accessed | tf_op | source)
XLA Modules:
  0.0 71.0 jit_solution(12367953338096204241)
XLA Ops:
  0.6 0.0 copy-start
  0.6 0.0 copy-start.4
  0.7 0.0 copy-start.5
  0.7 0.0 copy-start.1
  0.7 0.0 copy-start.2
  0.7 0.0 copy-start.6
  0.7 1.6 %reduce_max.54 = f32[128]{0:T(128)S(1)} reduce(f32[1,2048,128]{2,1,0:T(8,128)} %param.9, f32[]{:T(128)} %constant.112.clone.1), dimensions={0,1}, to_apply=%region_0.0 | reduce | flops 262016 | bytes 1049092 | tf_op jit(solution)/shard_map/reduce_max | solution.py:223
  2.3 0.0 copy-done
  2.3 0.3 fusion.8
  2.6 0.0 copy-done.4
  2.6 0.0 copy-done.5
  2.6 3.1 %collective-permute-start = (f32[1280]{0:T(1024)S(1)}, f32[1280]{0:T(1024)S(1)}, u32[]{:S(2)}, u32[]{:S(2)}) collective-permute-start(f32[1280]{0:T(1024)S(1)} %pad_maximum_fusion.1), channel_id=1, source_target_pairs={{0,1},{1,0},{2,3},{3,2},{4,5},{5,4},{6,7},{7,6},{8,9},{9,8},{10,11... | collective-permute-start | bytes 15368 | tf_op jit(solution)/shard_map/ppermute | solution.py:68
  5.7 0.0 copy-done.1
  5.7 0.0 copy-done.2
  5.7 0.1 fusion.147
  5.9 0.1 concatenate.67
  6.1 0.1 concatenate.68
  6.1 1.2 %collective-permute-done = f32[1280]{0:T(1024)S(1)} collective-permute-done((f32[1280]{0:T(1024)S(1)}, f32[1280]{0:T(1024)S(1)}, u32[]{:S(2)}, u32[]{:S(2)}) %collective-permute-start) | collective-permute-done | bytes 5152 | tf_op jit(solution)/shard_map/ppermute | solution.py:68
  7.4 0.1 fusion.148
  7.6 0.0 copy-done.6
  7.6 0.1 select_reduce_fusion
  7.7 0.0 copy-start.3
  7.7 1.5 %fusion.6 = bf16[1024,128]{1,0:T(8,128)(2,1)S(1)} fusion(s32[1024]{0:T(1024)S(1)} %fusion.57, f32[1,2048,128]{2,1,0:T(8,128)S(1)} %copy-done, f32[128]{0:T(128)S(1)} %log_add_fusion), kind=kOutput, calls=%fused_computation.8 | convolution fusion | flops 539885568 | bytes 1315328 | tf_op jit(solution)/shard_map/dot_general | solution.py:262
  9.3 2.1 %collective-permute-start.1 = (bf16[2,512,128]{2,1,0:T(8,128)(2,1)S(1)}, bf16[2,512,128]{2,1,0:T(8,128)(2,1)S(1)}, u32[]{:S(2)}, u32[]{:S(2)}) collective-permute-start(bf16[2,512,128]{2,1,0:T(8,128)(2,1)S(1)} %bitcast.450), channel_id=1, source_target_pairs={{0,1},{1,0},{2,3},{3,2},{4,5},{5,4},{6,7},{7,6},{8,9},{9,8},{10,11... | collective-permute-start | bytes 786440 | tf_op jit(solution)/shard_map/ppermute | solution.py:68
  11.4 0.0 copy-done.3
  11.4 0.1 fusion.59
  11.5 5.0 %collective-permute-done.1 = bf16[2,512,128]{2,1,0:T(8,128)(2,1)S(1)} collective-permute-done((bf16[2,512,128]{2,1,0:T(8,128)(2,1)S(1)}, bf16[2,512,128]{2,1,0:T(8,128)(2,1)S(1)}, u32[]{:S(2)}, u32[]{:S(2)}) %collective-permute-start.1) | collective-permute-done | bytes 262176 | tf_op jit(solution)/shard_map/ppermute | solution.py:68
  16.6 0.2 fusion.45
  16.8 0.4 fusion.47
  17.2 0.4 fusion.14
  17.6 0.1 fusion.61
  17.6 0.2 fusion.41
  17.9 0.4 fusion.43
  18.3 0.3 fusion.18
  18.6 0.1 fusion.63
  18.7 0.2 fusion.37
  18.9 0.4 fusion.39
  19.3 0.3 fusion.22
  19.7 0.1 fusion.65
  19.7 0.2 fusion.29
  19.9 0.4 fusion.32
  20.3 0.5 fusion.35
  20.8 2.8 %fusion.5 = f32[2048,128]{1,0:T(8,128)} fusion(bf16[1024,128]{1,0:T(8,128)(2,1)S(1)} %fusion.35, s32[1024]{0:T(1024)S(1)} %fusion.57, f32[1,2048,128]{2,1,0:T(8,128)S(1)} %copy-done), kind=kOutput, calls=%fused_computation.7 | convolution fusion | flops 539230208 | bytes 2363392 | tf_op jit(solution)/shard_map/dot_general | solution.py:275
  23.6 4.0 %all-to-all-start = ((f32[8,256,128]{2,1,0:T(8,128)}), f32[8,256,128]{2,1,0:T(8,128)S(1)}, u32[]{:S(2)}, u32[]{:S(2)}) async-start(f32[8,256,128]{2,1,0:T(8,128)} %bitcast.133), calls=%async_computation | async-start | bytes 2097152 | tf_op jit(solution)/shard_map/all_to_all | solution.py:299
  27.6 0.2 multiply_add_fusion.10
  27.8 0.1 multiply_add_fusion.2
  27.9 0.1 stack.8
  28.1 14.0 %all-to-all-done = f32[8,256,128]{2,1,0:T(8,128)S(1)} async-done(((f32[8,256,128]{2,1,0:T(8,128)}), f32[8,256,128]{2,1,0:T(8,128)S(1)}, u32[]{:S(2)}, u32[]{:S(2)}) %all-to-all-start) | async-done | bytes 1048608 | tf_op jit(solution)/shard_map/all_to_all | solution.py:299
  42.1 0.2 add_select_fusion
  42.3 2.7 %collective-permute-start.2 = (f32[256,128]{1,0:T(8,128)S(1)}, f32[256,128]{1,0:T(8,128)S(1)}, u32[]{:S(2)}, u32[]{:S(2)}) collective-permute-start(f32[256,128]{1,0:T(8,128)S(1)} %add_select_fusion), channel_id=1, source_target_pairs={{0,16},{16,0},{1,17},{17,1},{2,18},{18,2},{3,19},{19,3},{4,20},{20... | collective-permute-start | bytes 393224 | tf_op jit(solution)/shard_map/ppermute | solution.py:68
  44.9 0.1 slice_bitcast_fusion.7
  45.0 0.1 multiply_bitcast_fusion
  45.1 0.6 multiply_add_fusion.1
  45.8 5.2 %collective-permute-done.2 = f32[256,128]{1,0:T(8,128)S(1)} collective-permute-done((f32[256,128]{1,0:T(8,128)S(1)}, f32[256,128]{1,0:T(8,128)S(1)}, u32[]{:S(2)}, u32[]{:S(2)}) %collective-permute-start.2) | collective-permute-done | bytes 131104 | tf_op jit(solution)/shard_map/ppermute | solution.py:68
  51.0 1.1 %multiply_add_fusion = f32[8,256,128]{2,1,0:T(8,128)} fusion(f32[8,256,128]{2,1,0:T(8,128)S(1)} %multiply_add_fusion.1, f32[256,128]{1,0:T(8,128)S(1)} %collective-permute-done.2, f32[8,128]{1,0:T(8,128)S(1)} %get-tuple-element.67), kind=kLoop, calls=%fused_computation.15 | loop fusion | flops 524288 | bytes 2232320 | tf_op jit(solution)/shard_map/add | solution.py:197
  52.1 3.6 %all-to-all-start.1 = ((f32[8,256,128]{2,1,0:T(8,128)}), f32[8,256,128]{2,1,0:T(8,128)S(1)}, u32[]{:S(2)}, u32[]{:S(2)}) async-start(f32[8,256,128]{2,1,0:T(8,128)} %multiply_add_fusion), calls=%async_computation.1 | async-start | bytes 2097152 | tf_op jit(solution)/shard_map/all_to_all | solution.py:332
  55.6 0.5 fusion.49
  56.1 0.6 slice_bitcast_fusion.17
  56.7 13.3 %all-to-all-done.1 = f32[8,256,128]{2,1,0:T(8,128)S(1)} async-done(((f32[8,256,128]{2,1,0:T(8,128)}), f32[8,256,128]{2,1,0:T(8,128)S(1)}, u32[]{:S(2)}, u32[]{:S(2)}) %all-to-all-start.1) | async-done | bytes 1048608 | tf_op jit(solution)/shard_map/all_to_all | solution.py:332
  70.0 1.0 %copy.13 = f32[1,2048,128]{2,1,0:T(8,128)} copy(f32[1,2048,128]{2,1,0:T(8,128)S(1)} %bitcast.448) | data formatting | bytes 2097152
  (38 shorter events, 0.5 us)
Async XLA Ops:
  0.6 1.6 %copy-start = (f32[1,2048,128]{2,1,0:T(8,128)S(1)}, f32[1,2048,128]{2,1,0:T(8,128)}, u32[]{:S(2)}) copy-start(f32[1,2048,128]{2,1,0:T(8,128)} %param.9) | copy-start | bytes 3145732
  0.6 1.9 %copy-start.4 = (s32[1,4,128]{2,1,0:T(4,128)S(1)}, s32[1,4,128]{2,1,0:T(4,128)}, u32[]{:S(2)}) copy-start(s32[1,4,128]{2,1,0:T(4,128)} %param.11) | copy-start | bytes 6148
  0.7 1.9 %copy-start.5 = (s32[1,4,128]{2,1,0:T(4,128)S(1)}, s32[1,4,128]{2,1,0:T(4,128)}, u32[]{:S(2)}) copy-start(s32[1,4,128]{2,1,0:T(4,128)} %param.10) | copy-start | bytes 6148
  0.7 5.0 %copy-start.1 = (f32[16,128]{1,0:T(8,128)S(1)}, f32[16,128]{1,0:T(8,128)}, u32[]{:S(2)}) copy-start(f32[16,128]{1,0:T(8,128)} %param.15) | copy-start | bytes 24580
  0.7 5.0 %copy-start.2 = (f32[128]{0:T(128)S(1)}, f32[128]{0:T(128)}, u32[]{:S(2)}) copy-start(f32[128]{0:T(128)} %param.14) | copy-start | bytes 1540
  0.7 6.9 %copy-start.6 = (s32[32]{0:T(128)S(1)}, s32[32]{0:T(128)}, u32[]{:S(2)}) copy-start(s32[32]{0:T(128)} %param.12) | copy-start | bytes 388
  2.6 4.7 %collective-permute-start = (f32[1280]{0:T(1024)S(1)}, f32[1280]{0:T(1024)S(1)}, u32[]{:S(2)}, u32[]{:S(2)}) collective-permute-start(f32[1280]{0:T(1024)S(1)} %pad_maximum_fusion.1), channel_id=1, source_target_pairs={{0,1},{1,0},{2,3},{3,2},{4,5},{5,4},{6,7},{7,6},{8,9},{9,8},{10,11... | collective-permute-start | bytes 15368 | tf_op jit(solution)/shard_map/ppermute | solution.py:68
  7.7 3.6 %copy-start.3 = (f32[128]{0:T(128)S(1)}, f32[128]{0:T(128)}, u32[]{:S(2)}) copy-start(f32[128]{0:T(128)} %param.13) | copy-start | bytes 1540
  9.3 7.2 %collective-permute-start.1 = (bf16[2,512,128]{2,1,0:T(8,128)(2,1)S(1)}, bf16[2,512,128]{2,1,0:T(8,128)(2,1)S(1)}, u32[]{:S(2)}, u32[]{:S(2)}) collective-permute-start(bf16[2,512,128]{2,1,0:T(8,128)(2,1)S(1)} %bitcast.450), channel_id=1, source_target_pairs={{0,1},{1,0},{2,3},{3,2},{4,5},{5,4},{6,7},{7,6},{8,9},{9,8},{10,11... | collective-permute-start | bytes 786440 | tf_op jit(solution)/shard_map/ppermute | solution.py:68
  23.6 18.5 %all-to-all-start = ((f32[8,256,128]{2,1,0:T(8,128)}), f32[8,256,128]{2,1,0:T(8,128)S(1)}, u32[]{:S(2)}, u32[]{:S(2)}) async-start(f32[8,256,128]{2,1,0:T(8,128)} %bitcast.133), calls=%async_computation | async-start | bytes 2097152 | tf_op jit(solution)/shard_map/all_to_all | solution.py:299
  42.3 8.7 %collective-permute-start.2 = (f32[256,128]{1,0:T(8,128)S(1)}, f32[256,128]{1,0:T(8,128)S(1)}, u32[]{:S(2)}, u32[]{:S(2)}) collective-permute-start(f32[256,128]{1,0:T(8,128)S(1)} %add_select_fusion), channel_id=1, source_target_pairs={{0,16},{16,0},{1,17},{17,1},{2,18},{18,2},{3,19},{19,3},{4,20},{20... | collective-permute-start | bytes 393224 | tf_op jit(solution)/shard_map/ppermute | solution.py:68
  52.1 18.0 %all-to-all-start.1 = ((f32[8,256,128]{2,1,0:T(8,128)}), f32[8,256,128]{2,1,0:T(8,128)S(1)}, u32[]{:S(2)}, u32[]{:S(2)}) async-start(f32[8,256,128]{2,1,0:T(8,128)} %multiply_add_fusion), calls=%async_computation.1 | async-start | bytes 2097152 | tf_op jit(solution)/shard_map/all_to_all | solution.py:332

commit v19 on v18

--- a/solution.py
+++ b/solution.py
@@ -272,7 +272,7 @@
     doc_topics = doc_topics_all[:local_docs]
 
     flat_weighted = weighted.reshape(-1, topics)
-    counts = jnp.dot(marks, flat_weighted, preferred_element_type=jnp.float32)
+    counts = jnp.dot(flat_weighted.T, slot_marks, preferred_element_type=jnp.float32).T
     pseudo = local_beta + jnp.log1p(counts)
 
     gains, filt_vars, shrinks, infos = variance_tables(obs_precision, drift_var)

time: 71.3 us -> 72.1 us (1.011)
  matrix products: 4.28 us -> 5.09 us
    dot_general x1, matrix products: 2.75 us -> 3.56 us  [body(): jnp.dot(flat_weighted.T, slot_marks, preferred_element_type=jnp.float32)]
where the time goes in v19:
time: 72.1 us; the launch traced here: 71.8 us
  waiting for transfers between devices  38.7 us (54%)
  starting transfers between devices  15.4 us (21%)
  other arithmetic  9.69 us (13%)
  matrix products  5.09 us (7%)
  local copies, waits for them, and re-layouts  1.94 us (3%)
  between operations  1.02 us (1%)
    all_to_all x1, waiting for transfers between devices, smooth_part(): lax.all_to_all(by_dest, 'tl', split_axis=0, concat_axis=0, tiled=True)  14 us
    all_to_all x1, waiting for transfers between devices, smooth_part(): lax.all_to_all(smoothed, 'tl', split_axis=0, concat_axis=0, tiled=True)  13.3 us
    ppermute x3, waiting for transfers between devices, shift_axis(): lax.ppermute(value, axis, [(i, (i + s) % count) for i in range(count)])  11.4 us
    ppermute x3, starting transfers between devices, shift_axis(): lax.ppermute(value, axis, [(i, (i + s) % count) for i in range(count)])  7.8 us
    all_to_all x1, starting transfers between devices, smooth_part(): lax.all_to_all(by_dest, 'tl', split_axis=0, concat_axis=0, tiled=True)  4 us
    dot_general x1, matrix products, body(): jnp.dot(flat_weighted.T, slot_marks, preferred_element_type=jnp.float32)  3.56 us
    all_to_all x1, starting transfers between devices, smooth_part(): lax.all_to_all(smoothed, 'tl', split_axis=0, concat_axis=0, tiled=True)  3.56 us
    reduce_max x1, other arithmetic, body(): local_peak = jnp.max(local_beta, axis=0)  1.59 us
  transfers between devices with their start and end apart: 5, of which 5 were waited for; matrix products, arithmetic and copies ran while one was open for 4% of the time, Pallas kernels for 0%

profile of v19, /device:TPU:0, one launch (start us, length us, event | category | flops | bytes accessed | tf_op | source)
XLA Modules:
  0.0 71.8 jit_solution(11538677703462360798)
XLA Ops:
  0.6 0.0 copy-start
  0.6 0.0 copy-start.4
  0.7 0.0 copy-start.5
  0.7 0.0 copy-start.1
  0.7 0.0 copy-start.2
  0.7 0.0 copy-start.6
  0.7 1.6 %reduce_max.54 = f32[128]{0:T(128)S(1)} reduce(f32[1,2048,128]{2,1,0:T(8,128)} %param.9, f32[]{:T(128)} %constant.110.clone.1), dimensions={0,1}, to_apply=%region_0.0 | reduce | flops 262016 | bytes 1049092 | tf_op jit(solution)/shard_map/reduce_max | solution.py:223
  2.3 0.0 copy-done
  2.3 0.3 fusion.8
  2.6 0.0 copy-done.4
  2.6 0.0 copy-done.5
  2.6 3.1 %collective-permute-start = (f32[1280]{0:T(1024)S(1)}, f32[1280]{0:T(1024)S(1)}, u32[]{:S(2)}, u32[]{:S(2)}) collective-permute-start(f32[1280]{0:T(1024)S(1)} %pad_maximum_fusion.1), channel_id=1, source_target_pairs={{0,1},{1,0},{2,3},{3,2},{4,5},{5,4},{6,7},{7,6},{8,9},{9,8},{10,11... | collective-permute-start | bytes 15368 | tf_op jit(solution)/shard_map/ppermute | solution.py:68
  5.7 0.0 copy-done.1
  5.7 0.0 copy-done.2
  5.7 0.1 fusion.147
  5.9 0.1 concatenate.67
  6.1 0.1 concatenate.68
  6.1 1.2 %collective-permute-done = f32[1280]{0:T(1024)S(1)} collective-permute-done((f32[1280]{0:T(1024)S(1)}, f32[1280]{0:T(1024)S(1)}, u32[]{:S(2)}, u32[]{:S(2)}) %collective-permute-start) | collective-permute-done | bytes 5152 | tf_op jit(solution)/shard_map/ppermute | solution.py:68
  7.4 0.1 fusion.148
  7.6 0.0 copy-done.6
  7.6 0.1 select_reduce_fusion
  7.7 0.0 copy-start.3
  7.7 1.5 %fusion.6 = bf16[1024,128]{1,0:T(8,128)(2,1)S(1)} fusion(s32[1024]{0:T(1024)S(1)} %fusion.57, f32[1,2048,128]{2,1,0:T(8,128)S(1)} %copy-done, f32[128]{0:T(128)S(1)} %log_add_fusion), kind=kOutput, calls=%fused_computation.7 | convolution fusion | flops 539885568 | bytes 1315328 | tf_op jit(solution)/shard_map/dot_general | solution.py:262
  9.3 2.1 %collective-permute-start.1 = (bf16[2,512,128]{2,1,0:T(8,128)(2,1)S(1)}, bf16[2,512,128]{2,1,0:T(8,128)(2,1)S(1)}, u32[]{:S(2)}, u32[]{:S(2)}) collective-permute-start(bf16[2,512,128]{2,1,0:T(8,128)(2,1)S(1)} %bitcast.450), channel_id=1, source_target_pairs={{0,1},{1,0},{2,3},{3,2},{4,5},{5,4},{6,7},{7,6},{8,9},{9,8},{10,11... | collective-permute-start | bytes 786440 | tf_op jit(solution)/shard_map/ppermute | solution.py:68
  11.4 0.0 copy-done.3
  11.4 0.1 fusion.59
  11.5 5.0 %collective-permute-done.1 = bf16[2,512,128]{2,1,0:T(8,128)(2,1)S(1)} collective-permute-done((bf16[2,512,128]{2,1,0:T(8,128)(2,1)S(1)}, bf16[2,512,128]{2,1,0:T(8,128)(2,1)S(1)}, u32[]{:S(2)}, u32[]{:S(2)}) %collective-permute-start.1) | collective-permute-done | bytes 262176 | tf_op jit(solution)/shard_map/ppermute | solution.py:68
  16.6 0.2 fusion.45
  16.8 0.4 fusion.47
  17.2 0.4 fusion.14
  17.6 0.1 fusion.61
  17.6 0.2 fusion.41
  17.9 0.4 fusion.43
  18.3 0.3 fusion.18
  18.6 0.1 fusion.63
  18.7 0.2 fusion.37
  18.9 0.4 fusion.39
  19.3 0.3 fusion.22
  19.7 0.1 fusion.65
  19.7 0.2 fusion.29
  19.9 0.4 fusion.32
  20.3 0.5 fusion.35
  20.8 3.6 %fusion.5 = f32[2048,128]{1,0:T(8,128)} fusion(bf16[1024,128]{1,0:T(8,128)(2,1)S(1)} %fusion.35, s32[1024]{0:T(1024)S(1)} %fusion.57, f32[1,2048,128]{2,1,0:T(8,128)S(1)} %copy-done), kind=kOutput, calls=%fused_computation.6 | convolution fusion | flops 539230208 | bytes 2363392 | tf_op jit(solution)/shard_map/dot_general | solution.py:275
  24.4 4.0 %all-to-all-start = ((f32[8,256,128]{2,1,0:T(8,128)}), f32[8,256,128]{2,1,0:T(8,128)S(1)}, u32[]{:S(2)}, u32[]{:S(2)}) async-start(f32[8,256,128]{2,1,0:T(8,128)} %bitcast.133), calls=%async_computation | async-start | bytes 2097152 | tf_op jit(solution)/shard_map/all_to_all | solution.py:299
  28.4 0.2 multiply_add_fusion.10
  28.6 0.1 multiply_add_fusion.2
  28.8 0.1 stack.8
  28.9 14.0 %all-to-all-done = f32[8,256,128]{2,1,0:T(8,128)S(1)} async-done(((f32[8,256,128]{2,1,0:T(8,128)}), f32[8,256,128]{2,1,0:T(8,128)S(1)}, u32[]{:S(2)}, u32[]{:S(2)}) %all-to-all-start) | async-done | bytes 1048608 | tf_op jit(solution)/shard_map/all_to_all | solution.py:299
  42.9 0.2 add_select_fusion
  43.1 2.7 %collective-permute-start.2 = (f32[256,128]{1,0:T(8,128)S(1)}, f32[256,128]{1,0:T(8,128)S(1)}, u32[]{:S(2)}, u32[]{:S(2)}) collective-permute-start(f32[256,128]{1,0:T(8,128)S(1)} %add_select_fusion), channel_id=1, source_target_pairs={{0,16},{16,0},{1,17},{17,1},{2,18},{18,2},{3,19},{19,3},{4,20},{20... | collective-permute-start | bytes 393224 | tf_op jit(solution)/shard_map/ppermute | solution.py:68
  45.7 0.1 slice_bitcast_fusion.7
  45.8 0.1 multiply_bitcast_fusion
  45.9 0.6 multiply_add_fusion.1
  46.6 5.2 %collective-permute-done.2 = f32[256,128]{1,0:T(8,128)S(1)} collective-permute-done((f32[256,128]{1,0:T(8,128)S(1)}, f32[256,128]{1,0:T(8,128)S(1)}, u32[]{:S(2)}, u32[]{:S(2)}) %collective-permute-start.2) | collective-permute-done | bytes 131104 | tf_op jit(solution)/shard_map/ppermute | solution.py:68
  51.8 1.1 %multiply_add_fusion = f32[8,256,128]{2,1,0:T(8,128)} fusion(f32[8,256,128]{2,1,0:T(8,128)S(1)} %multiply_add_fusion.1, f32[256,128]{1,0:T(8,128)S(1)} %collective-permute-done.2, f32[8,128]{1,0:T(8,128)S(1)} %get-tuple-element.67), kind=kLoop, calls=%fused_computation.14 | loop fusion | flops 524288 | bytes 2232320 | tf_op jit(solution)/shard_map/add | solution.py:197
  52.9 3.6 %all-to-all-start.1 = ((f32[8,256,128]{2,1,0:T(8,128)}), f32[8,256,128]{2,1,0:T(8,128)S(1)}, u32[]{:S(2)}, u32[]{:S(2)}) async-start(f32[8,256,128]{2,1,0:T(8,128)} %multiply_add_fusion), calls=%async_computation.1 | async-start | bytes 2097152 | tf_op jit(solution)/shard_map/all_to_all | solution.py:332
  56.5 0.5 fusion.49
  57.0 0.6 slice_bitcast_fusion.17
  57.5 13.3 %all-to-all-done.1 = f32[8,256,128]{2,1,0:T(8,128)S(1)} async-done(((f32[8,256,128]{2,1,0:T(8,128)}), f32[8,256,128]{2,1,0:T(8,128)S(1)}, u32[]{:S(2)}, u32[]{:S(2)}) %all-to-all-start.1) | async-done | bytes 1048608 | tf_op jit(solution)/shard_map/all_to_all | solution.py:332
  70.8 1.0 %copy.13 = f32[1,2048,128]{2,1,0:T(8,128)} copy(f32[1,2048,128]{2,1,0:T(8,128)S(1)} %bitcast.448) | data formatting | bytes 2097152
  (38 shorter events, 0.5 us)
Async XLA Ops:
  0.6 1.6 %copy-start = (f32[1,2048,128]{2,1,0:T(8,128)S(1)}, f32[1,2048,128]{2,1,0:T(8,128)}, u32[]{:S(2)}) copy-start(f32[1,2048,128]{2,1,0:T(8,128)} %param.9) | copy-start | bytes 3145732
  0.6 1.9 %copy-start.4 = (s32[1,4,128]{2,1,0:T(4,128)S(1)}, s32[1,4,128]{2,1,0:T(4,128)}, u32[]{:S(2)}) copy-start(s32[1,4,128]{2,1,0:T(4,128)} %param.11) | copy-start | bytes 6148
  0.7 1.9 %copy-start.5 = (s32[1,4,128]{2,1,0:T(4,128)S(1)}, s32[1,4,128]{2,1,0:T(4,128)}, u32[]{:S(2)}) copy-start(s32[1,4,128]{2,1,0:T(4,128)} %param.10) | copy-start | bytes 6148
  0.7 5.0 %copy-start.1 = (f32[16,128]{1,0:T(8,128)S(1)}, f32[16,128]{1,0:T(8,128)}, u32[]{:S(2)}) copy-start(f32[16,128]{1,0:T(8,128)} %param.15) | copy-start | bytes 24580
  0.7 5.0 %copy-start.2 = (f32[128]{0:T(128)S(1)}, f32[128]{0:T(128)}, u32[]{:S(2)}) copy-start(f32[128]{0:T(128)} %param.14) | copy-start | bytes 1540
  0.7 6.9 %copy-start.6 = (s32[32]{0:T(128)S(1)}, s32[32]{0:T(128)}, u32[]{:S(2)}) copy-start(s32[32]{0:T(128)} %param.12) | copy-start | bytes 388
  2.6 4.7 %collective-permute-start = (f32[1280]{0:T(1024)S(1)}, f32[1280]{0:T(1024)S(1)}, u32[]{:S(2)}, u32[]{:S(2)}) collective-permute-start(f32[1280]{0:T(1024)S(1)} %pad_maximum_fusion.1), channel_id=1, source_target_pairs={{0,1},{1,0},{2,3},{3,2},{4,5},{5,4},{6,7},{7,6},{8,9},{9,8},{10,11... | collective-permute-start | bytes 15368 | tf_op jit(solution)/shard_map/ppermute | solution.py:68
  7.7 3.6 %copy-start.3 = (f32[128]{0:T(128)S(1)}, f32[128]{0:T(128)}, u32[]{:S(2)}) copy-start(f32[128]{0:T(128)} %param.13) | copy-start | bytes 1540
  9.3 7.2 %collective-permute-start.1 = (bf16[2,512,128]{2,1,0:T(8,128)(2,1)S(1)}, bf16[2,512,128]{2,1,0:T(8,128)(2,1)S(1)}, u32[]{:S(2)}, u32[]{:S(2)}) collective-permute-start(bf16[2,512,128]{2,1,0:T(8,128)(2,1)S(1)} %bitcast.450), channel_id=1, source_target_pairs={{0,1},{1,0},{2,3},{3,2},{4,5},{5,4},{6,7},{7,6},{8,9},{9,8},{10,11... | collective-permute-start | bytes 786440 | tf_op jit(solution)/shard_map/ppermute | solution.py:68
  24.4 18.5 %all-to-all-start = ((f32[8,256,128]{2,1,0:T(8,128)}), f32[8,256,128]{2,1,0:T(8,128)S(1)}, u32[]{:S(2)}, u32[]{:S(2)}) async-start(f32[8,256,128]{2,1,0:T(8,128)} %bitcast.133), calls=%async_computation | async-start | bytes 2097152 | tf_op jit(solution)/shard_map/all_to_all | solution.py:299
  43.1 8.7 %collective-permute-start.2 = (f32[256,128]{1,0:T(8,128)S(1)}, f32[256,128]{1,0:T(8,128)S(1)}, u32[]{:S(2)}, u32[]{:S(2)}) collective-permute-start(f32[256,128]{1,0:T(8,128)S(1)} %add_select_fusion), channel_id=1, source_target_pairs={{0,16},{16,0},{1,17},{17,1},{2,18},{18,2},{3,19},{19,3},{4,20},{20... | collective-permute-start | bytes 393224 | tf_op jit(solution)/shard_map/ppermute | solution.py:68
  52.9 18.0 %all-to-all-start.1 = ((f32[8,256,128]{2,1,0:T(8,128)}), f32[8,256,128]{2,1,0:T(8,128)S(1)}, u32[]{:S(2)}, u32[]{:S(2)}) async-start(f32[8,256,128]{2,1,0:T(8,128)} %multiply_add_fusion), calls=%async_computation.1 | async-start | bytes 2097152 | tf_op jit(solution)/shard_map/all_to_all | solution.py:332
